TPU v7x, 32 devices: a whole 2x2x4 slice. The times are simulated.
32 devices in a mesh: groups: 2 (over y), ctx: 4 (over z), head: 4 (over x, core).
Axes of the slice: x: 2, y: 2, z: 4, core: 2. Of those that a mesh axis runs over, the one named last changes fastest.
Arguments:
- query_nope: bfloat16 [16, 128, 128], P('groups', 'head'), parts along dimension 0, may hold values from -9 to 9
- query_rope: bfloat16 [16, 128, 64], P('groups', 'head'), parts along dimension 0, may hold values from -500 to 500
- kv_cache: bfloat16 [8, 2048, 576], P('groups', 'ctx'), parts along dimension 0, may hold values from -8 to 8
- lengths: int32 [8], P('groups'), parts along dimension 0, may hold values from 2 to 2048, as said below
- w_absorb: bfloat16 [128, 128, 512], P('head', None, 'ctx'), may hold values from -0.5 to 0.5
- w_value: bfloat16 [128, 512, 128], P('head', 'ctx'), may hold values from -0.25 to 0.25
- w_output: bfloat16 [16384, 7168], P('head', 'ctx'), may hold values from -0.046875 to 0.046875
Outputs:
- mixed: float32 [16, 7168], P('groups', ('ctx', 'head')), parts along dimension 0
There are 2 independent parts, one for each index of `groups`. A program takes and returns all parts, laid end to end along the dimension named above; an argument that names none is the same for every part. Nothing has to cross between parts.
Inputs may be any that keep to these rules, and one draw needn't show every extreme that they name: lengths[s] counts the cached positions of sequence s including its 2 new tokens; the largest equals 2048 in every draw.
All inputs are finite; a program needn't handle non-finite values.
Results may differ from a plain program's by a relative error of at most 0.0055.
Values may be sent and summed in bfloat16 or wider, within the bound.
No kernel may reach another device: no remote copies, remote signals or barrier semaphores. Data moves between devices by JAX's collectives and lax.ppermute only.
A program may use at most 64 MiB of HBM per device.

v0:
```python
import jax
import jax.numpy as jnp
from jax import lax
from jax.sharding import PartitionSpec as P

ROTARY_CHANNELS = 64
PLAIN_CHANNELS = 128
DRAFT = 2


def per_device(query_nope, query_rope, kv_cache, lengths, w_absorb, w_value, w_output):
    seq_count, ctx_rows, channels = kv_cache.shape
    head_count = query_nope.shape[1]
    latent_width = channels - query_rope.shape[2]
    slice_width = w_value.shape[1]
    q_part = jnp.einsum(
        "rhn,hnl->rhl", query_nope, w_absorb, preferred_element_type=jnp.float32
    ).astype(jnp.bfloat16)
    q_latent = lax.all_gather(q_part, "ctx", axis=2, tiled=True)
    query_rows = jnp.concatenate([q_latent, query_rope], axis=2).reshape(
        seq_count, DRAFT * head_count, channels
    )
    logit_scores = jnp.einsum(
        "sqc,skc->sqk", query_rows, kv_cache, preferred_element_type=jnp.float32
    ) * (PLAIN_CHANNELS + ROTARY_CHANNELS) ** (-0.5)
    position = lax.axis_index("ctx") * ctx_rows + jnp.arange(ctx_rows, dtype=jnp.int32)
    draft_index = jnp.arange(DRAFT * head_count, dtype=jnp.int32) // head_count
    row_limit = lengths[:, None] - DRAFT + draft_index[None, :]
    is_valid = position[None, None, :] <= row_limit[:, :, None]
    masked = jnp.where(is_valid, logit_scores, jnp.float32(-1e30))
    row_top = jnp.max(masked, axis=2)
    expo_f = jnp.where(is_valid, jnp.exp(masked - row_top[:, :, None]), jnp.float32(0.0))
    row_total = jnp.sum(expo_f, axis=2)
    weighted = jnp.einsum(
        "sqk,skl->sql",
        expo_f.astype(jnp.bfloat16),
        kv_cache[:, :, :latent_width],
        preferred_element_type=jnp.float32,
    )
    merged_top = lax.pmax(row_top, "ctx")
    factor = jnp.exp(row_top - merged_top)
    merged_total = lax.psum(row_total * factor, "ctx")
    own_sum = lax.psum_scatter(
        weighted * factor[:, :, None], "ctx", scatter_dimension=2, tiled=True
    )
    latent_out = (own_sum / merged_total[:, :, None]).astype(jnp.bfloat16)
    latent_out = latent_out.reshape(seq_count * DRAFT, head_count, slice_width)
    value_part = jnp.einsum("rhl,hlv->rhv", latent_out, w_value, preferred_element_type=jnp.float32)
    values = lax.psum(value_part, "ctx").astype(jnp.bfloat16)
    partial_value = jnp.dot(
        values.reshape(values.shape[0], -1), w_output, preferred_element_type=jnp.float32
    )
    return lax.psum_scatter(partial_value, "head", scatter_dimension=1, tiled=True)


def solution(mesh):
    return jax.shard_map(
        per_device,
        mesh=mesh,
        in_specs=(
            P("groups", "head", None),
            P("groups", "head", None),
            P("groups", "ctx", None),
            P("groups"),
            P("head", None, "ctx"),
            P("head", "ctx", None),
            P("head", "ctx"),
        ),
        out_specs=P("groups", ("ctx", "head")),
        check_vma=False,
    )
```

profile of v0, /device:TPU:1, one launch (start us, length us, event | category | flops | bytes accessed | tf_op | source)
XLA Modules:
  0.0 122.5 jit_solution(3374330247635600044)
XLA Ops:
  6.5 0.0 copy-start
  6.5 0.0 copy-start.1
  6.5 0.0 reduce-scatter.5.cloned.1.call-start
  6.6 0.8 broadcast_add_fusion.1
  7.4 1.1 copy.18
  8.4 0.0 copy-done
  8.5 1.2 fusion.6
  9.7 12.4 %all_gather.3 = bf16[8,32,512]{2,0,1:T(8,128)(2,1)S(1)} all-gather(bf16[8,32,128]{2,0,1:T(8,128)(2,1)S(1)} %fusion.6), channel_id=1, replica_groups=mesh['groups'=2,'ctx'=4,'head'=4] {'ctx'}, dimensions={2}, use_global_device_ids=true | all-gather | bytes 327680 | tf_op jit(solution)/shard_map/all_gather | solution.py:19
  22.2 0.1 broadcast_add_fusion
  22.2 0.0 copy-done.1
  22.2 1.4 %fusion.20 = (f32[4,64]{1,0:T(4,128)S(1)}, f32[4,64,512]{2,1,0:T(8,128)}) fusion(bf16[4,64,576]{2,1,0:T(8,128)(2,1)S(1)} %bitcast.17, bf16[4,512,576]{1,2,0:T(8,128)(2,1)S(1)} %copy-done.1, s32[4,64]{1,0:T(4,128)S(1)} %broadcast_add_fusion, s32[512]{0:T(512)S(1)} %iota_add_fusion), kind=kOutput, calls=%fused_computation.32 | convolution fusion | flops 151518976 | bytes 3182592 | tf_op jit(solution)/shard_map/sqc,skc->sqk/dot_general | solution.py:23
  23.6 7.9 %pmax.7 = f32[4,64]{1,0:T(4,128)S(1)} all-reduce(f32[4,64]{1,0:T(4,128)S(1)} %get-tuple-element.7), channel_id=1, replica_groups=mesh['groups'=2,'ctx'=4,'head'=4] {'ctx'}, use_global_device_ids=true, to_apply=%region_1.2 | all-reduce | flops 256 | bytes 2048 | tf_op jit(solution)/shard_map/pmax | solution.py:40
  31.5 1.3 %fusion.7 = f32[4,64]{1,0:T(4,128)S(1)} fusion(f32[4,64,512]{2,1,0:T(8,128)} %get-tuple-element.8, f32[4,64]{1,0:T(4,128)S(1)} %get-tuple-element.7, s32[4,64]{1,0:T(4,128)S(1)} %broadcast_add_fusion, s32[512]{0:T(512)S(1)} %iota_add_fusion), kind=kLoop, calls=%fused_computation.10 | loop fusion | flops 524032 | bytes 529408 | tf_op jit(solution)/shard_map/reduce_sum | solution.py:33
  32.8 2.6 %fusion.2 = f32[4,64,512]{2,1,0:T(8,128)} fusion(bf16[4,512,576]{1,2,0:T(8,128)(2,1)S(1)} %copy-done.1, f32[4,64,512]{2,1,0:T(8,128)} %get-tuple-element.8, f32[4,64]{1,0:T(4,128)S(1)} %get-tuple-element.6, f32[4,64]{1,0:T(4,128)S(1)} %get-tuple-element.7, s32[4,64]{1,0:T(4,128)S(1)} %broadcast_add_fusion, s32[512]{0:T(512)S(1)} %iota_add_fusion), kind=kOutput, calls=%fused_computation.3 | convolution fusion | flops 134873088 | bytes 3153920 | tf_op jit(solution)/shard_map/sqk,skl->sql/dot_general | solution.py:34
  35.4 0.0 reduce-scatter.5.cloned.1.call-update
  35.4 0.0 reduce-scatter.7.cloned.1.call-start
  35.5 6.8 %psum.14 = f32[4,64]{1,0:T(4,128)S(1)} all-reduce(f32[4,64]{1,0:T(4,128)S(1)} %get-tuple-element.5), channel_id=1, replica_groups=mesh['groups'=2,'ctx'=4,'head'=4] {'ctx'}, use_global_device_ids=true, to_apply=%region_4.5 | all-reduce | flops 256 | bytes 2048 | tf_op jit(solution)/shard_map/psum | solution.py:42
  42.3 16.1 %reduce-scatter.5.cloned.1.call-done = f32[4,64,128]{2,1,0:T(8,128)} async-done(((f32[4,64,512]{2,1,0:T(8,128)}), f32[4,64,128]{2,1,0:T(8,128)}) %reduce-scatter.5.cloned.1.call-update) | async-done | bytes 131088 | tf_op jit(solution)/shard_map/reduce_scatter | solution.py:43
  58.3 1.0 divide_convert_fusion
  59.4 1.6 %convolution_bitcast_fusion.1 = f32[8,32,128]{2,0,1:T(8,128)S(1)} fusion(bf16[32,128,128]{2,1,0:T(8,128)(2,1)} %param.12, bf16[8,32,128]{2,1,0:T(8,128)(2,1)S(1)} %bitcast.18), kind=kOutput, calls=%fused_computation.6 | convolution fusion | flops 8388608 | bytes 1245184 | tf_op jit(solution)/shard_map/rhl,hlv->rhv/dot_general | solution.py:48
  61.0 15.8 %all-reduce.1 = bf16[8,32,128]{2,0,1:T(8,128)(2,1)S(1)} all-reduce(f32[8,32,128]{2,0,1:T(8,128)S(1)} %convolution_bitcast_fusion.1), channel_id=1, replica_groups=mesh['groups'=2,'ctx'=4,'head'=4] {'ctx'}, use_global_device_ids=true, to_apply=%region_5.6 | all-reduce | flops 32768 | bytes 196608 | tf_op jit(solution)/shard_map/psum | solution.py:49
  76.8 9.9 %convolution_bitcast_fusion = f32[1792,8]{1,0:T(8,128)} fusion(bf16[4096,1792]{1,0:T(8,128)(2,1)} %param.13, bf16[8,32,128]{2,0,1:T(8,128)(2,1)S(1)} %all-reduce.1), kind=kOutput, calls=%fused_computation | convolution fusion | flops 117440512 | bytes 14802944
  86.7 0.0 reduce-scatter.7.cloned.1.call-update
  86.8 27.3 %reduce-scatter.7.cloned.1.call-done = f32[448,8]{1,0:T(8,128)} async-done(((f32[1792,8]{1,0:T(8,128)}), f32[448,8]{1,0:T(8,128)}) %reduce-scatter.7.cloned.1.call-update) | async-done | bytes 14352
  114.0 1.6 %copy.23 = f32[8,448]{1,0:T(8,128)} copy(f32[8,448]{0,1:T(8,128)} %bitcast.19) | data formatting | bytes 28672
  (5 shorter events, 0.1 us)
Async XLA Ops:
  6.5 1.9 %copy-start = (bf16[32,128,128]{2,1,0:T(8,128)(2,1)S(1)}, bf16[32,128,128]{2,1,0:T(8,128)(2,1)}, u32[]{:S(2)}) copy-start(bf16[32,128,128]{2,1,0:T(8,128)(2,1)} %param.11) | copy-start | bytes 3145732
  6.5 15.7 %copy-start.1 = (bf16[4,512,576]{1,2,0:T(8,128)(2,1)S(1)}, bf16[4,512,576]{1,2,0:T(8,128)(2,1)}, u32[]{:S(2)}) copy-start(bf16[4,512,576]{1,2,0:T(8,128)(2,1)} %param.9) | copy-start | bytes 7077892
  6.5 51.8 %reduce-scatter.5.cloned.1.call-start = ((), (), s32[]{:S(2)}) async-start(), calls=%async_computation.2 | async-start | bytes 655360 | tf_op jit(solution)/shard_map/reduce_scatter | solution.py:43
  35.4 78.6 %reduce-scatter.7.cloned.1.call-start = ((), (), s32[]{:S(2)}) async-start(), calls=%async_computation.3 | async-start | bytes 1146880
Sparse Core Ops, SparseCore 0:
  35.6 22.7 reduce-scatter.4
  86.9 27.1 reduce-scatter.6
where the time goes:
time: 124 us; the launch traced here: 123 us
  waiting for transfers between devices  43.4 us (35%)
  blocking collectives  42.9 us (35%)
  matrix products  16.7 us (13%)
  between operations  13.5 us (11%)
  other arithmetic  3.22 us (3%)
  local copies, waits for them, and re-layouts  2.77 us (2%)
    unnamed x3, waiting for transfers between devices  27.3 us
    reduce_scatter x1, waiting for transfers between devices, per_device(): lax.psum_scatter(weighted * factor[:, :, None], 'ctx', scatter_dimension=...  16.1 us
    psum x1, blocking collectives, per_device(): values = lax.psum(value_part, 'ctx').astype(jnp.bfloat16)  15.8 us
    all_gather x1, blocking collectives, per_device(): q_latent = lax.all_gather(q_part, 'ctx', axis=2, tiled=True)  12.4 us
    unnamed x1, matrix products  9.94 us
    pmax x1, blocking collectives, per_device(): merged_top = lax.pmax(row_top, 'ctx')  7.91 us
    psum x1, blocking collectives, per_device(): merged_total = lax.psum(row_total * factor, 'ctx')  6.77 us
    unnamed x6, local copies, waits for them, and re-layouts  2.73 us
  transfers between devices with their start and end apart: 2, of which 2 were waited for; matrix products, arithmetic and copies ran while one was open for 0% of the time, Pallas kernels for 0%

commit v1 on v0

v1 whole, which is shorter than its diff:
```python
import functools

import jax
import jax.numpy as jnp
from jax import lax
from jax.sharding import PartitionSpec as P

ROTARY_CHANNELS = 64
PLAIN_CHANNELS = 128
DRAFT = 2
PERMUTE_MAX = 8


def shift_pairs(n, k):
    return [(i, (i + k) % n) for i in range(n)]


def gather_pieces(x, axis, n):
    if n > PERMUTE_MAX:
        return lax.all_gather(x, axis, axis=0, tiled=False)
    me = lax.axis_index(axis)
    received = [x] + [lax.ppermute(x, axis, shift_pairs(n, k)) for k in range(1, n)]
    back = jnp.stack([received[(-j) % n] for j in range(n)])
    return jnp.roll(back, me, axis=0)


def exchange_sum(chunks, axis, n, combine):
    if n > PERMUTE_MAX:
        got = lax.all_to_all(chunks, axis, 0, 0, tiled=False)
        return combine([got[j] for j in range(n)])
    me = lax.axis_index(axis)
    mine = [lax.dynamic_index_in_dim(chunks, me, axis=0, keepdims=False)]
    for k in range(1, n):
        out = lax.dynamic_index_in_dim(chunks, (me + k) % n, axis=0, keepdims=False)
        mine.append(lax.ppermute(out, axis, shift_pairs(n, k)))
    return combine(mine)


def per_device(n_ctx, n_head, query_nope, query_rope, kv_cache, lengths, w_absorb, w_value, w_output):
    seq_count, ctx_rows, channels = kv_cache.shape
    row_count, head_count = query_nope.shape[:2]
    latent_width = channels - query_rope.shape[2]
    slice_width = w_value.shape[1]

    q_part = jnp.einsum(
        "rhn,hnl->rhl", query_nope, w_absorb, preferred_element_type=jnp.float32
    ).astype(jnp.bfloat16)
    q_pieces = gather_pieces(q_part, "ctx", n_ctx)
    q_latent = jnp.concatenate([q_pieces[j] for j in range(n_ctx)], axis=2)
    query_rows = jnp.concatenate([q_latent, query_rope], axis=2).reshape(
        seq_count, DRAFT * head_count, channels
    )
    logit_scores = jnp.einsum(
        "sqc,skc->sqk", query_rows, kv_cache, preferred_element_type=jnp.float32
    ) * (PLAIN_CHANNELS + ROTARY_CHANNELS) ** (-0.5)
    position = lax.axis_index("ctx") * ctx_rows + jnp.arange(ctx_rows, dtype=jnp.int32)
    draft_index = jnp.arange(DRAFT * head_count, dtype=jnp.int32) // head_count
    row_limit = lengths[:, None] - DRAFT + draft_index[None, :]
    is_valid = position[None, None, :] <= row_limit[:, :, None]
    masked = jnp.where(is_valid, logit_scores, jnp.float32(-1e30))
    block_top = jnp.max(masked, axis=2)
    expo_f = jnp.where(is_valid, jnp.exp(masked - block_top[:, :, None]), jnp.float32(0.0))
    block_total = jnp.sum(expo_f, axis=2)
    weighted = jnp.einsum(
        "sqk,skl->sql",
        expo_f.astype(jnp.bfloat16),
        kv_cache[:, :, :latent_width],
        preferred_element_type=jnp.float32,
    )
    sums = jnp.moveaxis(weighted.reshape(seq_count, DRAFT * head_count, n_ctx, slice_width), 2, 0)
    stats = jnp.broadcast_to(
        jnp.stack([block_top, block_total])[None], (n_ctx, 2) + block_top.shape
    )

    def combine_blocks(parts):
        tops = [st[0] for _, st in parts]
        row_top = functools.reduce(jnp.maximum, tops)
        factors = [jnp.exp(t - row_top) for t in tops]
        total = sum(f * st[1] for f, (_, st) in zip(factors, parts))
        acc = sum(f[:, :, None] * s for f, (s, _) in zip(factors, parts))
        return (acc / total[:, :, None]).astype(jnp.bfloat16)

    if n_ctx > PERMUTE_MAX:
        got_s = lax.all_to_all(sums, "ctx", 0, 0, tiled=False)
        got_t = lax.all_to_all(stats, "ctx", 0, 0, tiled=False)
        latent_out = combine_blocks([(got_s[j], got_t[j]) for j in range(n_ctx)])
    else:
        me = lax.axis_index("ctx")
        parts = [(
            lax.dynamic_index_in_dim(sums, me, axis=0, keepdims=False),
            jnp.stack([block_top, block_total]),
        )]
        for k in range(1, n_ctx):
            out = lax.dynamic_index_in_dim(sums, (me + k) % n_ctx, axis=0, keepdims=False)
            parts.append((
                lax.ppermute(out, "ctx", shift_pairs(n_ctx, k)),
                lax.ppermute(jnp.stack([block_top, block_total]), "ctx", shift_pairs(n_ctx, k)),
            ))
        latent_out = combine_blocks(parts)

    latent_out = latent_out.reshape(row_count, head_count, slice_width)
    value_part = jnp.einsum("rhl,hlv->rhv", latent_out, w_value, preferred_element_type=jnp.float32)
    if n_ctx > PERMUTE_MAX:
        values = lax.psum(value_part, "ctx").astype(jnp.bfloat16)
    else:
        received = [value_part] + [
            lax.ppermute(value_part, "ctx", shift_pairs(n_ctx, k)) for k in range(1, n_ctx)
        ]
        values = sum(received).astype(jnp.bfloat16)
    partial_value = jnp.dot(
        values.reshape(row_count, -1), w_output, preferred_element_type=jnp.float32
    )
    if n_head > PERMUTE_MAX:
        return lax.psum_scatter(partial_value, "head", scatter_dimension=1, tiled=True)
    out_width = partial_value.shape[1] // n_head
    chunks = jnp.moveaxis(partial_value.reshape(row_count, n_head, out_width), 1, 0)
    return exchange_sum(chunks, "head", n_head, sum)


def solution(mesh):
    return jax.shard_map(
        functools.partial(per_device, mesh.shape["ctx"], mesh.shape["head"]),
        mesh=mesh,
        in_specs=(
            P("groups", "head", None),
            P("groups", "head", None),
            P("groups", "ctx", None),
            P("groups"),
            P("head", None, "ctx"),
            P("head", "ctx", None),
            P("head", "ctx"),
        ),
        out_specs=P("groups", ("ctx", "head")),
        check_vma=False,
    )
```

time: 124 us -> 85.6 us (0.69)
  blocking collectives: 42.9 us -> 0 us
  local copies, waits for them, and re-layouts: 2.77 us -> 31.9 us
  waiting for transfers between devices: 43.4 us -> 15.3 us
  starting transfers between devices: 0.04 us -> 20.6 us
  between operations: 13.5 us -> 0.16 us
  matrix products: 16.7 us -> 14.7 us
  other arithmetic: 3.22 us -> 1.86 us
    unnamed x3 -> x0, waiting for transfers between devices: 27.3 us -> none
    unnamed x6 -> x17, local copies, waits for them, and re-layouts: 2.73 us -> 27.6 us
    psum x2 -> x0, blocking collectives: 22.6 us -> none  [the longest x1 15.8 us: per_device(): values = lax.psum(value_part, 'ctx').astype(jnp.bfloat16)]
    ppermute x0 -> x15, starting transfers between devices: none -> 20.6 us  [the longest x3 5.54 us: per_device(): lax.ppermute(value_part, 'ctx', shift_pairs(n_ctx, k))]
    reduce_scatter x1 -> x0, waiting for transfers between devices: 16.1 us -> none  [per_device(): lax.psum_scatter(weighted * factor[:, :, None], 'ctx', scatter_dimension=...]
    ppermute x0 -> x15, waiting for transfers between devices: none -> 15.3 us  [the longest x3 7.33 us: per_device(): lax.ppermute(out, 'ctx', shift_pairs(n_ctx, k))]
    all_gather x1 -> x0, blocking collectives: 12.4 us -> none  [per_device(): q_latent = lax.all_gather(q_part, 'ctx', axis=2, tiled=True)]
    unnamed x1 -> x0, matrix products: 9.94 us -> none
  transfers between devices with their start and end apart: 2 -> 15, of which waited for: 2 -> 7; matrix products, arithmetic and copies ran while one was open for 0% -> 31% of each run, Pallas kernels for 0% -> 0%
where the time goes in v1:
time: 85.6 us; the launch traced here: 84.6 us
  local copies, waits for them, and re-layouts  31.9 us (37%)
  starting transfers between devices  20.6 us (24%)
  waiting for transfers between devices  15.3 us (18%)
  matrix products  14.7 us (17%)
  other arithmetic  1.86 us (2%)
    unnamed x17, local copies, waits for them, and re-layouts  27.6 us
    dot_general x1, matrix products, per_device(): jnp.dot(values.reshape(row_count, -1), w_output, preferred_element_type=j...  9.05 us
    ppermute x3, waiting for transfers between devices, per_device(): lax.ppermute(out, 'ctx', shift_pairs(n_ctx, k))  7.33 us
    ppermute x3, starting transfers between devices, per_device(): lax.ppermute(value_part, 'ctx', shift_pairs(n_ctx, k))  5.54 us
    ppermute x3, waiting for transfers between devices, gather_pieces(): lax.ppermute(x, axis, shift_pairs(n, k))  5.02 us
    ppermute x3, starting transfers between devices, gather_pieces(): lax.ppermute(x, axis, shift_pairs(n, k))  4.6 us
    ppermute x3, starting transfers between devices, per_device(): lax.ppermute(out, 'ctx', shift_pairs(n_ctx, k))  3.89 us
    ppermute x3, starting transfers between devices, exchange_sum(): mine.append(lax.ppermute(out, axis, shift_pairs(n, k)))  3.31 us
  transfers between devices with their start and end apart: 15, of which 7 were waited for; matrix products, arithmetic and copies ran while one was open for 31% of the time, Pallas kernels for 0%

profile of v1, /device:TPU:1, one launch (start us, length us, event | category | flops | bytes accessed | tf_op | source)
XLA Modules:
  0.0 84.6 jit_solution(14355227812105146481)
XLA Ops:
  0.0 1.2 %copy-done = bf16[32,128,128]{2,1,0:T(8,128)(2,1)S(1)} copy-done((bf16[32,128,128]{2,1,0:T(8,128)(2,1)S(1)}, bf16[32,128,128]{2,1,0:T(8,128)(2,1)}, u32[]{:S(2)}) %copy-start) | copy-done | bytes 1048600
  1.2 1.9 %bitcast_dynamic-update-slice_fusion = (bf16[8,8,32,128]{3,1,2,0:T(8,128)(2,1)}, bf16[32,128,8]{1,2,0:T(8,128)(2,1)S(1)}) fusion(bf16[32,128,128]{2,1,0:T(8,128)(2,1)S(1)} %copy-done, bf16[8,32,128]{2,1,0:T(8,128)(2,1)} %param.7), kind=kOutput, calls=%fused_computation.17 | convolution fusion | flops 8421375 | bytes 1245184 | tf_op jit(solution)/shard_map/rhn,hnl->rhl/dot_general | solution.py:45
  3.1 4.2 %collective-permute-start = (bf16[8,32,128]{2,0,1:T(8,128)(2,1)S(1)}, bf16[8,32,128]{2,0,1:T(8,128)(2,1)S(1)}, u32[]{:S(2)}, u32[]{:S(2)}) collective-permute-start(bf16[8,32,128]{2,0,1:T(8,128)(2,1)S(1)} %bitcast.101), channel_id=1, source_target_pairs={{0,12},{4,0},{8,4},{12,8},{1,13},{5,1},{9,5},{13,9},{2,14},{6,2},{... | collective-permute-start | bytes 196616 | tf_op jit(solution)/shard_map/ppermute | solution.py:22
  7.2 0.0 collective-permute-start.1
  7.2 0.5 collective-permute-start.2
  7.7 0.7 broadcast_add_fusion.1
  8.4 0.1 broadcast_add_fusion
  8.4 0.1 collective-permute-done
  8.6 0.6 bitcast_dynamic-update-slice_fusion.7
  9.2 4.9 %collective-permute-done.1 = bf16[8,32,128]{2,0,1:T(8,128)(2,1)} collective-permute-done((bf16[8,32,128]{2,0,1:T(8,128)(2,1)S(1)}, bf16[8,32,128]{2,0,1:T(8,128)(2,1)}, u32[]{:S(2)}, u32[]{:S(2)}) %collective-permute-start.1) | collective-permute-done | bytes 65568 | tf_op jit(solution)/shard_map/ppermute | solution.py:22
  14.1 1.5 %bitcast_dynamic-update-slice_fusion.5 = bf16[8,8,32,128]{3,1,2,0:T(8,128)(2,1)} fusion(bf16[8,8,32,128]{3,1,2,0:T(8,128)(2,1)} %bitcast_dynamic-update-slice_fusion.7, bf16[8,32,128]{2,0,1:T(8,128)(2,1)} %collective-permute-done.1), kind=kLoop, calls=%fused_computation.22 | loop fusion | bytes 131072
  15.6 0.0 collective-permute-done.2
  15.6 1.5 %bitcast_dynamic-update-slice_fusion.3 = bf16[8,8,32,128]{3,1,2,0:T(8,128)(2,1)} fusion(bf16[8,8,32,128]{3,1,2,0:T(8,128)(2,1)} %bitcast_dynamic-update-slice_fusion.5, bf16[8,32,128]{2,0,1:T(8,128)(2,1)} %collective-permute-done.2), kind=kLoop, calls=%fused_computation.20 | loop fusion | bytes 131072
  17.0 0.6 bitcast_dynamic-update-slice_fusion.1
  17.7 0.6 bitcast_dynamic-update-slice_fusion.8
  18.3 1.5 %bitcast_dynamic-update-slice_fusion.6 = bf16[8,8,32,128]{3,1,2,0:T(8,128)(2,1)} fusion(bf16[8,8,32,128]{3,1,2,0:T(8,128)(2,1)} %bitcast_dynamic-update-slice_fusion.8, bf16[8,32,128]{2,0,1:T(8,128)(2,1)} %collective-permute-done.1), kind=kLoop, calls=%fused_computation.23 | loop fusion | bytes 131072
  19.8 1.5 %bitcast_dynamic-update-slice_fusion.4 = bf16[8,8,32,128]{3,1,2,0:T(8,128)(2,1)} fusion(bf16[8,8,32,128]{3,1,2,0:T(8,128)(2,1)} %bitcast_dynamic-update-slice_fusion.6, bf16[8,32,128]{2,0,1:T(8,128)(2,1)} %collective-permute-done.2), kind=kLoop, calls=%fused_computation.21 | loop fusion | bytes 131072 | tf_op jit(solution)/shard_map/jit(_roll_dynamic)/concatenate | solution.py:24
  21.2 1.0 %constant_dynamic-slice_fusion.7 = (bf16[1,8,32,128]{3,1,2,0:T(8,128)(2,1)S(1)}, bf16[1,8,32,128]{3,1,2,0:T(8,128)(2,1)S(1)}, bf16[1,8,32,128]{3,1,2,0:T(8,128)(2,1)S(1)}, bf16[1,8,32,128]{3,1,2,0:T(8,128)(2,1)S(1)}) fusion(bf16[8,8,32,128]{3,1,2,0:T(8,128)(2,1)} %bitcast_dynamic-update-slice_fusion.4, s32[]{:T(128)S(6)} %add.196, s32[]{:T(128)S(6)} %add.195, ...), kind=kLoop, calls=%fused_computation.46 | loop fusion | bytes 524304 | tf_op jit(solution)/shard_map/slice | solution.py:49
  22.4 0.6 fusion.24
  23.0 0.3 fusion.4
  23.3 0.1 collective-permute-start.3
  23.4 0.1 collective-permute-start.4
  23.4 3.2 %collective-permute-start.5 = (f32[2,4,64]{2,1,0:T(4,128)S(1)}, f32[2,4,64]{2,1,0:T(4,128)S(1)}, u32[]{:S(2)}, u32[]{:S(2)}) collective-permute-start(f32[2,4,64]{2,1,0:T(4,128)S(1)} %pad_maximum_fusion), channel_id=1, source_target_pairs={{0,12},{4,0},{8,4},{12,8},{1,13},{5,1},{9,5},{13,9},{2,14},{6,2},{... | collective-permute-start | bytes 6152 | tf_op jit(solution)/shard_map/ppermute | solution.py:97
  26.6 1.6 %fusion = f32[4,64,512]{2,1,0:T(8,128)} fusion(bf16[4,512,576]{1,2,0:T(8,128)(2,1)S(1)} %copy-done.1, f32[4,64,512]{2,1,0:T(8,128)S(1)} %get-tuple-element.24, f32[4,64]{1,0:T(4,128)S(1)} %get-tuple-element.23, s32[4,64]{1,0:T(4,128)S(1)} %broadcast_add_fusion, s32[512]{0:T(512)S(1)} %iota_add_fusion), kind=kOutput, calls=%fused_computation | convolution fusion | flops 134742016 | bytes 3151872 | tf_op jit(solution)/shard_map/sqk,skl->sql/dot_general | solution.py:64
  28.2 1.2 %reshape.189 = f32[4,64,4,128]{3,2,1,0:T(4,128)S(1)} reshape(f32[4,64,512]{2,1,0:T(8,128)} %fusion) | data formatting | bytes 1048576 | tf_op jit(solution)/shard_map/reshape | solution.py:70
  29.4 0.6 constant_dynamic-slice_fusion.6
  30.0 0.3 collective-permute-start.6
  30.3 1.3 %collective-permute-start.7 = (f32[4,64,128]{2,1,0:T(8,128)S(1)}, f32[4,64,128]{2,1,0:T(8,128)S(1)}, u32[]{:S(2)}, u32[]{:S(2)}) collective-permute-start(f32[4,64,128]{2,1,0:T(8,128)S(1)} %bitcast.109), channel_id=1, source_target_pairs={{0,8},{4,12},{8,0},{12,4},{1,9},{5,13},{9,1},{13,5},{2,10},{6,14},... | collective-permute-start | bytes 393224 | tf_op jit(solution)/shard_map/ppermute | solution.py:96
  31.6 2.3 %collective-permute-start.8 = (f32[4,64,128]{2,1,0:T(8,128)S(1)}, f32[4,64,128]{2,1,0:T(8,128)S(1)}, u32[]{:S(2)}, u32[]{:S(2)}) collective-permute-start(f32[4,64,128]{2,1,0:T(8,128)S(1)} %bitcast.108), channel_id=1, source_target_pairs={{0,12},{4,0},{8,4},{12,8},{1,13},{5,1},{9,5},{13,9},{2,14},{6,2},{... | collective-permute-start | bytes 393224 | tf_op jit(solution)/shard_map/ppermute | solution.py:96
  33.9 0.0 collective-permute-done.4
  33.9 2.0 %collective-permute-done.6 = f32[4,64,128]{2,1,0:T(8,128)S(1)} collective-permute-done((f32[4,64,128]{2,1,0:T(8,128)S(1)}, f32[4,64,128]{2,1,0:T(8,128)S(1)}, u32[]{:S(2)}, u32[]{:S(2)}) %collective-permute-start.6) | collective-permute-done | bytes 131104 | tf_op jit(solution)/shard_map/ppermute | solution.py:96
  35.9 5.4 %collective-permute-done.7 = f32[4,64,128]{2,1,0:T(8,128)S(1)} collective-permute-done((f32[4,64,128]{2,1,0:T(8,128)S(1)}, f32[4,64,128]{2,1,0:T(8,128)S(1)}, u32[]{:S(2)}, u32[]{:S(2)}) %collective-permute-start.7) | collective-permute-done | bytes 131104 | tf_op jit(solution)/shard_map/ppermute | solution.py:96
  41.2 0.0 collective-permute-done.8
  41.3 0.2 divide_convert_fusion
  41.5 1.6 %convolution_bitcast_fusion = f32[8,32,128]{2,0,1:T(8,128)S(1)} fusion(bf16[32,128,128]{2,1,0:T(8,128)(2,1)} %param.12, bf16[8,32,128]{2,1,0:T(8,128)(2,1)S(1)} %bitcast.100), kind=kOutput, calls=%fused_computation.4 | convolution fusion | flops 8388608 | bytes 1245184 | tf_op jit(solution)/shard_map/rhl,hlv->rhv/dot_general | solution.py:102
  43.1 2.4 %collective-permute-start.10 = (f32[8,32,128]{2,0,1:T(8,128)S(1)}, f32[8,32,128]{2,0,1:T(8,128)S(1)}, u32[]{:S(2)}, u32[]{:S(2)}) collective-permute-start(f32[8,32,128]{2,0,1:T(8,128)S(1)} %convolution_bitcast_fusion), channel_id=1, source_target_pairs={{0,8},{4,12},{8,0},{12,4},{1,9},{5,13},{9,1},{13,5},{2,10},{6,14},... | collective-permute-start | bytes 393224 | tf_op jit(solution)/shard_map/ppermute | solution.py:107
  45.5 3.1 %collective-permute-start.11 = (f32[8,32,128]{2,0,1:T(8,128)S(1)}, f32[8,32,128]{2,0,1:T(8,128)S(1)}, u32[]{:S(2)}, u32[]{:S(2)}) collective-permute-start(f32[8,32,128]{2,0,1:T(8,128)S(1)} %convolution_bitcast_fusion), channel_id=1, source_target_pairs={{0,12},{4,0},{8,4},{12,8},{1,13},{5,1},{9,5},{13,9},{2,14},{6,2},{... | collective-permute-start | bytes 393224 | tf_op jit(solution)/shard_map/ppermute | solution.py:107
  48.6 20.0 %copy.18 = bf16[4096,1792]{0,1:T(8,128)(2,1)} copy(bf16[4096,1792]{1,0:T(8,128)(2,1)} %param.13) | data formatting | bytes 29360128 | tf_op args[6]
  68.7 0.0 collective-permute-done.10
  68.7 0.0 collective-permute-done.11
  68.7 9.0 %fusion.11 = f32[8,4,448]{2,0,1:T(8,128)S(1)} fusion(bf16[4,448,4096]{2,1,0:T(8,128)(2,1)} %bitcast.98, f32[8,32,128]{2,0,1:T(8,128)S(1)} %collective-permute-done.11, f32[8,32,128]{2,0,1:T(8,128)S(1)} %collective-permute-done.10, f32[8,32,128]{2,0,1:T(8,128)S(1)} %convolution_bitcast_fusion, f32[8,32,128]{2,0,1:T(8,128)S(1)} %collective-permute-done.9), kind=kOutput, calls=%fused_computation.16 | convolution fusion | flops 117571584 | bytes 15261696 | tf_op jit(solution)/shard_map/dot_general | solution.py:110
  77.8 2.8 %collective-permute-start.12 = (f32[8,448]{1,0:T(8,128)S(1)}, f32[8,448]{1,0:T(8,128)S(1)}, u32[]{:S(2)}, u32[]{:S(2)}) collective-permute-start(f32[8,448]{1,0:T(8,128)S(1)} %get-tuple-element.18), channel_id=1, source_target_pairs={{0,1},{1,2},{2,3},{3,0},{4,5},{5,6},{6,7},{7,4},{8,9},{9,10},{10,1... | collective-permute-start | bytes 43016 | tf_op jit(solution)/shard_map/ppermute | solution.py:35
  80.6 0.3 collective-permute-start.13
  80.9 0.2 collective-permute-start.14
  81.1 0.4 collective-permute-done.12
  81.5 1.7 %collective-permute-done.13 = f32[8,448]{1,0:T(8,128)S(1)} collective-permute-done((f32[8,448]{1,0:T(8,128)S(1)}, f32[8,448]{1,0:T(8,128)S(1)}, u32[]{:S(2)}, u32[]{:S(2)}) %collective-permute-start.13) | collective-permute-done | bytes 14368 | tf_op jit(solution)/shard_map/ppermute | solution.py:35
  83.2 0.8 collective-permute-done.14
  84.0 0.6 fusion.16
  (23 shorter events, 0.2 us)
Async XLA Ops:
  0.0 1.2 %copy-start = (bf16[32,128,128]{2,1,0:T(8,128)(2,1)S(1)}, bf16[32,128,128]{2,1,0:T(8,128)(2,1)}, u32[]{:S(2)}) copy-start(bf16[32,128,128]{2,1,0:T(8,128)(2,1)} %param.11) | copy-start | bytes 3145732
  0.0 22.4 %copy-start.1 = (bf16[4,512,576]{1,2,0:T(8,128)(2,1)S(1)}, bf16[4,512,576]{1,2,0:T(8,128)(2,1)}, u32[]{:S(2)}) copy-start(bf16[4,512,576]{1,2,0:T(8,128)(2,1)} %param.9) | copy-start | bytes 7077892
  3.1 5.5 %collective-permute-start = (bf16[8,32,128]{2,0,1:T(8,128)(2,1)S(1)}, bf16[8,32,128]{2,0,1:T(8,128)(2,1)S(1)}, u32[]{:S(2)}, u32[]{:S(2)}) collective-permute-start(bf16[8,32,128]{2,0,1:T(8,128)(2,1)S(1)} %bitcast.101), channel_id=1, source_target_pairs={{0,12},{4,0},{8,4},{12,8},{1,13},{5,1},{9,5},{13,9},{2,14},{6,2},{... | collective-permute-start | bytes 196616 | tf_op jit(solution)/shard_map/ppermute | solution.py:22
  7.2 6.8 %collective-permute-start.1 = (bf16[8,32,128]{2,0,1:T(8,128)(2,1)S(1)}, bf16[8,32,128]{2,0,1:T(8,128)(2,1)}, u32[]{:S(2)}, u32[]{:S(2)}) collective-permute-start(bf16[8,32,128]{2,0,1:T(8,128)(2,1)S(1)} %bitcast.102), channel_id=1, source_target_pairs={{0,8},{4,12},{8,0},{12,4},{1,9},{5,13},{9,1},{13,5},{2,10},{6,14},... | collective-permute-start | bytes 196616 | tf_op jit(solution)/shard_map/ppermute | solution.py:22
  7.2 8.3 %collective-permute-start.2 = (bf16[8,32,128]{2,0,1:T(8,128)(2,1)S(1)}, bf16[8,32,128]{2,0,1:T(8,128)(2,1)}, u32[]{:S(2)}, u32[]{:S(2)}) collective-permute-start(bf16[8,32,128]{2,0,1:T(8,128)(2,1)S(1)} %bitcast.103), channel_id=1, source_target_pairs={{0,4},{4,8},{8,12},{12,0},{1,5},{5,9},{9,13},{13,1},{2,6},{6,10},{... | collective-permute-start | bytes 196616 | tf_op jit(solution)/shard_map/ppermute | solution.py:22
  8.4 13.9 %copy-start.2 = (bf16[8,32,64]{2,1,0:T(8,128)(2,1)S(1)}, bf16[8,32,64]{2,1,0:T(8,128)(2,1)}, u32[]{:S(2)}) copy-start(bf16[8,32,64]{2,1,0:T(8,128)(2,1)} %param.8) | copy-start | bytes 98308
  23.3 8.3 %collective-permute-start.3 = (f32[2,4,64]{2,1,0:T(4,128)S(1)}, f32[2,4,64]{2,1,0:T(4,128)S(1)}, u32[]{:S(2)}, u32[]{:S(2)}) collective-permute-start(f32[2,4,64]{2,1,0:T(4,128)S(1)} %pad_maximum_fusion), channel_id=1, source_target_pairs={{0,4},{4,8},{8,12},{12,0},{1,5},{5,9},{9,13},{13,1},{2,6},{6,10},{... | collective-permute-start | bytes 6152 | tf_op jit(solution)/shard_map/ppermute | solution.py:97
  23.4 10.5 %collective-permute-start.4 = (f32[2,4,64]{2,1,0:T(4,128)S(1)}, f32[2,4,64]{2,1,0:T(4,128)S(1)}, u32[]{:S(2)}, u32[]{:S(2)}) collective-permute-start(f32[2,4,64]{2,1,0:T(4,128)S(1)} %pad_maximum_fusion), channel_id=1, source_target_pairs={{0,8},{4,12},{8,0},{12,4},{1,9},{5,13},{9,1},{13,5},{2,10},{6,14},... | collective-permute-start | bytes 6152 | tf_op jit(solution)/shard_map/ppermute | solution.py:97
  23.4 10.5 %collective-permute-start.5 = (f32[2,4,64]{2,1,0:T(4,128)S(1)}, f32[2,4,64]{2,1,0:T(4,128)S(1)}, u32[]{:S(2)}, u32[]{:S(2)}) collective-permute-start(f32[2,4,64]{2,1,0:T(4,128)S(1)} %pad_maximum_fusion), channel_id=1, source_target_pairs={{0,12},{4,0},{8,4},{12,8},{1,13},{5,1},{9,5},{13,9},{2,14},{6,2},{... | collective-permute-start | bytes 6152 | tf_op jit(solution)/shard_map/ppermute | solution.py:97
  30.0 5.9 %collective-permute-start.6 = (f32[4,64,128]{2,1,0:T(8,128)S(1)}, f32[4,64,128]{2,1,0:T(8,128)S(1)}, u32[]{:S(2)}, u32[]{:S(2)}) collective-permute-start(f32[4,64,128]{2,1,0:T(8,128)S(1)} %bitcast.110), channel_id=1, source_target_pairs={{0,4},{4,8},{8,12},{12,0},{1,5},{5,9},{9,13},{13,1},{2,6},{6,10},{... | collective-permute-start | bytes 393224 | tf_op jit(solution)/shard_map/ppermute | solution.py:96
  30.3 10.9 %collective-permute-start.7 = (f32[4,64,128]{2,1,0:T(8,128)S(1)}, f32[4,64,128]{2,1,0:T(8,128)S(1)}, u32[]{:S(2)}, u32[]{:S(2)}) collective-permute-start(f32[4,64,128]{2,1,0:T(8,128)S(1)} %bitcast.109), channel_id=1, source_target_pairs={{0,8},{4,12},{8,0},{12,4},{1,9},{5,13},{9,1},{13,5},{2,10},{6,14},... | collective-permute-start | bytes 393224 | tf_op jit(solution)/shard_map/ppermute | solution.py:96
  31.6 9.6 %collective-permute-start.8 = (f32[4,64,128]{2,1,0:T(8,128)S(1)}, f32[4,64,128]{2,1,0:T(8,128)S(1)}, u32[]{:S(2)}, u32[]{:S(2)}) collective-permute-start(f32[4,64,128]{2,1,0:T(8,128)S(1)} %bitcast.108), channel_id=1, source_target_pairs={{0,12},{4,0},{8,4},{12,8},{1,13},{5,1},{9,5},{13,9},{2,14},{6,2},{... | collective-permute-start | bytes 393224 | tf_op jit(solution)/shard_map/ppermute | solution.py:96
  43.1 25.6 %collective-permute-start.10 = (f32[8,32,128]{2,0,1:T(8,128)S(1)}, f32[8,32,128]{2,0,1:T(8,128)S(1)}, u32[]{:S(2)}, u32[]{:S(2)}) collective-permute-start(f32[8,32,128]{2,0,1:T(8,128)S(1)} %convolution_bitcast_fusion), channel_id=1, source_target_pairs={{0,8},{4,12},{8,0},{12,4},{1,9},{5,13},{9,1},{13,5},{2,10},{6,14},... | collective-permute-start | bytes 393224 | tf_op jit(solution)/shard_map/ppermute | solution.py:107
  45.5 23.2 %collective-permute-start.11 = (f32[8,32,128]{2,0,1:T(8,128)S(1)}, f32[8,32,128]{2,0,1:T(8,128)S(1)}, u32[]{:S(2)}, u32[]{:S(2)}) collective-permute-start(f32[8,32,128]{2,0,1:T(8,128)S(1)} %convolution_bitcast_fusion), channel_id=1, source_target_pairs={{0,12},{4,0},{8,4},{12,8},{1,13},{5,1},{9,5},{13,9},{2,14},{6,2},{... | collective-permute-start | bytes 393224 | tf_op jit(solution)/shard_map/ppermute | solution.py:107
  48.6 20.1 %collective-permute-start.9 = (f32[8,32,128]{2,0,1:T(8,128)S(1)}, f32[8,32,128]{2,0,1:T(8,128)S(1)}, u32[]{:S(2)}, u32[]{:S(2)}) collective-permute-start(f32[8,32,128]{2,0,1:T(8,128)S(1)} %convolution_bitcast_fusion), channel_id=1, source_target_pairs={{0,4},{4,8},{8,12},{12,0},{1,5},{5,9},{9,13},{13,1},{2,6},{6,10},{... | collective-permute-start | bytes 393224 | tf_op jit(solution)/shard_map/ppermute | solution.py:107
  77.8 3.7 %collective-permute-start.12 = (f32[8,448]{1,0:T(8,128)S(1)}, f32[8,448]{1,0:T(8,128)S(1)}, u32[]{:S(2)}, u32[]{:S(2)}) collective-permute-start(f32[8,448]{1,0:T(8,128)S(1)} %get-tuple-element.18), channel_id=1, source_target_pairs={{0,1},{1,2},{2,3},{3,0},{4,5},{5,6},{6,7},{7,4},{8,9},{9,10},{10,1... | collective-permute-start | bytes 43016 | tf_op jit(solution)/shard_map/ppermute | solution.py:35
  80.6 2.6 %collective-permute-start.13 = (f32[8,448]{1,0:T(8,128)S(1)}, f32[8,448]{1,0:T(8,128)S(1)}, u32[]{:S(2)}, u32[]{:S(2)}) collective-permute-start(f32[8,448]{1,0:T(8,128)S(1)} %get-tuple-element.20), channel_id=1, source_target_pairs={{0,2},{1,3},{2,0},{3,1},{4,6},{5,7},{6,4},{7,5},{8,10},{9,11},{10,... | collective-permute-start | bytes 43016 | tf_op jit(solution)/shard_map/ppermute | solution.py:35
  80.9 3.2 %collective-permute-start.14 = (f32[8,448]{1,0:T(8,128)S(1)}, f32[8,448]{1,0:T(8,128)S(1)}, u32[]{:S(2)}, u32[]{:S(2)}) collective-permute-start(f32[8,448]{1,0:T(8,128)S(1)} %get-tuple-element.19), channel_id=1, source_target_pairs={{0,3},{1,0},{2,1},{3,2},{4,7},{5,4},{6,5},{7,6},{8,11},{9,8},{10,9... | collective-permute-start | bytes 43016 | tf_op jit(solution)/shard_map/ppermute | solution.py:35

commit v2 on v0

v2 whole, which is shorter than its diff:
```python
import functools

import jax
import jax.numpy as jnp
from jax import lax
from jax.sharding import PartitionSpec as P

ROTARY_CHANNELS = 64
PLAIN_CHANNELS = 128
DRAFT = 2
PERMUTE_MAX = 8


def shift_pairs(n, k):
    return [(i, (i + k) % n) for i in range(n)]


def pick(index, options):
    chosen = options[-1]
    for j in range(len(options) - 2, -1, -1):
        chosen = jnp.where(index == j, options[j], chosen)
    return chosen


def per_device(n_ctx, n_head, query_nope, query_rope, kv_cache, lengths, w_absorb, w_value, w_output):
    seq_count, ctx_rows, channels = kv_cache.shape
    row_count, head_count = query_nope.shape[:2]
    latent_width = channels - query_rope.shape[2]
    slice_width = w_value.shape[1]
    small_ctx = n_ctx <= PERMUTE_MAX
    me_ctx = lax.axis_index("ctx")

    q_part = jnp.einsum(
        "rhn,hnl->rhl", query_nope, w_absorb, preferred_element_type=jnp.float32
    ).astype(jnp.bfloat16)
    if small_ctx:
        received = [q_part] + [
            lax.ppermute(q_part, "ctx", shift_pairs(n_ctx, k)) for k in range(1, n_ctx)
        ]
        slots = [pick((me_ctx - j) % n_ctx, received) for j in range(n_ctx)]
        q_latent = jnp.concatenate(slots, axis=2)
    else:
        q_latent = lax.all_gather(q_part, "ctx", axis=2, tiled=True)
    query_rows = jnp.concatenate([q_latent, query_rope], axis=2).reshape(
        seq_count, DRAFT * head_count, channels
    )
    logit_scores = jnp.einsum(
        "sqc,skc->sqk", query_rows, kv_cache, preferred_element_type=jnp.float32
    ) * (PLAIN_CHANNELS + ROTARY_CHANNELS) ** (-0.5)
    position = me_ctx * ctx_rows + jnp.arange(ctx_rows, dtype=jnp.int32)
    draft_index = jnp.arange(DRAFT * head_count, dtype=jnp.int32) // head_count
    row_limit = lengths[:, None] - DRAFT + draft_index[None, :]
    is_valid = position[None, None, :] <= row_limit[:, :, None]
    masked = jnp.where(is_valid, logit_scores, jnp.float32(-1e30))
    block_top = jnp.max(masked, axis=2)
    expo_f = jnp.where(is_valid, jnp.exp(masked - block_top[:, :, None]), jnp.float32(0.0))
    block_total = jnp.sum(expo_f, axis=2)
    weighted = jnp.einsum(
        "sqk,skl->sql",
        expo_f.astype(jnp.bfloat16),
        kv_cache[:, :, :latent_width],
        preferred_element_type=jnp.float32,
    )
    q_rows = DRAFT * head_count
    stats = jnp.stack([block_top, block_total]).reshape(-1, slice_width)
    sum_slices = [
        weighted[:, :, j * slice_width:(j + 1) * slice_width].reshape(-1, slice_width)
        for j in range(n_ctx)
    ]

    def packed_for(target):
        return jnp.concatenate([pick(target, sum_slices), stats], axis=0)

    def combine_blocks(parts):
        split = seq_count * q_rows
        sums = [p[:split].reshape(seq_count, q_rows, slice_width) for p in parts]
        st = [p[split:].reshape(2, seq_count, q_rows) for p in parts]
        row_top = functools.reduce(jnp.maximum, [t[0] for t in st])
        factors = [jnp.exp(t[0] - row_top) for t in st]
        total = sum(f * t[1] for f, t in zip(factors, st))
        acc = sum(f[:, :, None] * a for f, a in zip(factors, sums))
        return (acc / total[:, :, None]).astype(jnp.bfloat16)

    if small_ctx:
        parts = [packed_for(me_ctx)] + [
            lax.ppermute(packed_for((me_ctx + k) % n_ctx), "ctx", shift_pairs(n_ctx, k))
            for k in range(1, n_ctx)
        ]
    else:
        packed = jnp.stack([jnp.concatenate([s, stats], axis=0) for s in sum_slices])
        got = lax.all_to_all(packed, "ctx", 0, 0, tiled=False)
        parts = [got[j] for j in range(n_ctx)]
    latent_out = combine_blocks(parts).reshape(row_count, head_count, slice_width)

    value_part = jnp.einsum("rhl,hlv->rhv", latent_out, w_value, preferred_element_type=jnp.float32)
    if small_ctx:
        received = [value_part] + [
            lax.ppermute(value_part, "ctx", shift_pairs(n_ctx, k)) for k in range(1, n_ctx)
        ]
        values = sum(received).astype(jnp.bfloat16)
    else:
        values = lax.psum(value_part, "ctx").astype(jnp.bfloat16)
    partial_value = jnp.dot(
        values.reshape(row_count, -1), w_output, preferred_element_type=jnp.float32
    )
    if n_head > PERMUTE_MAX:
        return lax.psum_scatter(partial_value, "head", scatter_dimension=1, tiled=True)
    me_head = lax.axis_index("head")
    out_width = partial_value.shape[1] // n_head
    col_slices = [partial_value[:, j * out_width:(j + 1) * out_width] for j in range(n_head)]
    total = pick(me_head, col_slices)
    for k in range(1, n_head):
        total = total + lax.ppermute(
            pick((me_head + k) % n_head, col_slices), "head", shift_pairs(n_head, k)
        )
    return total


def solution(mesh):
    return jax.shard_map(
        functools.partial(per_device, mesh.shape["ctx"], mesh.shape["head"]),
        mesh=mesh,
        in_specs=(
            P("groups", "head", None),
            P("groups", "head", None),
            P("groups", "ctx", None),
            P("groups"),
            P("head", None, "ctx"),
            P("head", "ctx", None),
            P("head", "ctx"),
        ),
        out_specs=P("groups", ("ctx", "head")),
        check_vma=False,
    )
```

time: 124 us -> 60.6 us (0.49)
  blocking collectives: 42.9 us -> 0 us
  waiting for transfers between devices: 43.4 us -> 27.1 us
  starting transfers between devices: 0.04 us -> 15.5 us
  between operations: 13.5 us -> 0.17 us
  matrix products: 16.7 us -> 10.2 us
    unnamed x3 -> x0, waiting for transfers between devices: 27.3 us -> none
    ppermute x0 -> x12, waiting for transfers between devices: none -> 27.1 us  [the longest x3 11.2 us: per_device(): lax.ppermute(value_part, 'ctx', shift_pairs(n_ctx, k))]
    psum x2 -> x0, blocking collectives: 22.6 us -> none  [the longest x1 15.8 us: per_device(): values = lax.psum(value_part, 'ctx').astype(jnp.bfloat16)]
    reduce_scatter x1 -> x0, waiting for transfers between devices: 16.1 us -> none  [per_device(): lax.psum_scatter(weighted * factor[:, :, None], 'ctx', scatter_dimension=...]
    ppermute x0 -> x12, starting transfers between devices: none -> 15.5 us  [the longest x3 4.62 us: per_device(): lax.ppermute(q_part, 'ctx', shift_pairs(n_ctx, k))]
    all_gather x1 -> x0, blocking collectives: 12.4 us -> none  [per_device(): q_latent = lax.all_gather(q_part, 'ctx', axis=2, tiled=True)]
    unnamed x1 -> x0, matrix products: 9.94 us -> none
    pmax x1 -> x0, blocking collectives: 7.91 us -> none  [per_device(): merged_top = lax.pmax(row_top, 'ctx')]
  transfers between devices with their start and end apart: 2 -> 12, of which waited for: 2 -> 8; matrix products, arithmetic and copies ran while one was open for 0% -> 2% of each run, Pallas kernels for 0% -> 0%
where the time goes in v2:
time: 60.6 us; the launch traced here: 60 us
  waiting for transfers between devices  27.1 us (45%)
  starting transfers between devices  15.5 us (26%)
  matrix products  10.2 us (17%)
  other arithmetic  4.27 us (7%)
  local copies, waits for them, and re-layouts  2.77 us (5%)
    ppermute x3, waiting for transfers between devices, per_device(): lax.ppermute(value_part, 'ctx', shift_pairs(n_ctx, k))  11.2 us
    ppermute x3, waiting for transfers between devices, per_device(): lax.ppermute(packed_for((me_ctx + k) % n_ctx), 'ctx', shift_pairs(n_ctx, k))  7.75 us
    dot_general x1, matrix products, per_device(): jnp.dot(values.reshape(row_count, -1), w_output, preferred_element_type=j...  7.17 us
    ppermute x3, waiting for transfers between devices, per_device(): lax.ppermute(q_part, 'ctx', shift_pairs(n_ctx, k))  5.65 us
    ppermute x3, starting transfers between devices, per_device(): lax.ppermute(q_part, 'ctx', shift_pairs(n_ctx, k))  4.62 us
    ppermute x3, starting transfers between devices, per_device(): lax.ppermute(value_part, 'ctx', shift_pairs(n_ctx, k))  4.22 us
    ppermute x3, starting transfers between devices, per_device(): lax.ppermute(packed_for((me_ctx + k) % n_ctx), 'ctx', shift_pairs(n_ctx, k))  3.55 us
    ppermute x3, starting transfers between devices, per_device(): lax.ppermute(pick((me_head + k) % n_head, col_slices), 'head', shift_pair...  3.07 us
  transfers between devices with their start and end apart: 12, of which 8 were waited for; matrix products, arithmetic and copies ran while one was open for 2% of the time, Pallas kernels for 0%

profile of v2, /device:TPU:1, one launch (start us, length us, event | category | flops | bytes accessed | tf_op | source)
XLA Modules:
  0.0 60.0 jit_solution(13130401105335144425)
XLA Ops:
  0.0 1.2 %copy-done = bf16[32,128,128]{2,1,0:T(8,128)(2,1)S(1)} copy-done((bf16[32,128,128]{2,1,0:T(8,128)(2,1)S(1)}, bf16[32,128,128]{2,1,0:T(8,128)(2,1)}, u32[]{:S(2)}) %copy-start) | copy-done | bytes 1048600
  1.2 1.2 %fusion.3 = bf16[8,32,128]{2,0,1:T(8,128)(2,1)S(1)} fusion(bf16[32,128,128]{2,1,0:T(8,128)(2,1)S(1)} %copy-done, bf16[8,32,128]{2,1,0:T(8,128)(2,1)} %param.7), kind=kOutput, calls=%fused_computation.6 | convolution fusion | flops 8421376 | bytes 1179648 | tf_op jit(solution)/shard_map/rhn,hnl->rhl/dot_general | solution.py:33
  2.4 4.2 %collective-permute-start.2 = (bf16[8,32,128]{2,0,1:T(8,128)(2,1)S(1)}, bf16[8,32,128]{2,0,1:T(8,128)(2,1)S(1)}, u32[]{:S(2)}, u32[]{:S(2)}) collective-permute-start(bf16[8,32,128]{2,0,1:T(8,128)(2,1)S(1)} %fusion.3), channel_id=1, source_target_pairs={{0,12},{4,0},{8,4},{12,8},{1,13},{5,1},{9,5},{13,9},{2,14},{6,2},{... | collective-permute-start | bytes 196616 | tf_op jit(solution)/shard_map/ppermute | solution.py:38
  6.6 0.5 collective-permute-start
  7.1 0.7 %broadcast_add_fusion.1 = s32[4]{0:T(128)S(1)} fusion(s32[4]{0:T(128)} %param.10), kind=kLoop, calls=%fused_computation.48 | loop fusion | flops 4 | bytes 32 | tf_op jit(solution)/shard_map/sub | solution.py:52
  7.7 0.1 broadcast_add_fusion
  7.8 0.1 collective-permute-done.2
  7.9 5.5 %collective-permute-done.1 = bf16[8,32,128]{2,0,1:T(8,128)(2,1)} collective-permute-done((bf16[8,32,128]{2,0,1:T(8,128)(2,1)S(1)}, bf16[8,32,128]{2,0,1:T(8,128)(2,1)}, u32[]{:S(2)}, u32[]{:S(2)}) %collective-permute-start.1) | collective-permute-done | bytes 65568 | tf_op jit(solution)/shard_map/ppermute | solution.py:38
  13.4 0.0 collective-permute-done
  13.5 0.1 select_dynamic-update-slice_fusion.2
  13.6 0.9 %select_dynamic-update-slice_fusion.1 = bf16[8,32,576]{2,0,1:T(8,128)(2,1)S(1)} fusion(bf16[8,32,576]{2,0,1:T(8,128)(2,1)S(1)} %select_dynamic-update-slice_fusion.2, bf16[8,32,128]{2,0,1:T(8,128)(2,1)S(1)} %fusion.3, bf16[8,32,128]{2,0,1:T(8,128)(2,1)} %collective-permute-done, bf16[8,32,128]{2,0,1:T(8,128)(2,1)} %collective-permute-done.1, ...), kind=kLoop, calls=%fused_computation.28 | loop fusion | flops 98304 | bytes 327683
  14.5 0.0 copy-start.2
  14.5 1.1 %select_dynamic-update-slice_fusion = bf16[8,32,576]{2,0,1:T(8,128)(2,1)S(1)} fusion(bf16[8,32,576]{2,0,1:T(8,128)(2,1)S(1)} %select_dynamic-update-slice_fusion.1, bf16[8,32,128]{2,0,1:T(8,128)(2,1)S(1)} %fusion.3, bf16[8,32,128]{2,0,1:T(8,128)(2,1)} %collective-permute-done, bf16[8,32,128]{2,0,1:T(8,128)(2,1)} %collective-permute-done.1, ...), kind=kLoop, calls=%fused_computation.27 | loop fusion | flops 98304 | bytes 327683
  15.6 0.9 %copy_dynamic-update-slice_fusion = bf16[8,32,576]{2,0,1:T(8,128)(2,1)S(1)} fusion(bf16[8,32,576]{2,0,1:T(8,128)(2,1)S(1)} %select_dynamic-update-slice_fusion, bf16[8,32,64]{2,1,0:T(8,128)(2,1)} %param.8), kind=kLoop, calls=%fused_computation.25 | loop fusion | bytes 98304 | tf_op jit(solution)/shard_map/concatenate | solution.py:44
  16.5 0.6 %fusion.20 = (f32[4,64]{1,0:T(4,128)S(1)}, f32[4,64,512]{2,1,0:T(8,128)S(1)}) fusion(bf16[4,64,576]{2,1,0:T(8,128)(2,1)S(1)} %bitcast.22, bf16[4,512,576]{1,2,0:T(8,128)(2,1)S(1)} %copy-done.1, s32[4,64]{1,0:T(4,128)S(1)} %broadcast_add_fusion, s32[512]{0:T(512)S(1)} %iota_add_fusion), kind=kOutput, calls=%fused_computation.53 | convolution fusion | flops 151518976 | bytes 3182592 | tf_op jit(solution)/shard_map/sqc,skc->sqk/dot_general | solution.py:47
  17.1 0.3 fusion.4
  17.4 0.8 %fusion = f32[4,64,512]{2,1,0:T(8,128)S(1)} fusion(bf16[4,512,576]{1,2,0:T(8,128)(2,1)S(1)} %copy-done.2, f32[4,64,512]{2,1,0:T(8,128)S(1)} %get-tuple-element.24, f32[4,64]{1,0:T(4,128)S(1)} %get-tuple-element.23, s32[4,64]{1,0:T(4,128)S(1)} %broadcast_add_fusion, s32[512]{0:T(512)S(1)} %iota_add_fusion), kind=kOutput, calls=%fused_computation | convolution fusion | flops 134742016 | bytes 3151872 | tf_op jit(solution)/shard_map/sqk,skl->sql/dot_general | solution.py:58
  18.2 0.0 copy-start.3
  18.2 0.1 reshape.212
  18.4 0.1 collective-permute-start.3
  18.5 1.2 %collective-permute-start.4 = (f32[260,128]{1,0:T(8,128)S(1)}, f32[260,128]{1,0:T(8,128)S(1)}, u32[]{:S(2)}, u32[]{:S(2)}) collective-permute-start(f32[260,128]{1,0:T(8,128)S(1)} %get-tuple-element.21), channel_id=1, source_target_pairs={{0,8},{4,12},{8,0},{12,4},{1,9},{5,13},{9,1},{13,5},{2,10},{6,14},... | collective-permute-start | bytes 399368 | tf_op jit(solution)/shard_map/ppermute | solution.py:86
  19.7 2.3 %collective-permute-start.5 = (f32[260,128]{1,0:T(8,128)S(1)}, f32[260,128]{1,0:T(8,128)S(1)}, u32[]{:S(2)}, u32[]{:S(2)}) collective-permute-start(f32[260,128]{1,0:T(8,128)S(1)} %get-tuple-element.22), channel_id=1, source_target_pairs={{0,12},{4,0},{8,4},{12,8},{1,13},{5,1},{9,5},{13,9},{2,14},{6,2},{... | collective-permute-start | bytes 399368 | tf_op jit(solution)/shard_map/ppermute | solution.py:86
  22.0 2.8 %collective-permute-done.3 = f32[260,128]{1,0:T(8,128)S(1)} collective-permute-done((f32[260,128]{1,0:T(8,128)S(1)}, f32[260,128]{1,0:T(8,128)S(1)}, u32[]{:S(2)}, u32[]{:S(2)}) %collective-permute-start.3) | collective-permute-done | bytes 133152 | tf_op jit(solution)/shard_map/ppermute | solution.py:86
  24.8 0.1 squeeze.21
  24.9 0.1 squeeze.24
  24.9 4.9 %collective-permute-done.4 = f32[260,128]{1,0:T(8,128)S(1)} collective-permute-done((f32[260,128]{1,0:T(8,128)S(1)}, f32[260,128]{1,0:T(8,128)S(1)}, u32[]{:S(2)}, u32[]{:S(2)}) %collective-permute-start.4) | collective-permute-done | bytes 133152 | tf_op jit(solution)/shard_map/ppermute | solution.py:86
  29.9 0.1 squeeze.22
  30.0 0.1 squeeze.25
  30.0 0.0 collective-permute-done.5
  30.0 0.1 squeeze.23
  30.1 0.1 squeeze.26
  30.3 0.2 divide_convert_fusion
  30.5 0.4 convolution_bitcast_fusion
  30.9 3.8 %collective-permute-start.8 = (f32[8,32,128]{2,0,1:T(8,128)S(1)}, f32[8,32,128]{2,0,1:T(8,128)S(1)}, u32[]{:S(2)}, u32[]{:S(2)}) collective-permute-start(f32[8,32,128]{2,0,1:T(8,128)S(1)} %convolution_bitcast_fusion), channel_id=1, source_target_pairs={{0,12},{4,0},{8,4},{12,8},{1,13},{5,1},{9,5},{13,9},{2,14},{6,2},{... | collective-permute-start | bytes 393224 | tf_op jit(solution)/shard_map/ppermute | solution.py:98
  34.8 0.4 collective-permute-start.7
  35.2 1.6 %collective-permute-done.8 = f32[8,32,128]{2,0,1:T(8,128)S(1)} collective-permute-done((f32[8,32,128]{2,0,1:T(8,128)S(1)}, f32[8,32,128]{2,0,1:T(8,128)S(1)}, u32[]{:S(2)}, u32[]{:S(2)}) %collective-permute-start.8) | collective-permute-done | bytes 131104 | tf_op jit(solution)/shard_map/ppermute | solution.py:98
  36.7 9.6 %collective-permute-done.7 = f32[8,32,128]{2,0,1:T(8,128)S(1)} collective-permute-done((f32[8,32,128]{2,0,1:T(8,128)S(1)}, f32[8,32,128]{2,0,1:T(8,128)S(1)}, u32[]{:S(2)}, u32[]{:S(2)}) %collective-permute-start.7) | collective-permute-done | bytes 131104 | tf_op jit(solution)/shard_map/ppermute | solution.py:98
  46.3 0.0 collective-permute-done.6
  46.3 7.2 %fusion.12 = f32[8,1792]{1,0:T(8,128)S(1)} fusion(bf16[4096,1792]{1,0:T(8,128)(2,1)} %param.13, f32[8,32,128]{2,0,1:T(8,128)S(1)} %collective-permute-done.8, f32[8,32,128]{2,0,1:T(8,128)S(1)} %collective-permute-done.7, f32[8,32,128]{2,0,1:T(8,128)S(1)} %convolution_bitcast_fusion, f32[8,32,128]{2,0,1:T(8,128)S(1)} %collective-permute-done.6), kind=kOutput, calls=%fused_computation.23 | convolution fusion | flops 117571584 | bytes 15261696 | tf_op jit(solution)/shard_map/dot_general | solution.py:103
  53.5 0.1 select_select_fusion.3
  53.6 1.7 %collective-permute-start.11 = (f32[8,448]{1,0:T(8,128)S(1)}, f32[8,448]{1,0:T(8,128)S(1)}, u32[]{:S(2)}, u32[]{:S(2)}) collective-permute-start(f32[8,448]{1,0:T(8,128)S(1)} %select_select_fusion.3), channel_id=1, source_target_pairs={{0,3},{1,0},{2,1},{3,2},{4,7},{5,4},{6,5},{7,6},{8,11},{9,8},{10,9... | collective-permute-start | bytes 43016 | tf_op jit(solution)/shard_map/ppermute | solution.py:113
  55.3 0.1 select_select_fusion.5
  55.4 1.1 %collective-permute-start.9 = (f32[8,448]{1,0:T(8,128)S(1)}, f32[8,448]{1,0:T(8,128)S(1)}, u32[]{:S(2)}, u32[]{:S(2)}) collective-permute-start(f32[8,448]{1,0:T(8,128)S(1)} %get-tuple-element.18), channel_id=1, source_target_pairs={{0,1},{1,2},{2,3},{3,0},{4,5},{5,6},{6,7},{7,4},{8,9},{9,10},{10,1... | collective-permute-start | bytes 43016 | tf_op jit(solution)/shard_map/ppermute | solution.py:113
  56.5 0.3 collective-permute-start.10
  56.7 1.5 %collective-permute-done.11 = f32[8,448]{1,0:T(8,128)S(1)} collective-permute-done((f32[8,448]{1,0:T(8,128)S(1)}, f32[8,448]{1,0:T(8,128)S(1)}, u32[]{:S(2)}, u32[]{:S(2)}) %collective-permute-start.11) | collective-permute-done | bytes 14368 | tf_op jit(solution)/shard_map/ppermute | solution.py:113
  58.2 0.0 collective-permute-done.9
  58.2 1.0 %collective-permute-done.10 = f32[8,448]{1,0:T(8,128)S(1)} collective-permute-done((f32[8,448]{1,0:T(8,128)S(1)}, f32[8,448]{1,0:T(8,128)S(1)}, u32[]{:S(2)}, u32[]{:S(2)}) %collective-permute-start.10) | collective-permute-done | bytes 14368 | tf_op jit(solution)/shard_map/ppermute | solution.py:113
  59.3 0.7 %add_add_fusion = f32[8,448]{1,0:T(8,128)} fusion(f32[8,448]{1,0:T(8,128)S(1)} %collective-permute-done.11, f32[8,448]{1,0:T(8,128)S(1)} %collective-permute-done.10, f32[8,448]{1,0:T(8,128)S(1)} %collective-permute-done.9, f32[8,1792]{1,0:T(8,128)S(1)} %fusion.12, pred[]{:T(512)S(6)} %eq.145, pred[]{:T(512)S(6)} %eq.144, pred[]{:T(512)S(6)} %eq.119), kind=kLoop, calls=%fused_computation.32 | loop fusion | flops 21504 | bytes 114691 | tf_op jit(solution)/shard_map/add | solution.py:113
  (22 shorter events, 0.3 us)
Async XLA Ops:
  0.0 1.2 %copy-start = (bf16[32,128,128]{2,1,0:T(8,128)(2,1)S(1)}, bf16[32,128,128]{2,1,0:T(8,128)(2,1)}, u32[]{:S(2)}) copy-start(bf16[32,128,128]{2,1,0:T(8,128)(2,1)} %param.11) | copy-start | bytes 3145732
  0.0 16.5 %copy-start.1 = (bf16[4,512,576]{1,2,0:T(8,128)(2,1)S(1)}, bf16[4,512,576]{1,2,0:T(8,128)(2,1)}, u32[]{:S(2)}) copy-start(bf16[4,512,576]{1,2,0:T(8,128)(2,1)} %param.9) | copy-start | bytes 7077892
  2.4 5.5 %collective-permute-start.2 = (bf16[8,32,128]{2,0,1:T(8,128)(2,1)S(1)}, bf16[8,32,128]{2,0,1:T(8,128)(2,1)S(1)}, u32[]{:S(2)}, u32[]{:S(2)}) collective-permute-start(bf16[8,32,128]{2,0,1:T(8,128)(2,1)S(1)} %fusion.3), channel_id=1, source_target_pairs={{0,12},{4,0},{8,4},{12,8},{1,13},{5,1},{9,5},{13,9},{2,14},{6,2},{... | collective-permute-start | bytes 196616 | tf_op jit(solution)/shard_map/ppermute | solution.py:38
  6.6 6.8 %collective-permute-start.1 = (bf16[8,32,128]{2,0,1:T(8,128)(2,1)S(1)}, bf16[8,32,128]{2,0,1:T(8,128)(2,1)}, u32[]{:S(2)}, u32[]{:S(2)}) collective-permute-start(bf16[8,32,128]{2,0,1:T(8,128)(2,1)S(1)} %fusion.3), channel_id=1, source_target_pairs={{0,8},{4,12},{8,0},{12,4},{1,9},{5,13},{9,1},{13,5},{2,10},{6,14},... | collective-permute-start | bytes 196616 | tf_op jit(solution)/shard_map/ppermute | solution.py:38
  6.6 6.8 %collective-permute-start = (bf16[8,32,128]{2,0,1:T(8,128)(2,1)S(1)}, bf16[8,32,128]{2,0,1:T(8,128)(2,1)}, u32[]{:S(2)}, u32[]{:S(2)}) collective-permute-start(bf16[8,32,128]{2,0,1:T(8,128)(2,1)S(1)} %fusion.3), channel_id=1, source_target_pairs={{0,4},{4,8},{8,12},{12,0},{1,5},{5,9},{9,13},{13,1},{2,6},{6,10},{... | collective-permute-start | bytes 196616 | tf_op jit(solution)/shard_map/ppermute | solution.py:38
  14.5 2.9 %copy-start.2 = (bf16[4,512,576]{1,2,0:T(8,128)(2,1)S(1)}, bf16[4,512,576]{1,2,0:T(8,128)(2,1)}, u32[]{:S(2)}) copy-start(bf16[4,512,576]{1,2,0:T(8,128)(2,1)} %param.9) | copy-start | bytes 7077892
  18.2 12.4 %copy-start.3 = (bf16[32,128,128]{2,1,0:T(8,128)(2,1)S(1)}, bf16[32,128,128]{2,1,0:T(8,128)(2,1)}, u32[]{:S(2)}) copy-start(bf16[32,128,128]{2,1,0:T(8,128)(2,1)} %param.12) | copy-start | bytes 3145732
  18.4 6.4 %collective-permute-start.3 = (f32[260,128]{1,0:T(8,128)S(1)}, f32[260,128]{1,0:T(8,128)S(1)}, u32[]{:S(2)}, u32[]{:S(2)}) collective-permute-start(f32[260,128]{1,0:T(8,128)S(1)} %get-tuple-element.20), channel_id=1, source_target_pairs={{0,4},{4,8},{8,12},{12,0},{1,5},{5,9},{9,13},{13,1},{2,6},{6,10},{... | collective-permute-start | bytes 399368 | tf_op jit(solution)/shard_map/ppermute | solution.py:86
  18.5 11.4 %collective-permute-start.4 = (f32[260,128]{1,0:T(8,128)S(1)}, f32[260,128]{1,0:T(8,128)S(1)}, u32[]{:S(2)}, u32[]{:S(2)}) collective-permute-start(f32[260,128]{1,0:T(8,128)S(1)} %get-tuple-element.21), channel_id=1, source_target_pairs={{0,8},{4,12},{8,0},{12,4},{1,9},{5,13},{9,1},{13,5},{2,10},{6,14},... | collective-permute-start | bytes 399368 | tf_op jit(solution)/shard_map/ppermute | solution.py:86
  19.7 10.4 %collective-permute-start.5 = (f32[260,128]{1,0:T(8,128)S(1)}, f32[260,128]{1,0:T(8,128)S(1)}, u32[]{:S(2)}, u32[]{:S(2)}) collective-permute-start(f32[260,128]{1,0:T(8,128)S(1)} %get-tuple-element.22), channel_id=1, source_target_pairs={{0,12},{4,0},{8,4},{12,8},{1,13},{5,1},{9,5},{13,9},{2,14},{6,2},{... | collective-permute-start | bytes 399368 | tf_op jit(solution)/shard_map/ppermute | solution.py:86
  30.9 5.8 %collective-permute-start.8 = (f32[8,32,128]{2,0,1:T(8,128)S(1)}, f32[8,32,128]{2,0,1:T(8,128)S(1)}, u32[]{:S(2)}, u32[]{:S(2)}) collective-permute-start(f32[8,32,128]{2,0,1:T(8,128)S(1)} %convolution_bitcast_fusion), channel_id=1, source_target_pairs={{0,12},{4,0},{8,4},{12,8},{1,13},{5,1},{9,5},{13,9},{2,14},{6,2},{... | collective-permute-start | bytes 393224 | tf_op jit(solution)/shard_map/ppermute | solution.py:98
  34.8 11.6 %collective-permute-start.7 = (f32[8,32,128]{2,0,1:T(8,128)S(1)}, f32[8,32,128]{2,0,1:T(8,128)S(1)}, u32[]{:S(2)}, u32[]{:S(2)}) collective-permute-start(f32[8,32,128]{2,0,1:T(8,128)S(1)} %convolution_bitcast_fusion), channel_id=1, source_target_pairs={{0,8},{4,12},{8,0},{12,4},{1,9},{5,13},{9,1},{13,5},{2,10},{6,14},... | collective-permute-start | bytes 393224 | tf_op jit(solution)/shard_map/ppermute | solution.py:98
  35.2 11.2 %collective-permute-start.6 = (f32[8,32,128]{2,0,1:T(8,128)S(1)}, f32[8,32,128]{2,0,1:T(8,128)S(1)}, u32[]{:S(2)}, u32[]{:S(2)}) collective-permute-start(f32[8,32,128]{2,0,1:T(8,128)S(1)} %convolution_bitcast_fusion), channel_id=1, source_target_pairs={{0,4},{4,8},{8,12},{12,0},{1,5},{5,9},{9,13},{13,1},{2,6},{6,10},{... | collective-permute-start | bytes 393224 | tf_op jit(solution)/shard_map/ppermute | solution.py:98
  53.6 4.6 %collective-permute-start.11 = (f32[8,448]{1,0:T(8,128)S(1)}, f32[8,448]{1,0:T(8,128)S(1)}, u32[]{:S(2)}, u32[]{:S(2)}) collective-permute-start(f32[8,448]{1,0:T(8,128)S(1)} %select_select_fusion.3), channel_id=1, source_target_pairs={{0,3},{1,0},{2,1},{3,2},{4,7},{5,4},{6,5},{7,6},{8,11},{9,8},{10,9... | collective-permute-start | bytes 43016 | tf_op jit(solution)/shard_map/ppermute | solution.py:113
  55.4 2.9 %collective-permute-start.9 = (f32[8,448]{1,0:T(8,128)S(1)}, f32[8,448]{1,0:T(8,128)S(1)}, u32[]{:S(2)}, u32[]{:S(2)}) collective-permute-start(f32[8,448]{1,0:T(8,128)S(1)} %get-tuple-element.18), channel_id=1, source_target_pairs={{0,1},{1,2},{2,3},{3,0},{4,5},{5,6},{6,7},{7,4},{8,9},{9,10},{10,1... | collective-permute-start | bytes 43016 | tf_op jit(solution)/shard_map/ppermute | solution.py:113
  56.5 2.8 %collective-permute-start.10 = (f32[8,448]{1,0:T(8,128)S(1)}, f32[8,448]{1,0:T(8,128)S(1)}, u32[]{:S(2)}, u32[]{:S(2)}) collective-permute-start(f32[8,448]{1,0:T(8,128)S(1)} %get-tuple-element.19), channel_id=1, source_target_pairs={{0,2},{1,3},{2,0},{3,1},{4,6},{5,7},{6,4},{7,5},{8,10},{9,11},{10,... | collective-permute-start | bytes 43016 | tf_op jit(solution)/shard_map/ppermute | solution.py:113

commit v3 on v2

--- a/solution.py
+++ b/solution.py
@@ -3,6 +3,8 @@
 import jax
 import jax.numpy as jnp
 from jax import lax
+from jax.experimental import pallas as pl
+from jax.experimental.pallas import tpu as pltpu
 from jax.sharding import PartitionSpec as P
 
 ROTARY_CHANNELS = 64
@@ -20,6 +22,45 @@
     for j in range(len(options) - 2, -1, -1):
         chosen = jnp.where(index == j, options[j], chosen)
     return chosen
+
+
+def out_proj_kernel(chunks, v_ref, w_hbm, o_ref, w_vmem, sems):
+    depth = w_hbm.shape[0] // chunks
+    copies = [
+        pltpu.make_async_copy(
+            w_hbm.at[pl.ds(i * depth, depth)], w_vmem.at[pl.ds(i * depth, depth)], sems.at[i]
+        )
+        for i in range(chunks)
+    ]
+    for c in copies:
+        c.start()
+    acc = jnp.zeros(o_ref.shape, jnp.float32)
+    for i in range(chunks):
+        copies[i].wait()
+        rows = pl.ds(i * depth, depth)
+        acc = acc + jnp.dot(v_ref[:, rows], w_vmem[rows, :], preferred_element_type=jnp.float32)
+    o_ref[...] = acc
+
+
+def out_proj(values, w_output):
+    depth, width = w_output.shape
+    chunks = 8 if depth % (8 * 256) == 0 else 1
+    vmem = pltpu.MemorySpace.VMEM
+    return pl.pallas_call(
+        functools.partial(out_proj_kernel, chunks),
+        out_shape=jax.ShapeDtypeStruct((values.shape[0], width), jnp.float32),
+        in_specs=[pl.BlockSpec(memory_space=vmem), pl.BlockSpec(memory_space=pl.ANY)],
+        out_specs=pl.BlockSpec(memory_space=vmem),
+        scratch_shapes=[
+            pltpu.VMEM(w_output.shape, w_output.dtype),
+            pltpu.SemaphoreType.DMA((chunks,)),
+        ],
+        cost_estimate=pl.CostEstimate(
+            flops=2 * values.shape[0] * depth * width,
+            transcendentals=0,
+            bytes_accessed=2 * depth * width + 2 * values.size + 4 * values.shape[0] * width,
+        ),
+    )(values, w_output)
 
 
 def per_device(n_ctx, n_head, query_nope, query_rope, kv_cache, lengths, w_absorb, w_value, w_output):
@@ -100,9 +141,7 @@
         values = sum(received).astype(jnp.bfloat16)
     else:
         values = lax.psum(value_part, "ctx").astype(jnp.bfloat16)
-    partial_value = jnp.dot(
-        values.reshape(row_count, -1), w_output, preferred_element_type=jnp.float32
-    )
+    partial_value = out_proj(values.reshape(row_count, -1), w_output)
     if n_head > PERMUTE_MAX:
         return lax.psum_scatter(partial_value, "head", scatter_dimension=1, tiled=True)
     me_head = lax.axis_index("head")

time: 60.6 us -> 63.8 us (1.053)
  matrix products: 10.2 us -> 3 us
  Pallas kernels: 0 us -> 7.15 us
  other arithmetic: 4.27 us -> 7.33 us
    dot_general x1 -> x0, matrix products: 7.17 us -> none  [per_device(): jnp.dot(values.reshape(row_count, -1), w_output, preferred_element_type=j...]
    pallas_call x0 -> x1, Pallas kernels: none -> 7.15 us  [out_proj(): pl.pallas_call(functools.partial(out_proj_kernel, chunks), out_shape=jax....]
    select_n x4, other arithmetic: 0.21 us -> 1.81 us  [pick(): chosen = jnp.where(index == j, options[j], chosen)]
    add x1, other arithmetic: 0.69 us -> 1.48 us  [per_device(): total + lax.ppermute(pick((me_head + k) % n_head, col_slices), 'head', sh...]
    reshape x0 -> x1, other arithmetic: none -> 0.66 us  [per_device(): partial_value = out_proj(values.reshape(row_count, -1), w_output)]
  transfers between devices with their start and end apart: 12 -> 12, of which waited for: 8 -> 9; matrix products, arithmetic and copies ran while one was open for 2% -> 3% of each run, Pallas kernels for 0% -> 0%
where the time goes in v3:
time: 63.8 us; the launch traced here: 63 us
  waiting for transfers between devices  27.1 us (42%)
  starting transfers between devices  15.5 us (24%)
  other arithmetic  7.33 us (11%)
  Pallas kernels  7.15 us (11%)
  matrix products  3 us (5%)
  local copies, waits for them, and re-layouts  2.77 us (4%)
    ppermute x3, waiting for transfers between devices, per_device(): lax.ppermute(value_part, 'ctx', shift_pairs(n_ctx, k))  11.2 us
    ppermute x3, waiting for transfers between devices, per_device(): lax.ppermute(packed_for((me_ctx + k) % n_ctx), 'ctx', shift_pairs(n_ctx, k))  7.75 us
    pallas_call x1, Pallas kernels, out_proj(): pl.pallas_call(functools.partial(out_proj_kernel, chunks), out_shape=jax....  7.15 us
    ppermute x3, waiting for transfers between devices, per_device(): lax.ppermute(q_part, 'ctx', shift_pairs(n_ctx, k))  5.65 us
    ppermute x3, starting transfers between devices, per_device(): lax.ppermute(q_part, 'ctx', shift_pairs(n_ctx, k))  4.62 us
    ppermute x3, starting transfers between devices, per_device(): lax.ppermute(value_part, 'ctx', shift_pairs(n_ctx, k))  4.22 us
    ppermute x3, starting transfers between devices, per_device(): lax.ppermute(packed_for((me_ctx + k) % n_ctx), 'ctx', shift_pairs(n_ctx, k))  3.55 us
    ppermute x3, starting transfers between devices, per_device(): lax.ppermute(pick((me_head + k) % n_head, col_slices), 'head', shift_pair...  3.09 us
  transfers between devices with their start and end apart: 12, of which 9 were waited for; matrix products, arithmetic and copies ran while one was open for 3% of the time, Pallas kernels for 0%

profile of v3, /device:TPU:1, one launch (start us, length us, event | category | flops | bytes accessed | tf_op | source)
XLA Modules:
  0.0 63.0 jit_solution(1069058684771811782)
XLA Ops:
  0.0 1.2 %copy-done = bf16[32,128,128]{2,1,0:T(8,128)(2,1)S(1)} copy-done((bf16[32,128,128]{2,1,0:T(8,128)(2,1)S(1)}, bf16[32,128,128]{2,1,0:T(8,128)(2,1)}, u32[]{:S(2)}) %copy-start) | copy-done | bytes 1048600
  1.2 1.2 %fusion.3 = bf16[8,32,128]{2,0,1:T(8,128)(2,1)S(1)} fusion(bf16[32,128,128]{2,1,0:T(8,128)(2,1)S(1)} %copy-done, bf16[8,32,128]{2,1,0:T(8,128)(2,1)} %param.7), kind=kOutput, calls=%fused_computation.6 | convolution fusion | flops 8421376 | bytes 1179648 | tf_op jit(solution)/shard_map/rhn,hnl->rhl/dot_general | solution.py:74
  2.4 4.2 %collective-permute-start.2 = (bf16[8,32,128]{2,0,1:T(8,128)(2,1)S(1)}, bf16[8,32,128]{2,0,1:T(8,128)(2,1)S(1)}, u32[]{:S(2)}, u32[]{:S(2)}) collective-permute-start(bf16[8,32,128]{2,0,1:T(8,128)(2,1)S(1)} %fusion.3), channel_id=1, source_target_pairs={{0,12},{4,0},{8,4},{12,8},{1,13},{5,1},{9,5},{13,9},{2,14},{6,2},{... | collective-permute-start | bytes 196616 | tf_op jit(solution)/shard_map/ppermute | solution.py:79
  6.6 0.0 collective-permute-start.1
  6.6 0.5 collective-permute-start
  7.1 0.7 %broadcast_add_fusion.1 = s32[4]{0:T(128)S(1)} fusion(s32[4]{0:T(128)} %param.10), kind=kLoop, calls=%fused_computation.47 | loop fusion | flops 4 | bytes 32 | tf_op jit(solution)/shard_map/sub | solution.py:93
  7.7 0.1 broadcast_add_fusion
  7.8 0.1 collective-permute-done.2
  7.9 5.5 %collective-permute-done.1 = bf16[8,32,128]{2,0,1:T(8,128)(2,1)} collective-permute-done((bf16[8,32,128]{2,0,1:T(8,128)(2,1)S(1)}, bf16[8,32,128]{2,0,1:T(8,128)(2,1)}, u32[]{:S(2)}, u32[]{:S(2)}) %collective-permute-start.1) | collective-permute-done | bytes 65568 | tf_op jit(solution)/shard_map/ppermute | solution.py:79
  13.5 0.1 select_dynamic-update-slice_fusion.2
  13.6 0.9 %select_dynamic-update-slice_fusion.1 = bf16[8,32,576]{2,0,1:T(8,128)(2,1)S(1)} fusion(bf16[8,32,576]{2,0,1:T(8,128)(2,1)S(1)} %select_dynamic-update-slice_fusion.2, bf16[8,32,128]{2,0,1:T(8,128)(2,1)S(1)} %fusion.3, bf16[8,32,128]{2,0,1:T(8,128)(2,1)} %collective-permute-done, bf16[8,32,128]{2,0,1:T(8,128)(2,1)} %collective-permute-done.1, ...), kind=kLoop, calls=%fused_computation.27 | loop fusion | flops 98304 | bytes 327683
  14.5 0.0 copy-start.2
  14.5 1.1 %select_dynamic-update-slice_fusion = bf16[8,32,576]{2,0,1:T(8,128)(2,1)S(1)} fusion(bf16[8,32,576]{2,0,1:T(8,128)(2,1)S(1)} %select_dynamic-update-slice_fusion.1, bf16[8,32,128]{2,0,1:T(8,128)(2,1)S(1)} %fusion.3, bf16[8,32,128]{2,0,1:T(8,128)(2,1)} %collective-permute-done, bf16[8,32,128]{2,0,1:T(8,128)(2,1)} %collective-permute-done.1, ...), kind=kLoop, calls=%fused_computation.26 | loop fusion | flops 98304 | bytes 327683
  15.6 0.9 %copy_dynamic-update-slice_fusion = bf16[8,32,576]{2,0,1:T(8,128)(2,1)S(1)} fusion(bf16[8,32,576]{2,0,1:T(8,128)(2,1)S(1)} %select_dynamic-update-slice_fusion, bf16[8,32,64]{2,1,0:T(8,128)(2,1)} %param.8), kind=kLoop, calls=%fused_computation.24 | loop fusion | bytes 98304 | tf_op jit(solution)/shard_map/concatenate | solution.py:85
  16.5 0.6 %fusion.18 = (f32[4,64]{1,0:T(4,128)S(1)}, f32[4,64,512]{2,1,0:T(8,128)S(1)}) fusion(bf16[4,64,576]{2,1,0:T(8,128)(2,1)S(1)} %bitcast.20, bf16[4,512,576]{1,2,0:T(8,128)(2,1)S(1)} %copy-done.1, s32[4,64]{1,0:T(4,128)S(1)} %broadcast_add_fusion, s32[512]{0:T(512)S(1)} %iota_add_fusion), kind=kOutput, calls=%fused_computation.52 | convolution fusion | flops 151518976 | bytes 3182592 | tf_op jit(solution)/shard_map/sqc,skc->sqk/dot_general | solution.py:88
  17.1 0.3 fusion.4
  17.4 0.8 %fusion = f32[4,64,512]{2,1,0:T(8,128)S(1)} fusion(bf16[4,512,576]{1,2,0:T(8,128)(2,1)S(1)} %copy-done.2, f32[4,64,512]{2,1,0:T(8,128)S(1)} %get-tuple-element.24, f32[4,64]{1,0:T(4,128)S(1)} %get-tuple-element.23, s32[4,64]{1,0:T(4,128)S(1)} %broadcast_add_fusion, s32[512]{0:T(512)S(1)} %iota_add_fusion), kind=kOutput, calls=%fused_computation | convolution fusion | flops 134742016 | bytes 3151872 | tf_op jit(solution)/shard_map/sqk,skl->sql/dot_general | solution.py:99
  18.2 0.0 copy-start.3
  18.2 0.1 reshape.212
  18.4 0.1 collective-permute-start.3
  18.5 1.2 %collective-permute-start.4 = (f32[260,128]{1,0:T(8,128)S(1)}, f32[260,128]{1,0:T(8,128)S(1)}, u32[]{:S(2)}, u32[]{:S(2)}) collective-permute-start(f32[260,128]{1,0:T(8,128)S(1)} %get-tuple-element.21), channel_id=1, source_target_pairs={{0,8},{4,12},{8,0},{12,4},{1,9},{5,13},{9,1},{13,5},{2,10},{6,14},... | collective-permute-start | bytes 399368 | tf_op jit(solution)/shard_map/ppermute | solution.py:127
  19.7 2.3 %collective-permute-start.5 = (f32[260,128]{1,0:T(8,128)S(1)}, f32[260,128]{1,0:T(8,128)S(1)}, u32[]{:S(2)}, u32[]{:S(2)}) collective-permute-start(f32[260,128]{1,0:T(8,128)S(1)} %get-tuple-element.22), channel_id=1, source_target_pairs={{0,12},{4,0},{8,4},{12,8},{1,13},{5,1},{9,5},{13,9},{2,14},{6,2},{... | collective-permute-start | bytes 399368 | tf_op jit(solution)/shard_map/ppermute | solution.py:127
  22.0 2.8 %collective-permute-done.3 = f32[260,128]{1,0:T(8,128)S(1)} collective-permute-done((f32[260,128]{1,0:T(8,128)S(1)}, f32[260,128]{1,0:T(8,128)S(1)}, u32[]{:S(2)}, u32[]{:S(2)}) %collective-permute-start.3) | collective-permute-done | bytes 133152 | tf_op jit(solution)/shard_map/ppermute | solution.py:127
  24.8 0.1 squeeze.21
  24.9 0.1 squeeze.24
  24.9 4.9 %collective-permute-done.4 = f32[260,128]{1,0:T(8,128)S(1)} collective-permute-done((f32[260,128]{1,0:T(8,128)S(1)}, f32[260,128]{1,0:T(8,128)S(1)}, u32[]{:S(2)}, u32[]{:S(2)}) %collective-permute-start.4) | collective-permute-done | bytes 133152 | tf_op jit(solution)/shard_map/ppermute | solution.py:127
  29.9 0.1 squeeze.22
  30.0 0.1 squeeze.25
  30.0 0.0 collective-permute-done.5
  30.0 0.1 squeeze.23
  30.1 0.1 squeeze.26
  30.3 0.2 divide_convert_fusion
  30.5 0.4 convolution_bitcast_fusion
  30.9 3.8 %collective-permute-start.8 = (f32[8,32,128]{2,0,1:T(8,128)S(1)}, f32[8,32,128]{2,0,1:T(8,128)S(1)}, u32[]{:S(2)}, u32[]{:S(2)}) collective-permute-start(f32[8,32,128]{2,0,1:T(8,128)S(1)} %convolution_bitcast_fusion), channel_id=1, source_target_pairs={{0,12},{4,0},{8,4},{12,8},{1,13},{5,1},{9,5},{13,9},{2,14},{6,2},{... | collective-permute-start | bytes 393224 | tf_op jit(solution)/shard_map/ppermute | solution.py:139
  34.8 0.4 collective-permute-start.7
  35.2 1.6 %collective-permute-done.8 = f32[8,32,128]{2,0,1:T(8,128)S(1)} collective-permute-done((f32[8,32,128]{2,0,1:T(8,128)S(1)}, f32[8,32,128]{2,0,1:T(8,128)S(1)}, u32[]{:S(2)}, u32[]{:S(2)}) %collective-permute-start.8) | collective-permute-done | bytes 131104 | tf_op jit(solution)/shard_map/ppermute | solution.py:139
  36.7 9.6 %collective-permute-done.7 = f32[8,32,128]{2,0,1:T(8,128)S(1)} collective-permute-done((f32[8,32,128]{2,0,1:T(8,128)S(1)}, f32[8,32,128]{2,0,1:T(8,128)S(1)}, u32[]{:S(2)}, u32[]{:S(2)}) %collective-permute-start.7) | collective-permute-done | bytes 131104 | tf_op jit(solution)/shard_map/ppermute | solution.py:139
  46.3 0.7 %fusion.11.v_ref = bf16[8,4096]{1,0:T(8,128)(2,1)} fusion(f32[8,32,128]{2,0,1:T(8,128)S(1)} %collective-permute-done.8, f32[8,32,128]{2,0,1:T(8,128)S(1)} %collective-permute-done.7, f32[8,32,128]{2,0,1:T(8,128)S(1)} %convolution_bitcast_fusion, f32[8,32,128]{2,0,1:T(8,128)S(1)} %collective-permute-done.6), kind=kLoop, calls=%fused_computation.22 | loop fusion | flops 131072 | bytes 589824 | tf_op jit(solution)/shard_map/reshape | solution.py:144
  47.0 7.2 %shard_map.73 = f32[8,1792]{1,0:T(8,128)} custom-call(bf16[8,4096]{1,0:T(8,128)(2,1)} %fusion.11.v_ref, bf16[4096,1792]{1,0:T(8,128)(2,1)} %w_hbm.1), custom_call_target="tpu_custom_call" | custom-call | flops 117440512 | bytes 14802944 | tf_op jit(solution)/shard_map/pallas_call | solution.py:49
  54.2 0.9 %select_select_fusion.3 = f32[8,448]{1,0:T(8,128)S(1)} fusion(f32[8,1792]{1,0:T(8,128)} %shard_map.73, pred[]{:T(512)S(6)} %eq.154, pred[]{:T(512)S(6)} %eq.153, pred[]{:T(512)S(6)} %eq.152), kind=kLoop, calls=%fused_computation.30 | loop fusion | flops 10752 | bytes 71683 | tf_op jit(solution)/shard_map/jit(_where)/select_n | solution.py:23
  55.0 1.7 %collective-permute-start.11 = (f32[8,448]{1,0:T(8,128)S(1)}, f32[8,448]{1,0:T(8,128)S(1)}, u32[]{:S(2)}, u32[]{:S(2)}) collective-permute-start(f32[8,448]{1,0:T(8,128)S(1)} %select_select_fusion.3), channel_id=1, source_target_pairs={{0,3},{1,0},{2,1},{3,2},{4,7},{5,4},{6,5},{7,6},{8,11},{9,8},{10,9... | collective-permute-start | bytes 43016 | tf_op jit(solution)/shard_map/ppermute | solution.py:152
  56.7 0.9 %select_select_fusion.5 = (f32[8,448]{1,0:T(8,128)S(1)}, f32[8,448]{1,0:T(8,128)S(1)}) fusion(f32[8,1792]{1,0:T(8,128)} %shard_map.73, pred[]{:T(512)S(6)} %eq.148, pred[]{:T(512)S(6)} %eq.147, pred[]{:T(512)S(6)} %eq.146, pred[]{:T(512)S(6)} %eq.151, pred[]{:T(512)S(6)} %eq.150, pred[]{:T(512)S(6)} %eq.149), kind=kLoop, calls=%fused_computation.33 | loop fusion | flops 21504 | bytes 86022 | tf_op jit(solution)/shard_map/jit(_where)/select_n | solution.py:23
  57.6 1.1 %collective-permute-start.9 = (f32[8,448]{1,0:T(8,128)S(1)}, f32[8,448]{1,0:T(8,128)S(1)}, u32[]{:S(2)}, u32[]{:S(2)}) collective-permute-start(f32[8,448]{1,0:T(8,128)S(1)} %get-tuple-element.18), channel_id=1, source_target_pairs={{0,1},{1,2},{2,3},{3,0},{4,5},{5,6},{6,7},{7,4},{8,9},{9,10},{10,1... | collective-permute-start | bytes 43016 | tf_op jit(solution)/shard_map/ppermute | solution.py:152
  58.7 0.3 collective-permute-start.10
  59.0 0.3 collective-permute-done.11
  59.2 0.4 collective-permute-done.9
  59.6 1.9 %collective-permute-done.10 = f32[8,448]{1,0:T(8,128)S(1)} collective-permute-done((f32[8,448]{1,0:T(8,128)S(1)}, f32[8,448]{1,0:T(8,128)S(1)}, u32[]{:S(2)}, u32[]{:S(2)}) %collective-permute-start.10) | collective-permute-done | bytes 14368 | tf_op jit(solution)/shard_map/ppermute | solution.py:152
  61.5 1.5 %add_add_fusion = f32[8,448]{1,0:T(8,128)} fusion(f32[8,448]{1,0:T(8,128)S(1)} %collective-permute-done.11, f32[8,448]{1,0:T(8,128)S(1)} %collective-permute-done.10, f32[8,448]{1,0:T(8,128)S(1)} %collective-permute-done.9, f32[8,1792]{1,0:T(8,128)} %shard_map.73, pred[]{:T(512)S(6)} %eq.145, pred[]{:T(512)S(6)} %eq.144, pred[]{:T(512)S(6)} %eq.119), kind=kLoop, calls=%fused_computation.31 | loop fusion | flops 21504 | bytes 114691 | tf_op jit(solution)/shard_map/add | solution.py:152
  (23 shorter events, 0.3 us)
Async XLA Ops:
  0.0 1.2 %copy-start = (bf16[32,128,128]{2,1,0:T(8,128)(2,1)S(1)}, bf16[32,128,128]{2,1,0:T(8,128)(2,1)}, u32[]{:S(2)}) copy-start(bf16[32,128,128]{2,1,0:T(8,128)(2,1)} %param.11) | copy-start | bytes 3145732
  0.0 16.5 %copy-start.1 = (bf16[4,512,576]{1,2,0:T(8,128)(2,1)S(1)}, bf16[4,512,576]{1,2,0:T(8,128)(2,1)}, u32[]{:S(2)}) copy-start(bf16[4,512,576]{1,2,0:T(8,128)(2,1)} %param.9) | copy-start | bytes 7077892
  2.4 5.5 %collective-permute-start.2 = (bf16[8,32,128]{2,0,1:T(8,128)(2,1)S(1)}, bf16[8,32,128]{2,0,1:T(8,128)(2,1)S(1)}, u32[]{:S(2)}, u32[]{:S(2)}) collective-permute-start(bf16[8,32,128]{2,0,1:T(8,128)(2,1)S(1)} %fusion.3), channel_id=1, source_target_pairs={{0,12},{4,0},{8,4},{12,8},{1,13},{5,1},{9,5},{13,9},{2,14},{6,2},{... | collective-permute-start | bytes 196616 | tf_op jit(solution)/shard_map/ppermute | solution.py:79
  6.6 6.8 %collective-permute-start.1 = (bf16[8,32,128]{2,0,1:T(8,128)(2,1)S(1)}, bf16[8,32,128]{2,0,1:T(8,128)(2,1)}, u32[]{:S(2)}, u32[]{:S(2)}) collective-permute-start(bf16[8,32,128]{2,0,1:T(8,128)(2,1)S(1)} %fusion.3), channel_id=1, source_target_pairs={{0,8},{4,12},{8,0},{12,4},{1,9},{5,13},{9,1},{13,5},{2,10},{6,14},... | collective-permute-start | bytes 196616 | tf_op jit(solution)/shard_map/ppermute | solution.py:79
  6.6 6.8 %collective-permute-start = (bf16[8,32,128]{2,0,1:T(8,128)(2,1)S(1)}, bf16[8,32,128]{2,0,1:T(8,128)(2,1)}, u32[]{:S(2)}, u32[]{:S(2)}) collective-permute-start(bf16[8,32,128]{2,0,1:T(8,128)(2,1)S(1)} %fusion.3), channel_id=1, source_target_pairs={{0,4},{4,8},{8,12},{12,0},{1,5},{5,9},{9,13},{13,1},{2,6},{6,10},{... | collective-permute-start | bytes 196616 | tf_op jit(solution)/shard_map/ppermute | solution.py:79
  14.5 2.9 %copy-start.2 = (bf16[4,512,576]{1,2,0:T(8,128)(2,1)S(1)}, bf16[4,512,576]{1,2,0:T(8,128)(2,1)}, u32[]{:S(2)}) copy-start(bf16[4,512,576]{1,2,0:T(8,128)(2,1)} %param.9) | copy-start | bytes 7077892
  18.2 12.4 %copy-start.3 = (bf16[32,128,128]{2,1,0:T(8,128)(2,1)S(1)}, bf16[32,128,128]{2,1,0:T(8,128)(2,1)}, u32[]{:S(2)}) copy-start(bf16[32,128,128]{2,1,0:T(8,128)(2,1)} %param.12) | copy-start | bytes 3145732
  18.4 6.4 %collective-permute-start.3 = (f32[260,128]{1,0:T(8,128)S(1)}, f32[260,128]{1,0:T(8,128)S(1)}, u32[]{:S(2)}, u32[]{:S(2)}) collective-permute-start(f32[260,128]{1,0:T(8,128)S(1)} %get-tuple-element.20), channel_id=1, source_target_pairs={{0,4},{4,8},{8,12},{12,0},{1,5},{5,9},{9,13},{13,1},{2,6},{6,10},{... | collective-permute-start | bytes 399368 | tf_op jit(solution)/shard_map/ppermute | solution.py:127
  18.5 11.4 %collective-permute-start.4 = (f32[260,128]{1,0:T(8,128)S(1)}, f32[260,128]{1,0:T(8,128)S(1)}, u32[]{:S(2)}, u32[]{:S(2)}) collective-permute-start(f32[260,128]{1,0:T(8,128)S(1)} %get-tuple-element.21), channel_id=1, source_target_pairs={{0,8},{4,12},{8,0},{12,4},{1,9},{5,13},{9,1},{13,5},{2,10},{6,14},... | collective-permute-start | bytes 399368 | tf_op jit(solution)/shard_map/ppermute | solution.py:127
  19.7 10.4 %collective-permute-start.5 = (f32[260,128]{1,0:T(8,128)S(1)}, f32[260,128]{1,0:T(8,128)S(1)}, u32[]{:S(2)}, u32[]{:S(2)}) collective-permute-start(f32[260,128]{1,0:T(8,128)S(1)} %get-tuple-element.22), channel_id=1, source_target_pairs={{0,12},{4,0},{8,4},{12,8},{1,13},{5,1},{9,5},{13,9},{2,14},{6,2},{... | collective-permute-start | bytes 399368 | tf_op jit(solution)/shard_map/ppermute | solution.py:127
  30.9 5.8 %collective-permute-start.8 = (f32[8,32,128]{2,0,1:T(8,128)S(1)}, f32[8,32,128]{2,0,1:T(8,128)S(1)}, u32[]{:S(2)}, u32[]{:S(2)}) collective-permute-start(f32[8,32,128]{2,0,1:T(8,128)S(1)} %convolution_bitcast_fusion), channel_id=1, source_target_pairs={{0,12},{4,0},{8,4},{12,8},{1,13},{5,1},{9,5},{13,9},{2,14},{6,2},{... | collective-permute-start | bytes 393224 | tf_op jit(solution)/shard_map/ppermute | solution.py:139
  34.8 11.6 %collective-permute-start.7 = (f32[8,32,128]{2,0,1:T(8,128)S(1)}, f32[8,32,128]{2,0,1:T(8,128)S(1)}, u32[]{:S(2)}, u32[]{:S(2)}) collective-permute-start(f32[8,32,128]{2,0,1:T(8,128)S(1)} %convolution_bitcast_fusion), channel_id=1, source_target_pairs={{0,8},{4,12},{8,0},{12,4},{1,9},{5,13},{9,1},{13,5},{2,10},{6,14},... | collective-permute-start | bytes 393224 | tf_op jit(solution)/shard_map/ppermute | solution.py:139
  35.2 11.2 %collective-permute-start.6 = (f32[8,32,128]{2,0,1:T(8,128)S(1)}, f32[8,32,128]{2,0,1:T(8,128)S(1)}, u32[]{:S(2)}, u32[]{:S(2)}) collective-permute-start(f32[8,32,128]{2,0,1:T(8,128)S(1)} %convolution_bitcast_fusion), channel_id=1, source_target_pairs={{0,4},{4,8},{8,12},{12,0},{1,5},{5,9},{9,13},{13,1},{2,6},{6,10},{... | collective-permute-start | bytes 393224 | tf_op jit(solution)/shard_map/ppermute | solution.py:139
  55.0 4.2 %collective-permute-start.11 = (f32[8,448]{1,0:T(8,128)S(1)}, f32[8,448]{1,0:T(8,128)S(1)}, u32[]{:S(2)}, u32[]{:S(2)}) collective-permute-start(f32[8,448]{1,0:T(8,128)S(1)} %select_select_fusion.3), channel_id=1, source_target_pairs={{0,3},{1,0},{2,1},{3,2},{4,7},{5,4},{6,5},{7,6},{8,11},{9,8},{10,9... | collective-permute-start | bytes 43016 | tf_op jit(solution)/shard_map/ppermute | solution.py:152
  57.6 2.0 %collective-permute-start.9 = (f32[8,448]{1,0:T(8,128)S(1)}, f32[8,448]{1,0:T(8,128)S(1)}, u32[]{:S(2)}, u32[]{:S(2)}) collective-permute-start(f32[8,448]{1,0:T(8,128)S(1)} %get-tuple-element.18), channel_id=1, source_target_pairs={{0,1},{1,2},{2,3},{3,0},{4,5},{5,6},{6,7},{7,4},{8,9},{9,10},{10,1... | collective-permute-start | bytes 43016 | tf_op jit(solution)/shard_map/ppermute | solution.py:152
  58.7 2.8 %collective-permute-start.10 = (f32[8,448]{1,0:T(8,128)S(1)}, f32[8,448]{1,0:T(8,128)S(1)}, u32[]{:S(2)}, u32[]{:S(2)}) collective-permute-start(f32[8,448]{1,0:T(8,128)S(1)} %get-tuple-element.19), channel_id=1, source_target_pairs={{0,2},{1,3},{2,0},{3,1},{4,6},{5,7},{6,4},{7,5},{8,10},{9,11},{10,... | collective-permute-start | bytes 43016 | tf_op jit(solution)/shard_map/ppermute | solution.py:152

commit v4 on v2

--- a/solution.py
+++ b/solution.py
@@ -37,16 +37,27 @@
         received = [q_part] + [
             lax.ppermute(q_part, "ctx", shift_pairs(n_ctx, k)) for k in range(1, n_ctx)
         ]
-        slots = [pick((me_ctx - j) % n_ctx, received) for j in range(n_ctx)]
-        q_latent = jnp.concatenate(slots, axis=2)
+        source = (me_ctx - jnp.arange(n_ctx, dtype=jnp.int32)[None, None, :, None]) % n_ctx
+        q_slots = received[-1][:, :, None, :]
+        for k in range(n_ctx - 2, -1, -1):
+            q_slots = jnp.where(source == k, received[k][:, :, None, :], q_slots)
+        q_latent = q_slots.reshape(row_count, head_count, latent_width)
     else:
         q_latent = lax.all_gather(q_part, "ctx", axis=2, tiled=True)
-    query_rows = jnp.concatenate([q_latent, query_rope], axis=2).reshape(
-        seq_count, DRAFT * head_count, channels
+    q_rows = DRAFT * head_count
+    latent_scores = jnp.einsum(
+        "sqc,skc->sqk",
+        q_latent.reshape(seq_count, q_rows, latent_width),
+        kv_cache[:, :, :latent_width],
+        preferred_element_type=jnp.float32,
     )
-    logit_scores = jnp.einsum(
-        "sqc,skc->sqk", query_rows, kv_cache, preferred_element_type=jnp.float32
-    ) * (PLAIN_CHANNELS + ROTARY_CHANNELS) ** (-0.5)
+    rope_scores = jnp.einsum(
+        "sqc,skc->sqk",
+        query_rope.reshape(seq_count, q_rows, channels - latent_width),
+        kv_cache[:, :, latent_width:],
+        preferred_element_type=jnp.float32,
+    )
+    logit_scores = (latent_scores + rope_scores) * (PLAIN_CHANNELS + ROTARY_CHANNELS) ** (-0.5)
     position = me_ctx * ctx_rows + jnp.arange(ctx_rows, dtype=jnp.int32)
     draft_index = jnp.arange(DRAFT * head_count, dtype=jnp.int32) // head_count
     row_limit = lengths[:, None] - DRAFT + draft_index[None, :]
@@ -61,7 +72,6 @@
         kv_cache[:, :, :latent_width],
         preferred_element_type=jnp.float32,
     )
-    q_rows = DRAFT * head_count
     stats = jnp.stack([block_top, block_total]).reshape(-1, slice_width)
     sum_slices = [
         weighted[:, :, j * slice_width:(j + 1) * slice_width].reshape(-1, slice_width)

time: 60.6 us -> 57.6 us (0.950)
  waiting for transfers between devices: 27.1 us -> 21.4 us
  matrix products: 10.2 us -> 13.1 us
  other arithmetic: 4.27 us -> 2.22 us
  starting transfers between devices: 15.5 us -> 16.7 us
    ppermute x3, waiting for transfers between devices: 5.65 us -> 1.25 us  [per_device(): lax.ppermute(q_part, 'ctx', shift_pairs(n_ctx, k))]
    ppermute x3, waiting for transfers between devices: 11.2 us -> 7.61 us  [per_device(): lax.ppermute(value_part, 'ctx', shift_pairs(n_ctx, k))]
    dot_general x1 -> x2, matrix products: 0.63 us -> 3.53 us  [the longest x1 2.34 us: per_device(): jnp.einsum('sqc,skc->sqk', q_latent.reshape(seq_count, q_rows, latent_wid...]
    unnamed x4 -> x0, other arithmetic: 2.08 us -> none
    ppermute x3, waiting for transfers between devices: 7.75 us -> 9.39 us  [per_device(): lax.ppermute(packed_for((me_ctx + k) % n_ctx), 'ctx', shift_pairs(n_ctx, k))]
    ppermute x3, starting transfers between devices: 4.22 us -> 5.23 us  [per_device(): lax.ppermute(value_part, 'ctx', shift_pairs(n_ctx, k))]
    broadcast_in_dim x0 -> x11, local copies, waits for them, and re-layouts: none -> 0.96 us  [per_device(): q_slots = jnp.where(source == k, received[k][:, :, None, :], q_slots)]
    concatenate x2 -> x0, local copies, waits for them, and re-layouts: 0.92 us -> none  [per_device(): jnp.concatenate([q_latent, query_rope], axis=2)]
  transfers between devices with their start and end apart: 12 -> 12, of which waited for: 8 -> 8; matrix products, arithmetic and copies ran while one was open for 2% -> 5% of each run, Pallas kernels for 0% -> 0%
where the time goes in v4:
time: 57.6 us; the launch traced here: 56.5 us
  waiting for transfers between devices  21.4 us (37%)
  starting transfers between devices  16.7 us (29%)
  matrix products  13.1 us (23%)
  local copies, waits for them, and re-layouts  2.85 us (5%)
  other arithmetic  2.22 us (4%)
    ppermute x3, waiting for transfers between devices, per_device(): lax.ppermute(packed_for((me_ctx + k) % n_ctx), 'ctx', shift_pairs(n_ctx, k))  9.39 us
    ppermute x3, waiting for transfers between devices, per_device(): lax.ppermute(value_part, 'ctx', shift_pairs(n_ctx, k))  7.61 us
    dot_general x1, matrix products, per_device(): jnp.dot(values.reshape(row_count, -1), w_output, preferred_element_type=j...  7.17 us
    ppermute x3, starting transfers between devices, per_device(): lax.ppermute(q_part, 'ctx', shift_pairs(n_ctx, k))  5.51 us
    ppermute x3, starting transfers between devices, per_device(): lax.ppermute(value_part, 'ctx', shift_pairs(n_ctx, k))  5.23 us
    ppermute x3, starting transfers between devices, per_device(): lax.ppermute(packed_for((me_ctx + k) % n_ctx), 'ctx', shift_pairs(n_ctx, k))  3.68 us
    ppermute x3, waiting for transfers between devices, per_device(): lax.ppermute(pick((me_head + k) % n_head, col_slices), 'head', shift_pair...  3.15 us
    dot_general x1, matrix products, per_device(): jnp.einsum('sqc,skc->sqk', q_latent.reshape(seq_count, q_rows, latent_wid...  2.34 us
  transfers between devices with their start and end apart: 12, of which 8 were waited for; matrix products, arithmetic and copies ran while one was open for 5% of the time, Pallas kernels for 0%

profile of v4, /device:TPU:1, one launch (start us, length us, event | category | flops | bytes accessed | tf_op | source)
XLA Modules:
  0.0 56.5 jit_solution(18104556373095619026)
XLA Ops:
  0.0 1.2 %copy-done = bf16[32,128,128]{2,1,0:T(8,128)(2,1)S(1)} copy-done((bf16[32,128,128]{2,1,0:T(8,128)(2,1)S(1)}, bf16[32,128,128]{2,1,0:T(8,128)(2,1)}, u32[]{:S(2)}) %copy-start) | copy-done | bytes 1048600
  1.2 1.2 %fusion.13 = bf16[8,32,128]{2,0,1:T(8,128)(2,1)S(1)} fusion(bf16[32,128,128]{2,1,0:T(8,128)(2,1)S(1)} %copy-done, bf16[8,32,128]{2,1,0:T(8,128)(2,1)} %param.7), kind=kOutput, calls=%fused_computation.9 | convolution fusion | flops 8421376 | bytes 1179648 | tf_op jit(solution)/shard_map/rhn,hnl->rhl/dot_general | solution.py:33
  2.4 2.1 %collective-permute-start = (bf16[8,32,128]{2,0,1:T(8,128)(2,1)S(1)}, bf16[8,32,128]{2,0,1:T(8,128)(2,1)S(1)}, u32[]{:S(2)}, u32[]{:S(2)}) collective-permute-start(bf16[8,32,128]{2,0,1:T(8,128)(2,1)S(1)} %fusion.13), channel_id=1, source_target_pairs={{0,4},{4,8},{8,12},{12,0},{1,5},{5,9},{9,13},{13,1},{2,6},{6,10},{... | collective-permute-start | bytes 196616 | tf_op jit(solution)/shard_map/ppermute | solution.py:38
  4.6 2.3 %collective-permute-start.1 = (bf16[8,32,128]{2,0,1:T(8,128)(2,1)S(1)}, bf16[8,32,128]{2,0,1:T(8,128)(2,1)S(1)}, u32[]{:S(2)}, u32[]{:S(2)}) collective-permute-start(bf16[8,32,128]{2,0,1:T(8,128)(2,1)S(1)} %fusion.13), channel_id=1, source_target_pairs={{0,8},{4,12},{8,0},{12,4},{1,9},{5,13},{9,1},{13,5},{2,10},{6,14},... | collective-permute-start | bytes 196616 | tf_op jit(solution)/shard_map/ppermute | solution.py:38
  6.9 1.1 %collective-permute-start.2 = (bf16[8,32,128]{2,0,1:T(8,128)(2,1)S(1)}, bf16[8,32,128]{2,0,1:T(8,128)(2,1)S(1)}, u32[]{:S(2)}, u32[]{:S(2)}) collective-permute-start(bf16[8,32,128]{2,0,1:T(8,128)(2,1)S(1)} %fusion.13), channel_id=1, source_target_pairs={{0,12},{4,0},{8,4},{12,8},{1,13},{5,1},{9,5},{13,9},{2,14},{6,2},{... | collective-permute-start | bytes 196616 | tf_op jit(solution)/shard_map/ppermute | solution.py:38
  8.1 0.1 broadcast_bitcast_fusion
  8.1 0.1 broadcast_bitcast_fusion.1
  8.3 0.1 broadcast_in_dim.95
  8.4 0.1 broadcast_in_dim.96
  8.5 0.7 %broadcast_add_fusion.1 = s32[4]{0:T(128)S(1)} fusion(s32[4]{0:T(128)} %param.10), kind=kLoop, calls=%fused_computation.64 | loop fusion | flops 4 | bytes 32 | tf_op jit(solution)/shard_map/sub | solution.py:63
  9.1 0.1 broadcast_add_fusion
  9.2 1.2 %fusion.19 = f32[4,64,512]{2,1,0:T(8,128)S(1)} fusion(bf16[4,64,64]{2,1,0:T(8,128)(2,1)} %bitcast.34, bf16[4,512,576]{1,2,0:T(8,128)(2,1)} %param.9), kind=kOutput, calls=%fused_computation.15 | convolution fusion | flops 16777216 | bytes 851968 | tf_op jit(solution)/shard_map/sqc,skc->sqk/dot_general | solution.py:54
  10.5 0.1 broadcast_in_dim.100
  10.5 0.1 broadcast_in_dim.101
  10.7 1.2 %collective-permute-done.1 = bf16[8,32,128]{2,0,1:T(8,128)(2,1)S(1)} collective-permute-done((bf16[8,32,128]{2,0,1:T(8,128)(2,1)S(1)}, bf16[8,32,128]{2,0,1:T(8,128)(2,1)S(1)}, u32[]{:S(2)}, u32[]{:S(2)}) %collective-permute-start.1) | collective-permute-done | bytes 65568 | tf_op jit(solution)/shard_map/ppermute | solution.py:38
  11.9 0.1 broadcast_in_dim.105
  12.0 0.1 broadcast_in_dim.106
  12.2 0.1 broadcast_in_dim.107
  12.2 0.1 broadcast_in_dim.108
  12.4 2.3 %fusion.39 = (f32[4,64]{1,0:T(4,128)S(1)}, f32[4,64,512]{2,1,0:T(8,128)S(1)}) fusion(f32[4,64,512]{2,1,0:T(8,128)S(1)} %fusion.19, bf16[4,512,576]{1,2,0:T(8,128)(2,1)} %param.9, bf16[4,64,512]{2,1,0:T(8,128)(2,1)S(1)} %broadcast_in_dim.96, bf16[4,64,512]{2,1,0:T(8,128)(2,1)S(1)} %broadcast_in_dim.101, bf16[4,64,512]{2,1,0:T(8,128)(2,1)S(1)} %broadcast_in_dim.106, ...), kind=kOutput, calls=%fused_computation.69 | convolution fusion | flops 135266048 | bytes 4199936 | tf_op jit(solution)/shard_map/sqc,skc->sqk/dot_general | solution.py:48
  14.7 0.8 %fusion.2 = f32[4,64,512]{2,1,0:T(8,128)S(1)} fusion(bf16[4,512,576]{1,2,0:T(8,128)(2,1)S(1)} %copy-done.2, f32[4,64,512]{2,1,0:T(8,128)S(1)} %get-tuple-element.24, f32[4,64]{1,0:T(4,128)S(1)} %get-tuple-element.23, s32[4,64]{1,0:T(4,128)S(1)} %broadcast_add_fusion, s32[512]{0:T(512)S(1)} %iota_add_fusion), kind=kOutput, calls=%fused_computation.2 | convolution fusion | flops 134742016 | bytes 3151872 | tf_op jit(solution)/shard_map/sqk,skl->sql/dot_general | solution.py:69
  15.5 0.2 fusion.14
  15.8 0.1 reshape.253
  16.0 1.5 %collective-permute-start.3 = (f32[260,128]{1,0:T(8,128)S(1)}, f32[260,128]{1,0:T(8,128)S(1)}, u32[]{:S(2)}, u32[]{:S(2)}) collective-permute-start(f32[260,128]{1,0:T(8,128)S(1)} %get-tuple-element.20), channel_id=1, source_target_pairs={{0,4},{4,8},{8,12},{12,0},{1,5},{5,9},{9,13},{13,1},{2,6},{6,10},{... | collective-permute-start | bytes 399368 | tf_op jit(solution)/shard_map/ppermute | solution.py:96
  17.5 2.2 %collective-permute-start.5 = (f32[260,128]{1,0:T(8,128)S(1)}, f32[260,128]{1,0:T(8,128)S(1)}, u32[]{:S(2)}, u32[]{:S(2)}) collective-permute-start(f32[260,128]{1,0:T(8,128)S(1)} %get-tuple-element.22), channel_id=1, source_target_pairs={{0,12},{4,0},{8,4},{12,8},{1,13},{5,1},{9,5},{13,9},{2,14},{6,2},{... | collective-permute-start | bytes 399368 | tf_op jit(solution)/shard_map/ppermute | solution.py:96
  19.6 2.6 %collective-permute-done.3 = f32[260,128]{1,0:T(8,128)S(1)} collective-permute-done((f32[260,128]{1,0:T(8,128)S(1)}, f32[260,128]{1,0:T(8,128)S(1)}, u32[]{:S(2)}, u32[]{:S(2)}) %collective-permute-start.3) | collective-permute-done | bytes 133152 | tf_op jit(solution)/shard_map/ppermute | solution.py:96
  22.2 0.1 squeeze.21
  22.3 6.8 %collective-permute-done.4 = f32[260,128]{1,0:T(8,128)S(1)} collective-permute-done((f32[260,128]{1,0:T(8,128)S(1)}, f32[260,128]{1,0:T(8,128)S(1)}, u32[]{:S(2)}, u32[]{:S(2)}) %collective-permute-start.4) | collective-permute-done | bytes 133152 | tf_op jit(solution)/shard_map/ppermute | solution.py:96
  29.1 0.1 squeeze.22
  29.2 0.1 squeeze.23
  29.3 0.1 squeeze.24
  29.4 0.1 squeeze.25
  29.5 0.1 squeeze.26
  29.6 0.2 divide_convert_fusion
  29.9 0.4 convolution_bitcast_fusion
  30.3 3.1 %collective-permute-start.6 = (f32[8,32,128]{2,0,1:T(8,128)S(1)}, f32[8,32,128]{2,0,1:T(8,128)S(1)}, u32[]{:S(2)}, u32[]{:S(2)}) collective-permute-start(f32[8,32,128]{2,0,1:T(8,128)S(1)} %convolution_bitcast_fusion), channel_id=1, source_target_pairs={{0,4},{4,8},{8,12},{12,0},{1,5},{5,9},{9,13},{13,1},{2,6},{6,10},{... | collective-permute-start | bytes 393224 | tf_op jit(solution)/shard_map/ppermute | solution.py:108
  33.4 2.1 %collective-permute-start.8 = (f32[8,32,128]{2,0,1:T(8,128)S(1)}, f32[8,32,128]{2,0,1:T(8,128)S(1)}, u32[]{:S(2)}, u32[]{:S(2)}) collective-permute-start(f32[8,32,128]{2,0,1:T(8,128)S(1)} %convolution_bitcast_fusion), channel_id=1, source_target_pairs={{0,12},{4,0},{8,4},{12,8},{1,13},{5,1},{9,5},{13,9},{2,14},{6,2},{... | collective-permute-start | bytes 393224 | tf_op jit(solution)/shard_map/ppermute | solution.py:108
  35.5 1.0 %collective-permute-done.6 = f32[8,32,128]{2,0,1:T(8,128)S(1)} collective-permute-done((f32[8,32,128]{2,0,1:T(8,128)S(1)}, f32[8,32,128]{2,0,1:T(8,128)S(1)}, u32[]{:S(2)}, u32[]{:S(2)}) %collective-permute-start.6) | collective-permute-done | bytes 131104 | tf_op jit(solution)/shard_map/ppermute | solution.py:108
  36.5 6.6 %collective-permute-done.7 = f32[8,32,128]{2,0,1:T(8,128)S(1)} collective-permute-done((f32[8,32,128]{2,0,1:T(8,128)S(1)}, f32[8,32,128]{2,0,1:T(8,128)S(1)}, u32[]{:S(2)}, u32[]{:S(2)}) %collective-permute-start.7) | collective-permute-done | bytes 131104 | tf_op jit(solution)/shard_map/ppermute | solution.py:108
  43.1 7.2 %fusion.30 = f32[8,1792]{1,0:T(8,128)S(1)} fusion(bf16[4096,1792]{1,0:T(8,128)(2,1)} %param.13, f32[8,32,128]{2,0,1:T(8,128)S(1)} %collective-permute-done.8, f32[8,32,128]{2,0,1:T(8,128)S(1)} %collective-permute-done.7, f32[8,32,128]{2,0,1:T(8,128)S(1)} %convolution_bitcast_fusion, f32[8,32,128]{2,0,1:T(8,128)S(1)} %collective-permute-done.6), kind=kOutput, calls=%fused_computation.34 | convolution fusion | flops 117571584 | bytes 15261696 | tf_op jit(solution)/shard_map/dot_general | solution.py:113
  50.3 0.1 select_select_fusion.5
  50.3 0.5 collective-permute-start.10
  50.8 1.7 %collective-permute-start.9 = (f32[8,448]{1,0:T(8,128)S(1)}, f32[8,448]{1,0:T(8,128)S(1)}, u32[]{:S(2)}, u32[]{:S(2)}) collective-permute-start(f32[8,448]{1,0:T(8,128)S(1)} %get-tuple-element.18), channel_id=1, source_target_pairs={{0,1},{1,2},{2,3},{3,0},{4,5},{5,6},{6,7},{7,4},{8,9},{9,10},{10,1... | collective-permute-start | bytes 43016 | tf_op jit(solution)/shard_map/ppermute | solution.py:123
  52.6 0.1 select_select_fusion.3
  52.7 0.3 collective-permute-done.10
  53.0 0.5 collective-permute-done.9
  53.5 2.4 %collective-permute-done.11 = f32[8,448]{1,0:T(8,128)S(1)} collective-permute-done((f32[8,448]{1,0:T(8,128)S(1)}, f32[8,448]{1,0:T(8,128)S(1)}, u32[]{:S(2)}, u32[]{:S(2)}) %collective-permute-start.11) | collective-permute-done | bytes 14368 | tf_op jit(solution)/shard_map/ppermute | solution.py:123
  55.8 0.7 %add_add_fusion = f32[8,448]{1,0:T(8,128)} fusion(f32[8,448]{1,0:T(8,128)S(1)} %collective-permute-done.11, f32[8,448]{1,0:T(8,128)S(1)} %collective-permute-done.10, f32[8,448]{1,0:T(8,128)S(1)} %collective-permute-done.9, f32[8,1792]{1,0:T(8,128)S(1)} %fusion.30, pred[]{:T(512)S(6)} %eq.122, pred[]{:T(512)S(6)} %eq.121, pred[]{:T(512)S(6)} %eq.105), kind=kLoop, calls=%fused_computation.38 | loop fusion | flops 21504 | bytes 114691 | tf_op jit(solution)/shard_map/add | solution.py:123
  (32 shorter events, 0.3 us)
Async XLA Ops:
  0.0 1.2 %copy-start = (bf16[32,128,128]{2,1,0:T(8,128)(2,1)S(1)}, bf16[32,128,128]{2,1,0:T(8,128)(2,1)}, u32[]{:S(2)}) copy-start(bf16[32,128,128]{2,1,0:T(8,128)(2,1)} %param.11) | copy-start | bytes 3145732
  2.4 8.0 %collective-permute-start = (bf16[8,32,128]{2,0,1:T(8,128)(2,1)S(1)}, bf16[8,32,128]{2,0,1:T(8,128)(2,1)S(1)}, u32[]{:S(2)}, u32[]{:S(2)}) collective-permute-start(bf16[8,32,128]{2,0,1:T(8,128)(2,1)S(1)} %fusion.13), channel_id=1, source_target_pairs={{0,4},{4,8},{8,12},{12,0},{1,5},{5,9},{9,13},{13,1},{2,6},{6,10},{... | collective-permute-start | bytes 196616 | tf_op jit(solution)/shard_map/ppermute | solution.py:38
  4.6 7.3 %collective-permute-start.1 = (bf16[8,32,128]{2,0,1:T(8,128)(2,1)S(1)}, bf16[8,32,128]{2,0,1:T(8,128)(2,1)S(1)}, u32[]{:S(2)}, u32[]{:S(2)}) collective-permute-start(bf16[8,32,128]{2,0,1:T(8,128)(2,1)S(1)} %fusion.13), channel_id=1, source_target_pairs={{0,8},{4,12},{8,0},{12,4},{1,9},{5,13},{9,1},{13,5},{2,10},{6,14},... | collective-permute-start | bytes 196616 | tf_op jit(solution)/shard_map/ppermute | solution.py:38
  6.9 5.2 %collective-permute-start.2 = (bf16[8,32,128]{2,0,1:T(8,128)(2,1)S(1)}, bf16[8,32,128]{2,0,1:T(8,128)(2,1)S(1)}, u32[]{:S(2)}, u32[]{:S(2)}) collective-permute-start(bf16[8,32,128]{2,0,1:T(8,128)(2,1)S(1)} %fusion.13), channel_id=1, source_target_pairs={{0,12},{4,0},{8,4},{12,8},{1,13},{5,1},{9,5},{13,9},{2,14},{6,2},{... | collective-permute-start | bytes 196616 | tf_op jit(solution)/shard_map/ppermute | solution.py:38
  12.4 2.4 %copy-start.2 = (bf16[4,512,576]{1,2,0:T(8,128)(2,1)S(1)}, bf16[4,512,576]{1,2,0:T(8,128)(2,1)}, u32[]{:S(2)}) copy-start(bf16[4,512,576]{1,2,0:T(8,128)(2,1)} %param.9) | copy-start | bytes 7077892
  15.5 14.4 %copy-start.1 = (bf16[32,128,128]{2,1,0:T(8,128)(2,1)S(1)}, bf16[32,128,128]{2,1,0:T(8,128)(2,1)}, u32[]{:S(2)}) copy-start(bf16[32,128,128]{2,1,0:T(8,128)(2,1)} %param.12) | copy-start | bytes 3145732
  16.0 6.3 %collective-permute-start.3 = (f32[260,128]{1,0:T(8,128)S(1)}, f32[260,128]{1,0:T(8,128)S(1)}, u32[]{:S(2)}, u32[]{:S(2)}) collective-permute-start(f32[260,128]{1,0:T(8,128)S(1)} %get-tuple-element.20), channel_id=1, source_target_pairs={{0,4},{4,8},{8,12},{12,0},{1,5},{5,9},{9,13},{13,1},{2,6},{6,10},{... | collective-permute-start | bytes 399368 | tf_op jit(solution)/shard_map/ppermute | solution.py:96
  17.5 11.6 %collective-permute-start.4 = (f32[260,128]{1,0:T(8,128)S(1)}, f32[260,128]{1,0:T(8,128)S(1)}, u32[]{:S(2)}, u32[]{:S(2)}) collective-permute-start(f32[260,128]{1,0:T(8,128)S(1)} %get-tuple-element.21), channel_id=1, source_target_pairs={{0,8},{4,12},{8,0},{12,4},{1,9},{5,13},{9,1},{13,5},{2,10},{6,14},... | collective-permute-start | bytes 399368 | tf_op jit(solution)/shard_map/ppermute | solution.py:96
  17.5 11.7 %collective-permute-start.5 = (f32[260,128]{1,0:T(8,128)S(1)}, f32[260,128]{1,0:T(8,128)S(1)}, u32[]{:S(2)}, u32[]{:S(2)}) collective-permute-start(f32[260,128]{1,0:T(8,128)S(1)} %get-tuple-element.22), channel_id=1, source_target_pairs={{0,12},{4,0},{8,4},{12,8},{1,13},{5,1},{9,5},{13,9},{2,14},{6,2},{... | collective-permute-start | bytes 399368 | tf_op jit(solution)/shard_map/ppermute | solution.py:96
  30.3 6.3 %collective-permute-start.6 = (f32[8,32,128]{2,0,1:T(8,128)S(1)}, f32[8,32,128]{2,0,1:T(8,128)S(1)}, u32[]{:S(2)}, u32[]{:S(2)}) collective-permute-start(f32[8,32,128]{2,0,1:T(8,128)S(1)} %convolution_bitcast_fusion), channel_id=1, source_target_pairs={{0,4},{4,8},{8,12},{12,0},{1,5},{5,9},{9,13},{13,1},{2,6},{6,10},{... | collective-permute-start | bytes 393224 | tf_op jit(solution)/shard_map/ppermute | solution.py:108
  33.4 9.7 %collective-permute-start.7 = (f32[8,32,128]{2,0,1:T(8,128)S(1)}, f32[8,32,128]{2,0,1:T(8,128)S(1)}, u32[]{:S(2)}, u32[]{:S(2)}) collective-permute-start(f32[8,32,128]{2,0,1:T(8,128)S(1)} %convolution_bitcast_fusion), channel_id=1, source_target_pairs={{0,8},{4,12},{8,0},{12,4},{1,9},{5,13},{9,1},{13,5},{2,10},{6,14},... | collective-permute-start | bytes 393224 | tf_op jit(solution)/shard_map/ppermute | solution.py:108
  33.4 9.7 %collective-permute-start.8 = (f32[8,32,128]{2,0,1:T(8,128)S(1)}, f32[8,32,128]{2,0,1:T(8,128)S(1)}, u32[]{:S(2)}, u32[]{:S(2)}) collective-permute-start(f32[8,32,128]{2,0,1:T(8,128)S(1)} %convolution_bitcast_fusion), channel_id=1, source_target_pairs={{0,12},{4,0},{8,4},{12,8},{1,13},{5,1},{9,5},{13,9},{2,14},{6,2},{... | collective-permute-start | bytes 393224 | tf_op jit(solution)/shard_map/ppermute | solution.py:108
  50.3 2.6 %collective-permute-start.10 = (f32[8,448]{1,0:T(8,128)S(1)}, f32[8,448]{1,0:T(8,128)S(1)}, u32[]{:S(2)}, u32[]{:S(2)}) collective-permute-start(f32[8,448]{1,0:T(8,128)S(1)} %get-tuple-element.19), channel_id=1, source_target_pairs={{0,2},{1,3},{2,0},{3,1},{4,6},{5,7},{6,4},{7,5},{8,10},{9,11},{10,... | collective-permute-start | bytes 43016 | tf_op jit(solution)/shard_map/ppermute | solution.py:123
  50.8 2.6 %collective-permute-start.9 = (f32[8,448]{1,0:T(8,128)S(1)}, f32[8,448]{1,0:T(8,128)S(1)}, u32[]{:S(2)}, u32[]{:S(2)}) collective-permute-start(f32[8,448]{1,0:T(8,128)S(1)} %get-tuple-element.18), channel_id=1, source_target_pairs={{0,1},{1,2},{2,3},{3,0},{4,5},{5,6},{6,7},{7,4},{8,9},{9,10},{10,1... | collective-permute-start | bytes 43016 | tf_op jit(solution)/shard_map/ppermute | solution.py:123
  52.7 3.2 %collective-permute-start.11 = (f32[8,448]{1,0:T(8,128)S(1)}, f32[8,448]{1,0:T(8,128)S(1)}, u32[]{:S(2)}, u32[]{:S(2)}) collective-permute-start(f32[8,448]{1,0:T(8,128)S(1)} %select_select_fusion.3), channel_id=1, source_target_pairs={{0,3},{1,0},{2,1},{3,2},{4,7},{5,4},{6,5},{7,6},{8,11},{9,8},{10,9... | collective-permute-start | bytes 43016 | tf_op jit(solution)/shard_map/ppermute | solution.py:123

commit v5 on v4

--- a/solution.py
+++ b/solution.py
@@ -78,13 +78,30 @@
         for j in range(n_ctx)
     ]
 
+    def to_bf16_grid(x):
+        return lax.reduce_precision(x, exponent_bits=8, mantissa_bits=7)
+
+    hi = to_bf16_grid(stats)
+    mid = to_bf16_grid(stats - hi)
+    stats_hi = hi.astype(jnp.bfloat16)
+    stats_mid = mid.astype(jnp.bfloat16)
+    stats_lo = ((stats - hi) - mid).astype(jnp.bfloat16)
+    stat_rows = stats.shape[0]
+
     def packed_for(target):
-        return jnp.concatenate([pick(target, sum_slices), stats], axis=0)
+        return jnp.concatenate(
+            [pick(target, sum_slices).astype(jnp.bfloat16), stats_hi, stats_mid, stats_lo], axis=0
+        )
+
+    def unpack(p):
+        split = seq_count * q_rows
+        f = p[split:].astype(jnp.float32)
+        whole = (f[:stat_rows] + f[stat_rows:2 * stat_rows]) + f[2 * stat_rows:]
+        return p[:split].astype(jnp.float32), whole
 
     def combine_blocks(parts):
-        split = seq_count * q_rows
-        sums = [p[:split].reshape(seq_count, q_rows, slice_width) for p in parts]
-        st = [p[split:].reshape(2, seq_count, q_rows) for p in parts]
+        sums = [a.reshape(seq_count, q_rows, slice_width) for a, _ in parts]
+        st = [b.reshape(2, seq_count, q_rows) for _, b in parts]
         row_top = functools.reduce(jnp.maximum, [t[0] for t in st])
         factors = [jnp.exp(t[0] - row_top) for t in st]
         total = sum(f * t[1] for f, t in zip(factors, st))
@@ -92,20 +109,23 @@
         return (acc / total[:, :, None]).astype(jnp.bfloat16)
 
     if small_ctx:
-        parts = [packed_for(me_ctx)] + [
-            lax.ppermute(packed_for((me_ctx + k) % n_ctx), "ctx", shift_pairs(n_ctx, k))
+        parts = [(pick(me_ctx, sum_slices), stats)] + [
+            unpack(lax.ppermute(packed_for((me_ctx + k) % n_ctx), "ctx", shift_pairs(n_ctx, k)))
             for k in range(1, n_ctx)
         ]
     else:
         packed = jnp.stack([jnp.concatenate([s, stats], axis=0) for s in sum_slices])
         got = lax.all_to_all(packed, "ctx", 0, 0, tiled=False)
-        parts = [got[j] for j in range(n_ctx)]
+        split = seq_count * q_rows
+        parts = [(got[j][:split], got[j][split:]) for j in range(n_ctx)]
     latent_out = combine_blocks(parts).reshape(row_count, head_count, slice_width)
 
     value_part = jnp.einsum("rhl,hlv->rhv", latent_out, w_value, preferred_element_type=jnp.float32)
     if small_ctx:
+        sent = value_part.astype(jnp.bfloat16)
         received = [value_part] + [
-            lax.ppermute(value_part, "ctx", shift_pairs(n_ctx, k)) for k in range(1, n_ctx)
+            lax.ppermute(sent, "ctx", shift_pairs(n_ctx, k)).astype(jnp.float32)
+            for k in range(1, n_ctx)
         ]
         values = sum(received).astype(jnp.bfloat16)
     else:

time: 57.6 us -> 47.6 us (0.83); the launches traced: 56.5 us -> 47.4 us
  waiting for transfers between devices: 21.4 us -> 14.5 us
  starting transfers between devices: 16.7 us -> 15.2 us
  local copies, waits for them, and re-layouts: 2.85 us -> 1.62 us
    ppermute x3, waiting for transfers between devices: 9.39 us -> 5.24 us  [per_device(): lax.ppermute(packed_for((me_ctx + k) % n_ctx), 'ctx', shift_pairs(n_ctx, k))]
    ppermute x3, waiting for transfers between devices: 7.61 us -> 4.87 us  [per_device(): lax.ppermute(sent, 'ctx', shift_pairs(n_ctx, k)).astype(jnp.float32)]
    ppermute x3, starting transfers between devices: 5.23 us -> 3.77 us  [per_device(): lax.ppermute(sent, 'ctx', shift_pairs(n_ctx, k)).astype(jnp.float32)]
    unnamed x6 -> x4, local copies, waits for them, and re-layouts: 1.24 us -> 0.01 us
  transfers between devices with their start and end apart: 12 -> 12, of which waited for: 8 -> 8; matrix products, arithmetic and copies ran while one was open for 5% -> 6% of each run, Pallas kernels for 0% -> 0%
where the time goes in v5:
time: 47.6 us; the launch traced here: 47.4 us
  starting transfers between devices  15.2 us (32%)
  waiting for transfers between devices  14.5 us (30%)
  matrix products  13.5 us (28%)
  other arithmetic  2.26 us (5%)
  local copies, waits for them, and re-layouts  1.62 us (3%)
    dot_general x1, matrix products, per_device(): jnp.dot(values.reshape(row_count, -1), w_output, preferred_element_type=j...  7.17 us
    ppermute x3, starting transfers between devices, per_device(): lax.ppermute(q_part, 'ctx', shift_pairs(n_ctx, k))  5.51 us
    ppermute x3, waiting for transfers between devices, per_device(): lax.ppermute(packed_for((me_ctx + k) % n_ctx), 'ctx', shift_pairs(n_ctx, k))  5.24 us
    ppermute x3, waiting for transfers between devices, per_device(): lax.ppermute(sent, 'ctx', shift_pairs(n_ctx, k)).astype(jnp.float32)  4.87 us
    ppermute x3, starting transfers between devices, per_device(): lax.ppermute(sent, 'ctx', shift_pairs(n_ctx, k)).astype(jnp.float32)  3.77 us
    ppermute x3, starting transfers between devices, per_device(): lax.ppermute(packed_for((me_ctx + k) % n_ctx), 'ctx', shift_pairs(n_ctx, k))  3.68 us
    ppermute x3, waiting for transfers between devices, per_device(): lax.ppermute(pick((me_head + k) % n_head, col_slices), 'head', shift_pair...  3.15 us
    dot_general x1, matrix products, per_device(): jnp.einsum('sqc,skc->sqk', q_latent.reshape(seq_count, q_rows, latent_wid...  2.32 us
  transfers between devices with their start and end apart: 12, of which 8 were waited for; matrix products, arithmetic and copies ran while one was open for 6% of the time, Pallas kernels for 0%

profile of v5, /device:TPU:1, one launch (start us, length us, event | category | flops | bytes accessed | tf_op | source)
XLA Modules:
  0.0 47.4 jit_solution(6545621628215055617)
XLA Ops:
  0.0 1.7 %fusion.13 = bf16[8,32,128]{2,0,1:T(8,128)(2,1)S(1)} fusion(bf16[32,128,128]{2,1,0:T(8,128)(2,1)} %param.11, bf16[8,32,128]{2,1,0:T(8,128)(2,1)} %param.7), kind=kOutput, calls=%fused_computation.9 | convolution fusion | flops 8421376 | bytes 1179648 | tf_op jit(solution)/shard_map/rhn,hnl->rhl/dot_general | solution.py:33
  1.7 2.1 %collective-permute-start = (bf16[8,32,128]{2,0,1:T(8,128)(2,1)S(1)}, bf16[8,32,128]{2,0,1:T(8,128)(2,1)S(1)}, u32[]{:S(2)}, u32[]{:S(2)}) collective-permute-start(bf16[8,32,128]{2,0,1:T(8,128)(2,1)S(1)} %fusion.13), channel_id=1, source_target_pairs={{0,4},{4,8},{8,12},{12,0},{1,5},{5,9},{9,13},{13,1},{2,6},{6,10},{... | collective-permute-start | bytes 196616 | tf_op jit(solution)/shard_map/ppermute | solution.py:38
  3.8 2.3 %collective-permute-start.1 = (bf16[8,32,128]{2,0,1:T(8,128)(2,1)S(1)}, bf16[8,32,128]{2,0,1:T(8,128)(2,1)S(1)}, u32[]{:S(2)}, u32[]{:S(2)}) collective-permute-start(bf16[8,32,128]{2,0,1:T(8,128)(2,1)S(1)} %fusion.13), channel_id=1, source_target_pairs={{0,8},{4,12},{8,0},{12,4},{1,9},{5,13},{9,1},{13,5},{2,10},{6,14},... | collective-permute-start | bytes 196616 | tf_op jit(solution)/shard_map/ppermute | solution.py:38
  6.1 1.1 %collective-permute-start.2 = (bf16[8,32,128]{2,0,1:T(8,128)(2,1)S(1)}, bf16[8,32,128]{2,0,1:T(8,128)(2,1)S(1)}, u32[]{:S(2)}, u32[]{:S(2)}) collective-permute-start(bf16[8,32,128]{2,0,1:T(8,128)(2,1)S(1)} %fusion.13), channel_id=1, source_target_pairs={{0,12},{4,0},{8,4},{12,8},{1,13},{5,1},{9,5},{13,9},{2,14},{6,2},{... | collective-permute-start | bytes 196616 | tf_op jit(solution)/shard_map/ppermute | solution.py:38
  7.3 0.1 broadcast_bitcast_fusion
  7.4 0.1 broadcast_bitcast_fusion.1
  7.5 0.1 broadcast_bitcast_fusion.2
  7.5 0.1 broadcast_in_dim.95
  7.6 0.1 broadcast_in_dim.96
  7.7 0.7 %broadcast_add_fusion.1 = s32[4]{0:T(128)S(1)} fusion(s32[4]{0:T(128)} %param.10), kind=kLoop, calls=%fused_computation.91 | loop fusion | flops 4 | bytes 32 | tf_op jit(solution)/shard_map/sub | solution.py:63
  8.4 0.1 broadcast_add_fusion
  8.5 1.2 %fusion.19 = f32[4,64,512]{2,1,0:T(8,128)S(1)} fusion(bf16[4,64,64]{2,1,0:T(8,128)(2,1)} %bitcast.37, bf16[4,512,576]{1,2,0:T(8,128)(2,1)} %param.9), kind=kOutput, calls=%fused_computation.15 | convolution fusion | flops 16777216 | bytes 851968 | tf_op jit(solution)/shard_map/sqc,skc->sqk/dot_general | solution.py:54
  9.7 0.1 broadcast_in_dim.100
  9.8 0.1 broadcast_in_dim.101
  9.9 1.3 %collective-permute-done.1 = bf16[8,32,128]{2,0,1:T(8,128)(2,1)S(1)} collective-permute-done((bf16[8,32,128]{2,0,1:T(8,128)(2,1)S(1)}, bf16[8,32,128]{2,0,1:T(8,128)(2,1)S(1)}, u32[]{:S(2)}, u32[]{:S(2)}) %collective-permute-start.1) | collective-permute-done | bytes 65568 | tf_op jit(solution)/shard_map/ppermute | solution.py:38
  11.2 0.1 broadcast_in_dim.105
  11.3 0.1 broadcast_in_dim.106
  11.4 0.1 broadcast_in_dim.107
  11.5 0.1 broadcast_in_dim.108
  11.6 2.3 %fusion.45 = (f32[4,64]{1,0:T(4,128)S(1)}, f32[4,64,512]{2,1,0:T(8,128)S(1)}) fusion(f32[4,64,512]{2,1,0:T(8,128)S(1)} %fusion.19, bf16[4,512,576]{1,2,0:T(8,128)(2,1)} %param.9, bf16[4,64,512]{2,1,0:T(8,128)(2,1)S(1)} %broadcast_in_dim.96, bf16[4,64,512]{2,1,0:T(8,128)(2,1)S(1)} %broadcast_in_dim.101, bf16[4,64,512]{2,1,0:T(8,128)(2,1)S(1)} %broadcast_in_dim.106, ...), kind=kOutput, calls=%fused_computation.96 | convolution fusion | flops 135266048 | bytes 4199936 | tf_op jit(solution)/shard_map/sqc,skc->sqk/dot_general | solution.py:48
  13.9 0.8 %fusion.2 = f32[4,64,512]{2,1,0:T(8,128)S(1)} fusion(bf16[4,512,576]{1,2,0:T(8,128)(2,1)S(1)} %copy-done.1, f32[4,64,512]{2,1,0:T(8,128)S(1)} %get-tuple-element.27, f32[4,64]{1,0:T(4,128)S(1)} %get-tuple-element.26, s32[4,64]{1,0:T(4,128)S(1)} %broadcast_add_fusion, s32[512]{0:T(512)S(1)} %iota_add_fusion), kind=kOutput, calls=%fused_computation.2 | convolution fusion | flops 134742016 | bytes 3151872 | tf_op jit(solution)/shard_map/sqk,skl->sql/dot_general | solution.py:69
  14.7 0.3 fusion.14
  15.0 0.1 reshape.265
  15.2 1.5 %collective-permute-start.3 = (bf16[268,128]{1,0:T(8,128)(2,1)S(1)}, bf16[268,128]{1,0:T(8,128)(2,1)S(1)}, u32[]{:S(2)}, u32[]{:S(2)}) collective-permute-start(bf16[268,128]{1,0:T(8,128)(2,1)S(1)} %get-tuple-element.14), channel_id=1, source_target_pairs={{0,4},{4,8},{8,12},{12,0},{1,5},{5,9},{9,13},{13,1},{2,6},{6,10},{... | collective-permute-start | bytes 205832 | tf_op jit(solution)/shard_map/ppermute | solution.py:113
  16.7 2.2 %collective-permute-start.5 = (bf16[268,128]{1,0:T(8,128)(2,1)S(1)}, bf16[268,128]{1,0:T(8,128)(2,1)S(1)}, u32[]{:S(2)}, u32[]{:S(2)}) collective-permute-start(bf16[268,128]{1,0:T(8,128)(2,1)S(1)} %get-tuple-element.16), channel_id=1, source_target_pairs={{0,12},{4,0},{8,4},{12,8},{1,13},{5,1},{9,5},{13,9},{2,14},{6,2},{... | collective-permute-start | bytes 205832 | tf_op jit(solution)/shard_map/ppermute | solution.py:113
  18.9 1.4 %collective-permute-done.3 = bf16[268,128]{1,0:T(8,128)(2,1)S(1)} collective-permute-done((bf16[268,128]{1,0:T(8,128)(2,1)S(1)}, bf16[268,128]{1,0:T(8,128)(2,1)S(1)}, u32[]{:S(2)}, u32[]{:S(2)}) %collective-permute-start.3) | collective-permute-done | bytes 68640 | tf_op jit(solution)/shard_map/ppermute | solution.py:113
  20.3 3.8 %collective-permute-done.4 = bf16[268,128]{1,0:T(8,128)(2,1)S(1)} collective-permute-done((bf16[268,128]{1,0:T(8,128)(2,1)S(1)}, bf16[268,128]{1,0:T(8,128)(2,1)S(1)}, u32[]{:S(2)}, u32[]{:S(2)}) %collective-permute-start.4) | collective-permute-done | bytes 68640 | tf_op jit(solution)/shard_map/ppermute | solution.py:113
  24.1 0.1 squeeze.21
  24.2 0.1 squeeze.22
  24.3 0.1 squeeze.23
  24.4 0.1 squeeze.24
  24.5 0.1 squeeze.25
  24.6 0.1 squeeze.26
  24.7 0.2 fusion.31
  25.0 0.4 fusion.46
  25.4 1.6 %collective-permute-start.6 = (bf16[8,32,128]{2,0,1:T(8,128)(2,1)S(1)}, bf16[8,32,128]{2,0,1:T(8,128)(2,1)S(1)}, u32[]{:S(2)}, u32[]{:S(2)}) collective-permute-start(bf16[8,32,128]{2,0,1:T(8,128)(2,1)S(1)} %get-tuple-element.28), channel_id=1, source_target_pairs={{0,4},{4,8},{8,12},{12,0},{1,5},{5,9},{9,13},{13,1},{2,6},{6,10},{... | collective-permute-start | bytes 196616 | tf_op jit(solution)/shard_map/ppermute | solution.py:127
  27.0 2.2 %collective-permute-start.8 = (bf16[8,32,128]{2,0,1:T(8,128)(2,1)S(1)}, bf16[8,32,128]{2,0,1:T(8,128)(2,1)S(1)}, u32[]{:S(2)}, u32[]{:S(2)}) collective-permute-start(bf16[8,32,128]{2,0,1:T(8,128)(2,1)S(1)} %get-tuple-element.28), channel_id=1, source_target_pairs={{0,12},{4,0},{8,4},{12,8},{1,13},{5,1},{9,5},{13,9},{2,14},{6,2},{... | collective-permute-start | bytes 196616 | tf_op jit(solution)/shard_map/ppermute | solution.py:127
  29.1 1.2 %collective-permute-done.6 = bf16[8,32,128]{2,0,1:T(8,128)(2,1)S(1)} collective-permute-done((bf16[8,32,128]{2,0,1:T(8,128)(2,1)S(1)}, bf16[8,32,128]{2,0,1:T(8,128)(2,1)S(1)}, u32[]{:S(2)}, u32[]{:S(2)}) %collective-permute-start.6) | collective-permute-done | bytes 65568 | tf_op jit(solution)/shard_map/ppermute | solution.py:127
  30.3 3.7 %collective-permute-done.7 = bf16[8,32,128]{2,0,1:T(8,128)(2,1)S(1)} collective-permute-done((bf16[8,32,128]{2,0,1:T(8,128)(2,1)S(1)}, bf16[8,32,128]{2,0,1:T(8,128)(2,1)S(1)}, u32[]{:S(2)}, u32[]{:S(2)}) %collective-permute-start.7) | collective-permute-done | bytes 65568 | tf_op jit(solution)/shard_map/ppermute | solution.py:127
  34.0 7.2 %fusion.35 = f32[8,1792]{1,0:T(8,128)S(1)} fusion(bf16[4096,1792]{1,0:T(8,128)(2,1)} %param.13, bf16[8,32,128]{2,0,1:T(8,128)(2,1)S(1)} %collective-permute-done.8, bf16[8,32,128]{2,0,1:T(8,128)(2,1)S(1)} %collective-permute-done.7, f32[8,32,128]{2,0,1:T(8,128)S(1)} %get-tuple-element.29, bf16[8,32,128]{2,0,1:T(8,128)(2,1)S(1)} %collective-permute-done.6), kind=kOutput, calls=%fused_computation.47 | convolution fusion | flops 117669888 | bytes 15065088 | tf_op jit(solution)/shard_map/dot_general | solution.py:133
  41.2 0.1 select_select_fusion.2
  41.3 0.0 collective-permute-start.10
  41.3 2.2 %collective-permute-start.9 = (f32[8,448]{1,0:T(8,128)S(1)}, f32[8,448]{1,0:T(8,128)S(1)}, u32[]{:S(2)}, u32[]{:S(2)}) collective-permute-start(f32[8,448]{1,0:T(8,128)S(1)} %get-tuple-element.12), channel_id=1, source_target_pairs={{0,1},{1,2},{2,3},{3,0},{4,5},{5,6},{6,7},{7,4},{8,9},{9,10},{10,1... | collective-permute-start | bytes 43016 | tf_op jit(solution)/shard_map/ppermute | solution.py:143
  43.5 0.1 select_select_fusion
  43.6 0.3 collective-permute-done.10
  43.9 0.5 %collective-permute-done.9 = f32[8,448]{1,0:T(8,128)S(1)} collective-permute-done((f32[8,448]{1,0:T(8,128)S(1)}, f32[8,448]{1,0:T(8,128)S(1)}, u32[]{:S(2)}, u32[]{:S(2)}) %collective-permute-start.9) | collective-permute-done | bytes 14368 | tf_op jit(solution)/shard_map/ppermute | solution.py:143
  44.4 2.4 %collective-permute-done.11 = f32[8,448]{1,0:T(8,128)S(1)} collective-permute-done((f32[8,448]{1,0:T(8,128)S(1)}, f32[8,448]{1,0:T(8,128)S(1)}, u32[]{:S(2)}, u32[]{:S(2)}) %collective-permute-start.11) | collective-permute-done | bytes 14368 | tf_op jit(solution)/shard_map/ppermute | solution.py:143
  46.7 0.7 %add_add_fusion = f32[8,448]{1,0:T(8,128)} fusion(f32[8,448]{1,0:T(8,128)S(1)} %collective-permute-done.11, f32[8,448]{1,0:T(8,128)S(1)} %collective-permute-done.10, f32[8,448]{1,0:T(8,128)S(1)} %collective-permute-done.9, f32[8,1792]{1,0:T(8,128)S(1)} %fusion.35, pred[]{:T(512)S(6)} %eq.122, pred[]{:T(512)S(6)} %eq.121, pred[]{:T(512)S(6)} %eq.105), kind=kLoop, calls=%fused_computation.51 | loop fusion | flops 21504 | bytes 114691 | tf_op jit(solution)/shard_map/add | solution.py:143
  (37 shorter events, 0.3 us)
Async XLA Ops:
  0.0 25.0 %copy-start = (bf16[32,128,128]{2,1,0:T(8,128)(2,1)S(1)}, bf16[32,128,128]{2,1,0:T(8,128)(2,1)}, u32[]{:S(2)}) copy-start(bf16[32,128,128]{2,1,0:T(8,128)(2,1)} %param.12) | copy-start | bytes 3145732
  1.7 8.0 %collective-permute-start = (bf16[8,32,128]{2,0,1:T(8,128)(2,1)S(1)}, bf16[8,32,128]{2,0,1:T(8,128)(2,1)S(1)}, u32[]{:S(2)}, u32[]{:S(2)}) collective-permute-start(bf16[8,32,128]{2,0,1:T(8,128)(2,1)S(1)} %fusion.13), channel_id=1, source_target_pairs={{0,4},{4,8},{8,12},{12,0},{1,5},{5,9},{9,13},{13,1},{2,6},{6,10},{... | collective-permute-start | bytes 196616 | tf_op jit(solution)/shard_map/ppermute | solution.py:38
  3.8 7.3 %collective-permute-start.1 = (bf16[8,32,128]{2,0,1:T(8,128)(2,1)S(1)}, bf16[8,32,128]{2,0,1:T(8,128)(2,1)S(1)}, u32[]{:S(2)}, u32[]{:S(2)}) collective-permute-start(bf16[8,32,128]{2,0,1:T(8,128)(2,1)S(1)} %fusion.13), channel_id=1, source_target_pairs={{0,8},{4,12},{8,0},{12,4},{1,9},{5,13},{9,1},{13,5},{2,10},{6,14},... | collective-permute-start | bytes 196616 | tf_op jit(solution)/shard_map/ppermute | solution.py:38
  6.1 5.2 %collective-permute-start.2 = (bf16[8,32,128]{2,0,1:T(8,128)(2,1)S(1)}, bf16[8,32,128]{2,0,1:T(8,128)(2,1)S(1)}, u32[]{:S(2)}, u32[]{:S(2)}) collective-permute-start(bf16[8,32,128]{2,0,1:T(8,128)(2,1)S(1)} %fusion.13), channel_id=1, source_target_pairs={{0,12},{4,0},{8,4},{12,8},{1,13},{5,1},{9,5},{13,9},{2,14},{6,2},{... | collective-permute-start | bytes 196616 | tf_op jit(solution)/shard_map/ppermute | solution.py:38
  11.6 2.3 %copy-start.1 = (bf16[4,512,576]{1,2,0:T(8,128)(2,1)S(1)}, bf16[4,512,576]{1,2,0:T(8,128)(2,1)}, u32[]{:S(2)}) copy-start(bf16[4,512,576]{1,2,0:T(8,128)(2,1)} %param.9) | copy-start | bytes 7077892
  15.2 5.1 %collective-permute-start.3 = (bf16[268,128]{1,0:T(8,128)(2,1)S(1)}, bf16[268,128]{1,0:T(8,128)(2,1)S(1)}, u32[]{:S(2)}, u32[]{:S(2)}) collective-permute-start(bf16[268,128]{1,0:T(8,128)(2,1)S(1)} %get-tuple-element.14), channel_id=1, source_target_pairs={{0,4},{4,8},{8,12},{12,0},{1,5},{5,9},{9,13},{13,1},{2,6},{6,10},{... | collective-permute-start | bytes 205832 | tf_op jit(solution)/shard_map/ppermute | solution.py:113
  16.7 7.4 %collective-permute-start.4 = (bf16[268,128]{1,0:T(8,128)(2,1)S(1)}, bf16[268,128]{1,0:T(8,128)(2,1)S(1)}, u32[]{:S(2)}, u32[]{:S(2)}) collective-permute-start(bf16[268,128]{1,0:T(8,128)(2,1)S(1)} %get-tuple-element.15), channel_id=1, source_target_pairs={{0,8},{4,12},{8,0},{12,4},{1,9},{5,13},{9,1},{13,5},{2,10},{6,14},... | collective-permute-start | bytes 205832 | tf_op jit(solution)/shard_map/ppermute | solution.py:113
  16.7 7.6 %collective-permute-start.5 = (bf16[268,128]{1,0:T(8,128)(2,1)S(1)}, bf16[268,128]{1,0:T(8,128)(2,1)S(1)}, u32[]{:S(2)}, u32[]{:S(2)}) collective-permute-start(bf16[268,128]{1,0:T(8,128)(2,1)S(1)} %get-tuple-element.16), channel_id=1, source_target_pairs={{0,12},{4,0},{8,4},{12,8},{1,13},{5,1},{9,5},{13,9},{2,14},{6,2},{... | collective-permute-start | bytes 205832 | tf_op jit(solution)/shard_map/ppermute | solution.py:113
  25.4 5.0 %collective-permute-start.6 = (bf16[8,32,128]{2,0,1:T(8,128)(2,1)S(1)}, bf16[8,32,128]{2,0,1:T(8,128)(2,1)S(1)}, u32[]{:S(2)}, u32[]{:S(2)}) collective-permute-start(bf16[8,32,128]{2,0,1:T(8,128)(2,1)S(1)} %get-tuple-element.28), channel_id=1, source_target_pairs={{0,4},{4,8},{8,12},{12,0},{1,5},{5,9},{9,13},{13,1},{2,6},{6,10},{... | collective-permute-start | bytes 196616 | tf_op jit(solution)/shard_map/ppermute | solution.py:127
  27.0 7.0 %collective-permute-start.7 = (bf16[8,32,128]{2,0,1:T(8,128)(2,1)S(1)}, bf16[8,32,128]{2,0,1:T(8,128)(2,1)S(1)}, u32[]{:S(2)}, u32[]{:S(2)}) collective-permute-start(bf16[8,32,128]{2,0,1:T(8,128)(2,1)S(1)} %get-tuple-element.28), channel_id=1, source_target_pairs={{0,8},{4,12},{8,0},{12,4},{1,9},{5,13},{9,1},{13,5},{2,10},{6,14},... | collective-permute-start | bytes 196616 | tf_op jit(solution)/shard_map/ppermute | solution.py:127
  27.0 7.0 %collective-permute-start.8 = (bf16[8,32,128]{2,0,1:T(8,128)(2,1)S(1)}, bf16[8,32,128]{2,0,1:T(8,128)(2,1)S(1)}, u32[]{:S(2)}, u32[]{:S(2)}) collective-permute-start(bf16[8,32,128]{2,0,1:T(8,128)(2,1)S(1)} %get-tuple-element.28), channel_id=1, source_target_pairs={{0,12},{4,0},{8,4},{12,8},{1,13},{5,1},{9,5},{13,9},{2,14},{6,2},{... | collective-permute-start | bytes 196616 | tf_op jit(solution)/shard_map/ppermute | solution.py:127
  41.3 2.6 %collective-permute-start.10 = (f32[8,448]{1,0:T(8,128)S(1)}, f32[8,448]{1,0:T(8,128)S(1)}, u32[]{:S(2)}, u32[]{:S(2)}) collective-permute-start(f32[8,448]{1,0:T(8,128)S(1)} %get-tuple-element.13), channel_id=1, source_target_pairs={{0,2},{1,3},{2,0},{3,1},{4,6},{5,7},{6,4},{7,5},{8,10},{9,11},{10,... | collective-permute-start | bytes 43016 | tf_op jit(solution)/shard_map/ppermute | solution.py:143
  41.3 3.1 %collective-permute-start.9 = (f32[8,448]{1,0:T(8,128)S(1)}, f32[8,448]{1,0:T(8,128)S(1)}, u32[]{:S(2)}, u32[]{:S(2)}) collective-permute-start(f32[8,448]{1,0:T(8,128)S(1)} %get-tuple-element.12), channel_id=1, source_target_pairs={{0,1},{1,2},{2,3},{3,0},{4,5},{5,6},{6,7},{7,4},{8,9},{9,10},{10,1... | collective-permute-start | bytes 43016 | tf_op jit(solution)/shard_map/ppermute | solution.py:143
  43.6 3.2 %collective-permute-start.11 = (f32[8,448]{1,0:T(8,128)S(1)}, f32[8,448]{1,0:T(8,128)S(1)}, u32[]{:S(2)}, u32[]{:S(2)}) collective-permute-start(f32[8,448]{1,0:T(8,128)S(1)} %select_select_fusion), channel_id=1, source_target_pairs={{0,3},{1,0},{2,1},{3,2},{4,7},{5,4},{6,5},{7,6},{8,11},{9,8},{10,9... | collective-permute-start | bytes 43016 | tf_op jit(solution)/shard_map/ppermute | solution.py:143

commit v6 on v5

--- a/solution.py
+++ b/solution.py
@@ -122,17 +122,27 @@
 
     value_part = jnp.einsum("rhl,hlv->rhv", latent_out, w_value, preferred_element_type=jnp.float32)
     if small_ctx:
-        sent = value_part.astype(jnp.bfloat16)
-        received = [value_part] + [
-            lax.ppermute(sent, "ctx", shift_pairs(n_ctx, k)).astype(jnp.float32)
-            for k in range(1, n_ctx)
-        ]
-        values = sum(received).astype(jnp.bfloat16)
+        halves = 2 if head_count % 2 == 0 else 1
+        span = head_count // halves
+        vdim = value_part.shape[2]
+        partial_value = 0
+        for i in range(halves):
+            own = value_part[:, i * span:(i + 1) * span]
+            sent = own.astype(jnp.bfloat16)
+            received = [own] + [
+                lax.ppermute(sent, "ctx", shift_pairs(n_ctx, k)).astype(jnp.float32)
+                for k in range(1, n_ctx)
+            ]
+            values = sum(received).astype(jnp.bfloat16)
+            rows = w_output[i * span * vdim:(i + 1) * span * vdim]
+            partial_value = partial_value + jnp.dot(
+                values.reshape(row_count, -1), rows, preferred_element_type=jnp.float32
+            )
     else:
         values = lax.psum(value_part, "ctx").astype(jnp.bfloat16)
-    partial_value = jnp.dot(
-        values.reshape(row_count, -1), w_output, preferred_element_type=jnp.float32
-    )
+        partial_value = jnp.dot(
+            values.reshape(row_count, -1), w_output, preferred_element_type=jnp.float32
+        )
     if n_head > PERMUTE_MAX:
         return lax.psum_scatter(partial_value, "head", scatter_dimension=1, tiled=True)
     me_head = lax.axis_index("head")

time: 47.6 us -> 51 us (1.071)
  starting transfers between devices: 15.2 us -> 20.4 us
  waiting for transfers between devices: 14.5 us -> 10.7 us
  local copies, waits for them, and re-layouts: 1.62 us -> 2.86 us
  matrix products: 13.5 us -> 14.2 us
    ppermute x3 -> x6, waiting for transfers between devices: 4.87 us -> 1.02 us  [per_device(): lax.ppermute(sent, 'ctx', shift_pairs(n_ctx, k)).astype(jnp.float32)]
    ppermute x3 -> x6, starting transfers between devices: 3.77 us -> 7.28 us  [per_device(): lax.ppermute(sent, 'ctx', shift_pairs(n_ctx, k)).astype(jnp.float32)]
    ppermute x3, starting transfers between devices: 2.22 us -> 3.96 us  [per_device(): lax.ppermute(pick((me_head + k) % n_head, col_slices), 'head', shift_pair...]
    unnamed x4 -> x6, local copies, waits for them, and re-layouts: 0.01 us -> 1.24 us
    dot_general x1 -> x2, matrix products: 7.17 us -> 8.27 us  [per_device(): jnp.dot(values.reshape(row_count, -1), rows, preferred_element_type=jnp.f...]
  transfers between devices with their start and end apart: 12 -> 15, of which waited for: 8 -> 6; matrix products, arithmetic and copies ran while one was open for 6% -> 14% of each run, Pallas kernels for 0% -> 0%
where the time goes in v6:
time: 51 us; the launch traced here: 50.7 us
  starting transfers between devices  20.4 us (40%)
  matrix products  14.2 us (28%)
  waiting for transfers between devices  10.7 us (21%)
  local copies, waits for them, and re-layouts  2.86 us (6%)
  other arithmetic  2.26 us (4%)
    dot_general x2, matrix products, per_device(): jnp.dot(values.reshape(row_count, -1), rows, preferred_element_type=jnp.f...  8.27 us
    ppermute x6, starting transfers between devices, per_device(): lax.ppermute(sent, 'ctx', shift_pairs(n_ctx, k)).astype(jnp.float32)  7.28 us
    ppermute x3, starting transfers between devices, per_device(): lax.ppermute(q_part, 'ctx', shift_pairs(n_ctx, k))  5.51 us
    ppermute x3, waiting for transfers between devices, per_device(): lax.ppermute(packed_for((me_ctx + k) % n_ctx), 'ctx', shift_pairs(n_ctx, k))  5.24 us
    ppermute x3, starting transfers between devices, per_device(): lax.ppermute(pick((me_head + k) % n_head, col_slices), 'head', shift_pair...  3.96 us
    ppermute x3, starting transfers between devices, per_device(): lax.ppermute(packed_for((me_ctx + k) % n_ctx), 'ctx', shift_pairs(n_ctx, k))  3.68 us
    ppermute x3, waiting for transfers between devices, per_device(): lax.ppermute(pick((me_head + k) % n_head, col_slices), 'head', shift_pair...  3.15 us
    dot_general x1, matrix products, per_device(): jnp.einsum('sqc,skc->sqk', q_latent.reshape(seq_count, q_rows, latent_wid...  2.34 us
  transfers between devices with their start and end apart: 15, of which 6 were waited for; matrix products, arithmetic and copies ran while one was open for 14% of the time, Pallas kernels for 0%

profile of v6, /device:TPU:1, one launch (start us, length us, event | category | flops | bytes accessed | tf_op | source)
XLA Modules:
  0.0 50.7 jit_solution(15582545418574287800)
XLA Ops:
  0.0 1.2 %copy-done = bf16[32,128,128]{2,1,0:T(8,128)(2,1)S(1)} copy-done((bf16[32,128,128]{2,1,0:T(8,128)(2,1)S(1)}, bf16[32,128,128]{2,1,0:T(8,128)(2,1)}, u32[]{:S(2)}) %copy-start) | copy-done | bytes 1048600
  1.2 1.2 %fusion.20 = bf16[8,32,128]{2,0,1:T(8,128)(2,1)S(1)} fusion(bf16[32,128,128]{2,1,0:T(8,128)(2,1)S(1)} %copy-done, bf16[8,32,128]{2,1,0:T(8,128)(2,1)} %param.7), kind=kOutput, calls=%fused_computation.14 | convolution fusion | flops 8421376 | bytes 1179648 | tf_op jit(solution)/shard_map/rhn,hnl->rhl/dot_general | solution.py:33
  2.4 2.1 %collective-permute-start = (bf16[8,32,128]{2,0,1:T(8,128)(2,1)S(1)}, bf16[8,32,128]{2,0,1:T(8,128)(2,1)S(1)}, u32[]{:S(2)}, u32[]{:S(2)}) collective-permute-start(bf16[8,32,128]{2,0,1:T(8,128)(2,1)S(1)} %fusion.20), channel_id=1, source_target_pairs={{0,4},{4,8},{8,12},{12,0},{1,5},{5,9},{9,13},{13,1},{2,6},{6,10},{... | collective-permute-start | bytes 196616 | tf_op jit(solution)/shard_map/ppermute | solution.py:38
  4.6 2.3 %collective-permute-start.1 = (bf16[8,32,128]{2,0,1:T(8,128)(2,1)S(1)}, bf16[8,32,128]{2,0,1:T(8,128)(2,1)S(1)}, u32[]{:S(2)}, u32[]{:S(2)}) collective-permute-start(bf16[8,32,128]{2,0,1:T(8,128)(2,1)S(1)} %fusion.20), channel_id=1, source_target_pairs={{0,8},{4,12},{8,0},{12,4},{1,9},{5,13},{9,1},{13,5},{2,10},{6,14},... | collective-permute-start | bytes 196616 | tf_op jit(solution)/shard_map/ppermute | solution.py:38
  6.9 1.1 %collective-permute-start.2 = (bf16[8,32,128]{2,0,1:T(8,128)(2,1)S(1)}, bf16[8,32,128]{2,0,1:T(8,128)(2,1)S(1)}, u32[]{:S(2)}, u32[]{:S(2)}) collective-permute-start(bf16[8,32,128]{2,0,1:T(8,128)(2,1)S(1)} %fusion.20), channel_id=1, source_target_pairs={{0,12},{4,0},{8,4},{12,8},{1,13},{5,1},{9,5},{13,9},{2,14},{6,2},{... | collective-permute-start | bytes 196616 | tf_op jit(solution)/shard_map/ppermute | solution.py:38
  8.1 0.1 broadcast_bitcast_fusion
  8.1 0.1 broadcast_bitcast_fusion.1
  8.3 0.1 broadcast_in_dim.95
  8.4 0.1 broadcast_in_dim.96
  8.5 0.7 %broadcast_add_fusion.1 = s32[4]{0:T(128)S(1)} fusion(s32[4]{0:T(128)} %param.10), kind=kLoop, calls=%fused_computation.99 | loop fusion | flops 4 | bytes 32 | tf_op jit(solution)/shard_map/sub | solution.py:63
  9.1 0.1 broadcast_add_fusion
  9.2 1.2 %fusion.26 = f32[4,64,512]{2,1,0:T(8,128)S(1)} fusion(bf16[4,64,64]{2,1,0:T(8,128)(2,1)} %bitcast.39, bf16[4,512,576]{1,2,0:T(8,128)(2,1)} %param.9), kind=kOutput, calls=%fused_computation.20 | convolution fusion | flops 16777216 | bytes 851968 | tf_op jit(solution)/shard_map/sqc,skc->sqk/dot_general | solution.py:54
  10.5 0.1 broadcast_in_dim.100
  10.5 0.1 broadcast_in_dim.101
  10.7 1.2 %collective-permute-done.1 = bf16[8,32,128]{2,0,1:T(8,128)(2,1)S(1)} collective-permute-done((bf16[8,32,128]{2,0,1:T(8,128)(2,1)S(1)}, bf16[8,32,128]{2,0,1:T(8,128)(2,1)S(1)}, u32[]{:S(2)}, u32[]{:S(2)}) %collective-permute-start.1) | collective-permute-done | bytes 65568 | tf_op jit(solution)/shard_map/ppermute | solution.py:38
  11.9 0.1 broadcast_in_dim.105
  12.0 0.1 broadcast_in_dim.106
  12.2 0.1 broadcast_in_dim.107
  12.2 0.1 broadcast_in_dim.108
  12.4 2.3 %fusion.54 = (f32[4,64]{1,0:T(4,128)S(1)}, f32[4,64,512]{2,1,0:T(8,128)S(1)}) fusion(f32[4,64,512]{2,1,0:T(8,128)S(1)} %fusion.26, bf16[4,512,576]{1,2,0:T(8,128)(2,1)} %param.9, bf16[4,64,512]{2,1,0:T(8,128)(2,1)S(1)} %broadcast_in_dim.96, bf16[4,64,512]{2,1,0:T(8,128)(2,1)S(1)} %broadcast_in_dim.101, bf16[4,64,512]{2,1,0:T(8,128)(2,1)S(1)} %broadcast_in_dim.106, ...), kind=kOutput, calls=%fused_computation.105 | convolution fusion | flops 135266048 | bytes 4199936 | tf_op jit(solution)/shard_map/sqc,skc->sqk/dot_general | solution.py:48
  14.7 0.8 %fusion.9 = f32[4,64,512]{2,1,0:T(8,128)S(1)} fusion(bf16[4,512,576]{1,2,0:T(8,128)(2,1)S(1)} %copy-done.2, f32[4,64,512]{2,1,0:T(8,128)S(1)} %get-tuple-element.29, f32[4,64]{1,0:T(4,128)S(1)} %get-tuple-element.28, s32[4,64]{1,0:T(4,128)S(1)} %broadcast_add_fusion, s32[512]{0:T(512)S(1)} %iota_add_fusion), kind=kOutput, calls=%fused_computation.7 | convolution fusion | flops 134742016 | bytes 3151872 | tf_op jit(solution)/shard_map/sqk,skl->sql/dot_general | solution.py:69
  15.5 0.3 fusion.21
  15.8 0.1 reshape.268
  16.0 1.5 %collective-permute-start.3 = (bf16[268,128]{1,0:T(8,128)(2,1)S(1)}, bf16[268,128]{1,0:T(8,128)(2,1)S(1)}, u32[]{:S(2)}, u32[]{:S(2)}) collective-permute-start(bf16[268,128]{1,0:T(8,128)(2,1)S(1)} %get-tuple-element.16), channel_id=1, source_target_pairs={{0,4},{4,8},{8,12},{12,0},{1,5},{5,9},{9,13},{13,1},{2,6},{6,10},{... | collective-permute-start | bytes 205832 | tf_op jit(solution)/shard_map/ppermute | solution.py:113
  17.5 2.2 %collective-permute-start.5 = (bf16[268,128]{1,0:T(8,128)(2,1)S(1)}, bf16[268,128]{1,0:T(8,128)(2,1)S(1)}, u32[]{:S(2)}, u32[]{:S(2)}) collective-permute-start(bf16[268,128]{1,0:T(8,128)(2,1)S(1)} %get-tuple-element.18), channel_id=1, source_target_pairs={{0,12},{4,0},{8,4},{12,8},{1,13},{5,1},{9,5},{13,9},{2,14},{6,2},{... | collective-permute-start | bytes 205832 | tf_op jit(solution)/shard_map/ppermute | solution.py:113
  19.6 1.4 %collective-permute-done.3 = bf16[268,128]{1,0:T(8,128)(2,1)S(1)} collective-permute-done((bf16[268,128]{1,0:T(8,128)(2,1)S(1)}, bf16[268,128]{1,0:T(8,128)(2,1)S(1)}, u32[]{:S(2)}, u32[]{:S(2)}) %collective-permute-start.3) | collective-permute-done | bytes 68640 | tf_op jit(solution)/shard_map/ppermute | solution.py:113
  21.1 3.8 %collective-permute-done.4 = bf16[268,128]{1,0:T(8,128)(2,1)S(1)} collective-permute-done((bf16[268,128]{1,0:T(8,128)(2,1)S(1)}, bf16[268,128]{1,0:T(8,128)(2,1)S(1)}, u32[]{:S(2)}, u32[]{:S(2)}) %collective-permute-start.4) | collective-permute-done | bytes 68640 | tf_op jit(solution)/shard_map/ppermute | solution.py:113
  24.9 0.1 squeeze.21
  25.0 0.1 squeeze.22
  25.1 0.1 squeeze.23
  25.2 0.1 squeeze.24
  25.3 0.1 squeeze.25
  25.4 0.1 squeeze.26
  25.5 0.2 fusion.38
  25.8 0.4 convolution_bitcast_fusion
  26.2 0.6 %collective-permute-start.10 = (bf16[8,16,128]{2,0,1:T(8,128)(2,1)S(1)}, bf16[8,16,128]{2,0,1:T(8,128)(2,1)S(1)}, u32[]{:S(2)}, u32[]{:S(2)}) collective-permute-start(bf16[8,16,128]{2,0,1:T(8,128)(2,1)S(1)} %get-tuple-element.13), channel_id=1, source_target_pairs={{0,8},{4,12},{8,0},{12,4},{1,9},{5,13},{9,1},{13,5},{2,10},{6,14},... | collective-permute-start | bytes 98312 | tf_op jit(solution)/shard_map/ppermute | solution.py:133
  26.8 3.1 %collective-permute-start.11 = (bf16[8,16,128]{2,0,1:T(8,128)(2,1)S(1)}, bf16[8,16,128]{2,0,1:T(8,128)(2,1)S(1)}, u32[]{:S(2)}, u32[]{:S(2)}) collective-permute-start(bf16[8,16,128]{2,0,1:T(8,128)(2,1)S(1)} %get-tuple-element.13), channel_id=1, source_target_pairs={{0,12},{4,0},{8,4},{12,8},{1,13},{5,1},{9,5},{13,9},{2,14},{6,2},{... | collective-permute-start | bytes 98312 | tf_op jit(solution)/shard_map/ppermute | solution.py:133
  29.9 3.5 %collective-permute-start.7 = (bf16[8,16,128]{2,0,1:T(8,128)(2,1)S(1)}, bf16[8,16,128]{2,0,1:T(8,128)(2,1)S(1)}, u32[]{:S(2)}, u32[]{:S(2)}) collective-permute-start(bf16[8,16,128]{2,0,1:T(8,128)(2,1)S(1)} %get-tuple-element.12), channel_id=1, source_target_pairs={{0,8},{4,12},{8,0},{12,4},{1,9},{5,13},{9,1},{13,5},{2,10},{6,14},... | collective-permute-start | bytes 98312 | tf_op jit(solution)/shard_map/ppermute | solution.py:133
  33.5 1.0 %collective-permute-done.9 = bf16[8,16,128]{2,0,1:T(8,128)(2,1)S(1)} collective-permute-done((bf16[8,16,128]{2,0,1:T(8,128)(2,1)S(1)}, bf16[8,16,128]{2,0,1:T(8,128)(2,1)S(1)}, u32[]{:S(2)}, u32[]{:S(2)}) %collective-permute-start.9) | collective-permute-done | bytes 32800 | tf_op jit(solution)/shard_map/ppermute | solution.py:133
  34.5 4.1 %fusion = f32[8,1792]{1,0:T(8,128)S(1)} fusion(bf16[4096,1792]{1,0:T(8,128)(2,1)} %param.13, bf16[8,16,128]{2,0,1:T(8,128)(2,1)S(1)} %collective-permute-done.11, bf16[8,16,128]{2,0,1:T(8,128)(2,1)S(1)} %collective-permute-done.10, bf16[8,16,128]{2,0,1:T(8,128)(2,1)S(1)} %collective-permute-done.9, f32[8,32,128]{2,0,1:T(8,128)S(1)} %convolution_bitcast_fusion), kind=kOutput, calls=%fused_computation | convolution fusion | flops 58834944 | bytes 7561216 | tf_op jit(solution)/shard_map/dot_general | solution.py:138
  38.6 4.1 %fusion.4 = f32[8,1792]{1,0:T(8,128)S(1)} fusion(f32[8,1792]{1,0:T(8,128)S(1)} %fusion, bf16[4096,1792]{1,0:T(8,128)(2,1)} %param.13, bf16[8,16,128]{2,0,1:T(8,128)(2,1)S(1)} %collective-permute-done.8, bf16[8,16,128]{2,0,1:T(8,128)(2,1)S(1)} %collective-permute-done.7, bf16[8,16,128]{2,0,1:T(8,128)(2,1)S(1)} %collective-permute-done.6, ...), kind=kOutput, calls=%fused_computation.4 | convolution fusion | flops 58849280 | bytes 7618560 | tf_op jit(solution)/shard_map/dot_general | solution.py:138
  42.8 0.1 select_select_fusion.2
  42.8 2.6 %collective-permute-start.12 = (f32[8,448]{1,0:T(8,128)S(1)}, f32[8,448]{1,0:T(8,128)S(1)}, u32[]{:S(2)}, u32[]{:S(2)}) collective-permute-start(f32[8,448]{1,0:T(8,128)S(1)} %get-tuple-element.14), channel_id=1, source_target_pairs={{0,1},{1,2},{2,3},{3,0},{4,5},{5,6},{6,7},{7,4},{8,9},{9,10},{10,1... | collective-permute-start | bytes 43016 | tf_op jit(solution)/shard_map/ppermute | solution.py:153
  45.5 1.3 %collective-permute-start.13 = (f32[8,448]{1,0:T(8,128)S(1)}, f32[8,448]{1,0:T(8,128)S(1)}, u32[]{:S(2)}, u32[]{:S(2)}) collective-permute-start(f32[8,448]{1,0:T(8,128)S(1)} %get-tuple-element.15), channel_id=1, source_target_pairs={{0,2},{1,3},{2,0},{3,1},{4,6},{5,7},{6,4},{7,5},{8,10},{9,11},{10,... | collective-permute-start | bytes 43016 | tf_op jit(solution)/shard_map/ppermute | solution.py:153
  46.8 0.1 select_select_fusion
  46.9 1.3 %collective-permute-done.13 = f32[8,448]{1,0:T(8,128)S(1)} collective-permute-done((f32[8,448]{1,0:T(8,128)S(1)}, f32[8,448]{1,0:T(8,128)S(1)}, u32[]{:S(2)}, u32[]{:S(2)}) %collective-permute-start.13) | collective-permute-done | bytes 14368 | tf_op jit(solution)/shard_map/ppermute | solution.py:153
  48.2 1.8 %collective-permute-done.14 = f32[8,448]{1,0:T(8,128)S(1)} collective-permute-done((f32[8,448]{1,0:T(8,128)S(1)}, f32[8,448]{1,0:T(8,128)S(1)}, u32[]{:S(2)}, u32[]{:S(2)}) %collective-permute-start.14) | collective-permute-done | bytes 14368 | tf_op jit(solution)/shard_map/ppermute | solution.py:153
  50.0 0.7 %add_add_fusion = f32[8,448]{1,0:T(8,128)} fusion(f32[8,448]{1,0:T(8,128)S(1)} %collective-permute-done.14, f32[8,448]{1,0:T(8,128)S(1)} %collective-permute-done.13, f32[8,448]{1,0:T(8,128)S(1)} %collective-permute-done.12, f32[8,1792]{1,0:T(8,128)S(1)} %fusion.4, pred[]{:T(512)S(6)} %eq.122, pred[]{:T(512)S(6)} %eq.121, pred[]{:T(512)S(6)} %eq.105), kind=kLoop, calls=%fused_computation.59 | loop fusion | flops 21504 | bytes 114691 | tf_op jit(solution)/shard_map/add | solution.py:153
  (47 shorter events, 0.4 us)
Async XLA Ops:
  0.0 1.2 %copy-start = (bf16[32,128,128]{2,1,0:T(8,128)(2,1)S(1)}, bf16[32,128,128]{2,1,0:T(8,128)(2,1)}, u32[]{:S(2)}) copy-start(bf16[32,128,128]{2,1,0:T(8,128)(2,1)} %param.11) | copy-start | bytes 3145732
  2.4 8.0 %collective-permute-start = (bf16[8,32,128]{2,0,1:T(8,128)(2,1)S(1)}, bf16[8,32,128]{2,0,1:T(8,128)(2,1)S(1)}, u32[]{:S(2)}, u32[]{:S(2)}) collective-permute-start(bf16[8,32,128]{2,0,1:T(8,128)(2,1)S(1)} %fusion.20), channel_id=1, source_target_pairs={{0,4},{4,8},{8,12},{12,0},{1,5},{5,9},{9,13},{13,1},{2,6},{6,10},{... | collective-permute-start | bytes 196616 | tf_op jit(solution)/shard_map/ppermute | solution.py:38
  4.6 7.3 %collective-permute-start.1 = (bf16[8,32,128]{2,0,1:T(8,128)(2,1)S(1)}, bf16[8,32,128]{2,0,1:T(8,128)(2,1)S(1)}, u32[]{:S(2)}, u32[]{:S(2)}) collective-permute-start(bf16[8,32,128]{2,0,1:T(8,128)(2,1)S(1)} %fusion.20), channel_id=1, source_target_pairs={{0,8},{4,12},{8,0},{12,4},{1,9},{5,13},{9,1},{13,5},{2,10},{6,14},... | collective-permute-start | bytes 196616 | tf_op jit(solution)/shard_map/ppermute | solution.py:38
  6.9 5.2 %collective-permute-start.2 = (bf16[8,32,128]{2,0,1:T(8,128)(2,1)S(1)}, bf16[8,32,128]{2,0,1:T(8,128)(2,1)S(1)}, u32[]{:S(2)}, u32[]{:S(2)}) collective-permute-start(bf16[8,32,128]{2,0,1:T(8,128)(2,1)S(1)} %fusion.20), channel_id=1, source_target_pairs={{0,12},{4,0},{8,4},{12,8},{1,13},{5,1},{9,5},{13,9},{2,14},{6,2},{... | collective-permute-start | bytes 196616 | tf_op jit(solution)/shard_map/ppermute | solution.py:38
  12.4 2.4 %copy-start.2 = (bf16[4,512,576]{1,2,0:T(8,128)(2,1)S(1)}, bf16[4,512,576]{1,2,0:T(8,128)(2,1)}, u32[]{:S(2)}) copy-start(bf16[4,512,576]{1,2,0:T(8,128)(2,1)} %param.9) | copy-start | bytes 7077892
  14.7 11.0 %copy-start.1 = (bf16[32,128,128]{2,1,0:T(8,128)(2,1)S(1)}, bf16[32,128,128]{2,1,0:T(8,128)(2,1)}, u32[]{:S(2)}) copy-start(bf16[32,128,128]{2,1,0:T(8,128)(2,1)} %param.12) | copy-start | bytes 3145732
  16.0 5.1 %collective-permute-start.3 = (bf16[268,128]{1,0:T(8,128)(2,1)S(1)}, bf16[268,128]{1,0:T(8,128)(2,1)S(1)}, u32[]{:S(2)}, u32[]{:S(2)}) collective-permute-start(bf16[268,128]{1,0:T(8,128)(2,1)S(1)} %get-tuple-element.16), channel_id=1, source_target_pairs={{0,4},{4,8},{8,12},{12,0},{1,5},{5,9},{9,13},{13,1},{2,6},{6,10},{... | collective-permute-start | bytes 205832 | tf_op jit(solution)/shard_map/ppermute | solution.py:113
  17.5 7.4 %collective-permute-start.4 = (bf16[268,128]{1,0:T(8,128)(2,1)S(1)}, bf16[268,128]{1,0:T(8,128)(2,1)S(1)}, u32[]{:S(2)}, u32[]{:S(2)}) collective-permute-start(bf16[268,128]{1,0:T(8,128)(2,1)S(1)} %get-tuple-element.17), channel_id=1, source_target_pairs={{0,8},{4,12},{8,0},{12,4},{1,9},{5,13},{9,1},{13,5},{2,10},{6,14},... | collective-permute-start | bytes 205832 | tf_op jit(solution)/shard_map/ppermute | solution.py:113
  17.5 7.6 %collective-permute-start.5 = (bf16[268,128]{1,0:T(8,128)(2,1)S(1)}, bf16[268,128]{1,0:T(8,128)(2,1)S(1)}, u32[]{:S(2)}, u32[]{:S(2)}) collective-permute-start(bf16[268,128]{1,0:T(8,128)(2,1)S(1)} %get-tuple-element.18), channel_id=1, source_target_pairs={{0,12},{4,0},{8,4},{12,8},{1,13},{5,1},{9,5},{13,9},{2,14},{6,2},{... | collective-permute-start | bytes 205832 | tf_op jit(solution)/shard_map/ppermute | solution.py:113
  26.2 7.3 %collective-permute-start.10 = (bf16[8,16,128]{2,0,1:T(8,128)(2,1)S(1)}, bf16[8,16,128]{2,0,1:T(8,128)(2,1)S(1)}, u32[]{:S(2)}, u32[]{:S(2)}) collective-permute-start(bf16[8,16,128]{2,0,1:T(8,128)(2,1)S(1)} %get-tuple-element.13), channel_id=1, source_target_pairs={{0,8},{4,12},{8,0},{12,4},{1,9},{5,13},{9,1},{13,5},{2,10},{6,14},... | collective-permute-start | bytes 98312 | tf_op jit(solution)/shard_map/ppermute | solution.py:133
  26.8 6.7 %collective-permute-start.11 = (bf16[8,16,128]{2,0,1:T(8,128)(2,1)S(1)}, bf16[8,16,128]{2,0,1:T(8,128)(2,1)S(1)}, u32[]{:S(2)}, u32[]{:S(2)}) collective-permute-start(bf16[8,16,128]{2,0,1:T(8,128)(2,1)S(1)} %get-tuple-element.13), channel_id=1, source_target_pairs={{0,12},{4,0},{8,4},{12,8},{1,13},{5,1},{9,5},{13,9},{2,14},{6,2},{... | collective-permute-start | bytes 98312 | tf_op jit(solution)/shard_map/ppermute | solution.py:133
  29.9 4.6 %collective-permute-start.9 = (bf16[8,16,128]{2,0,1:T(8,128)(2,1)S(1)}, bf16[8,16,128]{2,0,1:T(8,128)(2,1)S(1)}, u32[]{:S(2)}, u32[]{:S(2)}) collective-permute-start(bf16[8,16,128]{2,0,1:T(8,128)(2,1)S(1)} %get-tuple-element.13), channel_id=1, source_target_pairs={{0,4},{4,8},{8,12},{12,0},{1,5},{5,9},{9,13},{13,1},{2,6},{6,10},{... | collective-permute-start | bytes 98312 | tf_op jit(solution)/shard_map/ppermute | solution.py:133
  29.9 8.7 %collective-permute-start.6 = (bf16[8,16,128]{2,0,1:T(8,128)(2,1)S(1)}, bf16[8,16,128]{2,0,1:T(8,128)(2,1)S(1)}, u32[]{:S(2)}, u32[]{:S(2)}) collective-permute-start(bf16[8,16,128]{2,0,1:T(8,128)(2,1)S(1)} %get-tuple-element.12), channel_id=1, source_target_pairs={{0,4},{4,8},{8,12},{12,0},{1,5},{5,9},{9,13},{13,1},{2,6},{6,10},{... | collective-permute-start | bytes 98312 | tf_op jit(solution)/shard_map/ppermute | solution.py:133
  29.9 8.7 %collective-permute-start.7 = (bf16[8,16,128]{2,0,1:T(8,128)(2,1)S(1)}, bf16[8,16,128]{2,0,1:T(8,128)(2,1)S(1)}, u32[]{:S(2)}, u32[]{:S(2)}) collective-permute-start(bf16[8,16,128]{2,0,1:T(8,128)(2,1)S(1)} %get-tuple-element.12), channel_id=1, source_target_pairs={{0,8},{4,12},{8,0},{12,4},{1,9},{5,13},{9,1},{13,5},{2,10},{6,14},... | collective-permute-start | bytes 98312 | tf_op jit(solution)/shard_map/ppermute | solution.py:133
  33.5 5.2 %collective-permute-start.8 = (bf16[8,16,128]{2,0,1:T(8,128)(2,1)S(1)}, bf16[8,16,128]{2,0,1:T(8,128)(2,1)S(1)}, u32[]{:S(2)}, u32[]{:S(2)}) collective-permute-start(bf16[8,16,128]{2,0,1:T(8,128)(2,1)S(1)} %get-tuple-element.12), channel_id=1, source_target_pairs={{0,12},{4,0},{8,4},{12,8},{1,13},{5,1},{9,5},{13,9},{2,14},{6,2},{... | collective-permute-start | bytes 98312 | tf_op jit(solution)/shard_map/ppermute | solution.py:133
  42.8 4.1 %collective-permute-start.12 = (f32[8,448]{1,0:T(8,128)S(1)}, f32[8,448]{1,0:T(8,128)S(1)}, u32[]{:S(2)}, u32[]{:S(2)}) collective-permute-start(f32[8,448]{1,0:T(8,128)S(1)} %get-tuple-element.14), channel_id=1, source_target_pairs={{0,1},{1,2},{2,3},{3,0},{4,5},{5,6},{6,7},{7,4},{8,9},{9,10},{10,1... | collective-permute-start | bytes 43016 | tf_op jit(solution)/shard_map/ppermute | solution.py:153
  45.5 2.7 %collective-permute-start.13 = (f32[8,448]{1,0:T(8,128)S(1)}, f32[8,448]{1,0:T(8,128)S(1)}, u32[]{:S(2)}, u32[]{:S(2)}) collective-permute-start(f32[8,448]{1,0:T(8,128)S(1)} %get-tuple-element.15), channel_id=1, source_target_pairs={{0,2},{1,3},{2,0},{3,1},{4,6},{5,7},{6,4},{7,5},{8,10},{9,11},{10,... | collective-permute-start | bytes 43016 | tf_op jit(solution)/shard_map/ppermute | solution.py:153
  46.9 3.2 %collective-permute-start.14 = (f32[8,448]{1,0:T(8,128)S(1)}, f32[8,448]{1,0:T(8,128)S(1)}, u32[]{:S(2)}, u32[]{:S(2)}) collective-permute-start(f32[8,448]{1,0:T(8,128)S(1)} %select_select_fusion), channel_id=1, source_target_pairs={{0,3},{1,0},{2,1},{3,2},{4,7},{5,4},{6,5},{7,6},{8,11},{9,8},{10,9... | collective-permute-start | bytes 43016 | tf_op jit(solution)/shard_map/ppermute | solution.py:153

commit v7 on v5

--- a/solution.py
+++ b/solution.py
@@ -41,7 +41,7 @@
         q_slots = received[-1][:, :, None, :]
         for k in range(n_ctx - 2, -1, -1):
             q_slots = jnp.where(source == k, received[k][:, :, None, :], q_slots)
-        q_latent = q_slots.reshape(row_count, head_count, latent_width)
+        q_latent = lax.optimization_barrier(q_slots.reshape(row_count, head_count, latent_width))
     else:
         q_latent = lax.all_gather(q_part, "ctx", axis=2, tiled=True)
     q_rows = DRAFT * head_count

time: 47.6 us -> 60.1 us (1.26)
  local copies, waits for them, and re-layouts: 1.62 us -> 11.6 us
  waiting for transfers between devices: 14.5 us -> 8.17 us
  starting transfers between devices: 15.2 us -> 19.3 us
  other arithmetic: 2.26 us -> 5.68 us
  matrix products: 13.5 us -> 14.6 us
    broadcast_in_dim x11, local copies, waits for them, and re-layouts: 0.96 us -> 9.27 us  [per_device(): q_slots = jnp.where(source == k, received[k][:, :, None, :], q_slots)]
    ppermute x3, starting transfers between devices: 2.22 us -> 5.28 us  [per_device(): lax.ppermute(pick((me_head + k) % n_head, col_slices), 'head', shift_pair...]
    ppermute x3, waiting for transfers between devices: 5.24 us -> 2.67 us  [per_device(): lax.ppermute(packed_for((me_ctx + k) % n_ctx), 'ctx', shift_pairs(n_ctx, k))]
    ppermute x3, waiting for transfers between devices: 4.87 us -> 2.35 us  [per_device(): lax.ppermute(sent, 'ctx', shift_pairs(n_ctx, k)).astype(jnp.float32)]
    convert_element_type x2, other arithmetic: 0.06 us -> 2.27 us  [packed_for(): pick(target, sum_slices).astype(jnp.bfloat16)]
    ppermute x3, local copies, waits for them, and re-layouts: 0.03 us -> 1.71 us  [per_device(): lax.ppermute(q_part, 'ctx', shift_pairs(n_ctx, k))]
    ppermute x3, starting transfers between devices: 3.77 us -> 5.18 us  [per_device(): lax.ppermute(sent, 'ctx', shift_pairs(n_ctx, k)).astype(jnp.float32)]
    ppermute x3, waiting for transfers between devices: 1.26 us -> 0.01 us  [per_device(): lax.ppermute(q_part, 'ctx', shift_pairs(n_ctx, k))]
  transfers between devices with their start and end apart: 12 -> 12, of which waited for: 8 -> 5; matrix products, arithmetic and copies ran while one was open for 6% -> 19% of each run, Pallas kernels for 0% -> 0%
where the time goes in v7:
time: 60.1 us; the launch traced here: 59.6 us
  starting transfers between devices  19.3 us (32%)
  matrix products  14.6 us (24%)
  local copies, waits for them, and re-layouts  11.6 us (19%)
  waiting for transfers between devices  8.17 us (14%)
  other arithmetic  5.68 us (9%)
    broadcast_in_dim x11, local copies, waits for them, and re-layouts, per_device(): q_slots = jnp.where(source == k, received[k][:, :, None, :], q_slots)  9.27 us
    dot_general x1, matrix products, per_device(): jnp.dot(values.reshape(row_count, -1), w_output, preferred_element_type=j...  7.17 us
    ppermute x3, starting transfers between devices, per_device(): lax.ppermute(q_part, 'ctx', shift_pairs(n_ctx, k))  5.51 us
    ppermute x3, starting transfers between devices, per_device(): lax.ppermute(pick((me_head + k) % n_head, col_slices), 'head', shift_pair...  5.28 us
    ppermute x3, starting transfers between devices, per_device(): lax.ppermute(sent, 'ctx', shift_pairs(n_ctx, k)).astype(jnp.float32)  5.18 us
    ppermute x3, starting transfers between devices, per_device(): lax.ppermute(packed_for((me_ctx + k) % n_ctx), 'ctx', shift_pairs(n_ctx, k))  3.32 us
    ppermute x3, waiting for transfers between devices, per_device(): lax.ppermute(pick((me_head + k) % n_head, col_slices), 'head', shift_pair...  3.15 us
    ppermute x3, waiting for transfers between devices, per_device(): lax.ppermute(packed_for((me_ctx + k) % n_ctx), 'ctx', shift_pairs(n_ctx, k))  2.67 us
  transfers between devices with their start and end apart: 12, of which 5 were waited for; matrix products, arithmetic and copies ran while one was open for 19% of the time, Pallas kernels for 0%

profile of v7, /device:TPU:1, one launch (start us, length us, event | category | flops | bytes accessed | tf_op | source)
XLA Modules:
  0.0 59.6 jit_solution(12732828805340681397)
XLA Ops:
  0.0 1.7 %fusion.13 = bf16[8,32,128]{2,0,1:T(8,128)(2,1)S(1)} fusion(bf16[32,128,128]{2,1,0:T(8,128)(2,1)} %param.11, bf16[8,32,128]{2,1,0:T(8,128)(2,1)} %param.7), kind=kOutput, calls=%fused_computation.9 | convolution fusion | flops 8421376 | bytes 1179648 | tf_op jit(solution)/shard_map/rhn,hnl->rhl/dot_general | solution.py:33
  1.7 2.1 %collective-permute-start = (bf16[8,32,128]{2,0,1:T(8,128)(2,1)S(1)}, bf16[8,32,128]{2,0,1:T(8,128)(2,1)}, u32[]{:S(2)}, u32[]{:S(2)}) collective-permute-start(bf16[8,32,128]{2,0,1:T(8,128)(2,1)S(1)} %fusion.13), channel_id=1, source_target_pairs={{0,4},{4,8},{8,12},{12,0},{1,5},{5,9},{9,13},{13,1},{2,6},{6,10},{... | collective-permute-start | bytes 196616 | tf_op jit(solution)/shard_map/ppermute | solution.py:38
  3.8 2.3 %collective-permute-start.1 = (bf16[8,32,128]{2,0,1:T(8,128)(2,1)S(1)}, bf16[8,32,128]{2,0,1:T(8,128)(2,1)}, u32[]{:S(2)}, u32[]{:S(2)}) collective-permute-start(bf16[8,32,128]{2,0,1:T(8,128)(2,1)S(1)} %fusion.13), channel_id=1, source_target_pairs={{0,8},{4,12},{8,0},{12,4},{1,9},{5,13},{9,1},{13,5},{2,10},{6,14},... | collective-permute-start | bytes 196616 | tf_op jit(solution)/shard_map/ppermute | solution.py:38
  6.1 1.1 %collective-permute-start.2 = (bf16[8,32,128]{2,0,1:T(8,128)(2,1)S(1)}, bf16[8,32,128]{2,0,1:T(8,128)(2,1)S(1)}, u32[]{:S(2)}, u32[]{:S(2)}) collective-permute-start(bf16[8,32,128]{2,0,1:T(8,128)(2,1)S(1)} %fusion.13), channel_id=1, source_target_pairs={{0,12},{4,0},{8,4},{12,8},{1,13},{5,1},{9,5},{13,9},{2,14},{6,2},{... | collective-permute-start | bytes 196616 | tf_op jit(solution)/shard_map/ppermute | solution.py:38
  7.3 0.1 broadcast_bitcast_fusion
  7.5 0.6 broadcast_bitcast_fusion.2
  8.1 0.1 broadcast_in_dim.95
  8.1 0.8 %broadcast_in_dim.96 = bf16[8,32,512]{2,1,0:T(8,128)(2,1)} reshape(bf16[8,32,4,128]{3,2,1,0:T(4,128)(2,1)S(1)} %broadcast_in_dim.95) | data formatting | bytes 524288 | tf_op jit(solution)/shard_map/jit(_where)/broadcast_in_dim | solution.py:43
  8.9 0.7 %broadcast_add_fusion.1 = s32[4]{0:T(128)S(1)} fusion(s32[4]{0:T(128)} %param.10), kind=kLoop, calls=%fused_computation.86 | loop fusion | flops 4 | bytes 32 | tf_op jit(solution)/shard_map/sub | solution.py:63
  9.7 2.1 %fusion.19 = f32[4,64,512]{2,1,0:T(8,128)} fusion(bf16[4,64,64]{2,1,0:T(8,128)(2,1)} %bitcast.40, bf16[4,512,576]{1,2,0:T(8,128)(2,1)} %param.9), kind=kOutput, calls=%fused_computation.15 | convolution fusion | flops 16777216 | bytes 851968 | tf_op jit(solution)/shard_map/sqc,skc->sqk/dot_general | solution.py:54
  11.8 0.9 %copy.10 = bf16[8,32,128]{2,1,0:T(8,128)(2,1)S(1)} copy(bf16[8,32,128]{2,0,1:T(8,128)(2,1)} %collective-permute-done) | data formatting | bytes 131072 | tf_op jit(solution)/shard_map/ppermute | solution.py:38
  12.7 0.8 %broadcast_in_dim.100 = bf16[8,32,4,128]{3,2,1,0:T(4,128)(2,1)} broadcast(bf16[8,32,128]{2,1,0:T(8,128)(2,1)S(1)} %copy.10), dimensions={0,1,3} | broadcast | bytes 327680 | tf_op jit(solution)/shard_map/jit(_where)/broadcast_in_dim | solution.py:43
  13.5 1.7 %broadcast_in_dim.101 = bf16[8,32,512]{2,1,0:T(8,128)(2,1)} reshape(bf16[8,32,4,128]{3,2,1,0:T(4,128)(2,1)} %broadcast_in_dim.100) | data formatting | bytes 524288 | tf_op jit(solution)/shard_map/jit(_where)/broadcast_in_dim | solution.py:43
  15.2 0.9 %copy.11 = bf16[8,32,128]{2,1,0:T(8,128)(2,1)S(1)} copy(bf16[8,32,128]{2,0,1:T(8,128)(2,1)} %collective-permute-done.1) | data formatting | bytes 131072 | tf_op jit(solution)/shard_map/ppermute | solution.py:38
  16.1 0.8 %broadcast_in_dim.105 = bf16[8,32,4,128]{3,2,1,0:T(4,128)(2,1)} broadcast(bf16[8,32,128]{2,1,0:T(8,128)(2,1)S(1)} %copy.11), dimensions={0,1,3} | broadcast | bytes 327680 | tf_op jit(solution)/shard_map/jit(_where)/broadcast_in_dim | solution.py:43
  16.9 1.8 %broadcast_in_dim.106 = bf16[8,32,512]{2,1,0:T(8,128)(2,1)} reshape(bf16[8,32,4,128]{3,2,1,0:T(4,128)(2,1)} %broadcast_in_dim.105) | data formatting | bytes 524288 | tf_op jit(solution)/shard_map/jit(_where)/broadcast_in_dim | solution.py:43
  18.7 0.8 %broadcast_in_dim.107 = bf16[8,32,4,128]{3,2,1,0:T(4,128)(2,1)} broadcast(bf16[8,32,128]{2,1,0:T(8,128)(2,1)S(1)} %copy.12), dimensions={0,1,3} | broadcast | bytes 327680 | tf_op jit(solution)/shard_map/jit(_where)/broadcast_in_dim | solution.py:43
  19.4 1.8 %broadcast_in_dim.108 = bf16[8,32,512]{2,1,0:T(8,128)(2,1)} reshape(bf16[8,32,4,128]{3,2,1,0:T(4,128)(2,1)} %broadcast_in_dim.107) | data formatting | bytes 524288 | tf_op jit(solution)/shard_map/jit(_where)/broadcast_in_dim | solution.py:43
  21.2 1.2 %select_select_fusion = bf16[8,32,512]{2,1,0:T(8,128)(2,1)S(1)} fusion(bf16[8,32,512]{2,1,0:T(8,128)(2,1)} %broadcast_in_dim.96, bf16[8,32,512]{2,1,0:T(8,128)(2,1)} %broadcast_in_dim.101, bf16[8,32,512]{2,1,0:T(8,128)(2,1)} %broadcast_in_dim.106, bf16[8,32,512]{2,1,0:T(8,128)(2,1)} %broadcast_in_dim.108, pred[512]{0:T(512)(128)(4,1)S(1)} %broadcast_bitcast_fusion, ...), kind=kLoop, calls=%fused_computation.17 | loop fusion | flops 393216 | bytes 1312256 | tf_op jit(solution)/shard_map/jit(_where)/select_n | solution.py:43
  22.4 1.6 %fusion.39 = (f32[4,64]{1,0:T(4,128)S(1)}, f32[4,64,512]{2,1,0:T(8,128)S(1)}) fusion(f32[4,64,512]{2,1,0:T(8,128)} %fusion.19, bf16[4,64,512]{2,1,0:T(8,128)(2,1)S(1)} %bitcast.32, bf16[4,512,576]{1,2,0:T(8,128)(2,1)S(1)} %copy-done.1, s32[4,64]{1,0:T(4,128)S(1)} %broadcast_add_fusion, s32[512]{0:T(512)S(1)} %iota_add_fusion), kind=kOutput, calls=%fused_computation.91 | convolution fusion | flops 134872832 | bytes 3412992 | tf_op jit(solution)/shard_map/sqc,skc->sqk/dot_general | solution.py:48
  24.1 1.6 %fusion.2 = f32[4,64,512]{2,1,0:T(8,128)} fusion(bf16[4,512,576]{1,2,0:T(8,128)(2,1)S(1)} %copy-done.1, f32[4,64,512]{2,1,0:T(8,128)S(1)} %get-tuple-element.27, f32[4,64]{1,0:T(4,128)S(1)} %get-tuple-element.26, s32[4,64]{1,0:T(4,128)S(1)} %broadcast_add_fusion, s32[512]{0:T(512)S(1)} %iota_add_fusion), kind=kOutput, calls=%fused_computation.2 | convolution fusion | flops 134742016 | bytes 3151872 | tf_op jit(solution)/shard_map/sqk,skl->sql/dot_general | solution.py:69
  25.6 0.2 fusion.14
  25.9 0.1 reshape.270
  26.0 1.1 %select_convert_fusion = bf16[4,64,128]{2,1,0:T(8,128)(2,1)S(1)} fusion(f32[4,64,512]{2,1,0:T(8,128)} %fusion.2, pred[]{:T(512)S(6)} %eq.117, pred[]{:T(512)S(6)} %eq.116, pred[]{:T(512)S(6)} %eq.115), kind=kLoop, calls=%fused_computation.29 | loop fusion | flops 98304 | bytes 327683 | tf_op jit(solution)/shard_map/convert_element_type | solution.py:93
  27.1 1.1 %select_convert_fusion.2 = (bf16[4,64,128]{2,1,0:T(8,128)(2,1)S(1)}, bf16[4,64,128]{2,1,0:T(8,128)(2,1)S(1)}) fusion(f32[4,64,512]{2,1,0:T(8,128)} %fusion.2, pred[]{:T(512)S(6)} %eq.111, pred[]{:T(512)S(6)} %eq.110, pred[]{:T(512)S(6)} %eq.109, pred[]{:T(512)S(6)} %eq.114, pred[]{:T(512)S(6)} %eq.113, pred[]{:T(512)S(6)} %eq.112), kind=kLoop, calls=%fused_computation.31 | loop fusion | flops 196608 | bytes 393222 | tf_op jit(solution)/shard_map/convert_element_type | solution.py:93
  28.3 0.5 collective-permute-start.3
  28.8 2.8 %collective-permute-start.5 = (bf16[268,128]{1,0:T(8,128)(2,1)S(1)}, bf16[268,128]{1,0:T(8,128)(2,1)S(1)}, u32[]{:S(2)}, u32[]{:S(2)}) collective-permute-start(bf16[268,128]{1,0:T(8,128)(2,1)S(1)} %get-tuple-element.16), channel_id=1, source_target_pairs={{0,12},{4,0},{8,4},{12,8},{1,13},{5,1},{9,5},{13,9},{2,14},{6,2},{... | collective-permute-start | bytes 205832 | tf_op jit(solution)/shard_map/ppermute | solution.py:113
  31.6 1.9 %collective-permute-done.3 = bf16[268,128]{1,0:T(8,128)(2,1)S(1)} collective-permute-done((bf16[268,128]{1,0:T(8,128)(2,1)S(1)}, bf16[268,128]{1,0:T(8,128)(2,1)S(1)}, u32[]{:S(2)}, u32[]{:S(2)}) %collective-permute-start.3) | collective-permute-done | bytes 68640 | tf_op jit(solution)/shard_map/ppermute | solution.py:113
  33.5 0.8 %collective-permute-done.4 = bf16[268,128]{1,0:T(8,128)(2,1)S(1)} collective-permute-done((bf16[268,128]{1,0:T(8,128)(2,1)S(1)}, bf16[268,128]{1,0:T(8,128)(2,1)S(1)}, u32[]{:S(2)}, u32[]{:S(2)}) %collective-permute-start.4) | collective-permute-done | bytes 68640 | tf_op jit(solution)/shard_map/ppermute | solution.py:113
  34.3 0.1 squeeze.21
  34.4 0.1 squeeze.22
  34.5 0.1 squeeze.23
  34.6 0.1 squeeze.24
  34.7 0.1 squeeze.25
  34.8 0.1 squeeze.26
  34.9 0.2 fusion.25
  35.2 0.4 fusion.40
  35.6 3.0 %collective-permute-start.6 = (bf16[8,32,128]{2,0,1:T(8,128)(2,1)S(1)}, bf16[8,32,128]{2,0,1:T(8,128)(2,1)S(1)}, u32[]{:S(2)}, u32[]{:S(2)}) collective-permute-start(bf16[8,32,128]{2,0,1:T(8,128)(2,1)S(1)} %get-tuple-element.28), channel_id=1, source_target_pairs={{0,4},{4,8},{8,12},{12,0},{1,5},{5,9},{9,13},{13,1},{2,6},{6,10},{... | collective-permute-start | bytes 196616 | tf_op jit(solution)/shard_map/ppermute | solution.py:127
  38.6 2.1 %collective-permute-start.8 = (bf16[8,32,128]{2,0,1:T(8,128)(2,1)S(1)}, bf16[8,32,128]{2,0,1:T(8,128)(2,1)S(1)}, u32[]{:S(2)}, u32[]{:S(2)}) collective-permute-start(bf16[8,32,128]{2,0,1:T(8,128)(2,1)S(1)} %get-tuple-element.28), channel_id=1, source_target_pairs={{0,12},{4,0},{8,4},{12,8},{1,13},{5,1},{9,5},{13,9},{2,14},{6,2},{... | collective-permute-start | bytes 196616 | tf_op jit(solution)/shard_map/ppermute | solution.py:127
  40.7 2.3 %collective-permute-done.7 = bf16[8,32,128]{2,0,1:T(8,128)(2,1)S(1)} collective-permute-done((bf16[8,32,128]{2,0,1:T(8,128)(2,1)S(1)}, bf16[8,32,128]{2,0,1:T(8,128)(2,1)S(1)}, u32[]{:S(2)}, u32[]{:S(2)}) %collective-permute-start.7) | collective-permute-done | bytes 65568 | tf_op jit(solution)/shard_map/ppermute | solution.py:127
  43.1 7.2 %fusion.29 = f32[8,1792]{1,0:T(8,128)S(1)} fusion(bf16[4096,1792]{1,0:T(8,128)(2,1)} %param.13, bf16[8,32,128]{2,0,1:T(8,128)(2,1)S(1)} %collective-permute-done.8, bf16[8,32,128]{2,0,1:T(8,128)(2,1)S(1)} %collective-permute-done.7, f32[8,32,128]{2,0,1:T(8,128)S(1)} %get-tuple-element.29, bf16[8,32,128]{2,0,1:T(8,128)(2,1)S(1)} %collective-permute-done.6), kind=kOutput, calls=%fused_computation.42 | convolution fusion | flops 117669888 | bytes 15065088 | tf_op jit(solution)/shard_map/dot_general | solution.py:133
  50.3 0.1 select_select_fusion.3
  50.3 1.3 %collective-permute-start.10 = (f32[8,448]{1,0:T(8,128)S(1)}, f32[8,448]{1,0:T(8,128)S(1)}, u32[]{:S(2)}, u32[]{:S(2)}) collective-permute-start(f32[8,448]{1,0:T(8,128)S(1)} %get-tuple-element.13), channel_id=1, source_target_pairs={{0,2},{1,3},{2,0},{3,1},{4,6},{5,7},{6,4},{7,5},{8,10},{9,11},{10,... | collective-permute-start | bytes 43016 | tf_op jit(solution)/shard_map/ppermute | solution.py:143
  51.7 4.0 %collective-permute-start.9 = (f32[8,448]{1,0:T(8,128)S(1)}, f32[8,448]{1,0:T(8,128)S(1)}, u32[]{:S(2)}, u32[]{:S(2)}) collective-permute-start(f32[8,448]{1,0:T(8,128)S(1)} %get-tuple-element.12), channel_id=1, source_target_pairs={{0,1},{1,2},{2,3},{3,0},{4,5},{5,6},{6,7},{7,4},{8,9},{9,10},{10,1... | collective-permute-start | bytes 43016 | tf_op jit(solution)/shard_map/ppermute | solution.py:143
  55.6 0.1 select_select_fusion.1
  55.7 0.8 %collective-permute-done.9 = f32[8,448]{1,0:T(8,128)S(1)} collective-permute-done((f32[8,448]{1,0:T(8,128)S(1)}, f32[8,448]{1,0:T(8,128)S(1)}, u32[]{:S(2)}, u32[]{:S(2)}) %collective-permute-start.9) | collective-permute-done | bytes 14368 | tf_op jit(solution)/shard_map/ppermute | solution.py:143
  56.5 2.4 %collective-permute-done.11 = f32[8,448]{1,0:T(8,128)S(1)} collective-permute-done((f32[8,448]{1,0:T(8,128)S(1)}, f32[8,448]{1,0:T(8,128)S(1)}, u32[]{:S(2)}, u32[]{:S(2)}) %collective-permute-start.11) | collective-permute-done | bytes 14368 | tf_op jit(solution)/shard_map/ppermute | solution.py:143
  58.9 0.7 %add_add_fusion = f32[8,448]{1,0:T(8,128)} fusion(f32[8,448]{1,0:T(8,128)S(1)} %collective-permute-done.11, f32[8,448]{1,0:T(8,128)S(1)} %collective-permute-done.10, f32[8,448]{1,0:T(8,128)S(1)} %collective-permute-done.9, f32[8,1792]{1,0:T(8,128)S(1)} %fusion.29, pred[]{:T(512)S(6)} %eq.122, pred[]{:T(512)S(6)} %eq.121, pred[]{:T(512)S(6)} %eq.105), kind=kLoop, calls=%fused_computation.46 | loop fusion | flops 21504 | bytes 114691 | tf_op jit(solution)/shard_map/add | solution.py:143
  (40 shorter events, 0.5 us)
Async XLA Ops:
  0.0 35.2 %copy-start = (bf16[32,128,128]{2,1,0:T(8,128)(2,1)S(1)}, bf16[32,128,128]{2,1,0:T(8,128)(2,1)}, u32[]{:S(2)}) copy-start(bf16[32,128,128]{2,1,0:T(8,128)(2,1)} %param.12) | copy-start | bytes 3145732
  1.7 10.1 %collective-permute-start = (bf16[8,32,128]{2,0,1:T(8,128)(2,1)S(1)}, bf16[8,32,128]{2,0,1:T(8,128)(2,1)}, u32[]{:S(2)}, u32[]{:S(2)}) collective-permute-start(bf16[8,32,128]{2,0,1:T(8,128)(2,1)S(1)} %fusion.13), channel_id=1, source_target_pairs={{0,4},{4,8},{8,12},{12,0},{1,5},{5,9},{9,13},{13,1},{2,6},{6,10},{... | collective-permute-start | bytes 196616 | tf_op jit(solution)/shard_map/ppermute | solution.py:38
  3.8 11.4 %collective-permute-start.1 = (bf16[8,32,128]{2,0,1:T(8,128)(2,1)S(1)}, bf16[8,32,128]{2,0,1:T(8,128)(2,1)}, u32[]{:S(2)}, u32[]{:S(2)}) collective-permute-start(bf16[8,32,128]{2,0,1:T(8,128)(2,1)S(1)} %fusion.13), channel_id=1, source_target_pairs={{0,8},{4,12},{8,0},{12,4},{1,9},{5,13},{9,1},{13,5},{2,10},{6,14},... | collective-permute-start | bytes 196616 | tf_op jit(solution)/shard_map/ppermute | solution.py:38
  6.1 12.5 %collective-permute-start.2 = (bf16[8,32,128]{2,0,1:T(8,128)(2,1)S(1)}, bf16[8,32,128]{2,0,1:T(8,128)(2,1)S(1)}, u32[]{:S(2)}, u32[]{:S(2)}) collective-permute-start(bf16[8,32,128]{2,0,1:T(8,128)(2,1)S(1)} %fusion.13), channel_id=1, source_target_pairs={{0,12},{4,0},{8,4},{12,8},{1,13},{5,1},{9,5},{13,9},{2,14},{6,2},{... | collective-permute-start | bytes 196616 | tf_op jit(solution)/shard_map/ppermute | solution.py:38
  9.7 12.8 %copy-start.1 = (bf16[4,512,576]{1,2,0:T(8,128)(2,1)S(1)}, bf16[4,512,576]{1,2,0:T(8,128)(2,1)}, u32[]{:S(2)}) copy-start(bf16[4,512,576]{1,2,0:T(8,128)(2,1)} %param.9) | copy-start | bytes 7077892
  25.6 9.3 %copy-start.2 = (f32[4,64,512]{2,1,0:T(8,128)S(1)}, f32[4,64,512]{2,1,0:T(8,128)}, u32[]{:S(2)}) copy-start(f32[4,64,512]{2,1,0:T(8,128)} %fusion.2) | copy-start | bytes 1572868
  28.3 5.2 %collective-permute-start.3 = (bf16[268,128]{1,0:T(8,128)(2,1)S(1)}, bf16[268,128]{1,0:T(8,128)(2,1)S(1)}, u32[]{:S(2)}, u32[]{:S(2)}) collective-permute-start(bf16[268,128]{1,0:T(8,128)(2,1)S(1)} %get-tuple-element.14), channel_id=1, source_target_pairs={{0,4},{4,8},{8,12},{12,0},{1,5},{5,9},{9,13},{13,1},{2,6},{6,10},{... | collective-permute-start | bytes 205832 | tf_op jit(solution)/shard_map/ppermute | solution.py:113
  28.8 5.6 %collective-permute-start.4 = (bf16[268,128]{1,0:T(8,128)(2,1)S(1)}, bf16[268,128]{1,0:T(8,128)(2,1)S(1)}, u32[]{:S(2)}, u32[]{:S(2)}) collective-permute-start(bf16[268,128]{1,0:T(8,128)(2,1)S(1)} %get-tuple-element.15), channel_id=1, source_target_pairs={{0,8},{4,12},{8,0},{12,4},{1,9},{5,13},{9,1},{13,5},{2,10},{6,14},... | collective-permute-start | bytes 205832 | tf_op jit(solution)/shard_map/ppermute | solution.py:113
  28.8 5.7 %collective-permute-start.5 = (bf16[268,128]{1,0:T(8,128)(2,1)S(1)}, bf16[268,128]{1,0:T(8,128)(2,1)S(1)}, u32[]{:S(2)}, u32[]{:S(2)}) collective-permute-start(bf16[268,128]{1,0:T(8,128)(2,1)S(1)} %get-tuple-element.16), channel_id=1, source_target_pairs={{0,12},{4,0},{8,4},{12,8},{1,13},{5,1},{9,5},{13,9},{2,14},{6,2},{... | collective-permute-start | bytes 205832 | tf_op jit(solution)/shard_map/ppermute | solution.py:113
  35.6 5.2 %collective-permute-start.6 = (bf16[8,32,128]{2,0,1:T(8,128)(2,1)S(1)}, bf16[8,32,128]{2,0,1:T(8,128)(2,1)S(1)}, u32[]{:S(2)}, u32[]{:S(2)}) collective-permute-start(bf16[8,32,128]{2,0,1:T(8,128)(2,1)S(1)} %get-tuple-element.28), channel_id=1, source_target_pairs={{0,4},{4,8},{8,12},{12,0},{1,5},{5,9},{9,13},{13,1},{2,6},{6,10},{... | collective-permute-start | bytes 196616 | tf_op jit(solution)/shard_map/ppermute | solution.py:127
  38.6 4.5 %collective-permute-start.7 = (bf16[8,32,128]{2,0,1:T(8,128)(2,1)S(1)}, bf16[8,32,128]{2,0,1:T(8,128)(2,1)S(1)}, u32[]{:S(2)}, u32[]{:S(2)}) collective-permute-start(bf16[8,32,128]{2,0,1:T(8,128)(2,1)S(1)} %get-tuple-element.28), channel_id=1, source_target_pairs={{0,8},{4,12},{8,0},{12,4},{1,9},{5,13},{9,1},{13,5},{2,10},{6,14},... | collective-permute-start | bytes 196616 | tf_op jit(solution)/shard_map/ppermute | solution.py:127
  38.6 4.4 %collective-permute-start.8 = (bf16[8,32,128]{2,0,1:T(8,128)(2,1)S(1)}, bf16[8,32,128]{2,0,1:T(8,128)(2,1)S(1)}, u32[]{:S(2)}, u32[]{:S(2)}) collective-permute-start(bf16[8,32,128]{2,0,1:T(8,128)(2,1)S(1)} %get-tuple-element.28), channel_id=1, source_target_pairs={{0,12},{4,0},{8,4},{12,8},{1,13},{5,1},{9,5},{13,9},{2,14},{6,2},{... | collective-permute-start | bytes 196616 | tf_op jit(solution)/shard_map/ppermute | solution.py:127
  50.3 5.4 %collective-permute-start.10 = (f32[8,448]{1,0:T(8,128)S(1)}, f32[8,448]{1,0:T(8,128)S(1)}, u32[]{:S(2)}, u32[]{:S(2)}) collective-permute-start(f32[8,448]{1,0:T(8,128)S(1)} %get-tuple-element.13), channel_id=1, source_target_pairs={{0,2},{1,3},{2,0},{3,1},{4,6},{5,7},{6,4},{7,5},{8,10},{9,11},{10,... | collective-permute-start | bytes 43016 | tf_op jit(solution)/shard_map/ppermute | solution.py:143
  51.7 4.8 %collective-permute-start.9 = (f32[8,448]{1,0:T(8,128)S(1)}, f32[8,448]{1,0:T(8,128)S(1)}, u32[]{:S(2)}, u32[]{:S(2)}) collective-permute-start(f32[8,448]{1,0:T(8,128)S(1)} %get-tuple-element.12), channel_id=1, source_target_pairs={{0,1},{1,2},{2,3},{3,0},{4,5},{5,6},{6,7},{7,4},{8,9},{9,10},{10,1... | collective-permute-start | bytes 43016 | tf_op jit(solution)/shard_map/ppermute | solution.py:143
  55.7 3.2 %collective-permute-start.11 = (f32[8,448]{1,0:T(8,128)S(1)}, f32[8,448]{1,0:T(8,128)S(1)}, u32[]{:S(2)}, u32[]{:S(2)}) collective-permute-start(f32[8,448]{1,0:T(8,128)S(1)} %select_select_fusion.1), channel_id=1, source_target_pairs={{0,3},{1,0},{2,1},{3,2},{4,7},{5,4},{6,5},{7,6},{8,11},{9,8},{10,9... | collective-permute-start | bytes 43016 | tf_op jit(solution)/shard_map/ppermute | solution.py:143

commit v8 on v7

--- a/solution.py
+++ b/solution.py
@@ -37,20 +37,25 @@
         received = [q_part] + [
             lax.ppermute(q_part, "ctx", shift_pairs(n_ctx, k)) for k in range(1, n_ctx)
         ]
-        source = (me_ctx - jnp.arange(n_ctx, dtype=jnp.int32)[None, None, :, None]) % n_ctx
-        q_slots = received[-1][:, :, None, :]
-        for k in range(n_ctx - 2, -1, -1):
-            q_slots = jnp.where(source == k, received[k][:, :, None, :], q_slots)
-        q_latent = lax.optimization_barrier(q_slots.reshape(row_count, head_count, latent_width))
+        kv_blocks = kv_cache[:, :, :latent_width].reshape(seq_count, ctx_rows, n_ctx, -1)
+        latent_scores = 0
+        for k in range(n_ctx):
+            block = lax.dynamic_index_in_dim(kv_blocks, (me_ctx - k) % n_ctx, axis=2, keepdims=False)
+            latent_scores = latent_scores + jnp.einsum(
+                "sqc,skc->sqk",
+                received[k].reshape(seq_count, DRAFT * head_count, -1),
+                block,
+                preferred_element_type=jnp.float32,
+            )
     else:
         q_latent = lax.all_gather(q_part, "ctx", axis=2, tiled=True)
+        latent_scores = jnp.einsum(
+            "sqc,skc->sqk",
+            q_latent.reshape(seq_count, DRAFT * head_count, latent_width),
+            kv_cache[:, :, :latent_width],
+            preferred_element_type=jnp.float32,
+        )
     q_rows = DRAFT * head_count
-    latent_scores = jnp.einsum(
-        "sqc,skc->sqk",
-        q_latent.reshape(seq_count, q_rows, latent_width),
-        kv_cache[:, :, :latent_width],
-        preferred_element_type=jnp.float32,
-    )
     rope_scores = jnp.einsum(
         "sqc,skc->sqk",
         query_rope.reshape(seq_count, q_rows, channels - latent_width),

time: 60.1 us -> 65.5 us (1.090)
  local copies, waits for them, and re-layouts: 11.6 us -> 19 us
  other arithmetic: 5.68 us -> 3.76 us
    unnamed x6 -> x20, local copies, waits for them, and re-layouts: 0.01 us -> 14.5 us
    broadcast_in_dim x11 -> x0, local copies, waits for them, and re-layouts: 9.27 us -> none  [per_device(): q_slots = jnp.where(source == k, received[k][:, :, None, :], q_slots)]
    dynamic_slice x0 -> x1, local copies, waits for them, and re-layouts: none -> 1.36 us  [per_device(): lax.dynamic_index_in_dim(kv_blocks, (me_ctx - k) % n_ctx, axis=2, keepdim...]
    select_n x1 -> x0, other arithmetic: 1.24 us -> none  [per_device(): q_slots = jnp.where(source == k, received[k][:, :, None, :], q_slots)]
    ppermute x3, starting transfers between devices: 3.32 us -> 4.4 us  [per_device(): lax.ppermute(packed_for((me_ctx + k) % n_ctx), 'ctx', shift_pairs(n_ctx, k))]
    dot_general x1, matrix products: 2.12 us -> 1.19 us  [per_device(): jnp.einsum('sqc,skc->sqk', query_rope.reshape(seq_count, q_rows, channels...]
    dot_general x1 -> x4, matrix products: 1.6 us -> 2.52 us  [per_device(): jnp.einsum('sqc,skc->sqk', received[k].reshape(seq_count, DRAFT * head_co...]
    ppermute x3, starting transfers between devices: 5.51 us -> 4.62 us  [per_device(): lax.ppermute(q_part, 'ctx', shift_pairs(n_ctx, k))]
  transfers between devices with their start and end apart: 12 -> 12, of which waited for: 5 -> 7; matrix products, arithmetic and copies ran while one was open for 19% -> 33% of each run, Pallas kernels for 0% -> 0%
where the time goes in v8:
time: 65.5 us; the launch traced here: 64.9 us
  local copies, waits for them, and re-layouts  19 us (29%)
  starting transfers between devices  18.9 us (29%)
  matrix products  14.6 us (22%)
  waiting for transfers between devices  8.33 us (13%)
  other arithmetic  3.76 us (6%)
    unnamed x20, local copies, waits for them, and re-layouts  14.5 us
    dot_general x1, matrix products, per_device(): jnp.dot(values.reshape(row_count, -1), w_output, preferred_element_type=j...  7.17 us
    ppermute x3, starting transfers between devices, per_device(): lax.ppermute(pick((me_head + k) % n_head, col_slices), 'head', shift_pair...  5.37 us
    ppermute x3, starting transfers between devices, per_device(): lax.ppermute(q_part, 'ctx', shift_pairs(n_ctx, k))  4.62 us
    ppermute x3, starting transfers between devices, per_device(): lax.ppermute(sent, 'ctx', shift_pairs(n_ctx, k)).astype(jnp.float32)  4.55 us
    ppermute x3, starting transfers between devices, per_device(): lax.ppermute(packed_for((me_ctx + k) % n_ctx), 'ctx', shift_pairs(n_ctx, k))  4.4 us
    ppermute x3, waiting for transfers between devices, per_device(): lax.ppermute(pick((me_head + k) % n_head, col_slices), 'head', shift_pair...  3.15 us
    ppermute x3, waiting for transfers between devices, per_device(): lax.ppermute(packed_for((me_ctx + k) % n_ctx), 'ctx', shift_pairs(n_ctx, k))  2.65 us
  transfers between devices with their start and end apart: 12, of which 7 were waited for; matrix products, arithmetic and copies ran while one was open for 33% of the time, Pallas kernels for 0%

profile of v8, /device:TPU:1, one launch (start us, length us, event | category | flops | bytes accessed | tf_op | source)
XLA Modules:
  0.0 64.9 jit_solution(12378714856647955931)
XLA Ops:
  0.0 1.7 %fusion.4 = bf16[8,32,128]{2,0,1:T(8,128)(2,1)S(1)} fusion(bf16[32,128,128]{2,1,0:T(8,128)(2,1)} %param.11, bf16[8,32,128]{2,1,0:T(8,128)(2,1)} %param.7), kind=kOutput, calls=%fused_computation.8 | convolution fusion | flops 8421376 | bytes 1179648 | tf_op jit(solution)/shard_map/rhn,hnl->rhl/dot_general | solution.py:33
  1.7 2.1 %collective-permute-start = (bf16[8,32,128]{2,0,1:T(8,128)(2,1)S(1)}, bf16[8,32,128]{2,0,1:T(8,128)(2,1)}, u32[]{:S(2)}, u32[]{:S(2)}) collective-permute-start(bf16[8,32,128]{2,0,1:T(8,128)(2,1)S(1)} %fusion.4), channel_id=1, source_target_pairs={{0,4},{4,8},{8,12},{12,0},{1,5},{5,9},{9,13},{13,1},{2,6},{6,10},{... | collective-permute-start | bytes 196616 | tf_op jit(solution)/shard_map/ppermute | solution.py:38
  3.8 2.1 %collective-permute-start.2 = (bf16[8,32,128]{2,0,1:T(8,128)(2,1)S(1)}, bf16[8,32,128]{2,0,1:T(8,128)(2,1)}, u32[]{:S(2)}, u32[]{:S(2)}) collective-permute-start(bf16[8,32,128]{2,0,1:T(8,128)(2,1)S(1)} %fusion.4), channel_id=1, source_target_pairs={{0,12},{4,0},{8,4},{12,8},{1,13},{5,1},{9,5},{13,9},{2,14},{6,2},{... | collective-permute-start | bytes 196616 | tf_op jit(solution)/shard_map/ppermute | solution.py:38
  5.9 0.4 collective-permute-start.1
  6.4 1.4 %constant_dynamic-slice_fusion.1 = (bf16[4,512,1,128]{1,3,2,0:T(8,128)(2,1)}, bf16[4,512,1,128]{1,3,2,0:T(8,128)(2,1)}, bf16[4,512,1,128]{1,3,2,0:T(8,128)(2,1)}, bf16[4,512,1,128]{1,3,2,0:T(8,128)(2,1)}) fusion(bf16[4,512,4,128]{1,3,2,0:T(8,128)(2,1)S(1)} %bitcast.47, s32[]{:T(128)S(6)} %select_n.239, s32[]{:T(128)S(6)} %select_n.237, s32[]{:T(128)S(6)} %select_n.235, ...), kind=kLoop, calls=%fused_computation.82 | loop fusion | bytes 4194320 | tf_op jit(solution)/shard_map/jit(dynamic_index_in_dim)/dynamic_slice | solution.py:43
  7.8 3.6 %copy.32 = bf16[4,512,1,128]{3,2,1,0:T(2,128)(2,1)} copy(bf16[4,512,1,128]{1,3,2,0:T(8,128)(2,1)} %get-tuple-element.12) | data formatting | bytes 1048576
  11.4 3.7 %copy.33 = bf16[4,512,1,128]{3,2,1,0:T(2,128)(2,1)} copy(bf16[4,512,1,128]{1,3,2,0:T(8,128)(2,1)} %get-tuple-element.11) | data formatting | bytes 1048576
  15.1 3.6 %copy.35 = bf16[4,512,1,128]{3,2,1,0:T(2,128)(2,1)} copy(bf16[4,512,1,128]{1,3,2,0:T(8,128)(2,1)} %get-tuple-element.13) | data formatting | bytes 1048576
  18.6 3.6 %copy.34 = bf16[4,512,1,128]{3,2,1,0:T(2,128)(2,1)} copy(bf16[4,512,1,128]{1,3,2,0:T(8,128)(2,1)} %get-tuple-element.10) | data formatting | bytes 1048576
  22.3 1.2 %fusion.13 = f32[4,64,512]{2,1,0:T(8,128)S(1)} fusion(bf16[4,64,64]{2,1,0:T(8,128)(2,1)} %bitcast.59, bf16[4,512,576]{1,2,0:T(8,128)(2,1)S(1)} %copy-done.1), kind=kOutput, calls=%fused_computation.21 | convolution fusion | flops 16777216 | bytes 819200 | tf_op jit(solution)/shard_map/sqc,skc->sqk/dot_general | solution.py:59
  23.5 1.5 %fusion.6 = f32[4,64,512]{2,1,0:T(8,128)S(1)} fusion(bf16[4,64,128]{2,1,0:T(8,128)(2,1)S(1)} %bitcast.49, bf16[4,512,1,128]{3,2,1,0:T(2,128)(2,1)} %copy.32), kind=kOutput, calls=%fused_computation.15 | convolution fusion | flops 33554432 | bytes 1114112 | tf_op jit(solution)/shard_map/sqc,skc->sqk/dot_general | solution.py:44
  25.1 0.9 %copy.19 = bf16[8,32,128]{2,1,0:T(8,128)(2,1)S(1)} copy(bf16[8,32,128]{2,0,1:T(8,128)(2,1)} %collective-permute-done) | data formatting | bytes 131072 | tf_op jit(solution)/shard_map/ppermute | solution.py:38
  25.9 0.3 convolution_add_fusion.1
  26.2 0.9 %copy.23 = bf16[8,32,128]{2,1,0:T(8,128)(2,1)S(1)} copy(bf16[8,32,128]{2,0,1:T(8,128)(2,1)} %collective-permute-done.2) | data formatting | bytes 131072 | tf_op jit(solution)/shard_map/ppermute | solution.py:38
  27.1 0.3 fusion.5
  27.4 0.9 %copy.21 = bf16[8,32,128]{2,1,0:T(8,128)(2,1)S(1)} copy(bf16[8,32,128]{2,0,1:T(8,128)(2,1)} %collective-permute-done.1) | data formatting | bytes 131072 | tf_op jit(solution)/shard_map/ppermute | solution.py:38
  28.3 0.4 fusion.33
  28.7 1.6 %fusion.9 = f32[4,64,512]{2,1,0:T(8,128)} fusion(f32[4,64,512]{2,1,0:T(8,128)S(1)} %get-tuple-element.31, f32[4,64]{1,0:T(4,128)S(1)} %get-tuple-element.30, s32[4,64]{1,0:T(4,128)S(1)} %broadcast_add_fusion, s32[512]{0:T(512)S(1)} %iota_add_fusion, bf16[4,512,576]{1,2,0:T(8,128)(2,1)S(1)} %copy-done.1), kind=kOutput, calls=%fused_computation.18 | convolution fusion | flops 134742016 | bytes 3151872 | tf_op jit(solution)/shard_map/sqk,skl->sql/dot_general | solution.py:74
  30.3 0.2 fusion.7
  30.5 0.1 reshape.244
  30.6 1.1 %select_convert_fusion = bf16[4,64,128]{2,1,0:T(8,128)(2,1)S(1)} fusion(f32[4,64,512]{2,1,0:T(8,128)} %fusion.9, pred[]{:T(512)S(6)} %eq.92, pred[]{:T(512)S(6)} %eq.91, pred[]{:T(512)S(6)} %eq.90), kind=kLoop, calls=%fused_computation.34 | loop fusion | flops 98304 | bytes 327683 | tf_op jit(solution)/shard_map/convert_element_type | solution.py:98
  31.8 1.1 %select_convert_fusion.2 = (bf16[4,64,128]{2,1,0:T(8,128)(2,1)S(1)}, bf16[4,64,128]{2,1,0:T(8,128)(2,1)S(1)}) fusion(f32[4,64,512]{2,1,0:T(8,128)} %fusion.9, pred[]{:T(512)S(6)} %eq.86, pred[]{:T(512)S(6)} %eq.85, pred[]{:T(512)S(6)} %eq.84, pred[]{:T(512)S(6)} %eq.89, pred[]{:T(512)S(6)} %eq.88, pred[]{:T(512)S(6)} %eq.87), kind=kLoop, calls=%fused_computation.36 | loop fusion | flops 196608 | bytes 393222 | tf_op jit(solution)/shard_map/convert_element_type | solution.py:98
  32.9 1.4 %collective-permute-start.3 = (bf16[268,128]{1,0:T(8,128)(2,1)S(1)}, bf16[268,128]{1,0:T(8,128)(2,1)S(1)}, u32[]{:S(2)}, u32[]{:S(2)}) collective-permute-start(bf16[268,128]{1,0:T(8,128)(2,1)S(1)} %get-tuple-element.18), channel_id=1, source_target_pairs={{0,4},{4,8},{8,12},{12,0},{1,5},{5,9},{9,13},{13,1},{2,6},{6,10},{... | collective-permute-start | bytes 205832 | tf_op jit(solution)/shard_map/ppermute | solution.py:118
  34.3 0.8 %collective-permute-start.4 = (bf16[268,128]{1,0:T(8,128)(2,1)S(1)}, bf16[268,128]{1,0:T(8,128)(2,1)S(1)}, u32[]{:S(2)}, u32[]{:S(2)}) collective-permute-start(bf16[268,128]{1,0:T(8,128)(2,1)S(1)} %get-tuple-element.19), channel_id=1, source_target_pairs={{0,8},{4,12},{8,0},{12,4},{1,9},{5,13},{9,1},{13,5},{2,10},{6,14},... | collective-permute-start | bytes 205832 | tf_op jit(solution)/shard_map/ppermute | solution.py:118
  35.1 2.3 %collective-permute-start.5 = (bf16[268,128]{1,0:T(8,128)(2,1)S(1)}, bf16[268,128]{1,0:T(8,128)(2,1)S(1)}, u32[]{:S(2)}, u32[]{:S(2)}) collective-permute-start(bf16[268,128]{1,0:T(8,128)(2,1)S(1)} %get-tuple-element.20), channel_id=1, source_target_pairs={{0,12},{4,0},{8,4},{12,8},{1,13},{5,1},{9,5},{13,9},{2,14},{6,2},{... | collective-permute-start | bytes 205832 | tf_op jit(solution)/shard_map/ppermute | solution.py:118
  37.3 0.7 %collective-permute-done.3 = bf16[268,128]{1,0:T(8,128)(2,1)S(1)} collective-permute-done((bf16[268,128]{1,0:T(8,128)(2,1)S(1)}, bf16[268,128]{1,0:T(8,128)(2,1)S(1)}, u32[]{:S(2)}, u32[]{:S(2)}) %collective-permute-start.3) | collective-permute-done | bytes 68640 | tf_op jit(solution)/shard_map/ppermute | solution.py:118
  38.0 2.0 %collective-permute-done.4 = bf16[268,128]{1,0:T(8,128)(2,1)S(1)} collective-permute-done((bf16[268,128]{1,0:T(8,128)(2,1)S(1)}, bf16[268,128]{1,0:T(8,128)(2,1)S(1)}, u32[]{:S(2)}, u32[]{:S(2)}) %collective-permute-start.4) | collective-permute-done | bytes 68640 | tf_op jit(solution)/shard_map/ppermute | solution.py:118
  40.0 0.1 squeeze.38
  40.1 0.1 squeeze.39
  40.2 0.1 squeeze.40
  40.3 0.1 squeeze.41
  40.4 0.1 squeeze.42
  40.5 0.1 squeeze.43
  40.6 0.2 fusion.19
  40.9 0.4 fusion.34
  41.3 2.4 %collective-permute-start.6 = (bf16[8,32,128]{2,0,1:T(8,128)(2,1)S(1)}, bf16[8,32,128]{2,0,1:T(8,128)(2,1)S(1)}, u32[]{:S(2)}, u32[]{:S(2)}) collective-permute-start(bf16[8,32,128]{2,0,1:T(8,128)(2,1)S(1)} %get-tuple-element.32), channel_id=1, source_target_pairs={{0,4},{4,8},{8,12},{12,0},{1,5},{5,9},{9,13},{13,1},{2,6},{6,10},{... | collective-permute-start | bytes 196616 | tf_op jit(solution)/shard_map/ppermute | solution.py:132
  43.7 0.9 %collective-permute-start.7 = (bf16[8,32,128]{2,0,1:T(8,128)(2,1)S(1)}, bf16[8,32,128]{2,0,1:T(8,128)(2,1)S(1)}, u32[]{:S(2)}, u32[]{:S(2)}) collective-permute-start(bf16[8,32,128]{2,0,1:T(8,128)(2,1)S(1)} %get-tuple-element.32), channel_id=1, source_target_pairs={{0,8},{4,12},{8,0},{12,4},{1,9},{5,13},{9,1},{13,5},{2,10},{6,14},... | collective-permute-start | bytes 196616 | tf_op jit(solution)/shard_map/ppermute | solution.py:132
  44.5 1.3 %collective-permute-start.8 = (bf16[8,32,128]{2,0,1:T(8,128)(2,1)S(1)}, bf16[8,32,128]{2,0,1:T(8,128)(2,1)S(1)}, u32[]{:S(2)}, u32[]{:S(2)}) collective-permute-start(bf16[8,32,128]{2,0,1:T(8,128)(2,1)S(1)} %get-tuple-element.32), channel_id=1, source_target_pairs={{0,12},{4,0},{8,4},{12,8},{1,13},{5,1},{9,5},{13,9},{2,14},{6,2},{... | collective-permute-start | bytes 196616 | tf_op jit(solution)/shard_map/ppermute | solution.py:132
  45.8 0.4 collective-permute-done.6
  46.2 2.1 %collective-permute-done.7 = bf16[8,32,128]{2,0,1:T(8,128)(2,1)S(1)} collective-permute-done((bf16[8,32,128]{2,0,1:T(8,128)(2,1)S(1)}, bf16[8,32,128]{2,0,1:T(8,128)(2,1)S(1)}, u32[]{:S(2)}, u32[]{:S(2)}) %collective-permute-start.7) | collective-permute-done | bytes 65568 | tf_op jit(solution)/shard_map/ppermute | solution.py:132
  48.3 7.2 %fusion.23 = f32[8,1792]{1,0:T(8,128)S(1)} fusion(bf16[4096,1792]{1,0:T(8,128)(2,1)} %param.13, bf16[8,32,128]{2,0,1:T(8,128)(2,1)S(1)} %collective-permute-done.8, bf16[8,32,128]{2,0,1:T(8,128)(2,1)S(1)} %collective-permute-done.7, f32[8,32,128]{2,0,1:T(8,128)S(1)} %get-tuple-element.33, bf16[8,32,128]{2,0,1:T(8,128)(2,1)S(1)} %collective-permute-done.6), kind=kOutput, calls=%fused_computation.47 | convolution fusion | flops 117669888 | bytes 15065088 | tf_op jit(solution)/shard_map/dot_general | solution.py:138
  55.5 0.1 select_select_fusion.2
  55.6 1.1 %collective-permute-start.10 = (f32[8,448]{1,0:T(8,128)S(1)}, f32[8,448]{1,0:T(8,128)S(1)}, u32[]{:S(2)}, u32[]{:S(2)}) collective-permute-start(f32[8,448]{1,0:T(8,128)S(1)} %get-tuple-element.17), channel_id=1, source_target_pairs={{0,2},{1,3},{2,0},{3,1},{4,6},{5,7},{6,4},{7,5},{8,10},{9,11},{10,... | collective-permute-start | bytes 43016 | tf_op jit(solution)/shard_map/ppermute | solution.py:148
  56.7 4.2 %collective-permute-start.9 = (f32[8,448]{1,0:T(8,128)S(1)}, f32[8,448]{1,0:T(8,128)S(1)}, u32[]{:S(2)}, u32[]{:S(2)}) collective-permute-start(f32[8,448]{1,0:T(8,128)S(1)} %get-tuple-element.16), channel_id=1, source_target_pairs={{0,1},{1,2},{2,3},{3,0},{4,5},{5,6},{6,7},{7,4},{8,9},{9,10},{10,1... | collective-permute-start | bytes 43016 | tf_op jit(solution)/shard_map/ppermute | solution.py:148
  61.0 0.1 select_select_fusion
  61.1 0.8 %collective-permute-done.9 = f32[8,448]{1,0:T(8,128)S(1)} collective-permute-done((f32[8,448]{1,0:T(8,128)S(1)}, f32[8,448]{1,0:T(8,128)S(1)}, u32[]{:S(2)}, u32[]{:S(2)}) %collective-permute-start.9) | collective-permute-done | bytes 14368 | tf_op jit(solution)/shard_map/ppermute | solution.py:148
  61.8 2.4 %collective-permute-done.11 = f32[8,448]{1,0:T(8,128)S(1)} collective-permute-done((f32[8,448]{1,0:T(8,128)S(1)}, f32[8,448]{1,0:T(8,128)S(1)}, u32[]{:S(2)}, u32[]{:S(2)}) %collective-permute-start.11) | collective-permute-done | bytes 14368 | tf_op jit(solution)/shard_map/ppermute | solution.py:148
  64.2 0.7 %add_add_fusion = f32[8,448]{1,0:T(8,128)} fusion(f32[8,448]{1,0:T(8,128)S(1)} %collective-permute-done.11, f32[8,448]{1,0:T(8,128)S(1)} %collective-permute-done.10, f32[8,448]{1,0:T(8,128)S(1)} %collective-permute-done.9, f32[8,1792]{1,0:T(8,128)S(1)} %fusion.23, pred[]{:T(512)S(6)} %eq.97, pred[]{:T(512)S(6)} %eq.96, pred[]{:T(512)S(6)} %eq.83), kind=kLoop, calls=%fused_computation.51 | loop fusion | flops 21504 | bytes 114691 | tf_op jit(solution)/shard_map/add | solution.py:148
  (44 shorter events, 0.3 us)
Async XLA Ops:
  0.0 40.9 %copy-start = (bf16[32,128,128]{2,1,0:T(8,128)(2,1)S(1)}, bf16[32,128,128]{2,1,0:T(8,128)(2,1)}, u32[]{:S(2)}) copy-start(bf16[32,128,128]{2,1,0:T(8,128)(2,1)} %param.12) | copy-start | bytes 3145732
  1.7 4.7 %slice-start = ((bf16[4,512,576]{1,2,0:T(8,128)(2,1)}), bf16[4,512,512]{1,2,0:T(8,128)(2,1)S(1)}, s32[]{:S(2)}) async-start(bf16[4,512,576]{1,2,0:T(8,128)(2,1)} %param.9), calls=%async_computation | async-start | bytes 4194304
  1.7 23.4 %collective-permute-start = (bf16[8,32,128]{2,0,1:T(8,128)(2,1)S(1)}, bf16[8,32,128]{2,0,1:T(8,128)(2,1)}, u32[]{:S(2)}, u32[]{:S(2)}) collective-permute-start(bf16[8,32,128]{2,0,1:T(8,128)(2,1)S(1)} %fusion.4), channel_id=1, source_target_pairs={{0,4},{4,8},{8,12},{12,0},{1,5},{5,9},{9,13},{13,1},{2,6},{6,10},{... | collective-permute-start | bytes 196616 | tf_op jit(solution)/shard_map/ppermute | solution.py:38
  3.8 22.4 %collective-permute-start.2 = (bf16[8,32,128]{2,0,1:T(8,128)(2,1)S(1)}, bf16[8,32,128]{2,0,1:T(8,128)(2,1)}, u32[]{:S(2)}, u32[]{:S(2)}) collective-permute-start(bf16[8,32,128]{2,0,1:T(8,128)(2,1)S(1)} %fusion.4), channel_id=1, source_target_pairs={{0,12},{4,0},{8,4},{12,8},{1,13},{5,1},{9,5},{13,9},{2,14},{6,2},{... | collective-permute-start | bytes 196616 | tf_op jit(solution)/shard_map/ppermute | solution.py:38
  5.9 21.5 %collective-permute-start.1 = (bf16[8,32,128]{2,0,1:T(8,128)(2,1)S(1)}, bf16[8,32,128]{2,0,1:T(8,128)(2,1)}, u32[]{:S(2)}, u32[]{:S(2)}) collective-permute-start(bf16[8,32,128]{2,0,1:T(8,128)(2,1)S(1)} %fusion.4), channel_id=1, source_target_pairs={{0,8},{4,12},{8,0},{12,4},{1,9},{5,13},{9,1},{13,5},{2,10},{6,14},... | collective-permute-start | bytes 196616 | tf_op jit(solution)/shard_map/ppermute | solution.py:38
  11.4 10.9 %copy-start.6 = (s32[4]{0:T(128)S(1)}, s32[4]{0:T(128)}, u32[]{:S(2)}) copy-start(s32[4]{0:T(128)} %param.10) | copy-start | bytes 52
  11.4 10.9 %copy-start.1 = (bf16[4,512,576]{1,2,0:T(8,128)(2,1)S(1)}, bf16[4,512,576]{1,2,0:T(8,128)(2,1)}, u32[]{:S(2)}) copy-start(bf16[4,512,576]{1,2,0:T(8,128)(2,1)} %param.9) | copy-start | bytes 7077892
  22.2 3.7 %copy-start.3 = (bf16[4,512,1,128]{3,2,1,0:T(2,128)(2,1)S(1)}, bf16[4,512,1,128]{3,2,1,0:T(2,128)(2,1)}, u32[]{:S(2)}) copy-start(bf16[4,512,1,128]{3,2,1,0:T(2,128)(2,1)} %copy.33) | copy-start | bytes 1572868
  22.2 4.9 %copy-start.2 = (bf16[4,512,1,128]{3,2,1,0:T(2,128)(2,1)S(1)}, bf16[4,512,1,128]{3,2,1,0:T(2,128)(2,1)}, u32[]{:S(2)}) copy-start(bf16[4,512,1,128]{3,2,1,0:T(2,128)(2,1)} %copy.35) | copy-start | bytes 1572868
  22.2 6.0 %copy-start.4 = (bf16[4,512,1,128]{3,2,1,0:T(2,128)(2,1)S(1)}, bf16[4,512,1,128]{3,2,1,0:T(2,128)(2,1)}, u32[]{:S(2)}) copy-start(bf16[4,512,1,128]{3,2,1,0:T(2,128)(2,1)} %copy.34) | copy-start | bytes 1572868
  30.3 10.3 %copy-start.5 = (f32[4,64,512]{2,1,0:T(8,128)S(1)}, f32[4,64,512]{2,1,0:T(8,128)}, u32[]{:S(2)}) copy-start(f32[4,64,512]{2,1,0:T(8,128)} %fusion.9) | copy-start | bytes 1572868
  32.9 5.1 %collective-permute-start.3 = (bf16[268,128]{1,0:T(8,128)(2,1)S(1)}, bf16[268,128]{1,0:T(8,128)(2,1)S(1)}, u32[]{:S(2)}, u32[]{:S(2)}) collective-permute-start(bf16[268,128]{1,0:T(8,128)(2,1)S(1)} %get-tuple-element.18), channel_id=1, source_target_pairs={{0,4},{4,8},{8,12},{12,0},{1,5},{5,9},{9,13},{13,1},{2,6},{6,10},{... | collective-permute-start | bytes 205832 | tf_op jit(solution)/shard_map/ppermute | solution.py:118
  34.3 5.7 %collective-permute-start.4 = (bf16[268,128]{1,0:T(8,128)(2,1)S(1)}, bf16[268,128]{1,0:T(8,128)(2,1)S(1)}, u32[]{:S(2)}, u32[]{:S(2)}) collective-permute-start(bf16[268,128]{1,0:T(8,128)(2,1)S(1)} %get-tuple-element.19), channel_id=1, source_target_pairs={{0,8},{4,12},{8,0},{12,4},{1,9},{5,13},{9,1},{13,5},{2,10},{6,14},... | collective-permute-start | bytes 205832 | tf_op jit(solution)/shard_map/ppermute | solution.py:118
  35.1 5.1 %collective-permute-start.5 = (bf16[268,128]{1,0:T(8,128)(2,1)S(1)}, bf16[268,128]{1,0:T(8,128)(2,1)S(1)}, u32[]{:S(2)}, u32[]{:S(2)}) collective-permute-start(bf16[268,128]{1,0:T(8,128)(2,1)S(1)} %get-tuple-element.20), channel_id=1, source_target_pairs={{0,12},{4,0},{8,4},{12,8},{1,13},{5,1},{9,5},{13,9},{2,14},{6,2},{... | collective-permute-start | bytes 205832 | tf_op jit(solution)/shard_map/ppermute | solution.py:118
  41.3 4.9 %collective-permute-start.6 = (bf16[8,32,128]{2,0,1:T(8,128)(2,1)S(1)}, bf16[8,32,128]{2,0,1:T(8,128)(2,1)S(1)}, u32[]{:S(2)}, u32[]{:S(2)}) collective-permute-start(bf16[8,32,128]{2,0,1:T(8,128)(2,1)S(1)} %get-tuple-element.32), channel_id=1, source_target_pairs={{0,4},{4,8},{8,12},{12,0},{1,5},{5,9},{9,13},{13,1},{2,6},{6,10},{... | collective-permute-start | bytes 196616 | tf_op jit(solution)/shard_map/ppermute | solution.py:132
  43.7 4.6 %collective-permute-start.7 = (bf16[8,32,128]{2,0,1:T(8,128)(2,1)S(1)}, bf16[8,32,128]{2,0,1:T(8,128)(2,1)S(1)}, u32[]{:S(2)}, u32[]{:S(2)}) collective-permute-start(bf16[8,32,128]{2,0,1:T(8,128)(2,1)S(1)} %get-tuple-element.32), channel_id=1, source_target_pairs={{0,8},{4,12},{8,0},{12,4},{1,9},{5,13},{9,1},{13,5},{2,10},{6,14},... | collective-permute-start | bytes 196616 | tf_op jit(solution)/shard_map/ppermute | solution.py:132
  44.5 3.8 %collective-permute-start.8 = (bf16[8,32,128]{2,0,1:T(8,128)(2,1)S(1)}, bf16[8,32,128]{2,0,1:T(8,128)(2,1)S(1)}, u32[]{:S(2)}, u32[]{:S(2)}) collective-permute-start(bf16[8,32,128]{2,0,1:T(8,128)(2,1)S(1)} %get-tuple-element.32), channel_id=1, source_target_pairs={{0,12},{4,0},{8,4},{12,8},{1,13},{5,1},{9,5},{13,9},{2,14},{6,2},{... | collective-permute-start | bytes 196616 | tf_op jit(solution)/shard_map/ppermute | solution.py:132
  55.6 5.5 %collective-permute-start.10 = (f32[8,448]{1,0:T(8,128)S(1)}, f32[8,448]{1,0:T(8,128)S(1)}, u32[]{:S(2)}, u32[]{:S(2)}) collective-permute-start(f32[8,448]{1,0:T(8,128)S(1)} %get-tuple-element.17), channel_id=1, source_target_pairs={{0,2},{1,3},{2,0},{3,1},{4,6},{5,7},{6,4},{7,5},{8,10},{9,11},{10,... | collective-permute-start | bytes 43016 | tf_op jit(solution)/shard_map/ppermute | solution.py:148
  56.7 5.1 %collective-permute-start.9 = (f32[8,448]{1,0:T(8,128)S(1)}, f32[8,448]{1,0:T(8,128)S(1)}, u32[]{:S(2)}, u32[]{:S(2)}) collective-permute-start(f32[8,448]{1,0:T(8,128)S(1)} %get-tuple-element.16), channel_id=1, source_target_pairs={{0,1},{1,2},{2,3},{3,0},{4,5},{5,6},{6,7},{7,4},{8,9},{9,10},{10,1... | collective-permute-start | bytes 43016 | tf_op jit(solution)/shard_map/ppermute | solution.py:148
  61.0 3.2 %collective-permute-start.11 = (f32[8,448]{1,0:T(8,128)S(1)}, f32[8,448]{1,0:T(8,128)S(1)}, u32[]{:S(2)}, u32[]{:S(2)}) collective-permute-start(f32[8,448]{1,0:T(8,128)S(1)} %select_select_fusion), channel_id=1, source_target_pairs={{0,3},{1,0},{2,1},{3,2},{4,7},{5,4},{6,5},{7,6},{8,11},{9,8},{10,9... | collective-permute-start | bytes 43016 | tf_op jit(solution)/shard_map/ppermute | solution.py:148

commit v9 on v5

--- a/solution.py
+++ b/solution.py
@@ -3,6 +3,7 @@
 import jax
 import jax.numpy as jnp
 from jax import lax
+from jax.experimental.layout import Layout, with_layout_constraint
 from jax.sharding import PartitionSpec as P
 
 ROTARY_CHANNELS = 64
@@ -33,6 +34,7 @@
     q_part = jnp.einsum(
         "rhn,hnl->rhl", query_nope, w_absorb, preferred_element_type=jnp.float32
     ).astype(jnp.bfloat16)
+    q_part = with_layout_constraint(q_part, Layout(major_to_minor=(0, 1, 2)))
     if small_ctx:
         received = [q_part] + [
             lax.ppermute(q_part, "ctx", shift_pairs(n_ctx, k)) for k in range(1, n_ctx)

time: 47.6 us -> 47.7 us (level)
  no operation moved by 1% of the time
where the time goes in v9:
time: 47.7 us; the launch traced here: 47.5 us
  starting transfers between devices  15.3 us (32%)
  waiting for transfers between devices  14.5 us (30%)
  matrix products  13.5 us (28%)
  other arithmetic  2.26 us (5%)
  local copies, waits for them, and re-layouts  1.59 us (3%)
    dot_general x1, matrix products, per_device(): jnp.dot(values.reshape(row_count, -1), w_output, preferred_element_type=j...  7.17 us
    ppermute x3, starting transfers between devices, per_device(): lax.ppermute(q_part, 'ctx', shift_pairs(n_ctx, k))  5.56 us
    ppermute x3, waiting for transfers between devices, per_device(): lax.ppermute(packed_for((me_ctx + k) % n_ctx), 'ctx', shift_pairs(n_ctx, k))  5.2 us
    ppermute x3, waiting for transfers between devices, per_device(): lax.ppermute(sent, 'ctx', shift_pairs(n_ctx, k)).astype(jnp.float32)  4.87 us
    ppermute x3, starting transfers between devices, per_device(): lax.ppermute(sent, 'ctx', shift_pairs(n_ctx, k)).astype(jnp.float32)  3.77 us
    ppermute x3, starting transfers between devices, per_device(): lax.ppermute(packed_for((me_ctx + k) % n_ctx), 'ctx', shift_pairs(n_ctx, k))  3.72 us
    ppermute x3, waiting for transfers between devices, per_device(): lax.ppermute(pick((me_head + k) % n_head, col_slices), 'head', shift_pair...  3.15 us
    dot_general x1, matrix products, per_device(): jnp.einsum('sqc,skc->sqk', q_latent.reshape(seq_count, q_rows, latent_wid...  2.32 us
  transfers between devices with their start and end apart: 12, of which 8 were waited for; matrix products, arithmetic and copies ran while one was open for 6% of the time, Pallas kernels for 0%

profile of v9, /device:TPU:1, one launch (start us, length us, event | category | flops | bytes accessed | tf_op | source)
XLA Modules:
  0.0 47.5 jit_solution(10353090478693966259)
XLA Ops:
  0.0 1.7 %fusion.38 = bf16[32,128,8]{1,2,0:T(8,128)(2,1)S(1)} fusion(bf16[32,128,128]{2,1,0:T(8,128)(2,1)} %param.11, bf16[8,32,128]{2,1,0:T(8,128)(2,1)} %param.7), kind=kOutput, calls=%fused_computation.49 | convolution fusion | flops 8388608 | bytes 1179648 | tf_op jit(solution)/shard_map/rhn,hnl->rhl/dot_general | solution.py:34
  1.7 2.2 %collective-permute-start = (bf16[8,32,128]{2,1,0:T(8,128)(2,1)S(1)}, bf16[8,32,128]{2,1,0:T(8,128)(2,1)S(1)}, u32[]{:S(2)}, u32[]{:S(2)}) collective-permute-start(bf16[8,32,128]{2,1,0:T(8,128)(2,1)S(1)} %bitcast.32), channel_id=1, source_target_pairs={{0,4},{4,8},{8,12},{12,0},{1,5},{5,9},{9,13},{13,1},{2,6},{6,10},{... | collective-permute-start | bytes 196616 | tf_op jit(solution)/shard_map/ppermute | solution.py:40
  3.9 2.3 %collective-permute-start.1 = (bf16[8,32,128]{2,1,0:T(8,128)(2,1)S(1)}, bf16[8,32,128]{2,1,0:T(8,128)(2,1)S(1)}, u32[]{:S(2)}, u32[]{:S(2)}) collective-permute-start(bf16[8,32,128]{2,1,0:T(8,128)(2,1)S(1)} %bitcast.33), channel_id=1, source_target_pairs={{0,8},{4,12},{8,0},{12,4},{1,9},{5,13},{9,1},{13,5},{2,10},{6,14},... | collective-permute-start | bytes 196616 | tf_op jit(solution)/shard_map/ppermute | solution.py:40
  6.2 1.1 %collective-permute-start.2 = (bf16[8,32,128]{2,1,0:T(8,128)(2,1)S(1)}, bf16[8,32,128]{2,1,0:T(8,128)(2,1)S(1)}, u32[]{:S(2)}, u32[]{:S(2)}) collective-permute-start(bf16[8,32,128]{2,1,0:T(8,128)(2,1)S(1)} %bitcast.34), channel_id=1, source_target_pairs={{0,12},{4,0},{8,4},{12,8},{1,13},{5,1},{9,5},{13,9},{2,14},{6,2},{... | collective-permute-start | bytes 196616 | tf_op jit(solution)/shard_map/ppermute | solution.py:40
  7.4 0.1 broadcast_bitcast_fusion
  7.4 0.1 broadcast_bitcast_fusion.1
  7.5 0.1 broadcast_bitcast_fusion.2
  7.6 0.1 broadcast_in_dim.95
  7.7 0.1 broadcast_in_dim.96
  7.8 0.7 %broadcast_add_fusion.1 = s32[4]{0:T(128)S(1)} fusion(s32[4]{0:T(128)} %param.10), kind=kLoop, calls=%fused_computation.92 | loop fusion | flops 4 | bytes 32 | tf_op jit(solution)/shard_map/sub | solution.py:65
  8.4 0.1 broadcast_add_fusion
  8.5 1.2 %fusion.18 = f32[4,64,512]{2,1,0:T(8,128)S(1)} fusion(bf16[4,64,64]{2,1,0:T(8,128)(2,1)} %bitcast.42, bf16[4,512,576]{1,2,0:T(8,128)(2,1)} %param.9), kind=kOutput, calls=%fused_computation.13 | convolution fusion | flops 16777216 | bytes 851968 | tf_op jit(solution)/shard_map/sqc,skc->sqk/dot_general | solution.py:56
  9.7 0.1 broadcast_in_dim.100
  9.8 0.1 broadcast_in_dim.101
  9.9 1.3 %collective-permute-done.1 = bf16[8,32,128]{2,1,0:T(8,128)(2,1)S(1)} collective-permute-done((bf16[8,32,128]{2,1,0:T(8,128)(2,1)S(1)}, bf16[8,32,128]{2,1,0:T(8,128)(2,1)S(1)}, u32[]{:S(2)}, u32[]{:S(2)}) %collective-permute-start.1) | collective-permute-done | bytes 65568 | tf_op jit(solution)/shard_map/ppermute | solution.py:40
  11.2 0.1 broadcast_in_dim.105
  11.3 0.1 broadcast_in_dim.106
  11.4 0.1 broadcast_in_dim.107
  11.5 0.1 broadcast_in_dim.108
  11.7 2.3 %fusion.46 = (f32[4,64]{1,0:T(4,128)S(1)}, f32[4,64,512]{2,1,0:T(8,128)S(1)}) fusion(f32[4,64,512]{2,1,0:T(8,128)S(1)} %fusion.18, bf16[4,512,576]{1,2,0:T(8,128)(2,1)} %param.9, bf16[4,64,512]{2,1,0:T(8,128)(2,1)S(1)} %broadcast_in_dim.96, bf16[4,64,512]{2,1,0:T(8,128)(2,1)S(1)} %broadcast_in_dim.101, bf16[4,64,512]{2,1,0:T(8,128)(2,1)S(1)} %broadcast_in_dim.106, ...), kind=kOutput, calls=%fused_computation.97 | convolution fusion | flops 135266048 | bytes 4199936 | tf_op jit(solution)/shard_map/sqc,skc->sqk/dot_general | solution.py:50
  14.0 0.8 %fusion.2 = f32[4,64,512]{2,1,0:T(8,128)S(1)} fusion(bf16[4,512,576]{1,2,0:T(8,128)(2,1)S(1)} %copy-done.1, f32[4,64,512]{2,1,0:T(8,128)S(1)} %get-tuple-element.27, f32[4,64]{1,0:T(4,128)S(1)} %get-tuple-element.26, s32[4,64]{1,0:T(4,128)S(1)} %broadcast_add_fusion, s32[512]{0:T(512)S(1)} %iota_add_fusion), kind=kOutput, calls=%fused_computation.2 | convolution fusion | flops 134742016 | bytes 3151872 | tf_op jit(solution)/shard_map/sqk,skl->sql/dot_general | solution.py:71
  14.8 0.3 fusion.13
  15.0 0.1 reshape.265
  15.2 1.6 %collective-permute-start.3 = (bf16[268,128]{1,0:T(8,128)(2,1)S(1)}, bf16[268,128]{1,0:T(8,128)(2,1)S(1)}, u32[]{:S(2)}, u32[]{:S(2)}) collective-permute-start(bf16[268,128]{1,0:T(8,128)(2,1)S(1)} %get-tuple-element.14), channel_id=1, source_target_pairs={{0,4},{4,8},{8,12},{12,0},{1,5},{5,9},{9,13},{13,1},{2,6},{6,10},{... | collective-permute-start | bytes 205832 | tf_op jit(solution)/shard_map/ppermute | solution.py:115
  16.8 2.2 %collective-permute-start.5 = (bf16[268,128]{1,0:T(8,128)(2,1)S(1)}, bf16[268,128]{1,0:T(8,128)(2,1)S(1)}, u32[]{:S(2)}, u32[]{:S(2)}) collective-permute-start(bf16[268,128]{1,0:T(8,128)(2,1)S(1)} %get-tuple-element.16), channel_id=1, source_target_pairs={{0,12},{4,0},{8,4},{12,8},{1,13},{5,1},{9,5},{13,9},{2,14},{6,2},{... | collective-permute-start | bytes 205832 | tf_op jit(solution)/shard_map/ppermute | solution.py:115
  18.9 1.3 %collective-permute-done.3 = bf16[268,128]{1,0:T(8,128)(2,1)S(1)} collective-permute-done((bf16[268,128]{1,0:T(8,128)(2,1)S(1)}, bf16[268,128]{1,0:T(8,128)(2,1)S(1)}, u32[]{:S(2)}, u32[]{:S(2)}) %collective-permute-start.3) | collective-permute-done | bytes 68640 | tf_op jit(solution)/shard_map/ppermute | solution.py:115
  20.3 3.8 %collective-permute-done.4 = bf16[268,128]{1,0:T(8,128)(2,1)S(1)} collective-permute-done((bf16[268,128]{1,0:T(8,128)(2,1)S(1)}, bf16[268,128]{1,0:T(8,128)(2,1)S(1)}, u32[]{:S(2)}, u32[]{:S(2)}) %collective-permute-start.4) | collective-permute-done | bytes 68640 | tf_op jit(solution)/shard_map/ppermute | solution.py:115
  24.2 0.1 squeeze.21
  24.3 0.1 squeeze.22
  24.4 0.1 squeeze.23
  24.4 0.1 squeeze.24
  24.5 0.1 squeeze.25
  24.6 0.1 squeeze.26
  24.7 0.2 fusion.30
  25.0 0.4 fusion.47
  25.4 1.6 %collective-permute-start.6 = (bf16[8,32,128]{2,0,1:T(8,128)(2,1)S(1)}, bf16[8,32,128]{2,0,1:T(8,128)(2,1)S(1)}, u32[]{:S(2)}, u32[]{:S(2)}) collective-permute-start(bf16[8,32,128]{2,0,1:T(8,128)(2,1)S(1)} %get-tuple-element.28), channel_id=1, source_target_pairs={{0,4},{4,8},{8,12},{12,0},{1,5},{5,9},{9,13},{13,1},{2,6},{6,10},{... | collective-permute-start | bytes 196616 | tf_op jit(solution)/shard_map/ppermute | solution.py:129
  27.0 2.2 %collective-permute-start.8 = (bf16[8,32,128]{2,0,1:T(8,128)(2,1)S(1)}, bf16[8,32,128]{2,0,1:T(8,128)(2,1)S(1)}, u32[]{:S(2)}, u32[]{:S(2)}) collective-permute-start(bf16[8,32,128]{2,0,1:T(8,128)(2,1)S(1)} %get-tuple-element.28), channel_id=1, source_target_pairs={{0,12},{4,0},{8,4},{12,8},{1,13},{5,1},{9,5},{13,9},{2,14},{6,2},{... | collective-permute-start | bytes 196616 | tf_op jit(solution)/shard_map/ppermute | solution.py:129
  29.2 1.2 %collective-permute-done.6 = bf16[8,32,128]{2,0,1:T(8,128)(2,1)S(1)} collective-permute-done((bf16[8,32,128]{2,0,1:T(8,128)(2,1)S(1)}, bf16[8,32,128]{2,0,1:T(8,128)(2,1)S(1)}, u32[]{:S(2)}, u32[]{:S(2)}) %collective-permute-start.6) | collective-permute-done | bytes 65568 | tf_op jit(solution)/shard_map/ppermute | solution.py:129
  30.4 3.7 %collective-permute-done.7 = bf16[8,32,128]{2,0,1:T(8,128)(2,1)S(1)} collective-permute-done((bf16[8,32,128]{2,0,1:T(8,128)(2,1)S(1)}, bf16[8,32,128]{2,0,1:T(8,128)(2,1)S(1)}, u32[]{:S(2)}, u32[]{:S(2)}) %collective-permute-start.7) | collective-permute-done | bytes 65568 | tf_op jit(solution)/shard_map/ppermute | solution.py:129
  34.0 7.2 %fusion.34 = f32[8,1792]{1,0:T(8,128)S(1)} fusion(bf16[4096,1792]{1,0:T(8,128)(2,1)} %param.13, bf16[8,32,128]{2,0,1:T(8,128)(2,1)S(1)} %collective-permute-done.8, bf16[8,32,128]{2,0,1:T(8,128)(2,1)S(1)} %collective-permute-done.7, f32[8,32,128]{2,0,1:T(8,128)S(1)} %get-tuple-element.29, bf16[8,32,128]{2,0,1:T(8,128)(2,1)S(1)} %collective-permute-done.6), kind=kOutput, calls=%fused_computation.46 | convolution fusion | flops 117669888 | bytes 15065088 | tf_op jit(solution)/shard_map/dot_general | solution.py:135
  41.2 0.1 select_select_fusion.2
  41.3 0.0 collective-permute-start.10
  41.3 2.2 %collective-permute-start.9 = (f32[8,448]{1,0:T(8,128)S(1)}, f32[8,448]{1,0:T(8,128)S(1)}, u32[]{:S(2)}, u32[]{:S(2)}) collective-permute-start(f32[8,448]{1,0:T(8,128)S(1)} %get-tuple-element.12), channel_id=1, source_target_pairs={{0,1},{1,2},{2,3},{3,0},{4,5},{5,6},{6,7},{7,4},{8,9},{9,10},{10,1... | collective-permute-start | bytes 43016 | tf_op jit(solution)/shard_map/ppermute | solution.py:145
  43.5 0.1 select_select_fusion
  43.6 0.3 collective-permute-done.10
  43.9 0.5 %collective-permute-done.9 = f32[8,448]{1,0:T(8,128)S(1)} collective-permute-done((f32[8,448]{1,0:T(8,128)S(1)}, f32[8,448]{1,0:T(8,128)S(1)}, u32[]{:S(2)}, u32[]{:S(2)}) %collective-permute-start.9) | collective-permute-done | bytes 14368 | tf_op jit(solution)/shard_map/ppermute | solution.py:145
  44.4 2.4 %collective-permute-done.11 = f32[8,448]{1,0:T(8,128)S(1)} collective-permute-done((f32[8,448]{1,0:T(8,128)S(1)}, f32[8,448]{1,0:T(8,128)S(1)}, u32[]{:S(2)}, u32[]{:S(2)}) %collective-permute-start.11) | collective-permute-done | bytes 14368 | tf_op jit(solution)/shard_map/ppermute | solution.py:145
  46.8 0.7 %add_add_fusion = f32[8,448]{1,0:T(8,128)} fusion(f32[8,448]{1,0:T(8,128)S(1)} %collective-permute-done.11, f32[8,448]{1,0:T(8,128)S(1)} %collective-permute-done.10, f32[8,448]{1,0:T(8,128)S(1)} %collective-permute-done.9, f32[8,1792]{1,0:T(8,128)S(1)} %fusion.34, pred[]{:T(512)S(6)} %eq.122, pred[]{:T(512)S(6)} %eq.121, pred[]{:T(512)S(6)} %eq.105), kind=kLoop, calls=%fused_computation.52 | loop fusion | flops 21504 | bytes 114691 | tf_op jit(solution)/shard_map/add | solution.py:145
  (34 shorter events, 0.3 us)
Async XLA Ops:
  0.0 25.0 %copy-start = (bf16[32,128,128]{2,1,0:T(8,128)(2,1)S(1)}, bf16[32,128,128]{2,1,0:T(8,128)(2,1)}, u32[]{:S(2)}) copy-start(bf16[32,128,128]{2,1,0:T(8,128)(2,1)} %param.12) | copy-start | bytes 3145732
  1.7 8.0 %collective-permute-start = (bf16[8,32,128]{2,1,0:T(8,128)(2,1)S(1)}, bf16[8,32,128]{2,1,0:T(8,128)(2,1)S(1)}, u32[]{:S(2)}, u32[]{:S(2)}) collective-permute-start(bf16[8,32,128]{2,1,0:T(8,128)(2,1)S(1)} %bitcast.32), channel_id=1, source_target_pairs={{0,4},{4,8},{8,12},{12,0},{1,5},{5,9},{9,13},{13,1},{2,6},{6,10},{... | collective-permute-start | bytes 196616 | tf_op jit(solution)/shard_map/ppermute | solution.py:40
  3.9 7.3 %collective-permute-start.1 = (bf16[8,32,128]{2,1,0:T(8,128)(2,1)S(1)}, bf16[8,32,128]{2,1,0:T(8,128)(2,1)S(1)}, u32[]{:S(2)}, u32[]{:S(2)}) collective-permute-start(bf16[8,32,128]{2,1,0:T(8,128)(2,1)S(1)} %bitcast.33), channel_id=1, source_target_pairs={{0,8},{4,12},{8,0},{12,4},{1,9},{5,13},{9,1},{13,5},{2,10},{6,14},... | collective-permute-start | bytes 196616 | tf_op jit(solution)/shard_map/ppermute | solution.py:40
  6.2 5.2 %collective-permute-start.2 = (bf16[8,32,128]{2,1,0:T(8,128)(2,1)S(1)}, bf16[8,32,128]{2,1,0:T(8,128)(2,1)S(1)}, u32[]{:S(2)}, u32[]{:S(2)}) collective-permute-start(bf16[8,32,128]{2,1,0:T(8,128)(2,1)S(1)} %bitcast.34), channel_id=1, source_target_pairs={{0,12},{4,0},{8,4},{12,8},{1,13},{5,1},{9,5},{13,9},{2,14},{6,2},{... | collective-permute-start | bytes 196616 | tf_op jit(solution)/shard_map/ppermute | solution.py:40
  11.6 2.3 %copy-start.1 = (bf16[4,512,576]{1,2,0:T(8,128)(2,1)S(1)}, bf16[4,512,576]{1,2,0:T(8,128)(2,1)}, u32[]{:S(2)}) copy-start(bf16[4,512,576]{1,2,0:T(8,128)(2,1)} %param.9) | copy-start | bytes 7077892
  15.2 5.1 %collective-permute-start.3 = (bf16[268,128]{1,0:T(8,128)(2,1)S(1)}, bf16[268,128]{1,0:T(8,128)(2,1)S(1)}, u32[]{:S(2)}, u32[]{:S(2)}) collective-permute-start(bf16[268,128]{1,0:T(8,128)(2,1)S(1)} %get-tuple-element.14), channel_id=1, source_target_pairs={{0,4},{4,8},{8,12},{12,0},{1,5},{5,9},{9,13},{13,1},{2,6},{6,10},{... | collective-permute-start | bytes 205832 | tf_op jit(solution)/shard_map/ppermute | solution.py:115
  16.8 7.4 %collective-permute-start.4 = (bf16[268,128]{1,0:T(8,128)(2,1)S(1)}, bf16[268,128]{1,0:T(8,128)(2,1)S(1)}, u32[]{:S(2)}, u32[]{:S(2)}) collective-permute-start(bf16[268,128]{1,0:T(8,128)(2,1)S(1)} %get-tuple-element.15), channel_id=1, source_target_pairs={{0,8},{4,12},{8,0},{12,4},{1,9},{5,13},{9,1},{13,5},{2,10},{6,14},... | collective-permute-start | bytes 205832 | tf_op jit(solution)/shard_map/ppermute | solution.py:115
  16.8 7.6 %collective-permute-start.5 = (bf16[268,128]{1,0:T(8,128)(2,1)S(1)}, bf16[268,128]{1,0:T(8,128)(2,1)S(1)}, u32[]{:S(2)}, u32[]{:S(2)}) collective-permute-start(bf16[268,128]{1,0:T(8,128)(2,1)S(1)} %get-tuple-element.16), channel_id=1, source_target_pairs={{0,12},{4,0},{8,4},{12,8},{1,13},{5,1},{9,5},{13,9},{2,14},{6,2},{... | collective-permute-start | bytes 205832 | tf_op jit(solution)/shard_map/ppermute | solution.py:115
  25.4 5.0 %collective-permute-start.6 = (bf16[8,32,128]{2,0,1:T(8,128)(2,1)S(1)}, bf16[8,32,128]{2,0,1:T(8,128)(2,1)S(1)}, u32[]{:S(2)}, u32[]{:S(2)}) collective-permute-start(bf16[8,32,128]{2,0,1:T(8,128)(2,1)S(1)} %get-tuple-element.28), channel_id=1, source_target_pairs={{0,4},{4,8},{8,12},{12,0},{1,5},{5,9},{9,13},{13,1},{2,6},{6,10},{... | collective-permute-start | bytes 196616 | tf_op jit(solution)/shard_map/ppermute | solution.py:129
  27.0 7.0 %collective-permute-start.7 = (bf16[8,32,128]{2,0,1:T(8,128)(2,1)S(1)}, bf16[8,32,128]{2,0,1:T(8,128)(2,1)S(1)}, u32[]{:S(2)}, u32[]{:S(2)}) collective-permute-start(bf16[8,32,128]{2,0,1:T(8,128)(2,1)S(1)} %get-tuple-element.28), channel_id=1, source_target_pairs={{0,8},{4,12},{8,0},{12,4},{1,9},{5,13},{9,1},{13,5},{2,10},{6,14},... | collective-permute-start | bytes 196616 | tf_op jit(solution)/shard_map/ppermute | solution.py:129
  27.0 7.0 %collective-permute-start.8 = (bf16[8,32,128]{2,0,1:T(8,128)(2,1)S(1)}, bf16[8,32,128]{2,0,1:T(8,128)(2,1)S(1)}, u32[]{:S(2)}, u32[]{:S(2)}) collective-permute-start(bf16[8,32,128]{2,0,1:T(8,128)(2,1)S(1)} %get-tuple-element.28), channel_id=1, source_target_pairs={{0,12},{4,0},{8,4},{12,8},{1,13},{5,1},{9,5},{13,9},{2,14},{6,2},{... | collective-permute-start | bytes 196616 | tf_op jit(solution)/shard_map/ppermute | solution.py:129
  41.3 2.6 %collective-permute-start.10 = (f32[8,448]{1,0:T(8,128)S(1)}, f32[8,448]{1,0:T(8,128)S(1)}, u32[]{:S(2)}, u32[]{:S(2)}) collective-permute-start(f32[8,448]{1,0:T(8,128)S(1)} %get-tuple-element.13), channel_id=1, source_target_pairs={{0,2},{1,3},{2,0},{3,1},{4,6},{5,7},{6,4},{7,5},{8,10},{9,11},{10,... | collective-permute-start | bytes 43016 | tf_op jit(solution)/shard_map/ppermute | solution.py:145
  41.3 3.1 %collective-permute-start.9 = (f32[8,448]{1,0:T(8,128)S(1)}, f32[8,448]{1,0:T(8,128)S(1)}, u32[]{:S(2)}, u32[]{:S(2)}) collective-permute-start(f32[8,448]{1,0:T(8,128)S(1)} %get-tuple-element.12), channel_id=1, source_target_pairs={{0,1},{1,2},{2,3},{3,0},{4,5},{5,6},{6,7},{7,4},{8,9},{9,10},{10,1... | collective-permute-start | bytes 43016 | tf_op jit(solution)/shard_map/ppermute | solution.py:145
  43.6 3.2 %collective-permute-start.11 = (f32[8,448]{1,0:T(8,128)S(1)}, f32[8,448]{1,0:T(8,128)S(1)}, u32[]{:S(2)}, u32[]{:S(2)}) collective-permute-start(f32[8,448]{1,0:T(8,128)S(1)} %select_select_fusion), channel_id=1, source_target_pairs={{0,3},{1,0},{2,1},{3,2},{4,7},{5,4},{6,5},{7,6},{8,11},{9,8},{10,9... | collective-permute-start | bytes 43016 | tf_op jit(solution)/shard_map/ppermute | solution.py:145

commit v10 on v5

--- a/solution.py
+++ b/solution.py
@@ -13,6 +13,10 @@
 
 def shift_pairs(n, k):
     return [(i, (i + k) % n) for i in range(n)]
+
+
+def shift_order(n):
+    return sorted(range(1, n), key=lambda k: -max(k, n - k))
 
 
 def pick(index, options):
@@ -34,9 +38,9 @@
         "rhn,hnl->rhl", query_nope, w_absorb, preferred_element_type=jnp.float32
     ).astype(jnp.bfloat16)
     if small_ctx:
-        received = [q_part] + [
-            lax.ppermute(q_part, "ctx", shift_pairs(n_ctx, k)) for k in range(1, n_ctx)
-        ]
+        received = [q_part] * n_ctx
+        for k in shift_order(n_ctx):
+            received[k] = lax.ppermute(q_part, "ctx", shift_pairs(n_ctx, k))
         source = (me_ctx - jnp.arange(n_ctx, dtype=jnp.int32)[None, None, :, None]) % n_ctx
         q_slots = received[-1][:, :, None, :]
         for k in range(n_ctx - 2, -1, -1):
@@ -111,7 +115,7 @@
     if small_ctx:
         parts = [(pick(me_ctx, sum_slices), stats)] + [
             unpack(lax.ppermute(packed_for((me_ctx + k) % n_ctx), "ctx", shift_pairs(n_ctx, k)))
-            for k in range(1, n_ctx)
+            for k in shift_order(n_ctx)
         ]
     else:
         packed = jnp.stack([jnp.concatenate([s, stats], axis=0) for s in sum_slices])
@@ -125,7 +129,7 @@
         sent = value_part.astype(jnp.bfloat16)
         received = [value_part] + [
             lax.ppermute(sent, "ctx", shift_pairs(n_ctx, k)).astype(jnp.float32)
-            for k in range(1, n_ctx)
+            for k in shift_order(n_ctx)
         ]
         values = sum(received).astype(jnp.bfloat16)
     else:

time: 47.6 us -> 49 us (1.029)
  starting transfers between devices: 15.2 us -> 15.9 us
  waiting for transfers between devices: 14.5 us -> 15.2 us
    ppermute x3, starting transfers between devices: 2.22 us -> 3.74 us  [per_device(): lax.ppermute(pick((me_head + k) % n_head, col_slices), 'head', shift_pair...]
    ppermute x3, waiting for transfers between devices: 5.24 us -> 6.33 us  [per_device(): lax.ppermute(packed_for((me_ctx + k) % n_ctx), 'ctx', shift_pairs(n_ctx, k))]
where the time goes in v10:
time: 49 us; the launch traced here: 48.8 us
  starting transfers between devices  15.9 us (32%)
  waiting for transfers between devices  15.2 us (31%)
  matrix products  13.5 us (28%)
  other arithmetic  2.26 us (5%)
  local copies, waits for them, and re-layouts  1.62 us (3%)
    dot_general x1, matrix products, per_device(): jnp.dot(values.reshape(row_count, -1), w_output, preferred_element_type=j...  7.17 us
    ppermute x3, waiting for transfers between devices, per_device(): lax.ppermute(packed_for((me_ctx + k) % n_ctx), 'ctx', shift_pairs(n_ctx, k))  6.33 us
    ppermute x3, starting transfers between devices, per_device(): received[k] = lax.ppermute(q_part, 'ctx', shift_pairs(n_ctx, k))  5.51 us
    ppermute x3, waiting for transfers between devices, per_device(): lax.ppermute(sent, 'ctx', shift_pairs(n_ctx, k)).astype(jnp.float32)  4.45 us
    ppermute x3, starting transfers between devices, per_device(): lax.ppermute(pick((me_head + k) % n_head, col_slices), 'head', shift_pair...  3.74 us
    ppermute x3, starting transfers between devices, per_device(): lax.ppermute(packed_for((me_ctx + k) % n_ctx), 'ctx', shift_pairs(n_ctx, k))  3.32 us
    ppermute x3, starting transfers between devices, per_device(): lax.ppermute(sent, 'ctx', shift_pairs(n_ctx, k)).astype(jnp.float32)  3.28 us
    ppermute x3, waiting for transfers between devices, per_device(): lax.ppermute(pick((me_head + k) % n_head, col_slices), 'head', shift_pair...  3.15 us
  transfers between devices with their start and end apart: 12, of which 8 were waited for; matrix products, arithmetic and copies ran while one was open for 6% of the time, Pallas kernels for 0%

profile of v10, /device:TPU:1, one launch (start us, length us, event | category | flops | bytes accessed | tf_op | source)
XLA Modules:
  0.0 48.8 jit_solution(4761901026583283083)
XLA Ops:
  0.0 1.7 %fusion.13 = bf16[8,32,128]{2,0,1:T(8,128)(2,1)S(1)} fusion(bf16[32,128,128]{2,1,0:T(8,128)(2,1)} %param.11, bf16[8,32,128]{2,1,0:T(8,128)(2,1)} %param.7), kind=kOutput, calls=%fused_computation.9 | convolution fusion | flops 8421376 | bytes 1179648 | tf_op jit(solution)/shard_map/rhn,hnl->rhl/dot_general | solution.py:37
  1.7 2.1 %collective-permute-start = (bf16[8,32,128]{2,0,1:T(8,128)(2,1)S(1)}, bf16[8,32,128]{2,0,1:T(8,128)(2,1)S(1)}, u32[]{:S(2)}, u32[]{:S(2)}) collective-permute-start(bf16[8,32,128]{2,0,1:T(8,128)(2,1)S(1)} %fusion.13), channel_id=1, source_target_pairs={{0,4},{4,8},{8,12},{12,0},{1,5},{5,9},{9,13},{13,1},{2,6},{6,10},{... | collective-permute-start | bytes 196616 | tf_op jit(solution)/shard_map/ppermute | solution.py:43
  3.8 2.3 %collective-permute-start.1 = (bf16[8,32,128]{2,0,1:T(8,128)(2,1)S(1)}, bf16[8,32,128]{2,0,1:T(8,128)(2,1)S(1)}, u32[]{:S(2)}, u32[]{:S(2)}) collective-permute-start(bf16[8,32,128]{2,0,1:T(8,128)(2,1)S(1)} %fusion.13), channel_id=1, source_target_pairs={{0,8},{4,12},{8,0},{12,4},{1,9},{5,13},{9,1},{13,5},{2,10},{6,14},... | collective-permute-start | bytes 196616 | tf_op jit(solution)/shard_map/ppermute | solution.py:43
  6.1 1.1 %collective-permute-start.2 = (bf16[8,32,128]{2,0,1:T(8,128)(2,1)S(1)}, bf16[8,32,128]{2,0,1:T(8,128)(2,1)S(1)}, u32[]{:S(2)}, u32[]{:S(2)}) collective-permute-start(bf16[8,32,128]{2,0,1:T(8,128)(2,1)S(1)} %fusion.13), channel_id=1, source_target_pairs={{0,12},{4,0},{8,4},{12,8},{1,13},{5,1},{9,5},{13,9},{2,14},{6,2},{... | collective-permute-start | bytes 196616 | tf_op jit(solution)/shard_map/ppermute | solution.py:43
  7.3 0.1 broadcast_bitcast_fusion
  7.4 0.1 broadcast_bitcast_fusion.1
  7.5 0.1 broadcast_bitcast_fusion.2
  7.5 0.1 broadcast_in_dim.95
  7.6 0.1 broadcast_in_dim.96
  7.7 0.7 %broadcast_add_fusion.1 = s32[4]{0:T(128)S(1)} fusion(s32[4]{0:T(128)} %param.10), kind=kLoop, calls=%fused_computation.91 | loop fusion | flops 4 | bytes 32 | tf_op jit(solution)/shard_map/sub | solution.py:67
  8.4 0.1 broadcast_add_fusion
  8.5 1.2 %fusion.19 = f32[4,64,512]{2,1,0:T(8,128)S(1)} fusion(bf16[4,64,64]{2,1,0:T(8,128)(2,1)} %bitcast.37, bf16[4,512,576]{1,2,0:T(8,128)(2,1)} %param.9), kind=kOutput, calls=%fused_computation.15 | convolution fusion | flops 16777216 | bytes 851968 | tf_op jit(solution)/shard_map/sqc,skc->sqk/dot_general | solution.py:58
  9.7 0.1 broadcast_in_dim.100
  9.8 0.1 broadcast_in_dim.101
  9.9 1.3 %collective-permute-done.1 = bf16[8,32,128]{2,0,1:T(8,128)(2,1)S(1)} collective-permute-done((bf16[8,32,128]{2,0,1:T(8,128)(2,1)S(1)}, bf16[8,32,128]{2,0,1:T(8,128)(2,1)S(1)}, u32[]{:S(2)}, u32[]{:S(2)}) %collective-permute-start.1) | collective-permute-done | bytes 65568 | tf_op jit(solution)/shard_map/ppermute | solution.py:43
  11.2 0.1 broadcast_in_dim.105
  11.3 0.1 broadcast_in_dim.106
  11.4 0.1 broadcast_in_dim.107
  11.5 0.1 broadcast_in_dim.108
  11.6 2.3 %fusion.45 = (f32[4,64]{1,0:T(4,128)S(1)}, f32[4,64,512]{2,1,0:T(8,128)S(1)}) fusion(f32[4,64,512]{2,1,0:T(8,128)S(1)} %fusion.19, bf16[4,512,576]{1,2,0:T(8,128)(2,1)} %param.9, bf16[4,64,512]{2,1,0:T(8,128)(2,1)S(1)} %broadcast_in_dim.96, bf16[4,64,512]{2,1,0:T(8,128)(2,1)S(1)} %broadcast_in_dim.101, bf16[4,64,512]{2,1,0:T(8,128)(2,1)S(1)} %broadcast_in_dim.106, ...), kind=kOutput, calls=%fused_computation.96 | convolution fusion | flops 135266048 | bytes 4199936 | tf_op jit(solution)/shard_map/sqc,skc->sqk/dot_general | solution.py:52
  13.9 0.8 %fusion.2 = f32[4,64,512]{2,1,0:T(8,128)S(1)} fusion(bf16[4,512,576]{1,2,0:T(8,128)(2,1)S(1)} %copy-done.1, f32[4,64,512]{2,1,0:T(8,128)S(1)} %get-tuple-element.27, f32[4,64]{1,0:T(4,128)S(1)} %get-tuple-element.26, s32[4,64]{1,0:T(4,128)S(1)} %broadcast_add_fusion, s32[512]{0:T(512)S(1)} %iota_add_fusion), kind=kOutput, calls=%fused_computation.2 | convolution fusion | flops 134742016 | bytes 3151872 | tf_op jit(solution)/shard_map/sqk,skl->sql/dot_general | solution.py:73
  14.7 0.3 fusion.14
  15.0 0.1 reshape.265
  15.2 1.5 %collective-permute-start.3 = (bf16[268,128]{1,0:T(8,128)(2,1)S(1)}, bf16[268,128]{1,0:T(8,128)(2,1)S(1)}, u32[]{:S(2)}, u32[]{:S(2)}) collective-permute-start(bf16[268,128]{1,0:T(8,128)(2,1)S(1)} %get-tuple-element.14), channel_id=1, source_target_pairs={{0,4},{4,8},{8,12},{12,0},{1,5},{5,9},{9,13},{13,1},{2,6},{6,10},{... | collective-permute-start | bytes 205832 | tf_op jit(solution)/shard_map/ppermute | solution.py:117
  16.7 1.8 %collective-permute-start.4 = (bf16[268,128]{1,0:T(8,128)(2,1)S(1)}, bf16[268,128]{1,0:T(8,128)(2,1)S(1)}, u32[]{:S(2)}, u32[]{:S(2)}) collective-permute-start(bf16[268,128]{1,0:T(8,128)(2,1)S(1)} %get-tuple-element.15), channel_id=1, source_target_pairs={{0,12},{4,0},{8,4},{12,8},{1,13},{5,1},{9,5},{13,9},{2,14},{6,2},{... | collective-permute-start | bytes 205832 | tf_op jit(solution)/shard_map/ppermute | solution.py:117
  18.5 1.8 %collective-permute-done.3 = bf16[268,128]{1,0:T(8,128)(2,1)S(1)} collective-permute-done((bf16[268,128]{1,0:T(8,128)(2,1)S(1)}, bf16[268,128]{1,0:T(8,128)(2,1)S(1)}, u32[]{:S(2)}, u32[]{:S(2)}) %collective-permute-start.3) | collective-permute-done | bytes 68640 | tf_op jit(solution)/shard_map/ppermute | solution.py:117
  20.4 0.8 %collective-permute-done.4 = bf16[268,128]{1,0:T(8,128)(2,1)S(1)} collective-permute-done((bf16[268,128]{1,0:T(8,128)(2,1)S(1)}, bf16[268,128]{1,0:T(8,128)(2,1)S(1)}, u32[]{:S(2)}, u32[]{:S(2)}) %collective-permute-start.4) | collective-permute-done | bytes 68640 | tf_op jit(solution)/shard_map/ppermute | solution.py:117
  21.2 0.1 squeeze.21
  21.3 0.1 squeeze.22
  21.4 3.7 %collective-permute-done.5 = bf16[268,128]{1,0:T(8,128)(2,1)S(1)} collective-permute-done((bf16[268,128]{1,0:T(8,128)(2,1)S(1)}, bf16[268,128]{1,0:T(8,128)(2,1)S(1)}, u32[]{:S(2)}, u32[]{:S(2)}) %collective-permute-start.5) | collective-permute-done | bytes 68640 | tf_op jit(solution)/shard_map/ppermute | solution.py:117
  25.1 0.1 squeeze.23
  25.1 0.1 squeeze.24
  25.2 0.1 squeeze.25
  25.3 0.1 squeeze.26
  25.4 0.2 fusion.31
  25.7 0.4 fusion.46
  26.1 0.0 collective-permute-start.6
  26.1 3.3 %collective-permute-start.7 = (bf16[8,32,128]{2,0,1:T(8,128)(2,1)S(1)}, bf16[8,32,128]{2,0,1:T(8,128)(2,1)S(1)}, u32[]{:S(2)}, u32[]{:S(2)}) collective-permute-start(bf16[8,32,128]{2,0,1:T(8,128)(2,1)S(1)} %get-tuple-element.28), channel_id=1, source_target_pairs={{0,12},{4,0},{8,4},{12,8},{1,13},{5,1},{9,5},{13,9},{2,14},{6,2},{... | collective-permute-start | bytes 196616 | tf_op jit(solution)/shard_map/ppermute | solution.py:131
  29.4 1.8 %collective-permute-done.6 = bf16[8,32,128]{2,0,1:T(8,128)(2,1)S(1)} collective-permute-done((bf16[8,32,128]{2,0,1:T(8,128)(2,1)S(1)}, bf16[8,32,128]{2,0,1:T(8,128)(2,1)S(1)}, u32[]{:S(2)}, u32[]{:S(2)}) %collective-permute-start.6) | collective-permute-done | bytes 65568 | tf_op jit(solution)/shard_map/ppermute | solution.py:131
  31.2 2.6 %collective-permute-done.8 = bf16[8,32,128]{2,0,1:T(8,128)(2,1)S(1)} collective-permute-done((bf16[8,32,128]{2,0,1:T(8,128)(2,1)S(1)}, bf16[8,32,128]{2,0,1:T(8,128)(2,1)S(1)}, u32[]{:S(2)}, u32[]{:S(2)}) %collective-permute-start.8) | collective-permute-done | bytes 65568 | tf_op jit(solution)/shard_map/ppermute | solution.py:131
  33.8 7.2 %fusion.35 = f32[8,1792]{1,0:T(8,128)S(1)} fusion(bf16[4096,1792]{1,0:T(8,128)(2,1)} %param.13, bf16[8,32,128]{2,0,1:T(8,128)(2,1)S(1)} %collective-permute-done.8, bf16[8,32,128]{2,0,1:T(8,128)(2,1)S(1)} %collective-permute-done.7, f32[8,32,128]{2,0,1:T(8,128)S(1)} %get-tuple-element.29, bf16[8,32,128]{2,0,1:T(8,128)(2,1)S(1)} %collective-permute-done.6), kind=kOutput, calls=%fused_computation.47 | convolution fusion | flops 117669888 | bytes 15065088 | tf_op jit(solution)/shard_map/dot_general | solution.py:137
  41.0 0.1 select_select_fusion.2
  41.1 1.1 %collective-permute-start.10 = (f32[8,448]{1,0:T(8,128)S(1)}, f32[8,448]{1,0:T(8,128)S(1)}, u32[]{:S(2)}, u32[]{:S(2)}) collective-permute-start(f32[8,448]{1,0:T(8,128)S(1)} %get-tuple-element.13), channel_id=1, source_target_pairs={{0,2},{1,3},{2,0},{3,1},{4,6},{5,7},{6,4},{7,5},{8,10},{9,11},{10,... | collective-permute-start | bytes 43016 | tf_op jit(solution)/shard_map/ppermute | solution.py:147
  42.2 2.6 %collective-permute-start.9 = (f32[8,448]{1,0:T(8,128)S(1)}, f32[8,448]{1,0:T(8,128)S(1)}, u32[]{:S(2)}, u32[]{:S(2)}) collective-permute-start(f32[8,448]{1,0:T(8,128)S(1)} %get-tuple-element.12), channel_id=1, source_target_pairs={{0,1},{1,2},{2,3},{3,0},{4,5},{5,6},{6,7},{7,4},{8,9},{9,10},{10,1... | collective-permute-start | bytes 43016 | tf_op jit(solution)/shard_map/ppermute | solution.py:147
  44.8 0.1 select_select_fusion
  44.9 0.8 %collective-permute-done.9 = f32[8,448]{1,0:T(8,128)S(1)} collective-permute-done((f32[8,448]{1,0:T(8,128)S(1)}, f32[8,448]{1,0:T(8,128)S(1)}, u32[]{:S(2)}, u32[]{:S(2)}) %collective-permute-start.9) | collective-permute-done | bytes 14368 | tf_op jit(solution)/shard_map/ppermute | solution.py:147
  45.7 2.4 %collective-permute-done.11 = f32[8,448]{1,0:T(8,128)S(1)} collective-permute-done((f32[8,448]{1,0:T(8,128)S(1)}, f32[8,448]{1,0:T(8,128)S(1)}, u32[]{:S(2)}, u32[]{:S(2)}) %collective-permute-start.11) | collective-permute-done | bytes 14368 | tf_op jit(solution)/shard_map/ppermute | solution.py:147
  48.1 0.7 %add_add_fusion = f32[8,448]{1,0:T(8,128)} fusion(f32[8,448]{1,0:T(8,128)S(1)} %collective-permute-done.11, f32[8,448]{1,0:T(8,128)S(1)} %collective-permute-done.10, f32[8,448]{1,0:T(8,128)S(1)} %collective-permute-done.9, f32[8,1792]{1,0:T(8,128)S(1)} %fusion.35, pred[]{:T(512)S(6)} %eq.122, pred[]{:T(512)S(6)} %eq.121, pred[]{:T(512)S(6)} %eq.105), kind=kLoop, calls=%fused_computation.51 | loop fusion | flops 21504 | bytes 114691 | tf_op jit(solution)/shard_map/add | solution.py:147
  (37 shorter events, 0.3 us)
Async XLA Ops:
  0.0 25.7 %copy-start = (bf16[32,128,128]{2,1,0:T(8,128)(2,1)S(1)}, bf16[32,128,128]{2,1,0:T(8,128)(2,1)}, u32[]{:S(2)}) copy-start(bf16[32,128,128]{2,1,0:T(8,128)(2,1)} %param.12) | copy-start | bytes 3145732
  1.7 8.0 %collective-permute-start = (bf16[8,32,128]{2,0,1:T(8,128)(2,1)S(1)}, bf16[8,32,128]{2,0,1:T(8,128)(2,1)S(1)}, u32[]{:S(2)}, u32[]{:S(2)}) collective-permute-start(bf16[8,32,128]{2,0,1:T(8,128)(2,1)S(1)} %fusion.13), channel_id=1, source_target_pairs={{0,4},{4,8},{8,12},{12,0},{1,5},{5,9},{9,13},{13,1},{2,6},{6,10},{... | collective-permute-start | bytes 196616 | tf_op jit(solution)/shard_map/ppermute | solution.py:43
  3.8 7.3 %collective-permute-start.1 = (bf16[8,32,128]{2,0,1:T(8,128)(2,1)S(1)}, bf16[8,32,128]{2,0,1:T(8,128)(2,1)S(1)}, u32[]{:S(2)}, u32[]{:S(2)}) collective-permute-start(bf16[8,32,128]{2,0,1:T(8,128)(2,1)S(1)} %fusion.13), channel_id=1, source_target_pairs={{0,8},{4,12},{8,0},{12,4},{1,9},{5,13},{9,1},{13,5},{2,10},{6,14},... | collective-permute-start | bytes 196616 | tf_op jit(solution)/shard_map/ppermute | solution.py:43
  6.1 5.2 %collective-permute-start.2 = (bf16[8,32,128]{2,0,1:T(8,128)(2,1)S(1)}, bf16[8,32,128]{2,0,1:T(8,128)(2,1)S(1)}, u32[]{:S(2)}, u32[]{:S(2)}) collective-permute-start(bf16[8,32,128]{2,0,1:T(8,128)(2,1)S(1)} %fusion.13), channel_id=1, source_target_pairs={{0,12},{4,0},{8,4},{12,8},{1,13},{5,1},{9,5},{13,9},{2,14},{6,2},{... | collective-permute-start | bytes 196616 | tf_op jit(solution)/shard_map/ppermute | solution.py:43
  11.6 2.3 %copy-start.1 = (bf16[4,512,576]{1,2,0:T(8,128)(2,1)S(1)}, bf16[4,512,576]{1,2,0:T(8,128)(2,1)}, u32[]{:S(2)}) copy-start(bf16[4,512,576]{1,2,0:T(8,128)(2,1)} %param.9) | copy-start | bytes 7077892
  15.2 5.2 %collective-permute-start.3 = (bf16[268,128]{1,0:T(8,128)(2,1)S(1)}, bf16[268,128]{1,0:T(8,128)(2,1)S(1)}, u32[]{:S(2)}, u32[]{:S(2)}) collective-permute-start(bf16[268,128]{1,0:T(8,128)(2,1)S(1)} %get-tuple-element.14), channel_id=1, source_target_pairs={{0,4},{4,8},{8,12},{12,0},{1,5},{5,9},{9,13},{13,1},{2,6},{6,10},{... | collective-permute-start | bytes 205832 | tf_op jit(solution)/shard_map/ppermute | solution.py:117
  16.7 4.5 %collective-permute-start.4 = (bf16[268,128]{1,0:T(8,128)(2,1)S(1)}, bf16[268,128]{1,0:T(8,128)(2,1)S(1)}, u32[]{:S(2)}, u32[]{:S(2)}) collective-permute-start(bf16[268,128]{1,0:T(8,128)(2,1)S(1)} %get-tuple-element.15), channel_id=1, source_target_pairs={{0,12},{4,0},{8,4},{12,8},{1,13},{5,1},{9,5},{13,9},{2,14},{6,2},{... | collective-permute-start | bytes 205832 | tf_op jit(solution)/shard_map/ppermute | solution.py:117
  18.5 6.5 %collective-permute-start.5 = (bf16[268,128]{1,0:T(8,128)(2,1)S(1)}, bf16[268,128]{1,0:T(8,128)(2,1)S(1)}, u32[]{:S(2)}, u32[]{:S(2)}) collective-permute-start(bf16[268,128]{1,0:T(8,128)(2,1)S(1)} %get-tuple-element.16), channel_id=1, source_target_pairs={{0,8},{4,12},{8,0},{12,4},{1,9},{5,13},{9,1},{13,5},{2,10},{6,14},... | collective-permute-start | bytes 205832 | tf_op jit(solution)/shard_map/ppermute | solution.py:117
  26.1 5.1 %collective-permute-start.6 = (bf16[8,32,128]{2,0,1:T(8,128)(2,1)S(1)}, bf16[8,32,128]{2,0,1:T(8,128)(2,1)S(1)}, u32[]{:S(2)}, u32[]{:S(2)}) collective-permute-start(bf16[8,32,128]{2,0,1:T(8,128)(2,1)S(1)} %get-tuple-element.28), channel_id=1, source_target_pairs={{0,4},{4,8},{8,12},{12,0},{1,5},{5,9},{9,13},{13,1},{2,6},{6,10},{... | collective-permute-start | bytes 196616 | tf_op jit(solution)/shard_map/ppermute | solution.py:131
  26.1 5.1 %collective-permute-start.7 = (bf16[8,32,128]{2,0,1:T(8,128)(2,1)S(1)}, bf16[8,32,128]{2,0,1:T(8,128)(2,1)S(1)}, u32[]{:S(2)}, u32[]{:S(2)}) collective-permute-start(bf16[8,32,128]{2,0,1:T(8,128)(2,1)S(1)} %get-tuple-element.28), channel_id=1, source_target_pairs={{0,12},{4,0},{8,4},{12,8},{1,13},{5,1},{9,5},{13,9},{2,14},{6,2},{... | collective-permute-start | bytes 196616 | tf_op jit(solution)/shard_map/ppermute | solution.py:131
  29.4 4.5 %collective-permute-start.8 = (bf16[8,32,128]{2,0,1:T(8,128)(2,1)S(1)}, bf16[8,32,128]{2,0,1:T(8,128)(2,1)S(1)}, u32[]{:S(2)}, u32[]{:S(2)}) collective-permute-start(bf16[8,32,128]{2,0,1:T(8,128)(2,1)S(1)} %get-tuple-element.28), channel_id=1, source_target_pairs={{0,8},{4,12},{8,0},{12,4},{1,9},{5,13},{9,1},{13,5},{2,10},{6,14},... | collective-permute-start | bytes 196616 | tf_op jit(solution)/shard_map/ppermute | solution.py:131
  41.1 3.8 %collective-permute-start.10 = (f32[8,448]{1,0:T(8,128)S(1)}, f32[8,448]{1,0:T(8,128)S(1)}, u32[]{:S(2)}, u32[]{:S(2)}) collective-permute-start(f32[8,448]{1,0:T(8,128)S(1)} %get-tuple-element.13), channel_id=1, source_target_pairs={{0,2},{1,3},{2,0},{3,1},{4,6},{5,7},{6,4},{7,5},{8,10},{9,11},{10,... | collective-permute-start | bytes 43016 | tf_op jit(solution)/shard_map/ppermute | solution.py:147
  42.2 3.5 %collective-permute-start.9 = (f32[8,448]{1,0:T(8,128)S(1)}, f32[8,448]{1,0:T(8,128)S(1)}, u32[]{:S(2)}, u32[]{:S(2)}) collective-permute-start(f32[8,448]{1,0:T(8,128)S(1)} %get-tuple-element.12), channel_id=1, source_target_pairs={{0,1},{1,2},{2,3},{3,0},{4,5},{5,6},{6,7},{7,4},{8,9},{9,10},{10,1... | collective-permute-start | bytes 43016 | tf_op jit(solution)/shard_map/ppermute | solution.py:147
  44.9 3.2 %collective-permute-start.11 = (f32[8,448]{1,0:T(8,128)S(1)}, f32[8,448]{1,0:T(8,128)S(1)}, u32[]{:S(2)}, u32[]{:S(2)}) collective-permute-start(f32[8,448]{1,0:T(8,128)S(1)} %select_select_fusion), channel_id=1, source_target_pairs={{0,3},{1,0},{2,1},{3,2},{4,7},{5,4},{6,5},{7,6},{8,11},{9,8},{10,9... | collective-permute-start | bytes 43016 | tf_op jit(solution)/shard_map/ppermute | solution.py:147

commit v11 on v8

--- a/solution.py
+++ b/solution.py
@@ -3,6 +3,7 @@
 import jax
 import jax.numpy as jnp
 from jax import lax
+from jax.experimental.layout import Layout, with_layout_constraint
 from jax.sharding import PartitionSpec as P
 
 ROTARY_CHANNELS = 64
@@ -33,18 +34,17 @@
     q_part = jnp.einsum(
         "rhn,hnl->rhl", query_nope, w_absorb, preferred_element_type=jnp.float32
     ).astype(jnp.bfloat16)
+    q_part = with_layout_constraint(q_part, Layout(major_to_minor=(0, 1, 2)))
     if small_ctx:
         received = [q_part] + [
             lax.ppermute(q_part, "ctx", shift_pairs(n_ctx, k)) for k in range(1, n_ctx)
         ]
-        kv_blocks = kv_cache[:, :, :latent_width].reshape(seq_count, ctx_rows, n_ctx, -1)
         latent_scores = 0
-        for k in range(n_ctx):
-            block = lax.dynamic_index_in_dim(kv_blocks, (me_ctx - k) % n_ctx, axis=2, keepdims=False)
+        for j in range(n_ctx):
             latent_scores = latent_scores + jnp.einsum(
                 "sqc,skc->sqk",
-                received[k].reshape(seq_count, DRAFT * head_count, -1),
-                block,
+                pick((me_ctx - j) % n_ctx, received).reshape(seq_count, DRAFT * head_count, -1),
+                kv_cache[:, :, j * slice_width:(j + 1) * slice_width],
                 preferred_element_type=jnp.float32,
             )
     else:

time: 65.5 us -> 50.2 us (0.77)
  local copies, waits for them, and re-layouts: 19 us -> 0.64 us
  waiting for transfers between devices: 8.33 us -> 15.2 us
  starting transfers between devices: 18.9 us -> 15.5 us
  other arithmetic: 3.76 us -> 5.37 us
  matrix products: 14.6 us -> 13.1 us
    unnamed x20 -> x6, local copies, waits for them, and re-layouts: 14.5 us -> 0.01 us
    ppermute x3, starting transfers between devices: 5.37 us -> 2.22 us  [per_device(): lax.ppermute(pick((me_head + k) % n_head, col_slices), 'head', shift_pair...]
    ppermute x3 -> x0, local copies, waits for them, and re-layouts: 2.55 us -> none  [per_device(): lax.ppermute(q_part, 'ctx', shift_pairs(n_ctx, k))]
    ppermute x3, waiting for transfers between devices: 2.65 us -> 5.01 us  [per_device(): lax.ppermute(packed_for((me_ctx + k) % n_ctx), 'ctx', shift_pairs(n_ctx, k))]
    ppermute x3, waiting for transfers between devices: 2.52 us -> 4.87 us  [per_device(): lax.ppermute(sent, 'ctx', shift_pairs(n_ctx, k)).astype(jnp.float32)]
    ppermute x3, waiting for transfers between devices: 0.01 us -> 2.11 us  [per_device(): lax.ppermute(q_part, 'ctx', shift_pairs(n_ctx, k))]
    dot_general x4, matrix products: 2.52 us -> 1.02 us  [per_device(): jnp.einsum('sqc,skc->sqk', pick((me_ctx - j) % n_ctx, received).reshape(s...]
    dynamic_slice x1 -> x0, local copies, waits for them, and re-layouts: 1.36 us -> none  [per_device(): lax.dynamic_index_in_dim(kv_blocks, (me_ctx - k) % n_ctx, axis=2, keepdim...]
  transfers between devices with their start and end apart: 12 -> 12, of which waited for: 7 -> 8; matrix products, arithmetic and copies ran while one was open for 33% -> 4% of each run, Pallas kernels for 0% -> 0%
where the time goes in v11:
time: 50.2 us; the launch traced here: 49.9 us
  starting transfers between devices  15.5 us (31%)
  waiting for transfers between devices  15.2 us (30%)
  matrix products  13.1 us (26%)
  other arithmetic  5.37 us (11%)
  local copies, waits for them, and re-layouts  0.64 us (1%)
    dot_general x1, matrix products, per_device(): jnp.dot(values.reshape(row_count, -1), w_output, preferred_element_type=j...  7.17 us
    ppermute x3, starting transfers between devices, per_device(): lax.ppermute(q_part, 'ctx', shift_pairs(n_ctx, k))  5.56 us
    ppermute x3, waiting for transfers between devices, per_device(): lax.ppermute(packed_for((me_ctx + k) % n_ctx), 'ctx', shift_pairs(n_ctx, k))  5.01 us
    ppermute x3, waiting for transfers between devices, per_device(): lax.ppermute(sent, 'ctx', shift_pairs(n_ctx, k)).astype(jnp.float32)  4.87 us
    ppermute x3, starting transfers between devices, per_device(): lax.ppermute(packed_for((me_ctx + k) % n_ctx), 'ctx', shift_pairs(n_ctx, k))  3.9 us
    ppermute x3, starting transfers between devices, per_device(): lax.ppermute(sent, 'ctx', shift_pairs(n_ctx, k)).astype(jnp.float32)  3.77 us
    ppermute x3, waiting for transfers between devices, per_device(): lax.ppermute(pick((me_head + k) % n_head, col_slices), 'head', shift_pair...  3.15 us
    convert_element_type x2, other arithmetic, packed_for(): pick(target, sum_slices).astype(jnp.bfloat16)  2.27 us
  transfers between devices with their start and end apart: 12, of which 8 were waited for; matrix products, arithmetic and copies ran while one was open for 4% of the time, Pallas kernels for 0%

profile of v11, /device:TPU:1, one launch (start us, length us, event | category | flops | bytes accessed | tf_op | source)
XLA Modules:
  0.0 49.9 jit_solution(12388472608098920628)
XLA Ops:
  0.0 1.8 %fusion.33 = bf16[32,128,8]{1,2,0:T(8,128)(2,1)S(1)} fusion(bf16[32,128,128]{2,1,0:T(8,128)(2,1)} %param.11, bf16[8,32,128]{2,1,0:T(8,128)(2,1)} %param.7), kind=kOutput, calls=%fused_computation.51 | convolution fusion | flops 8388608 | bytes 1179648 | tf_op jit(solution)/shard_map/rhn,hnl->rhl/dot_general | solution.py:34
  1.8 2.2 %collective-permute-start = (bf16[8,32,128]{2,1,0:T(8,128)(2,1)S(1)}, bf16[8,32,128]{2,1,0:T(8,128)(2,1)}, u32[]{:S(2)}, u32[]{:S(2)}) collective-permute-start(bf16[8,32,128]{2,1,0:T(8,128)(2,1)S(1)} %bitcast.46), channel_id=1, source_target_pairs={{0,4},{4,8},{8,12},{12,0},{1,5},{5,9},{9,13},{13,1},{2,6},{6,10},{... | collective-permute-start | bytes 196616 | tf_op jit(solution)/shard_map/ppermute | solution.py:40
  4.0 2.3 %collective-permute-start.1 = (bf16[8,32,128]{2,1,0:T(8,128)(2,1)S(1)}, bf16[8,32,128]{2,1,0:T(8,128)(2,1)}, u32[]{:S(2)}, u32[]{:S(2)}) collective-permute-start(bf16[8,32,128]{2,1,0:T(8,128)(2,1)S(1)} %bitcast.47), channel_id=1, source_target_pairs={{0,8},{4,12},{8,0},{12,4},{1,9},{5,13},{9,1},{13,5},{2,10},{6,14},... | collective-permute-start | bytes 196616 | tf_op jit(solution)/shard_map/ppermute | solution.py:40
  6.3 1.1 %collective-permute-start.2 = (bf16[8,32,128]{2,1,0:T(8,128)(2,1)S(1)}, bf16[8,32,128]{2,1,0:T(8,128)(2,1)}, u32[]{:S(2)}, u32[]{:S(2)}) collective-permute-start(bf16[8,32,128]{2,1,0:T(8,128)(2,1)S(1)} %bitcast.48), channel_id=1, source_target_pairs={{0,12},{4,0},{8,4},{12,8},{1,13},{5,1},{9,5},{13,9},{2,14},{6,2},{... | collective-permute-start | bytes 196616 | tf_op jit(solution)/shard_map/ppermute | solution.py:40
  7.3 0.7 %broadcast_add_fusion.1 = s32[4]{0:T(128)S(1)} fusion(s32[4]{0:T(128)} %param.10), kind=kLoop, calls=%fused_computation.88 | loop fusion | flops 4 | bytes 32 | tf_op jit(solution)/shard_map/sub | solution.py:68
  8.0 0.1 broadcast_add_fusion
  8.1 1.2 %fusion.19 = f32[4,64,512]{2,1,0:T(8,128)S(1)} fusion(bf16[4,64,64]{2,1,0:T(8,128)(2,1)} %bitcast.49, bf16[4,512,576]{1,2,0:T(8,128)(2,1)} %param.9), kind=kOutput, calls=%fused_computation.21 | convolution fusion | flops 16777216 | bytes 851968 | tf_op jit(solution)/shard_map/sqc,skc->sqk/dot_general | solution.py:59
  9.3 0.0 collective-permute-done
  9.3 2.1 %collective-permute-done.1 = bf16[8,32,128]{2,1,0:T(8,128)(2,1)} collective-permute-done((bf16[8,32,128]{2,1,0:T(8,128)(2,1)S(1)}, bf16[8,32,128]{2,1,0:T(8,128)(2,1)}, u32[]{:S(2)}, u32[]{:S(2)}) %collective-permute-start.1) | collective-permute-done | bytes 65568 | tf_op jit(solution)/shard_map/ppermute | solution.py:40
  11.4 0.0 collective-permute-done.2
  11.4 0.9 %select_select_fusion.3 = (bf16[8,32,128]{2,1,0:T(8,128)(2,1)S(1)}, bf16[8,32,128]{2,1,0:T(8,128)(2,1)S(1)}, bf16[8,32,128]{2,1,0:T(8,128)(2,1)S(1)}, bf16[8,32,128]{2,1,0:T(8,128)(2,1)S(1)}) fusion(bf16[8,32,128]{2,1,0:T(8,128)(2,1)} %collective-permute-done, bf16[8,32,128]{2,1,0:T(8,128)(2,1)} %collective-permute-done.1, ...), kind=kLoop, calls=%fused_computation.56 | loop fusion | flops 393216 | bytes 524300 | tf_op jit(solution)/shard_map/jit(_where)/select_n | solution.py:22
  12.4 0.2 fusion.11
  12.6 0.2 fusion.7
  12.8 0.2 fusion.9
  13.0 0.4 fusion.40
  13.4 1.6 %fusion = f32[4,64,512]{2,1,0:T(8,128)} fusion(bf16[4,512,576]{1,2,0:T(8,128)(2,1)S(1)} %copy-done.1, f32[4,64,512]{2,1,0:T(8,128)S(1)} %get-tuple-element.31, f32[4,64]{1,0:T(4,128)S(1)} %get-tuple-element.30, s32[4,64]{1,0:T(4,128)S(1)} %broadcast_add_fusion, s32[512]{0:T(512)S(1)} %iota_add_fusion), kind=kOutput, calls=%fused_computation | convolution fusion | flops 134742016 | bytes 3151872 | tf_op jit(solution)/shard_map/sqk,skl->sql/dot_general | solution.py:74
  15.0 0.2 fusion.14
  15.3 0.1 reshape.240
  15.3 1.1 %select_convert_fusion = bf16[4,64,128]{2,1,0:T(8,128)(2,1)S(1)} fusion(f32[4,64,512]{2,1,0:T(8,128)} %fusion, pred[]{:T(512)S(6)} %eq.140, pred[]{:T(512)S(6)} %eq.139, pred[]{:T(512)S(6)} %eq.138), kind=kLoop, calls=%fused_computation.35 | loop fusion | flops 98304 | bytes 327683 | tf_op jit(solution)/shard_map/convert_element_type | solution.py:98
  16.5 1.1 %select_convert_fusion.2 = (bf16[4,64,128]{2,1,0:T(8,128)(2,1)S(1)}, bf16[4,64,128]{2,1,0:T(8,128)(2,1)S(1)}) fusion(f32[4,64,512]{2,1,0:T(8,128)} %fusion, pred[]{:T(512)S(6)} %eq.134, pred[]{:T(512)S(6)} %eq.133, pred[]{:T(512)S(6)} %eq.132, pred[]{:T(512)S(6)} %eq.137, pred[]{:T(512)S(6)} %eq.136, pred[]{:T(512)S(6)} %eq.135), kind=kLoop, calls=%fused_computation.37 | loop fusion | flops 196608 | bytes 393222 | tf_op jit(solution)/shard_map/convert_element_type | solution.py:98
  17.6 1.7 %collective-permute-start.3 = (bf16[268,128]{1,0:T(8,128)(2,1)S(1)}, bf16[268,128]{1,0:T(8,128)(2,1)S(1)}, u32[]{:S(2)}, u32[]{:S(2)}) collective-permute-start(bf16[268,128]{1,0:T(8,128)(2,1)S(1)} %get-tuple-element.18), channel_id=1, source_target_pairs={{0,4},{4,8},{8,12},{12,0},{1,5},{5,9},{9,13},{13,1},{2,6},{6,10},{... | collective-permute-start | bytes 205832 | tf_op jit(solution)/shard_map/ppermute | solution.py:118
  19.4 0.0 collective-permute-start.4
  19.4 2.2 %collective-permute-start.5 = (bf16[268,128]{1,0:T(8,128)(2,1)S(1)}, bf16[268,128]{1,0:T(8,128)(2,1)S(1)}, u32[]{:S(2)}, u32[]{:S(2)}) collective-permute-start(bf16[268,128]{1,0:T(8,128)(2,1)S(1)} %get-tuple-element.20), channel_id=1, source_target_pairs={{0,12},{4,0},{8,4},{12,8},{1,13},{5,1},{9,5},{13,9},{2,14},{6,2},{... | collective-permute-start | bytes 205832 | tf_op jit(solution)/shard_map/ppermute | solution.py:118
  21.5 1.2 %collective-permute-done.3 = bf16[268,128]{1,0:T(8,128)(2,1)S(1)} collective-permute-done((bf16[268,128]{1,0:T(8,128)(2,1)S(1)}, bf16[268,128]{1,0:T(8,128)(2,1)S(1)}, u32[]{:S(2)}, u32[]{:S(2)}) %collective-permute-start.3) | collective-permute-done | bytes 68640 | tf_op jit(solution)/shard_map/ppermute | solution.py:118
  22.7 3.9 %collective-permute-done.4 = bf16[268,128]{1,0:T(8,128)(2,1)S(1)} collective-permute-done((bf16[268,128]{1,0:T(8,128)(2,1)S(1)}, bf16[268,128]{1,0:T(8,128)(2,1)S(1)}, u32[]{:S(2)}, u32[]{:S(2)}) %collective-permute-start.4) | collective-permute-done | bytes 68640 | tf_op jit(solution)/shard_map/ppermute | solution.py:118
  26.6 0.1 squeeze.21
  26.7 0.1 squeeze.22
  26.8 0.0 collective-permute-done.5
  26.8 0.1 squeeze.23
  26.9 0.1 squeeze.24
  27.0 0.1 squeeze.25
  27.0 0.1 squeeze.26
  27.2 0.2 fusion.25
  27.4 0.4 fusion.41
  27.8 1.6 %collective-permute-start.6 = (bf16[8,32,128]{2,0,1:T(8,128)(2,1)S(1)}, bf16[8,32,128]{2,0,1:T(8,128)(2,1)S(1)}, u32[]{:S(2)}, u32[]{:S(2)}) collective-permute-start(bf16[8,32,128]{2,0,1:T(8,128)(2,1)S(1)} %get-tuple-element.32), channel_id=1, source_target_pairs={{0,4},{4,8},{8,12},{12,0},{1,5},{5,9},{9,13},{13,1},{2,6},{6,10},{... | collective-permute-start | bytes 196616 | tf_op jit(solution)/shard_map/ppermute | solution.py:132
  29.4 0.0 collective-permute-start.7
  29.4 2.2 %collective-permute-start.8 = (bf16[8,32,128]{2,0,1:T(8,128)(2,1)S(1)}, bf16[8,32,128]{2,0,1:T(8,128)(2,1)S(1)}, u32[]{:S(2)}, u32[]{:S(2)}) collective-permute-start(bf16[8,32,128]{2,0,1:T(8,128)(2,1)S(1)} %get-tuple-element.32), channel_id=1, source_target_pairs={{0,12},{4,0},{8,4},{12,8},{1,13},{5,1},{9,5},{13,9},{2,14},{6,2},{... | collective-permute-start | bytes 196616 | tf_op jit(solution)/shard_map/ppermute | solution.py:132
  31.6 1.2 %collective-permute-done.6 = bf16[8,32,128]{2,0,1:T(8,128)(2,1)S(1)} collective-permute-done((bf16[8,32,128]{2,0,1:T(8,128)(2,1)S(1)}, bf16[8,32,128]{2,0,1:T(8,128)(2,1)S(1)}, u32[]{:S(2)}, u32[]{:S(2)}) %collective-permute-start.6) | collective-permute-done | bytes 65568 | tf_op jit(solution)/shard_map/ppermute | solution.py:132
  32.8 3.7 %collective-permute-done.7 = bf16[8,32,128]{2,0,1:T(8,128)(2,1)S(1)} collective-permute-done((bf16[8,32,128]{2,0,1:T(8,128)(2,1)S(1)}, bf16[8,32,128]{2,0,1:T(8,128)(2,1)S(1)}, u32[]{:S(2)}, u32[]{:S(2)}) %collective-permute-start.7) | collective-permute-done | bytes 65568 | tf_op jit(solution)/shard_map/ppermute | solution.py:132
  36.5 7.2 %fusion.29 = f32[8,1792]{1,0:T(8,128)S(1)} fusion(bf16[4096,1792]{1,0:T(8,128)(2,1)} %param.13, bf16[8,32,128]{2,0,1:T(8,128)(2,1)S(1)} %collective-permute-done.8, bf16[8,32,128]{2,0,1:T(8,128)(2,1)S(1)} %collective-permute-done.7, f32[8,32,128]{2,0,1:T(8,128)S(1)} %get-tuple-element.33, bf16[8,32,128]{2,0,1:T(8,128)(2,1)S(1)} %collective-permute-done.6), kind=kOutput, calls=%fused_computation.48 | convolution fusion | flops 117669888 | bytes 15065088 | tf_op jit(solution)/shard_map/dot_general | solution.py:138
  43.7 0.1 select_select_fusion.6
  43.7 0.0 collective-permute-start.10
  43.8 2.2 %collective-permute-start.9 = (f32[8,448]{1,0:T(8,128)S(1)}, f32[8,448]{1,0:T(8,128)S(1)}, u32[]{:S(2)}, u32[]{:S(2)}) collective-permute-start(f32[8,448]{1,0:T(8,128)S(1)} %get-tuple-element.16), channel_id=1, source_target_pairs={{0,1},{1,2},{2,3},{3,0},{4,5},{5,6},{6,7},{7,4},{8,9},{9,10},{10,1... | collective-permute-start | bytes 43016 | tf_op jit(solution)/shard_map/ppermute | solution.py:148
  46.0 0.1 select_select_fusion.4
  46.0 0.3 collective-permute-done.10
  46.3 0.5 %collective-permute-done.9 = f32[8,448]{1,0:T(8,128)S(1)} collective-permute-done((f32[8,448]{1,0:T(8,128)S(1)}, f32[8,448]{1,0:T(8,128)S(1)}, u32[]{:S(2)}, u32[]{:S(2)}) %collective-permute-start.9) | collective-permute-done | bytes 14368 | tf_op jit(solution)/shard_map/ppermute | solution.py:148
  46.8 2.4 %collective-permute-done.11 = f32[8,448]{1,0:T(8,128)S(1)} collective-permute-done((f32[8,448]{1,0:T(8,128)S(1)}, f32[8,448]{1,0:T(8,128)S(1)}, u32[]{:S(2)}, u32[]{:S(2)}) %collective-permute-start.11) | collective-permute-done | bytes 14368 | tf_op jit(solution)/shard_map/ppermute | solution.py:148
  49.2 0.7 %add_add_fusion = f32[8,448]{1,0:T(8,128)} fusion(f32[8,448]{1,0:T(8,128)S(1)} %collective-permute-done.11, f32[8,448]{1,0:T(8,128)S(1)} %collective-permute-done.10, f32[8,448]{1,0:T(8,128)S(1)} %collective-permute-done.9, f32[8,1792]{1,0:T(8,128)S(1)} %fusion.29, pred[]{:T(512)S(6)} %eq.145, pred[]{:T(512)S(6)} %eq.144, pred[]{:T(512)S(6)} %eq.119), kind=kLoop, calls=%fused_computation.58 | loop fusion | flops 21504 | bytes 114691 | tf_op jit(solution)/shard_map/add | solution.py:148
  (27 shorter events, 0.2 us)
Async XLA Ops:
  0.0 27.4 %copy-start = (bf16[32,128,128]{2,1,0:T(8,128)(2,1)S(1)}, bf16[32,128,128]{2,1,0:T(8,128)(2,1)}, u32[]{:S(2)}) copy-start(bf16[32,128,128]{2,1,0:T(8,128)(2,1)} %param.12) | copy-start | bytes 3145732
  0.0 12.4 %copy-start.1 = (bf16[4,512,576]{1,2,0:T(8,128)(2,1)S(1)}, bf16[4,512,576]{1,2,0:T(8,128)(2,1)}, u32[]{:S(2)}) copy-start(bf16[4,512,576]{1,2,0:T(8,128)(2,1)} %param.9) | copy-start | bytes 7077892
  1.8 7.5 %collective-permute-start = (bf16[8,32,128]{2,1,0:T(8,128)(2,1)S(1)}, bf16[8,32,128]{2,1,0:T(8,128)(2,1)}, u32[]{:S(2)}, u32[]{:S(2)}) collective-permute-start(bf16[8,32,128]{2,1,0:T(8,128)(2,1)S(1)} %bitcast.46), channel_id=1, source_target_pairs={{0,4},{4,8},{8,12},{12,0},{1,5},{5,9},{9,13},{13,1},{2,6},{6,10},{... | collective-permute-start | bytes 196616 | tf_op jit(solution)/shard_map/ppermute | solution.py:40
  4.0 7.4 %collective-permute-start.1 = (bf16[8,32,128]{2,1,0:T(8,128)(2,1)S(1)}, bf16[8,32,128]{2,1,0:T(8,128)(2,1)}, u32[]{:S(2)}, u32[]{:S(2)}) collective-permute-start(bf16[8,32,128]{2,1,0:T(8,128)(2,1)S(1)} %bitcast.47), channel_id=1, source_target_pairs={{0,8},{4,12},{8,0},{12,4},{1,9},{5,13},{9,1},{13,5},{2,10},{6,14},... | collective-permute-start | bytes 196616 | tf_op jit(solution)/shard_map/ppermute | solution.py:40
  6.3 5.1 %collective-permute-start.2 = (bf16[8,32,128]{2,1,0:T(8,128)(2,1)S(1)}, bf16[8,32,128]{2,1,0:T(8,128)(2,1)}, u32[]{:S(2)}, u32[]{:S(2)}) collective-permute-start(bf16[8,32,128]{2,1,0:T(8,128)(2,1)S(1)} %bitcast.48), channel_id=1, source_target_pairs={{0,12},{4,0},{8,4},{12,8},{1,13},{5,1},{9,5},{13,9},{2,14},{6,2},{... | collective-permute-start | bytes 196616 | tf_op jit(solution)/shard_map/ppermute | solution.py:40
  15.0 12.2 %copy-start.2 = (f32[4,64,512]{2,1,0:T(8,128)S(1)}, f32[4,64,512]{2,1,0:T(8,128)}, u32[]{:S(2)}) copy-start(f32[4,64,512]{2,1,0:T(8,128)} %fusion) | copy-start | bytes 1572868
  17.6 5.1 %collective-permute-start.3 = (bf16[268,128]{1,0:T(8,128)(2,1)S(1)}, bf16[268,128]{1,0:T(8,128)(2,1)S(1)}, u32[]{:S(2)}, u32[]{:S(2)}) collective-permute-start(bf16[268,128]{1,0:T(8,128)(2,1)S(1)} %get-tuple-element.18), channel_id=1, source_target_pairs={{0,4},{4,8},{8,12},{12,0},{1,5},{5,9},{9,13},{13,1},{2,6},{6,10},{... | collective-permute-start | bytes 205832 | tf_op jit(solution)/shard_map/ppermute | solution.py:118
  19.4 7.2 %collective-permute-start.4 = (bf16[268,128]{1,0:T(8,128)(2,1)S(1)}, bf16[268,128]{1,0:T(8,128)(2,1)S(1)}, u32[]{:S(2)}, u32[]{:S(2)}) collective-permute-start(bf16[268,128]{1,0:T(8,128)(2,1)S(1)} %get-tuple-element.19), channel_id=1, source_target_pairs={{0,8},{4,12},{8,0},{12,4},{1,9},{5,13},{9,1},{13,5},{2,10},{6,14},... | collective-permute-start | bytes 205832 | tf_op jit(solution)/shard_map/ppermute | solution.py:118
  19.4 7.4 %collective-permute-start.5 = (bf16[268,128]{1,0:T(8,128)(2,1)S(1)}, bf16[268,128]{1,0:T(8,128)(2,1)S(1)}, u32[]{:S(2)}, u32[]{:S(2)}) collective-permute-start(bf16[268,128]{1,0:T(8,128)(2,1)S(1)} %get-tuple-element.20), channel_id=1, source_target_pairs={{0,12},{4,0},{8,4},{12,8},{1,13},{5,1},{9,5},{13,9},{2,14},{6,2},{... | collective-permute-start | bytes 205832 | tf_op jit(solution)/shard_map/ppermute | solution.py:118
  27.8 5.0 %collective-permute-start.6 = (bf16[8,32,128]{2,0,1:T(8,128)(2,1)S(1)}, bf16[8,32,128]{2,0,1:T(8,128)(2,1)S(1)}, u32[]{:S(2)}, u32[]{:S(2)}) collective-permute-start(bf16[8,32,128]{2,0,1:T(8,128)(2,1)S(1)} %get-tuple-element.32), channel_id=1, source_target_pairs={{0,4},{4,8},{8,12},{12,0},{1,5},{5,9},{9,13},{13,1},{2,6},{6,10},{... | collective-permute-start | bytes 196616 | tf_op jit(solution)/shard_map/ppermute | solution.py:132
  29.4 7.0 %collective-permute-start.7 = (bf16[8,32,128]{2,0,1:T(8,128)(2,1)S(1)}, bf16[8,32,128]{2,0,1:T(8,128)(2,1)S(1)}, u32[]{:S(2)}, u32[]{:S(2)}) collective-permute-start(bf16[8,32,128]{2,0,1:T(8,128)(2,1)S(1)} %get-tuple-element.32), channel_id=1, source_target_pairs={{0,8},{4,12},{8,0},{12,4},{1,9},{5,13},{9,1},{13,5},{2,10},{6,14},... | collective-permute-start | bytes 196616 | tf_op jit(solution)/shard_map/ppermute | solution.py:132
  29.4 7.0 %collective-permute-start.8 = (bf16[8,32,128]{2,0,1:T(8,128)(2,1)S(1)}, bf16[8,32,128]{2,0,1:T(8,128)(2,1)S(1)}, u32[]{:S(2)}, u32[]{:S(2)}) collective-permute-start(bf16[8,32,128]{2,0,1:T(8,128)(2,1)S(1)} %get-tuple-element.32), channel_id=1, source_target_pairs={{0,12},{4,0},{8,4},{12,8},{1,13},{5,1},{9,5},{13,9},{2,14},{6,2},{... | collective-permute-start | bytes 196616 | tf_op jit(solution)/shard_map/ppermute | solution.py:132
  43.7 2.6 %collective-permute-start.10 = (f32[8,448]{1,0:T(8,128)S(1)}, f32[8,448]{1,0:T(8,128)S(1)}, u32[]{:S(2)}, u32[]{:S(2)}) collective-permute-start(f32[8,448]{1,0:T(8,128)S(1)} %get-tuple-element.17), channel_id=1, source_target_pairs={{0,2},{1,3},{2,0},{3,1},{4,6},{5,7},{6,4},{7,5},{8,10},{9,11},{10,... | collective-permute-start | bytes 43016 | tf_op jit(solution)/shard_map/ppermute | solution.py:148
  43.8 3.1 %collective-permute-start.9 = (f32[8,448]{1,0:T(8,128)S(1)}, f32[8,448]{1,0:T(8,128)S(1)}, u32[]{:S(2)}, u32[]{:S(2)}) collective-permute-start(f32[8,448]{1,0:T(8,128)S(1)} %get-tuple-element.16), channel_id=1, source_target_pairs={{0,1},{1,2},{2,3},{3,0},{4,5},{5,6},{6,7},{7,4},{8,9},{9,10},{10,1... | collective-permute-start | bytes 43016 | tf_op jit(solution)/shard_map/ppermute | solution.py:148
  46.0 3.2 %collective-permute-start.11 = (f32[8,448]{1,0:T(8,128)S(1)}, f32[8,448]{1,0:T(8,128)S(1)}, u32[]{:S(2)}, u32[]{:S(2)}) collective-permute-start(f32[8,448]{1,0:T(8,128)S(1)} %select_select_fusion.4), channel_id=1, source_target_pairs={{0,3},{1,0},{2,1},{3,2},{4,7},{5,4},{6,5},{7,6},{8,11},{9,8},{10,9... | collective-permute-start | bytes 43016 | tf_op jit(solution)/shard_map/ppermute | solution.py:148

commit v12 on v5

--- a/solution.py
+++ b/solution.py
@@ -139,6 +139,11 @@
     out_width = partial_value.shape[1] // n_head
     col_slices = [partial_value[:, j * out_width:(j + 1) * out_width] for j in range(n_head)]
     total = pick(me_head, col_slices)
+    if n_head & (n_head - 1) == 0:
+        for m in range(1, n_head):
+            pairs = [(i, i ^ m) for i in range(n_head)]
+            total = total + lax.ppermute(pick(me_head ^ m, col_slices), "head", pairs)
+        return total
     for k in range(1, n_head):
         total = total + lax.ppermute(
             pick((me_head + k) % n_head, col_slices), "head", shift_pairs(n_head, k)

time: 47.6 us -> 46.6 us (0.979)
  waiting for transfers between devices: 14.5 us -> 13.4 us
    ppermute x3, waiting for transfers between devices: 3.15 us -> 1.99 us  [per_device(): total = total + lax.ppermute(pick(me_head ^ m, col_slices), 'head', pairs)]
  transfers between devices with their start and end apart: 12 -> 12, of which waited for: 8 -> 7; matrix products, arithmetic and copies ran while one was open for 6% -> 7% of each run, Pallas kernels for 0% -> 0%
where the time goes in v12:
time: 46.6 us; the launch traced here: 46.3 us
  starting transfers between devices  15.2 us (33%)
  matrix products  13.5 us (29%)
  waiting for transfers between devices  13.4 us (29%)
  other arithmetic  2.26 us (5%)
  local copies, waits for them, and re-layouts  1.62 us (3%)
    dot_general x1, matrix products, per_device(): jnp.dot(values.reshape(row_count, -1), w_output, preferred_element_type=j...  7.17 us
    ppermute x3, starting transfers between devices, per_device(): lax.ppermute(q_part, 'ctx', shift_pairs(n_ctx, k))  5.51 us
    ppermute x3, waiting for transfers between devices, per_device(): lax.ppermute(packed_for((me_ctx + k) % n_ctx), 'ctx', shift_pairs(n_ctx, k))  5.24 us
    ppermute x3, waiting for transfers between devices, per_device(): lax.ppermute(sent, 'ctx', shift_pairs(n_ctx, k)).astype(jnp.float32)  4.87 us
    ppermute x3, starting transfers between devices, per_device(): lax.ppermute(sent, 'ctx', shift_pairs(n_ctx, k)).astype(jnp.float32)  3.77 us
    ppermute x3, starting transfers between devices, per_device(): lax.ppermute(packed_for((me_ctx + k) % n_ctx), 'ctx', shift_pairs(n_ctx, k))  3.68 us
    dot_general x1, matrix products, per_device(): jnp.einsum('sqc,skc->sqk', q_latent.reshape(seq_count, q_rows, latent_wid...  2.32 us
    ppermute x3, starting transfers between devices, per_device(): total = total + lax.ppermute(pick(me_head ^ m, col_slices), 'head', pairs)  2.23 us
  transfers between devices with their start and end apart: 12, of which 7 were waited for; matrix products, arithmetic and copies ran while one was open for 7% of the time, Pallas kernels for 0%

profile of v12, /device:TPU:1, one launch (start us, length us, event | category | flops | bytes accessed | tf_op | source)
XLA Modules:
  0.0 46.3 jit_solution(3413199480248459535)
XLA Ops:
  0.0 1.7 %fusion.13 = bf16[8,32,128]{2,0,1:T(8,128)(2,1)S(1)} fusion(bf16[32,128,128]{2,1,0:T(8,128)(2,1)} %param.11, bf16[8,32,128]{2,1,0:T(8,128)(2,1)} %param.7), kind=kOutput, calls=%fused_computation.9 | convolution fusion | flops 8421376 | bytes 1179648 | tf_op jit(solution)/shard_map/rhn,hnl->rhl/dot_general | solution.py:33
  1.7 2.1 %collective-permute-start = (bf16[8,32,128]{2,0,1:T(8,128)(2,1)S(1)}, bf16[8,32,128]{2,0,1:T(8,128)(2,1)S(1)}, u32[]{:S(2)}, u32[]{:S(2)}) collective-permute-start(bf16[8,32,128]{2,0,1:T(8,128)(2,1)S(1)} %fusion.13), channel_id=1, source_target_pairs={{0,4},{4,8},{8,12},{12,0},{1,5},{5,9},{9,13},{13,1},{2,6},{6,10},{... | collective-permute-start | bytes 196616 | tf_op jit(solution)/shard_map/ppermute | solution.py:38
  3.8 2.3 %collective-permute-start.1 = (bf16[8,32,128]{2,0,1:T(8,128)(2,1)S(1)}, bf16[8,32,128]{2,0,1:T(8,128)(2,1)S(1)}, u32[]{:S(2)}, u32[]{:S(2)}) collective-permute-start(bf16[8,32,128]{2,0,1:T(8,128)(2,1)S(1)} %fusion.13), channel_id=1, source_target_pairs={{0,8},{4,12},{8,0},{12,4},{1,9},{5,13},{9,1},{13,5},{2,10},{6,14},... | collective-permute-start | bytes 196616 | tf_op jit(solution)/shard_map/ppermute | solution.py:38
  6.1 1.1 %collective-permute-start.2 = (bf16[8,32,128]{2,0,1:T(8,128)(2,1)S(1)}, bf16[8,32,128]{2,0,1:T(8,128)(2,1)S(1)}, u32[]{:S(2)}, u32[]{:S(2)}) collective-permute-start(bf16[8,32,128]{2,0,1:T(8,128)(2,1)S(1)} %fusion.13), channel_id=1, source_target_pairs={{0,12},{4,0},{8,4},{12,8},{1,13},{5,1},{9,5},{13,9},{2,14},{6,2},{... | collective-permute-start | bytes 196616 | tf_op jit(solution)/shard_map/ppermute | solution.py:38
  7.3 0.1 broadcast_bitcast_fusion
  7.4 0.1 broadcast_bitcast_fusion.1
  7.5 0.1 broadcast_bitcast_fusion.2
  7.5 0.1 broadcast_in_dim.95
  7.6 0.1 broadcast_in_dim.96
  7.7 0.7 %broadcast_add_fusion.1 = s32[4]{0:T(128)S(1)} fusion(s32[4]{0:T(128)} %param.10), kind=kLoop, calls=%fused_computation.91 | loop fusion | flops 4 | bytes 32 | tf_op jit(solution)/shard_map/sub | solution.py:63
  8.4 0.1 broadcast_add_fusion
  8.5 1.2 %fusion.19 = f32[4,64,512]{2,1,0:T(8,128)S(1)} fusion(bf16[4,64,64]{2,1,0:T(8,128)(2,1)} %bitcast.37, bf16[4,512,576]{1,2,0:T(8,128)(2,1)} %param.9), kind=kOutput, calls=%fused_computation.15 | convolution fusion | flops 16777216 | bytes 851968 | tf_op jit(solution)/shard_map/sqc,skc->sqk/dot_general | solution.py:54
  9.7 0.1 broadcast_in_dim.100
  9.8 0.1 broadcast_in_dim.101
  9.9 1.3 %collective-permute-done.1 = bf16[8,32,128]{2,0,1:T(8,128)(2,1)S(1)} collective-permute-done((bf16[8,32,128]{2,0,1:T(8,128)(2,1)S(1)}, bf16[8,32,128]{2,0,1:T(8,128)(2,1)S(1)}, u32[]{:S(2)}, u32[]{:S(2)}) %collective-permute-start.1) | collective-permute-done | bytes 65568 | tf_op jit(solution)/shard_map/ppermute | solution.py:38
  11.2 0.1 broadcast_in_dim.105
  11.3 0.1 broadcast_in_dim.106
  11.4 0.1 broadcast_in_dim.107
  11.5 0.1 broadcast_in_dim.108
  11.6 2.3 %fusion.45 = (f32[4,64]{1,0:T(4,128)S(1)}, f32[4,64,512]{2,1,0:T(8,128)S(1)}) fusion(f32[4,64,512]{2,1,0:T(8,128)S(1)} %fusion.19, bf16[4,512,576]{1,2,0:T(8,128)(2,1)} %param.9, bf16[4,64,512]{2,1,0:T(8,128)(2,1)S(1)} %broadcast_in_dim.96, bf16[4,64,512]{2,1,0:T(8,128)(2,1)S(1)} %broadcast_in_dim.101, bf16[4,64,512]{2,1,0:T(8,128)(2,1)S(1)} %broadcast_in_dim.106, ...), kind=kOutput, calls=%fused_computation.96 | convolution fusion | flops 135266048 | bytes 4199936 | tf_op jit(solution)/shard_map/sqc,skc->sqk/dot_general | solution.py:48
  13.9 0.8 %fusion.2 = f32[4,64,512]{2,1,0:T(8,128)S(1)} fusion(bf16[4,512,576]{1,2,0:T(8,128)(2,1)S(1)} %copy-done.1, f32[4,64,512]{2,1,0:T(8,128)S(1)} %get-tuple-element.27, f32[4,64]{1,0:T(4,128)S(1)} %get-tuple-element.26, s32[4,64]{1,0:T(4,128)S(1)} %broadcast_add_fusion, s32[512]{0:T(512)S(1)} %iota_add_fusion), kind=kOutput, calls=%fused_computation.2 | convolution fusion | flops 134742016 | bytes 3151872 | tf_op jit(solution)/shard_map/sqk,skl->sql/dot_general | solution.py:69
  14.7 0.3 fusion.14
  15.0 0.1 reshape.265
  15.2 1.5 %collective-permute-start.3 = (bf16[268,128]{1,0:T(8,128)(2,1)S(1)}, bf16[268,128]{1,0:T(8,128)(2,1)S(1)}, u32[]{:S(2)}, u32[]{:S(2)}) collective-permute-start(bf16[268,128]{1,0:T(8,128)(2,1)S(1)} %get-tuple-element.14), channel_id=1, source_target_pairs={{0,4},{4,8},{8,12},{12,0},{1,5},{5,9},{9,13},{13,1},{2,6},{6,10},{... | collective-permute-start | bytes 205832 | tf_op jit(solution)/shard_map/ppermute | solution.py:113
  16.7 2.2 %collective-permute-start.5 = (bf16[268,128]{1,0:T(8,128)(2,1)S(1)}, bf16[268,128]{1,0:T(8,128)(2,1)S(1)}, u32[]{:S(2)}, u32[]{:S(2)}) collective-permute-start(bf16[268,128]{1,0:T(8,128)(2,1)S(1)} %get-tuple-element.16), channel_id=1, source_target_pairs={{0,12},{4,0},{8,4},{12,8},{1,13},{5,1},{9,5},{13,9},{2,14},{6,2},{... | collective-permute-start | bytes 205832 | tf_op jit(solution)/shard_map/ppermute | solution.py:113
  18.9 1.4 %collective-permute-done.3 = bf16[268,128]{1,0:T(8,128)(2,1)S(1)} collective-permute-done((bf16[268,128]{1,0:T(8,128)(2,1)S(1)}, bf16[268,128]{1,0:T(8,128)(2,1)S(1)}, u32[]{:S(2)}, u32[]{:S(2)}) %collective-permute-start.3) | collective-permute-done | bytes 68640 | tf_op jit(solution)/shard_map/ppermute | solution.py:113
  20.3 3.8 %collective-permute-done.4 = bf16[268,128]{1,0:T(8,128)(2,1)S(1)} collective-permute-done((bf16[268,128]{1,0:T(8,128)(2,1)S(1)}, bf16[268,128]{1,0:T(8,128)(2,1)S(1)}, u32[]{:S(2)}, u32[]{:S(2)}) %collective-permute-start.4) | collective-permute-done | bytes 68640 | tf_op jit(solution)/shard_map/ppermute | solution.py:113
  24.1 0.1 squeeze.21
  24.2 0.1 squeeze.22
  24.3 0.1 squeeze.23
  24.4 0.1 squeeze.24
  24.5 0.1 squeeze.25
  24.6 0.1 squeeze.26
  24.7 0.2 fusion.31
  25.0 0.4 fusion.46
  25.4 1.6 %collective-permute-start.6 = (bf16[8,32,128]{2,0,1:T(8,128)(2,1)S(1)}, bf16[8,32,128]{2,0,1:T(8,128)(2,1)S(1)}, u32[]{:S(2)}, u32[]{:S(2)}) collective-permute-start(bf16[8,32,128]{2,0,1:T(8,128)(2,1)S(1)} %get-tuple-element.28), channel_id=1, source_target_pairs={{0,4},{4,8},{8,12},{12,0},{1,5},{5,9},{9,13},{13,1},{2,6},{6,10},{... | collective-permute-start | bytes 196616 | tf_op jit(solution)/shard_map/ppermute | solution.py:127
  27.0 2.2 %collective-permute-start.8 = (bf16[8,32,128]{2,0,1:T(8,128)(2,1)S(1)}, bf16[8,32,128]{2,0,1:T(8,128)(2,1)S(1)}, u32[]{:S(2)}, u32[]{:S(2)}) collective-permute-start(bf16[8,32,128]{2,0,1:T(8,128)(2,1)S(1)} %get-tuple-element.28), channel_id=1, source_target_pairs={{0,12},{4,0},{8,4},{12,8},{1,13},{5,1},{9,5},{13,9},{2,14},{6,2},{... | collective-permute-start | bytes 196616 | tf_op jit(solution)/shard_map/ppermute | solution.py:127
  29.1 1.2 %collective-permute-done.6 = bf16[8,32,128]{2,0,1:T(8,128)(2,1)S(1)} collective-permute-done((bf16[8,32,128]{2,0,1:T(8,128)(2,1)S(1)}, bf16[8,32,128]{2,0,1:T(8,128)(2,1)S(1)}, u32[]{:S(2)}, u32[]{:S(2)}) %collective-permute-start.6) | collective-permute-done | bytes 65568 | tf_op jit(solution)/shard_map/ppermute | solution.py:127
  30.3 3.7 %collective-permute-done.7 = bf16[8,32,128]{2,0,1:T(8,128)(2,1)S(1)} collective-permute-done((bf16[8,32,128]{2,0,1:T(8,128)(2,1)S(1)}, bf16[8,32,128]{2,0,1:T(8,128)(2,1)S(1)}, u32[]{:S(2)}, u32[]{:S(2)}) %collective-permute-start.7) | collective-permute-done | bytes 65568 | tf_op jit(solution)/shard_map/ppermute | solution.py:127
  34.0 7.2 %fusion.35 = f32[8,1792]{1,0:T(8,128)S(1)} fusion(bf16[4096,1792]{1,0:T(8,128)(2,1)} %param.13, bf16[8,32,128]{2,0,1:T(8,128)(2,1)S(1)} %collective-permute-done.8, bf16[8,32,128]{2,0,1:T(8,128)(2,1)S(1)} %collective-permute-done.7, f32[8,32,128]{2,0,1:T(8,128)S(1)} %get-tuple-element.29, bf16[8,32,128]{2,0,1:T(8,128)(2,1)S(1)} %collective-permute-done.6), kind=kOutput, calls=%fused_computation.47 | convolution fusion | flops 117669888 | bytes 15065088 | tf_op jit(solution)/shard_map/dot_general | solution.py:133
  41.2 0.1 select_select_fusion.2
  41.3 0.0 collective-permute-start.10
  41.3 1.0 %collective-permute-start.9 = (f32[8,448]{1,0:T(8,128)S(1)}, f32[8,448]{1,0:T(8,128)S(1)}, u32[]{:S(2)}, u32[]{:S(2)}) collective-permute-start(f32[8,448]{1,0:T(8,128)S(1)} %get-tuple-element.12), channel_id=1, source_target_pairs={{0,1},{1,0},{2,3},{3,2},{4,5},{5,4},{6,7},{7,6},{8,9},{9,8},{10,11... | collective-permute-start | bytes 43016 | tf_op jit(solution)/shard_map/ppermute | solution.py:145
  42.3 0.1 select_select_fusion
  42.4 1.2 %collective-permute-start.11 = (f32[8,448]{1,0:T(8,128)S(1)}, f32[8,448]{1,0:T(8,128)S(1)}, u32[]{:S(2)}, u32[]{:S(2)}) collective-permute-start(f32[8,448]{1,0:T(8,128)S(1)} %select_select_fusion), channel_id=1, source_target_pairs={{0,3},{1,2},{2,1},{3,0},{4,7},{5,6},{6,5},{7,4},{8,11},{9,10},{10,... | collective-permute-start | bytes 43016 | tf_op jit(solution)/shard_map/ppermute | solution.py:145
  43.6 0.3 collective-permute-done.10
  43.9 1.7 %collective-permute-done.11 = f32[8,448]{1,0:T(8,128)S(1)} collective-permute-done((f32[8,448]{1,0:T(8,128)S(1)}, f32[8,448]{1,0:T(8,128)S(1)}, u32[]{:S(2)}, u32[]{:S(2)}) %collective-permute-start.11) | collective-permute-done | bytes 14368 | tf_op jit(solution)/shard_map/ppermute | solution.py:145
  45.6 0.7 %add_add_fusion = f32[8,448]{1,0:T(8,128)} fusion(f32[8,448]{1,0:T(8,128)S(1)} %collective-permute-done.11, f32[8,448]{1,0:T(8,128)S(1)} %collective-permute-done.10, f32[8,448]{1,0:T(8,128)S(1)} %collective-permute-done.9, f32[8,1792]{1,0:T(8,128)S(1)} %fusion.35, pred[]{:T(512)S(6)} %eq.119, pred[]{:T(512)S(6)} %eq.118, pred[]{:T(512)S(6)} %eq.102), kind=kLoop, calls=%fused_computation.51 | loop fusion | flops 21504 | bytes 114691 | tf_op jit(solution)/shard_map/add | solution.py:145
  (37 shorter events, 0.3 us)
Async XLA Ops:
  0.0 25.0 %copy-start = (bf16[32,128,128]{2,1,0:T(8,128)(2,1)S(1)}, bf16[32,128,128]{2,1,0:T(8,128)(2,1)}, u32[]{:S(2)}) copy-start(bf16[32,128,128]{2,1,0:T(8,128)(2,1)} %param.12) | copy-start | bytes 3145732
  1.7 8.0 %collective-permute-start = (bf16[8,32,128]{2,0,1:T(8,128)(2,1)S(1)}, bf16[8,32,128]{2,0,1:T(8,128)(2,1)S(1)}, u32[]{:S(2)}, u32[]{:S(2)}) collective-permute-start(bf16[8,32,128]{2,0,1:T(8,128)(2,1)S(1)} %fusion.13), channel_id=1, source_target_pairs={{0,4},{4,8},{8,12},{12,0},{1,5},{5,9},{9,13},{13,1},{2,6},{6,10},{... | collective-permute-start | bytes 196616 | tf_op jit(solution)/shard_map/ppermute | solution.py:38
  3.8 7.3 %collective-permute-start.1 = (bf16[8,32,128]{2,0,1:T(8,128)(2,1)S(1)}, bf16[8,32,128]{2,0,1:T(8,128)(2,1)S(1)}, u32[]{:S(2)}, u32[]{:S(2)}) collective-permute-start(bf16[8,32,128]{2,0,1:T(8,128)(2,1)S(1)} %fusion.13), channel_id=1, source_target_pairs={{0,8},{4,12},{8,0},{12,4},{1,9},{5,13},{9,1},{13,5},{2,10},{6,14},... | collective-permute-start | bytes 196616 | tf_op jit(solution)/shard_map/ppermute | solution.py:38
  6.1 5.2 %collective-permute-start.2 = (bf16[8,32,128]{2,0,1:T(8,128)(2,1)S(1)}, bf16[8,32,128]{2,0,1:T(8,128)(2,1)S(1)}, u32[]{:S(2)}, u32[]{:S(2)}) collective-permute-start(bf16[8,32,128]{2,0,1:T(8,128)(2,1)S(1)} %fusion.13), channel_id=1, source_target_pairs={{0,12},{4,0},{8,4},{12,8},{1,13},{5,1},{9,5},{13,9},{2,14},{6,2},{... | collective-permute-start | bytes 196616 | tf_op jit(solution)/shard_map/ppermute | solution.py:38
  11.6 2.3 %copy-start.1 = (bf16[4,512,576]{1,2,0:T(8,128)(2,1)S(1)}, bf16[4,512,576]{1,2,0:T(8,128)(2,1)}, u32[]{:S(2)}) copy-start(bf16[4,512,576]{1,2,0:T(8,128)(2,1)} %param.9) | copy-start | bytes 7077892
  15.2 5.1 %collective-permute-start.3 = (bf16[268,128]{1,0:T(8,128)(2,1)S(1)}, bf16[268,128]{1,0:T(8,128)(2,1)S(1)}, u32[]{:S(2)}, u32[]{:S(2)}) collective-permute-start(bf16[268,128]{1,0:T(8,128)(2,1)S(1)} %get-tuple-element.14), channel_id=1, source_target_pairs={{0,4},{4,8},{8,12},{12,0},{1,5},{5,9},{9,13},{13,1},{2,6},{6,10},{... | collective-permute-start | bytes 205832 | tf_op jit(solution)/shard_map/ppermute | solution.py:113
  16.7 7.4 %collective-permute-start.4 = (bf16[268,128]{1,0:T(8,128)(2,1)S(1)}, bf16[268,128]{1,0:T(8,128)(2,1)S(1)}, u32[]{:S(2)}, u32[]{:S(2)}) collective-permute-start(bf16[268,128]{1,0:T(8,128)(2,1)S(1)} %get-tuple-element.15), channel_id=1, source_target_pairs={{0,8},{4,12},{8,0},{12,4},{1,9},{5,13},{9,1},{13,5},{2,10},{6,14},... | collective-permute-start | bytes 205832 | tf_op jit(solution)/shard_map/ppermute | solution.py:113
  16.7 7.6 %collective-permute-start.5 = (bf16[268,128]{1,0:T(8,128)(2,1)S(1)}, bf16[268,128]{1,0:T(8,128)(2,1)S(1)}, u32[]{:S(2)}, u32[]{:S(2)}) collective-permute-start(bf16[268,128]{1,0:T(8,128)(2,1)S(1)} %get-tuple-element.16), channel_id=1, source_target_pairs={{0,12},{4,0},{8,4},{12,8},{1,13},{5,1},{9,5},{13,9},{2,14},{6,2},{... | collective-permute-start | bytes 205832 | tf_op jit(solution)/shard_map/ppermute | solution.py:113
  25.4 5.0 %collective-permute-start.6 = (bf16[8,32,128]{2,0,1:T(8,128)(2,1)S(1)}, bf16[8,32,128]{2,0,1:T(8,128)(2,1)S(1)}, u32[]{:S(2)}, u32[]{:S(2)}) collective-permute-start(bf16[8,32,128]{2,0,1:T(8,128)(2,1)S(1)} %get-tuple-element.28), channel_id=1, source_target_pairs={{0,4},{4,8},{8,12},{12,0},{1,5},{5,9},{9,13},{13,1},{2,6},{6,10},{... | collective-permute-start | bytes 196616 | tf_op jit(solution)/shard_map/ppermute | solution.py:127
  27.0 7.0 %collective-permute-start.7 = (bf16[8,32,128]{2,0,1:T(8,128)(2,1)S(1)}, bf16[8,32,128]{2,0,1:T(8,128)(2,1)S(1)}, u32[]{:S(2)}, u32[]{:S(2)}) collective-permute-start(bf16[8,32,128]{2,0,1:T(8,128)(2,1)S(1)} %get-tuple-element.28), channel_id=1, source_target_pairs={{0,8},{4,12},{8,0},{12,4},{1,9},{5,13},{9,1},{13,5},{2,10},{6,14},... | collective-permute-start | bytes 196616 | tf_op jit(solution)/shard_map/ppermute | solution.py:127
  27.0 7.0 %collective-permute-start.8 = (bf16[8,32,128]{2,0,1:T(8,128)(2,1)S(1)}, bf16[8,32,128]{2,0,1:T(8,128)(2,1)S(1)}, u32[]{:S(2)}, u32[]{:S(2)}) collective-permute-start(bf16[8,32,128]{2,0,1:T(8,128)(2,1)S(1)} %get-tuple-element.28), channel_id=1, source_target_pairs={{0,12},{4,0},{8,4},{12,8},{1,13},{5,1},{9,5},{13,9},{2,14},{6,2},{... | collective-permute-start | bytes 196616 | tf_op jit(solution)/shard_map/ppermute | solution.py:127
  41.3 2.6 %collective-permute-start.10 = (f32[8,448]{1,0:T(8,128)S(1)}, f32[8,448]{1,0:T(8,128)S(1)}, u32[]{:S(2)}, u32[]{:S(2)}) collective-permute-start(f32[8,448]{1,0:T(8,128)S(1)} %get-tuple-element.13), channel_id=1, source_target_pairs={{0,2},{1,3},{2,0},{3,1},{4,6},{5,7},{6,4},{7,5},{8,10},{9,11},{10,... | collective-permute-start | bytes 43016 | tf_op jit(solution)/shard_map/ppermute | solution.py:145
  41.3 2.6 %collective-permute-start.9 = (f32[8,448]{1,0:T(8,128)S(1)}, f32[8,448]{1,0:T(8,128)S(1)}, u32[]{:S(2)}, u32[]{:S(2)}) collective-permute-start(f32[8,448]{1,0:T(8,128)S(1)} %get-tuple-element.12), channel_id=1, source_target_pairs={{0,1},{1,0},{2,3},{3,2},{4,5},{5,4},{6,7},{7,6},{8,9},{9,8},{10,11... | collective-permute-start | bytes 43016 | tf_op jit(solution)/shard_map/ppermute | solution.py:145
  42.4 3.2 %collective-permute-start.11 = (f32[8,448]{1,0:T(8,128)S(1)}, f32[8,448]{1,0:T(8,128)S(1)}, u32[]{:S(2)}, u32[]{:S(2)}) collective-permute-start(f32[8,448]{1,0:T(8,128)S(1)} %select_select_fusion), channel_id=1, source_target_pairs={{0,3},{1,2},{2,1},{3,0},{4,7},{5,6},{6,5},{7,4},{8,11},{9,10},{10,... | collective-permute-start | bytes 43016 | tf_op jit(solution)/shard_map/ppermute | solution.py:145

commit v13 on v12

--- a/solution.py
+++ b/solution.py
@@ -140,7 +140,7 @@
     col_slices = [partial_value[:, j * out_width:(j + 1) * out_width] for j in range(n_head)]
     total = pick(me_head, col_slices)
     if n_head & (n_head - 1) == 0:
-        for m in range(1, n_head):
+        for m in sorted(range(1, n_head), key=lambda m: (m == 1, -m & 2, m)):
             pairs = [(i, i ^ m) for i in range(n_head)]
             total = total + lax.ppermute(pick(me_head ^ m, col_slices), "head", pairs)
         return total

time: 46.6 us -> 46.5 us (level)
  no operation moved by 1% of the time
where the time goes in v13:
time: 46.5 us; the launch traced here: 46 us
  starting transfers between devices  15.2 us (33%)
  matrix products  13.5 us (29%)
  waiting for transfers between devices  13 us (28%)
  other arithmetic  2.26 us (5%)
  local copies, waits for them, and re-layouts  1.62 us (3%)
    dot_general x1, matrix products, per_device(): jnp.dot(values.reshape(row_count, -1), w_output, preferred_element_type=j...  7.17 us
    ppermute x3, starting transfers between devices, per_device(): lax.ppermute(q_part, 'ctx', shift_pairs(n_ctx, k))  5.51 us
    ppermute x3, waiting for transfers between devices, per_device(): lax.ppermute(packed_for((me_ctx + k) % n_ctx), 'ctx', shift_pairs(n_ctx, k))  5.24 us
    ppermute x3, waiting for transfers between devices, per_device(): lax.ppermute(sent, 'ctx', shift_pairs(n_ctx, k)).astype(jnp.float32)  4.87 us
    ppermute x3, starting transfers between devices, per_device(): lax.ppermute(sent, 'ctx', shift_pairs(n_ctx, k)).astype(jnp.float32)  3.77 us
    ppermute x3, starting transfers between devices, per_device(): lax.ppermute(packed_for((me_ctx + k) % n_ctx), 'ctx', shift_pairs(n_ctx, k))  3.68 us
    dot_general x1, matrix products, per_device(): jnp.einsum('sqc,skc->sqk', q_latent.reshape(seq_count, q_rows, latent_wid...  2.32 us
    ppermute x3, starting transfers between devices, per_device(): total = total + lax.ppermute(pick(me_head ^ m, col_slices), 'head', pairs)  2.23 us
  transfers between devices with their start and end apart: 12, of which 7 were waited for; matrix products, arithmetic and copies ran while one was open for 7% of the time, Pallas kernels for 0%

profile of v13, /device:TPU:1, one launch (start us, length us, event | category | flops | bytes accessed | tf_op | source)
XLA Modules:
  0.0 46.0 jit_solution(3440836517977634931)
XLA Ops:
  0.0 1.7 %fusion.13 = bf16[8,32,128]{2,0,1:T(8,128)(2,1)S(1)} fusion(bf16[32,128,128]{2,1,0:T(8,128)(2,1)} %param.11, bf16[8,32,128]{2,1,0:T(8,128)(2,1)} %param.7), kind=kOutput, calls=%fused_computation.9 | convolution fusion | flops 8421376 | bytes 1179648 | tf_op jit(solution)/shard_map/rhn,hnl->rhl/dot_general | solution.py:33
  1.7 2.1 %collective-permute-start = (bf16[8,32,128]{2,0,1:T(8,128)(2,1)S(1)}, bf16[8,32,128]{2,0,1:T(8,128)(2,1)S(1)}, u32[]{:S(2)}, u32[]{:S(2)}) collective-permute-start(bf16[8,32,128]{2,0,1:T(8,128)(2,1)S(1)} %fusion.13), channel_id=1, source_target_pairs={{0,4},{4,8},{8,12},{12,0},{1,5},{5,9},{9,13},{13,1},{2,6},{6,10},{... | collective-permute-start | bytes 196616 | tf_op jit(solution)/shard_map/ppermute | solution.py:38
  3.8 2.3 %collective-permute-start.1 = (bf16[8,32,128]{2,0,1:T(8,128)(2,1)S(1)}, bf16[8,32,128]{2,0,1:T(8,128)(2,1)S(1)}, u32[]{:S(2)}, u32[]{:S(2)}) collective-permute-start(bf16[8,32,128]{2,0,1:T(8,128)(2,1)S(1)} %fusion.13), channel_id=1, source_target_pairs={{0,8},{4,12},{8,0},{12,4},{1,9},{5,13},{9,1},{13,5},{2,10},{6,14},... | collective-permute-start | bytes 196616 | tf_op jit(solution)/shard_map/ppermute | solution.py:38
  6.1 1.1 %collective-permute-start.2 = (bf16[8,32,128]{2,0,1:T(8,128)(2,1)S(1)}, bf16[8,32,128]{2,0,1:T(8,128)(2,1)S(1)}, u32[]{:S(2)}, u32[]{:S(2)}) collective-permute-start(bf16[8,32,128]{2,0,1:T(8,128)(2,1)S(1)} %fusion.13), channel_id=1, source_target_pairs={{0,12},{4,0},{8,4},{12,8},{1,13},{5,1},{9,5},{13,9},{2,14},{6,2},{... | collective-permute-start | bytes 196616 | tf_op jit(solution)/shard_map/ppermute | solution.py:38
  7.3 0.1 broadcast_bitcast_fusion
  7.4 0.1 broadcast_bitcast_fusion.1
  7.5 0.1 broadcast_bitcast_fusion.2
  7.5 0.1 broadcast_in_dim.95
  7.6 0.1 broadcast_in_dim.96
  7.7 0.7 %broadcast_add_fusion.1 = s32[4]{0:T(128)S(1)} fusion(s32[4]{0:T(128)} %param.10), kind=kLoop, calls=%fused_computation.91 | loop fusion | flops 4 | bytes 32 | tf_op jit(solution)/shard_map/sub | solution.py:63
  8.4 0.1 broadcast_add_fusion
  8.5 1.2 %fusion.19 = f32[4,64,512]{2,1,0:T(8,128)S(1)} fusion(bf16[4,64,64]{2,1,0:T(8,128)(2,1)} %bitcast.37, bf16[4,512,576]{1,2,0:T(8,128)(2,1)} %param.9), kind=kOutput, calls=%fused_computation.15 | convolution fusion | flops 16777216 | bytes 851968 | tf_op jit(solution)/shard_map/sqc,skc->sqk/dot_general | solution.py:54
  9.7 0.1 broadcast_in_dim.100
  9.8 0.1 broadcast_in_dim.101
  9.9 1.3 %collective-permute-done.1 = bf16[8,32,128]{2,0,1:T(8,128)(2,1)S(1)} collective-permute-done((bf16[8,32,128]{2,0,1:T(8,128)(2,1)S(1)}, bf16[8,32,128]{2,0,1:T(8,128)(2,1)S(1)}, u32[]{:S(2)}, u32[]{:S(2)}) %collective-permute-start.1) | collective-permute-done | bytes 65568 | tf_op jit(solution)/shard_map/ppermute | solution.py:38
  11.2 0.1 broadcast_in_dim.105
  11.3 0.1 broadcast_in_dim.106
  11.4 0.1 broadcast_in_dim.107
  11.5 0.1 broadcast_in_dim.108
  11.6 2.3 %fusion.45 = (f32[4,64]{1,0:T(4,128)S(1)}, f32[4,64,512]{2,1,0:T(8,128)S(1)}) fusion(f32[4,64,512]{2,1,0:T(8,128)S(1)} %fusion.19, bf16[4,512,576]{1,2,0:T(8,128)(2,1)} %param.9, bf16[4,64,512]{2,1,0:T(8,128)(2,1)S(1)} %broadcast_in_dim.96, bf16[4,64,512]{2,1,0:T(8,128)(2,1)S(1)} %broadcast_in_dim.101, bf16[4,64,512]{2,1,0:T(8,128)(2,1)S(1)} %broadcast_in_dim.106, ...), kind=kOutput, calls=%fused_computation.96 | convolution fusion | flops 135266048 | bytes 4199936 | tf_op jit(solution)/shard_map/sqc,skc->sqk/dot_general | solution.py:48
  13.9 0.8 %fusion.2 = f32[4,64,512]{2,1,0:T(8,128)S(1)} fusion(bf16[4,512,576]{1,2,0:T(8,128)(2,1)S(1)} %copy-done.1, f32[4,64,512]{2,1,0:T(8,128)S(1)} %get-tuple-element.27, f32[4,64]{1,0:T(4,128)S(1)} %get-tuple-element.26, s32[4,64]{1,0:T(4,128)S(1)} %broadcast_add_fusion, s32[512]{0:T(512)S(1)} %iota_add_fusion), kind=kOutput, calls=%fused_computation.2 | convolution fusion | flops 134742016 | bytes 3151872 | tf_op jit(solution)/shard_map/sqk,skl->sql/dot_general | solution.py:69
  14.7 0.3 fusion.14
  15.0 0.1 reshape.265
  15.2 1.5 %collective-permute-start.3 = (bf16[268,128]{1,0:T(8,128)(2,1)S(1)}, bf16[268,128]{1,0:T(8,128)(2,1)S(1)}, u32[]{:S(2)}, u32[]{:S(2)}) collective-permute-start(bf16[268,128]{1,0:T(8,128)(2,1)S(1)} %get-tuple-element.14), channel_id=1, source_target_pairs={{0,4},{4,8},{8,12},{12,0},{1,5},{5,9},{9,13},{13,1},{2,6},{6,10},{... | collective-permute-start | bytes 205832 | tf_op jit(solution)/shard_map/ppermute | solution.py:113
  16.7 2.2 %collective-permute-start.5 = (bf16[268,128]{1,0:T(8,128)(2,1)S(1)}, bf16[268,128]{1,0:T(8,128)(2,1)S(1)}, u32[]{:S(2)}, u32[]{:S(2)}) collective-permute-start(bf16[268,128]{1,0:T(8,128)(2,1)S(1)} %get-tuple-element.16), channel_id=1, source_target_pairs={{0,12},{4,0},{8,4},{12,8},{1,13},{5,1},{9,5},{13,9},{2,14},{6,2},{... | collective-permute-start | bytes 205832 | tf_op jit(solution)/shard_map/ppermute | solution.py:113
  18.9 1.4 %collective-permute-done.3 = bf16[268,128]{1,0:T(8,128)(2,1)S(1)} collective-permute-done((bf16[268,128]{1,0:T(8,128)(2,1)S(1)}, bf16[268,128]{1,0:T(8,128)(2,1)S(1)}, u32[]{:S(2)}, u32[]{:S(2)}) %collective-permute-start.3) | collective-permute-done | bytes 68640 | tf_op jit(solution)/shard_map/ppermute | solution.py:113
  20.3 3.8 %collective-permute-done.4 = bf16[268,128]{1,0:T(8,128)(2,1)S(1)} collective-permute-done((bf16[268,128]{1,0:T(8,128)(2,1)S(1)}, bf16[268,128]{1,0:T(8,128)(2,1)S(1)}, u32[]{:S(2)}, u32[]{:S(2)}) %collective-permute-start.4) | collective-permute-done | bytes 68640 | tf_op jit(solution)/shard_map/ppermute | solution.py:113
  24.1 0.1 squeeze.21
  24.2 0.1 squeeze.22
  24.3 0.1 squeeze.23
  24.4 0.1 squeeze.24
  24.5 0.1 squeeze.25
  24.6 0.1 squeeze.26
  24.7 0.2 fusion.31
  25.0 0.4 fusion.46
  25.4 1.6 %collective-permute-start.6 = (bf16[8,32,128]{2,0,1:T(8,128)(2,1)S(1)}, bf16[8,32,128]{2,0,1:T(8,128)(2,1)S(1)}, u32[]{:S(2)}, u32[]{:S(2)}) collective-permute-start(bf16[8,32,128]{2,0,1:T(8,128)(2,1)S(1)} %get-tuple-element.28), channel_id=1, source_target_pairs={{0,4},{4,8},{8,12},{12,0},{1,5},{5,9},{9,13},{13,1},{2,6},{6,10},{... | collective-permute-start | bytes 196616 | tf_op jit(solution)/shard_map/ppermute | solution.py:127
  27.0 2.2 %collective-permute-start.8 = (bf16[8,32,128]{2,0,1:T(8,128)(2,1)S(1)}, bf16[8,32,128]{2,0,1:T(8,128)(2,1)S(1)}, u32[]{:S(2)}, u32[]{:S(2)}) collective-permute-start(bf16[8,32,128]{2,0,1:T(8,128)(2,1)S(1)} %get-tuple-element.28), channel_id=1, source_target_pairs={{0,12},{4,0},{8,4},{12,8},{1,13},{5,1},{9,5},{13,9},{2,14},{6,2},{... | collective-permute-start | bytes 196616 | tf_op jit(solution)/shard_map/ppermute | solution.py:127
  29.1 1.2 %collective-permute-done.6 = bf16[8,32,128]{2,0,1:T(8,128)(2,1)S(1)} collective-permute-done((bf16[8,32,128]{2,0,1:T(8,128)(2,1)S(1)}, bf16[8,32,128]{2,0,1:T(8,128)(2,1)S(1)}, u32[]{:S(2)}, u32[]{:S(2)}) %collective-permute-start.6) | collective-permute-done | bytes 65568 | tf_op jit(solution)/shard_map/ppermute | solution.py:127
  30.3 3.7 %collective-permute-done.7 = bf16[8,32,128]{2,0,1:T(8,128)(2,1)S(1)} collective-permute-done((bf16[8,32,128]{2,0,1:T(8,128)(2,1)S(1)}, bf16[8,32,128]{2,0,1:T(8,128)(2,1)S(1)}, u32[]{:S(2)}, u32[]{:S(2)}) %collective-permute-start.7) | collective-permute-done | bytes 65568 | tf_op jit(solution)/shard_map/ppermute | solution.py:127
  34.0 7.2 %fusion.35 = f32[8,1792]{1,0:T(8,128)S(1)} fusion(bf16[4096,1792]{1,0:T(8,128)(2,1)} %param.13, bf16[8,32,128]{2,0,1:T(8,128)(2,1)S(1)} %collective-permute-done.8, bf16[8,32,128]{2,0,1:T(8,128)(2,1)S(1)} %collective-permute-done.7, f32[8,32,128]{2,0,1:T(8,128)S(1)} %get-tuple-element.29, bf16[8,32,128]{2,0,1:T(8,128)(2,1)S(1)} %collective-permute-done.6), kind=kOutput, calls=%fused_computation.47 | convolution fusion | flops 117669888 | bytes 15065088 | tf_op jit(solution)/shard_map/dot_general | solution.py:133
  41.2 0.1 select_select_fusion.2
  41.3 0.0 collective-permute-start.10
  41.3 2.2 %collective-permute-start.9 = (f32[8,448]{1,0:T(8,128)S(1)}, f32[8,448]{1,0:T(8,128)S(1)}, u32[]{:S(2)}, u32[]{:S(2)}) collective-permute-start(f32[8,448]{1,0:T(8,128)S(1)} %get-tuple-element.12), channel_id=1, source_target_pairs={{0,3},{1,2},{2,1},{3,0},{4,7},{5,6},{6,5},{7,4},{8,11},{9,10},{10,... | collective-permute-start | bytes 43016 | tf_op jit(solution)/shard_map/ppermute | solution.py:145
  43.5 0.1 select_select_fusion
  43.6 0.0 collective-permute-start.11
  43.6 0.3 collective-permute-done.10
  43.9 1.4 %collective-permute-done.9 = f32[8,448]{1,0:T(8,128)S(1)} collective-permute-done((f32[8,448]{1,0:T(8,128)S(1)}, f32[8,448]{1,0:T(8,128)S(1)}, u32[]{:S(2)}, u32[]{:S(2)}) %collective-permute-start.9) | collective-permute-done | bytes 14368 | tf_op jit(solution)/shard_map/ppermute | solution.py:145
  45.3 0.7 %add_add_fusion = f32[8,448]{1,0:T(8,128)} fusion(f32[8,448]{1,0:T(8,128)S(1)} %collective-permute-done.11, f32[8,448]{1,0:T(8,128)S(1)} %collective-permute-done.10, f32[8,448]{1,0:T(8,128)S(1)} %collective-permute-done.9, f32[8,1792]{1,0:T(8,128)S(1)} %fusion.35, pred[]{:T(512)S(6)} %eq.119, pred[]{:T(512)S(6)} %eq.118, pred[]{:T(512)S(6)} %eq.102), kind=kLoop, calls=%fused_computation.51 | loop fusion | flops 21504 | bytes 114691 | tf_op jit(solution)/shard_map/add | solution.py:145
  (37 shorter events, 0.3 us)
Async XLA Ops:
  0.0 25.0 %copy-start = (bf16[32,128,128]{2,1,0:T(8,128)(2,1)S(1)}, bf16[32,128,128]{2,1,0:T(8,128)(2,1)}, u32[]{:S(2)}) copy-start(bf16[32,128,128]{2,1,0:T(8,128)(2,1)} %param.12) | copy-start | bytes 3145732
  1.7 8.0 %collective-permute-start = (bf16[8,32,128]{2,0,1:T(8,128)(2,1)S(1)}, bf16[8,32,128]{2,0,1:T(8,128)(2,1)S(1)}, u32[]{:S(2)}, u32[]{:S(2)}) collective-permute-start(bf16[8,32,128]{2,0,1:T(8,128)(2,1)S(1)} %fusion.13), channel_id=1, source_target_pairs={{0,4},{4,8},{8,12},{12,0},{1,5},{5,9},{9,13},{13,1},{2,6},{6,10},{... | collective-permute-start | bytes 196616 | tf_op jit(solution)/shard_map/ppermute | solution.py:38
  3.8 7.3 %collective-permute-start.1 = (bf16[8,32,128]{2,0,1:T(8,128)(2,1)S(1)}, bf16[8,32,128]{2,0,1:T(8,128)(2,1)S(1)}, u32[]{:S(2)}, u32[]{:S(2)}) collective-permute-start(bf16[8,32,128]{2,0,1:T(8,128)(2,1)S(1)} %fusion.13), channel_id=1, source_target_pairs={{0,8},{4,12},{8,0},{12,4},{1,9},{5,13},{9,1},{13,5},{2,10},{6,14},... | collective-permute-start | bytes 196616 | tf_op jit(solution)/shard_map/ppermute | solution.py:38
  6.1 5.2 %collective-permute-start.2 = (bf16[8,32,128]{2,0,1:T(8,128)(2,1)S(1)}, bf16[8,32,128]{2,0,1:T(8,128)(2,1)S(1)}, u32[]{:S(2)}, u32[]{:S(2)}) collective-permute-start(bf16[8,32,128]{2,0,1:T(8,128)(2,1)S(1)} %fusion.13), channel_id=1, source_target_pairs={{0,12},{4,0},{8,4},{12,8},{1,13},{5,1},{9,5},{13,9},{2,14},{6,2},{... | collective-permute-start | bytes 196616 | tf_op jit(solution)/shard_map/ppermute | solution.py:38
  11.6 2.3 %copy-start.1 = (bf16[4,512,576]{1,2,0:T(8,128)(2,1)S(1)}, bf16[4,512,576]{1,2,0:T(8,128)(2,1)}, u32[]{:S(2)}) copy-start(bf16[4,512,576]{1,2,0:T(8,128)(2,1)} %param.9) | copy-start | bytes 7077892
  15.2 5.1 %collective-permute-start.3 = (bf16[268,128]{1,0:T(8,128)(2,1)S(1)}, bf16[268,128]{1,0:T(8,128)(2,1)S(1)}, u32[]{:S(2)}, u32[]{:S(2)}) collective-permute-start(bf16[268,128]{1,0:T(8,128)(2,1)S(1)} %get-tuple-element.14), channel_id=1, source_target_pairs={{0,4},{4,8},{8,12},{12,0},{1,5},{5,9},{9,13},{13,1},{2,6},{6,10},{... | collective-permute-start | bytes 205832 | tf_op jit(solution)/shard_map/ppermute | solution.py:113
  16.7 7.4 %collective-permute-start.4 = (bf16[268,128]{1,0:T(8,128)(2,1)S(1)}, bf16[268,128]{1,0:T(8,128)(2,1)S(1)}, u32[]{:S(2)}, u32[]{:S(2)}) collective-permute-start(bf16[268,128]{1,0:T(8,128)(2,1)S(1)} %get-tuple-element.15), channel_id=1, source_target_pairs={{0,8},{4,12},{8,0},{12,4},{1,9},{5,13},{9,1},{13,5},{2,10},{6,14},... | collective-permute-start | bytes 205832 | tf_op jit(solution)/shard_map/ppermute | solution.py:113
  16.7 7.6 %collective-permute-start.5 = (bf16[268,128]{1,0:T(8,128)(2,1)S(1)}, bf16[268,128]{1,0:T(8,128)(2,1)S(1)}, u32[]{:S(2)}, u32[]{:S(2)}) collective-permute-start(bf16[268,128]{1,0:T(8,128)(2,1)S(1)} %get-tuple-element.16), channel_id=1, source_target_pairs={{0,12},{4,0},{8,4},{12,8},{1,13},{5,1},{9,5},{13,9},{2,14},{6,2},{... | collective-permute-start | bytes 205832 | tf_op jit(solution)/shard_map/ppermute | solution.py:113
  25.4 5.0 %collective-permute-start.6 = (bf16[8,32,128]{2,0,1:T(8,128)(2,1)S(1)}, bf16[8,32,128]{2,0,1:T(8,128)(2,1)S(1)}, u32[]{:S(2)}, u32[]{:S(2)}) collective-permute-start(bf16[8,32,128]{2,0,1:T(8,128)(2,1)S(1)} %get-tuple-element.28), channel_id=1, source_target_pairs={{0,4},{4,8},{8,12},{12,0},{1,5},{5,9},{9,13},{13,1},{2,6},{6,10},{... | collective-permute-start | bytes 196616 | tf_op jit(solution)/shard_map/ppermute | solution.py:127
  27.0 7.0 %collective-permute-start.7 = (bf16[8,32,128]{2,0,1:T(8,128)(2,1)S(1)}, bf16[8,32,128]{2,0,1:T(8,128)(2,1)S(1)}, u32[]{:S(2)}, u32[]{:S(2)}) collective-permute-start(bf16[8,32,128]{2,0,1:T(8,128)(2,1)S(1)} %get-tuple-element.28), channel_id=1, source_target_pairs={{0,8},{4,12},{8,0},{12,4},{1,9},{5,13},{9,1},{13,5},{2,10},{6,14},... | collective-permute-start | bytes 196616 | tf_op jit(solution)/shard_map/ppermute | solution.py:127
  27.0 7.0 %collective-permute-start.8 = (bf16[8,32,128]{2,0,1:T(8,128)(2,1)S(1)}, bf16[8,32,128]{2,0,1:T(8,128)(2,1)S(1)}, u32[]{:S(2)}, u32[]{:S(2)}) collective-permute-start(bf16[8,32,128]{2,0,1:T(8,128)(2,1)S(1)} %get-tuple-element.28), channel_id=1, source_target_pairs={{0,12},{4,0},{8,4},{12,8},{1,13},{5,1},{9,5},{13,9},{2,14},{6,2},{... | collective-permute-start | bytes 196616 | tf_op jit(solution)/shard_map/ppermute | solution.py:127
  41.3 2.6 %collective-permute-start.10 = (f32[8,448]{1,0:T(8,128)S(1)}, f32[8,448]{1,0:T(8,128)S(1)}, u32[]{:S(2)}, u32[]{:S(2)}) collective-permute-start(f32[8,448]{1,0:T(8,128)S(1)} %get-tuple-element.13), channel_id=1, source_target_pairs={{0,2},{1,3},{2,0},{3,1},{4,6},{5,7},{6,4},{7,5},{8,10},{9,11},{10,... | collective-permute-start | bytes 43016 | tf_op jit(solution)/shard_map/ppermute | solution.py:145
  41.3 4.0 %collective-permute-start.9 = (f32[8,448]{1,0:T(8,128)S(1)}, f32[8,448]{1,0:T(8,128)S(1)}, u32[]{:S(2)}, u32[]{:S(2)}) collective-permute-start(f32[8,448]{1,0:T(8,128)S(1)} %get-tuple-element.12), channel_id=1, source_target_pairs={{0,3},{1,2},{2,1},{3,0},{4,7},{5,6},{6,5},{7,4},{8,11},{9,10},{10,... | collective-permute-start | bytes 43016 | tf_op jit(solution)/shard_map/ppermute | solution.py:145
  43.6 1.7 %collective-permute-start.11 = (f32[8,448]{1,0:T(8,128)S(1)}, f32[8,448]{1,0:T(8,128)S(1)}, u32[]{:S(2)}, u32[]{:S(2)}) collective-permute-start(f32[8,448]{1,0:T(8,128)S(1)} %select_select_fusion), channel_id=1, source_target_pairs={{0,1},{1,0},{2,3},{3,2},{4,5},{5,4},{6,7},{7,6},{8,9},{9,8},{10,11... | collective-permute-start | bytes 43016 | tf_op jit(solution)/shard_map/ppermute | solution.py:145

commit v14 on v13

--- a/solution.py
+++ b/solution.py
@@ -69,9 +69,9 @@
     weighted = jnp.einsum(
         "sqk,skl->sql",
         expo_f.astype(jnp.bfloat16),
-        kv_cache[:, :, :latent_width],
+        kv_cache,
         preferred_element_type=jnp.float32,
-    )
+    )[:, :, :latent_width]
     stats = jnp.stack([block_top, block_total]).reshape(-1, slice_width)
     sum_slices = [
         weighted[:, :, j * slice_width:(j + 1) * slice_width].reshape(-1, slice_width)

time: 46.5 us -> 59.5 us (1.28)
  the two profiles are of different devices: /device:TPU:1 before, /device:TPU:0 now
where the time goes in v14:
time: 59.5 us; the launch traced here: 59 us
  starting transfers between devices  16.9 us (28%)
  local copies, waits for them, and re-layouts  15.2 us (26%)
  matrix products  14.2 us (24%)
  waiting for transfers between devices  10.3 us (17%)
  other arithmetic  2.24 us (4%)
    broadcast_in_dim x11, local copies, waits for them, and re-layouts, per_device(): q_slots = jnp.where(source == k, received[k][:, :, None, :], q_slots)  12 us
    dot_general x1, matrix products, per_device(): jnp.dot(values.reshape(row_count, -1), w_output, preferred_element_type=j...  7.17 us
    ppermute x3, starting transfers between devices, per_device(): lax.ppermute(q_part, 'ctx', shift_pairs(n_ctx, k))  6.97 us
    ppermute x3, waiting for transfers between devices, per_device(): lax.ppermute(packed_for((me_ctx + k) % n_ctx), 'ctx', shift_pairs(n_ctx, k))  4.26 us
    ppermute x3, starting transfers between devices, per_device(): lax.ppermute(packed_for((me_ctx + k) % n_ctx), 'ctx', shift_pairs(n_ctx, k))  3.88 us
    ppermute x3, starting transfers between devices, per_device(): lax.ppermute(sent, 'ctx', shift_pairs(n_ctx, k)).astype(jnp.float32)  3.85 us
    ppermute x3, waiting for transfers between devices, per_device(): lax.ppermute(sent, 'ctx', shift_pairs(n_ctx, k)).astype(jnp.float32)  3.64 us
    ppermute x3, local copies, waits for them, and re-layouts, per_device(): lax.ppermute(q_part, 'ctx', shift_pairs(n_ctx, k))  2.55 us
  transfers between devices with their start and end apart: 12, of which 6 were waited for; matrix products, arithmetic and copies ran while one was open for 24% of the time, Pallas kernels for 0%

profile of v14, /device:TPU:0, one launch (start us, length us, event | category | flops | bytes accessed | tf_op | source)
XLA Modules:
  0.0 59.0 jit_solution(12996496446909956205)
XLA Ops:
  0.0 1.7 %fusion.11 = bf16[8,32,128]{2,0,1:T(8,128)(2,1)S(1)} fusion(bf16[32,128,128]{2,1,0:T(8,128)(2,1)} %param.11, bf16[8,32,128]{2,1,0:T(8,128)(2,1)} %param.7), kind=kOutput, calls=%fused_computation.7 | convolution fusion | flops 8421376 | bytes 1179648 | tf_op jit(solution)/shard_map/rhn,hnl->rhl/dot_general | solution.py:33
  1.7 3.0 %collective-permute-start = (bf16[8,32,128]{2,0,1:T(8,128)(2,1)S(1)}, bf16[8,32,128]{2,0,1:T(8,128)(2,1)}, u32[]{:S(2)}, u32[]{:S(2)}) collective-permute-start(bf16[8,32,128]{2,0,1:T(8,128)(2,1)S(1)} %fusion.11), channel_id=1, source_target_pairs={{0,4},{4,8},{8,12},{12,0},{1,5},{5,9},{9,13},{13,1},{2,6},{6,10},{... | collective-permute-start | bytes 196616 | tf_op jit(solution)/shard_map/ppermute | solution.py:38
  4.7 2.6 %collective-permute-start.1 = (bf16[8,32,128]{2,0,1:T(8,128)(2,1)S(1)}, bf16[8,32,128]{2,0,1:T(8,128)(2,1)}, u32[]{:S(2)}, u32[]{:S(2)}) collective-permute-start(bf16[8,32,128]{2,0,1:T(8,128)(2,1)S(1)} %fusion.11), channel_id=1, source_target_pairs={{0,8},{4,12},{8,0},{12,4},{1,9},{5,13},{9,1},{13,5},{2,10},{6,14},... | collective-permute-start | bytes 196616 | tf_op jit(solution)/shard_map/ppermute | solution.py:38
  7.3 1.3 %collective-permute-start.2 = (bf16[8,32,128]{2,0,1:T(8,128)(2,1)S(1)}, bf16[8,32,128]{2,0,1:T(8,128)(2,1)}, u32[]{:S(2)}, u32[]{:S(2)}) collective-permute-start(bf16[8,32,128]{2,0,1:T(8,128)(2,1)S(1)} %fusion.11), channel_id=1, source_target_pairs={{0,12},{4,0},{8,4},{12,8},{1,13},{5,1},{9,5},{13,9},{2,14},{6,2},{... | collective-permute-start | bytes 196616 | tf_op jit(solution)/shard_map/ppermute | solution.py:38
  8.8 0.6 broadcast_bitcast_fusion
  9.4 0.6 %broadcast_bitcast_fusion.1 = pred[512]{0:T(512)(128)(4,1)} fusion(pred[4]{0:T(512)(128)(4,1)S(1)} %get-tuple-element.31), kind=kLoop, calls=%fused_computation.84 | loop fusion | bytes 516 | tf_op jit(solution)/shard_map/jit(_where)/broadcast_in_dim | solution.py:43
  10.0 0.6 %broadcast_bitcast_fusion.2 = pred[512]{0:T(512)(128)(4,1)} fusion(pred[4]{0:T(512)(128)(4,1)S(1)} %broadcast_compare_fusion.2), kind=kLoop, calls=%fused_computation.85 | loop fusion | bytes 516 | tf_op jit(solution)/shard_map/jit(_where)/broadcast_in_dim | solution.py:43
  10.7 0.8 %broadcast_in_dim.95 = bf16[8,32,4,128]{3,2,1,0:T(4,128)(2,1)} broadcast(bf16[8,32,128]{2,1,0:T(8,128)(2,1)S(1)} %copy.9), dimensions={0,1,3} | broadcast | bytes 327680 | tf_op jit(solution)/shard_map/jit(_where)/broadcast_in_dim | solution.py:43
  11.5 1.7 %broadcast_in_dim.96 = bf16[4,64,512]{2,1,0:T(8,128)(2,1)} reshape(bf16[8,32,4,128]{3,2,1,0:T(4,128)(2,1)} %broadcast_in_dim.95) | data formatting | bytes 524288 | tf_op jit(solution)/shard_map/jit(_where)/broadcast_in_dim | solution.py:43
  13.2 0.7 %broadcast_add_fusion.1 = s32[4]{0:T(128)S(1)} fusion(s32[4]{0:T(128)} %param.10), kind=kLoop, calls=%fused_computation.90 | loop fusion | flops 4 | bytes 32 | tf_op jit(solution)/shard_map/sub | solution.py:63
  13.9 2.0 %fusion.18 = f32[4,64,512]{2,1,0:T(8,128)} fusion(bf16[4,64,64]{2,1,0:T(8,128)(2,1)} %bitcast.38, bf16[4,512,576]{1,2,0:T(8,128)(2,1)} %param.9), kind=kOutput, calls=%fused_computation.14 | convolution fusion | flops 16777216 | bytes 851968 | tf_op jit(solution)/shard_map/sqc,skc->sqk/dot_general | solution.py:54
  15.9 0.9 %copy.10 = bf16[8,32,128]{2,1,0:T(8,128)(2,1)S(1)} copy(bf16[8,32,128]{2,0,1:T(8,128)(2,1)} %collective-permute-done) | data formatting | bytes 131072 | tf_op jit(solution)/shard_map/ppermute | solution.py:38
  16.8 0.8 %broadcast_in_dim.100 = bf16[8,32,4,128]{3,2,1,0:T(4,128)(2,1)} broadcast(bf16[8,32,128]{2,1,0:T(8,128)(2,1)S(1)} %copy.10), dimensions={0,1,3} | broadcast | bytes 327680 | tf_op jit(solution)/shard_map/jit(_where)/broadcast_in_dim | solution.py:43
  17.6 1.8 %broadcast_in_dim.101 = bf16[4,64,512]{2,1,0:T(8,128)(2,1)} reshape(bf16[8,32,4,128]{3,2,1,0:T(4,128)(2,1)} %broadcast_in_dim.100) | data formatting | bytes 524288 | tf_op jit(solution)/shard_map/jit(_where)/broadcast_in_dim | solution.py:43
  19.3 0.9 %copy.11 = bf16[8,32,128]{2,1,0:T(8,128)(2,1)S(1)} copy(bf16[8,32,128]{2,0,1:T(8,128)(2,1)} %collective-permute-done.1) | data formatting | bytes 131072 | tf_op jit(solution)/shard_map/ppermute | solution.py:38
  20.2 0.8 %broadcast_in_dim.105 = bf16[8,32,4,128]{3,2,1,0:T(4,128)(2,1)} broadcast(bf16[8,32,128]{2,1,0:T(8,128)(2,1)S(1)} %copy.11), dimensions={0,1,3} | broadcast | bytes 327680 | tf_op jit(solution)/shard_map/jit(_where)/broadcast_in_dim | solution.py:43
  21.0 1.7 %broadcast_in_dim.106 = bf16[4,64,512]{2,1,0:T(8,128)(2,1)} reshape(bf16[8,32,4,128]{3,2,1,0:T(4,128)(2,1)} %broadcast_in_dim.105) | data formatting | bytes 524288 | tf_op jit(solution)/shard_map/jit(_where)/broadcast_in_dim | solution.py:43
  22.7 0.9 %copy.12 = bf16[8,32,128]{2,1,0:T(8,128)(2,1)S(1)} copy(bf16[8,32,128]{2,0,1:T(8,128)(2,1)} %collective-permute-done.2) | data formatting | bytes 131072 | tf_op jit(solution)/shard_map/ppermute | solution.py:38
  23.6 0.8 %broadcast_in_dim.107 = bf16[8,32,4,128]{3,2,1,0:T(4,128)(2,1)} broadcast(bf16[8,32,128]{2,1,0:T(8,128)(2,1)S(1)} %copy.12), dimensions={0,1,3} | broadcast | bytes 327680 | tf_op jit(solution)/shard_map/jit(_where)/broadcast_in_dim | solution.py:43
  24.3 1.7 %broadcast_in_dim.108 = bf16[4,64,512]{2,1,0:T(8,128)(2,1)} reshape(bf16[8,32,4,128]{3,2,1,0:T(4,128)(2,1)} %broadcast_in_dim.107) | data formatting | bytes 524288 | tf_op jit(solution)/shard_map/jit(_where)/broadcast_in_dim | solution.py:43
  26.1 2.1 %fusion.44 = (f32[4,64]{1,0:T(4,128)S(1)}, f32[4,64,512]{2,1,0:T(8,128)S(1)}) fusion(f32[4,64,512]{2,1,0:T(8,128)} %fusion.18, bf16[4,512,576]{1,2,0:T(8,128)(2,1)S(1)} %copy-done.1, bf16[4,64,512]{2,1,0:T(8,128)(2,1)} %broadcast_in_dim.96, bf16[4,64,512]{2,1,0:T(8,128)(2,1)} %broadcast_in_dim.101, bf16[4,64,512]{2,1,0:T(8,128)(2,1)} %broadcast_in_dim.106, ...), kind=kOutput, calls=%fused_computation.95 | convolution fusion | flops 135266048 | bytes 4200960 | tf_op jit(solution)/shard_map/sqc,skc->sqk/dot_general | solution.py:48
  28.2 0.8 %fusion.14 = f32[4,64,576]{2,1,0:T(8,128)S(1)} fusion(bf16[4,512,576]{1,2,0:T(8,128)(2,1)S(1)} %copy-done.2, f32[4,64,512]{2,1,0:T(8,128)S(1)} %get-tuple-element.27, f32[4,64]{1,0:T(4,128)S(1)} %get-tuple-element.26, s32[4,64]{1,0:T(4,128)S(1)} %broadcast_add_fusion, s32[512]{0:T(512)S(1)} %iota_add_fusion), kind=kOutput, calls=%fused_computation.11 | convolution fusion | flops 151519232 | bytes 3477504 | tf_op jit(solution)/shard_map/sqk,skl->sql/dot_general | solution.py:69
  29.1 0.2 fusion.12
  29.3 0.1 reshape.265
  29.5 0.7 %collective-permute-start.3 = (bf16[268,128]{1,0:T(8,128)(2,1)S(1)}, bf16[268,128]{1,0:T(8,128)(2,1)S(1)}, u32[]{:S(2)}, u32[]{:S(2)}) collective-permute-start(bf16[268,128]{1,0:T(8,128)(2,1)S(1)} %get-tuple-element.14), channel_id=1, source_target_pairs={{0,4},{4,8},{8,12},{12,0},{1,5},{5,9},{9,13},{13,1},{2,6},{6,10},{... | collective-permute-start | bytes 205832 | tf_op jit(solution)/shard_map/ppermute | solution.py:113
  30.2 0.3 collective-permute-start.4
  30.6 2.8 %collective-permute-start.5 = (bf16[268,128]{1,0:T(8,128)(2,1)S(1)}, bf16[268,128]{1,0:T(8,128)(2,1)S(1)}, u32[]{:S(2)}, u32[]{:S(2)}) collective-permute-start(bf16[268,128]{1,0:T(8,128)(2,1)S(1)} %get-tuple-element.16), channel_id=1, source_target_pairs={{0,12},{4,0},{8,4},{12,8},{1,13},{5,1},{9,5},{13,9},{2,14},{6,2},{... | collective-permute-start | bytes 205832 | tf_op jit(solution)/shard_map/ppermute | solution.py:113
  33.4 2.8 %collective-permute-done.3 = bf16[268,128]{1,0:T(8,128)(2,1)S(1)} collective-permute-done((bf16[268,128]{1,0:T(8,128)(2,1)S(1)}, bf16[268,128]{1,0:T(8,128)(2,1)S(1)}, u32[]{:S(2)}, u32[]{:S(2)}) %collective-permute-start.3) | collective-permute-done | bytes 68640 | tf_op jit(solution)/shard_map/ppermute | solution.py:113
  36.2 1.5 %collective-permute-done.4 = bf16[268,128]{1,0:T(8,128)(2,1)S(1)} collective-permute-done((bf16[268,128]{1,0:T(8,128)(2,1)S(1)}, bf16[268,128]{1,0:T(8,128)(2,1)S(1)}, u32[]{:S(2)}, u32[]{:S(2)}) %collective-permute-start.4) | collective-permute-done | bytes 68640 | tf_op jit(solution)/shard_map/ppermute | solution.py:113
  37.7 0.1 squeeze.21
  37.8 0.1 squeeze.22
  37.9 0.1 squeeze.23
  38.0 0.1 squeeze.24
  38.1 0.1 squeeze.25
  38.1 0.1 squeeze.26
  38.3 0.2 fusion.30
  38.5 0.4 fusion.45
  38.9 1.1 %collective-permute-start.6 = (bf16[8,32,128]{2,0,1:T(8,128)(2,1)S(1)}, bf16[8,32,128]{2,0,1:T(8,128)(2,1)S(1)}, u32[]{:S(2)}, u32[]{:S(2)}) collective-permute-start(bf16[8,32,128]{2,0,1:T(8,128)(2,1)S(1)} %get-tuple-element.28), channel_id=1, source_target_pairs={{0,4},{4,8},{8,12},{12,0},{1,5},{5,9},{9,13},{13,1},{2,6},{6,10},{... | collective-permute-start | bytes 196616 | tf_op jit(solution)/shard_map/ppermute | solution.py:127
  40.1 1.1 %collective-permute-start.7 = (bf16[8,32,128]{2,0,1:T(8,128)(2,1)S(1)}, bf16[8,32,128]{2,0,1:T(8,128)(2,1)S(1)}, u32[]{:S(2)}, u32[]{:S(2)}) collective-permute-start(bf16[8,32,128]{2,0,1:T(8,128)(2,1)S(1)} %get-tuple-element.28), channel_id=1, source_target_pairs={{0,8},{4,12},{8,0},{12,4},{1,9},{5,13},{9,1},{13,5},{2,10},{6,14},... | collective-permute-start | bytes 196616 | tf_op jit(solution)/shard_map/ppermute | solution.py:127
  41.1 1.6 %collective-permute-start.8 = (bf16[8,32,128]{2,0,1:T(8,128)(2,1)S(1)}, bf16[8,32,128]{2,0,1:T(8,128)(2,1)S(1)}, u32[]{:S(2)}, u32[]{:S(2)}) collective-permute-start(bf16[8,32,128]{2,0,1:T(8,128)(2,1)S(1)} %get-tuple-element.28), channel_id=1, source_target_pairs={{0,12},{4,0},{8,4},{12,8},{1,13},{5,1},{9,5},{13,9},{2,14},{6,2},{... | collective-permute-start | bytes 196616 | tf_op jit(solution)/shard_map/ppermute | solution.py:127
  42.8 2.3 %collective-permute-done.6 = bf16[8,32,128]{2,0,1:T(8,128)(2,1)S(1)} collective-permute-done((bf16[8,32,128]{2,0,1:T(8,128)(2,1)S(1)}, bf16[8,32,128]{2,0,1:T(8,128)(2,1)S(1)}, u32[]{:S(2)}, u32[]{:S(2)}) %collective-permute-start.6) | collective-permute-done | bytes 65568 | tf_op jit(solution)/shard_map/ppermute | solution.py:127
  45.1 1.3 %collective-permute-done.7 = bf16[8,32,128]{2,0,1:T(8,128)(2,1)S(1)} collective-permute-done((bf16[8,32,128]{2,0,1:T(8,128)(2,1)S(1)}, bf16[8,32,128]{2,0,1:T(8,128)(2,1)S(1)}, u32[]{:S(2)}, u32[]{:S(2)}) %collective-permute-start.7) | collective-permute-done | bytes 65568 | tf_op jit(solution)/shard_map/ppermute | solution.py:127
  46.4 7.2 %fusion.34 = f32[8,1792]{1,0:T(8,128)S(1)} fusion(bf16[4096,1792]{1,0:T(8,128)(2,1)} %param.13, bf16[8,32,128]{2,0,1:T(8,128)(2,1)S(1)} %collective-permute-done.8, bf16[8,32,128]{2,0,1:T(8,128)(2,1)S(1)} %collective-permute-done.7, f32[8,32,128]{2,0,1:T(8,128)S(1)} %get-tuple-element.29, bf16[8,32,128]{2,0,1:T(8,128)(2,1)S(1)} %collective-permute-done.6), kind=kOutput, calls=%fused_computation.46 | convolution fusion | flops 117669888 | bytes 15065088 | tf_op jit(solution)/shard_map/dot_general | solution.py:133
  53.7 1.5 %collective-permute-start.10 = (f32[8,448]{1,0:T(8,128)S(1)}, f32[8,448]{1,0:T(8,128)S(1)}, u32[]{:S(2)}, u32[]{:S(2)}) collective-permute-start(f32[8,448]{1,0:T(8,128)S(1)} %get-tuple-element.13), channel_id=1, source_target_pairs={{0,2},{1,3},{2,0},{3,1},{4,6},{5,7},{6,4},{7,5},{8,10},{9,11},{10,... | collective-permute-start | bytes 43016 | tf_op jit(solution)/shard_map/ppermute | solution.py:145
  55.2 0.7 %collective-permute-start.11 = (f32[8,448]{1,0:T(8,128)S(1)}, f32[8,448]{1,0:T(8,128)S(1)}, u32[]{:S(2)}, u32[]{:S(2)}) collective-permute-start(f32[8,448]{1,0:T(8,128)S(1)} %select_select_fusion), channel_id=1, source_target_pairs={{0,1},{1,0},{2,3},{3,2},{4,5},{5,4},{6,7},{7,6},{8,9},{9,8},{10,11... | collective-permute-start | bytes 43016 | tf_op jit(solution)/shard_map/ppermute | solution.py:145
  55.9 1.5 %collective-permute-done.10 = f32[8,448]{1,0:T(8,128)S(1)} collective-permute-done((f32[8,448]{1,0:T(8,128)S(1)}, f32[8,448]{1,0:T(8,128)S(1)}, u32[]{:S(2)}, u32[]{:S(2)}) %collective-permute-start.10) | collective-permute-done | bytes 14368 | tf_op jit(solution)/shard_map/ppermute | solution.py:145
  57.4 0.9 %collective-permute-done.9 = f32[8,448]{1,0:T(8,128)S(1)} collective-permute-done((f32[8,448]{1,0:T(8,128)S(1)}, f32[8,448]{1,0:T(8,128)S(1)}, u32[]{:S(2)}, u32[]{:S(2)}) %collective-permute-start.9) | collective-permute-done | bytes 14368 | tf_op jit(solution)/shard_map/ppermute | solution.py:145
  58.3 0.7 %add_add_fusion = f32[8,448]{1,0:T(8,128)} fusion(f32[8,448]{1,0:T(8,128)S(1)} %collective-permute-done.11, f32[8,448]{1,0:T(8,128)S(1)} %collective-permute-done.10, f32[8,448]{1,0:T(8,128)S(1)} %collective-permute-done.9, f32[8,1792]{1,0:T(8,128)S(1)} %fusion.34, pred[]{:T(512)S(6)} %eq.119, pred[]{:T(512)S(6)} %eq.118, pred[]{:T(512)S(6)} %eq.102), kind=kLoop, calls=%fused_computation.50 | loop fusion | flops 21504 | bytes 114691 | tf_op jit(solution)/shard_map/add | solution.py:145
  (45 shorter events, 0.5 us)
Async XLA Ops:
  0.0 38.5 %copy-start = (bf16[32,128,128]{2,1,0:T(8,128)(2,1)S(1)}, bf16[32,128,128]{2,1,0:T(8,128)(2,1)}, u32[]{:S(2)}) copy-start(bf16[32,128,128]{2,1,0:T(8,128)(2,1)} %param.12) | copy-start | bytes 3145732
  1.7 14.2 %collective-permute-start = (bf16[8,32,128]{2,0,1:T(8,128)(2,1)S(1)}, bf16[8,32,128]{2,0,1:T(8,128)(2,1)}, u32[]{:S(2)}, u32[]{:S(2)}) collective-permute-start(bf16[8,32,128]{2,0,1:T(8,128)(2,1)S(1)} %fusion.11), channel_id=1, source_target_pairs={{0,4},{4,8},{8,12},{12,0},{1,5},{5,9},{9,13},{13,1},{2,6},{6,10},{... | collective-permute-start | bytes 196616 | tf_op jit(solution)/shard_map/ppermute | solution.py:38
  4.7 14.6 %collective-permute-start.1 = (bf16[8,32,128]{2,0,1:T(8,128)(2,1)S(1)}, bf16[8,32,128]{2,0,1:T(8,128)(2,1)}, u32[]{:S(2)}, u32[]{:S(2)}) collective-permute-start(bf16[8,32,128]{2,0,1:T(8,128)(2,1)S(1)} %fusion.11), channel_id=1, source_target_pairs={{0,8},{4,12},{8,0},{12,4},{1,9},{5,13},{9,1},{13,5},{2,10},{6,14},... | collective-permute-start | bytes 196616 | tf_op jit(solution)/shard_map/ppermute | solution.py:38
  7.3 15.4 %collective-permute-start.2 = (bf16[8,32,128]{2,0,1:T(8,128)(2,1)S(1)}, bf16[8,32,128]{2,0,1:T(8,128)(2,1)}, u32[]{:S(2)}, u32[]{:S(2)}) collective-permute-start(bf16[8,32,128]{2,0,1:T(8,128)(2,1)S(1)} %fusion.11), channel_id=1, source_target_pairs={{0,12},{4,0},{8,4},{12,8},{1,13},{5,1},{9,5},{13,9},{2,14},{6,2},{... | collective-permute-start | bytes 196616 | tf_op jit(solution)/shard_map/ppermute | solution.py:38
  8.7 17.3 %copy-start.1 = (bf16[4,512,576]{1,2,0:T(8,128)(2,1)S(1)}, bf16[4,512,576]{1,2,0:T(8,128)(2,1)}, u32[]{:S(2)}) copy-start(bf16[4,512,576]{1,2,0:T(8,128)(2,1)} %param.9) | copy-start | bytes 7077892
  9.4 16.7 %copy-start.3 = (pred[512]{0:T(512)(128)(4,1)S(1)}, pred[512]{0:T(512)(128)(4,1)}, u32[]{:S(2)}) copy-start(pred[512]{0:T(512)(128)(4,1)} %broadcast_bitcast_fusion) | copy-start | bytes 1540
  10.0 16.1 %copy-start.4 = (pred[512]{0:T(512)(128)(4,1)S(1)}, pred[512]{0:T(512)(128)(4,1)}, u32[]{:S(2)}) copy-start(pred[512]{0:T(512)(128)(4,1)} %broadcast_bitcast_fusion.1) | copy-start | bytes 1540
  10.7 15.4 %copy-start.5 = (pred[512]{0:T(512)(128)(4,1)S(1)}, pred[512]{0:T(512)(128)(4,1)}, u32[]{:S(2)}) copy-start(pred[512]{0:T(512)(128)(4,1)} %broadcast_bitcast_fusion.2) | copy-start | bytes 1540
  26.1 2.1 %copy-start.2 = (bf16[4,512,576]{1,2,0:T(8,128)(2,1)S(1)}, bf16[4,512,576]{1,2,0:T(8,128)(2,1)}, u32[]{:S(2)}) copy-start(bf16[4,512,576]{1,2,0:T(8,128)(2,1)} %param.9) | copy-start | bytes 7077892
  29.5 6.7 %collective-permute-start.3 = (bf16[268,128]{1,0:T(8,128)(2,1)S(1)}, bf16[268,128]{1,0:T(8,128)(2,1)S(1)}, u32[]{:S(2)}, u32[]{:S(2)}) collective-permute-start(bf16[268,128]{1,0:T(8,128)(2,1)S(1)} %get-tuple-element.14), channel_id=1, source_target_pairs={{0,4},{4,8},{8,12},{12,0},{1,5},{5,9},{9,13},{13,1},{2,6},{6,10},{... | collective-permute-start | bytes 205832 | tf_op jit(solution)/shard_map/ppermute | solution.py:113
  30.2 7.4 %collective-permute-start.4 = (bf16[268,128]{1,0:T(8,128)(2,1)S(1)}, bf16[268,128]{1,0:T(8,128)(2,1)S(1)}, u32[]{:S(2)}, u32[]{:S(2)}) collective-permute-start(bf16[268,128]{1,0:T(8,128)(2,1)S(1)} %get-tuple-element.15), channel_id=1, source_target_pairs={{0,8},{4,12},{8,0},{12,4},{1,9},{5,13},{9,1},{13,5},{2,10},{6,14},... | collective-permute-start | bytes 205832 | tf_op jit(solution)/shard_map/ppermute | solution.py:113
  30.6 7.3 %collective-permute-start.5 = (bf16[268,128]{1,0:T(8,128)(2,1)S(1)}, bf16[268,128]{1,0:T(8,128)(2,1)S(1)}, u32[]{:S(2)}, u32[]{:S(2)}) collective-permute-start(bf16[268,128]{1,0:T(8,128)(2,1)S(1)} %get-tuple-element.16), channel_id=1, source_target_pairs={{0,12},{4,0},{8,4},{12,8},{1,13},{5,1},{9,5},{13,9},{2,14},{6,2},{... | collective-permute-start | bytes 205832 | tf_op jit(solution)/shard_map/ppermute | solution.py:113
  38.9 6.2 %collective-permute-start.6 = (bf16[8,32,128]{2,0,1:T(8,128)(2,1)S(1)}, bf16[8,32,128]{2,0,1:T(8,128)(2,1)S(1)}, u32[]{:S(2)}, u32[]{:S(2)}) collective-permute-start(bf16[8,32,128]{2,0,1:T(8,128)(2,1)S(1)} %get-tuple-element.28), channel_id=1, source_target_pairs={{0,4},{4,8},{8,12},{12,0},{1,5},{5,9},{9,13},{13,1},{2,6},{6,10},{... | collective-permute-start | bytes 196616 | tf_op jit(solution)/shard_map/ppermute | solution.py:127
  40.1 6.3 %collective-permute-start.7 = (bf16[8,32,128]{2,0,1:T(8,128)(2,1)S(1)}, bf16[8,32,128]{2,0,1:T(8,128)(2,1)S(1)}, u32[]{:S(2)}, u32[]{:S(2)}) collective-permute-start(bf16[8,32,128]{2,0,1:T(8,128)(2,1)S(1)} %get-tuple-element.28), channel_id=1, source_target_pairs={{0,8},{4,12},{8,0},{12,4},{1,9},{5,13},{9,1},{13,5},{2,10},{6,14},... | collective-permute-start | bytes 196616 | tf_op jit(solution)/shard_map/ppermute | solution.py:127
  41.1 5.3 %collective-permute-start.8 = (bf16[8,32,128]{2,0,1:T(8,128)(2,1)S(1)}, bf16[8,32,128]{2,0,1:T(8,128)(2,1)S(1)}, u32[]{:S(2)}, u32[]{:S(2)}) collective-permute-start(bf16[8,32,128]{2,0,1:T(8,128)(2,1)S(1)} %get-tuple-element.28), channel_id=1, source_target_pairs={{0,12},{4,0},{8,4},{12,8},{1,13},{5,1},{9,5},{13,9},{2,14},{6,2},{... | collective-permute-start | bytes 196616 | tf_op jit(solution)/shard_map/ppermute | solution.py:127
  53.7 3.8 %collective-permute-start.10 = (f32[8,448]{1,0:T(8,128)S(1)}, f32[8,448]{1,0:T(8,128)S(1)}, u32[]{:S(2)}, u32[]{:S(2)}) collective-permute-start(f32[8,448]{1,0:T(8,128)S(1)} %get-tuple-element.13), channel_id=1, source_target_pairs={{0,2},{1,3},{2,0},{3,1},{4,6},{5,7},{6,4},{7,5},{8,10},{9,11},{10,... | collective-permute-start | bytes 43016 | tf_op jit(solution)/shard_map/ppermute | solution.py:145
  55.2 3.2 %collective-permute-start.9 = (f32[8,448]{1,0:T(8,128)S(1)}, f32[8,448]{1,0:T(8,128)S(1)}, u32[]{:S(2)}, u32[]{:S(2)}) collective-permute-start(f32[8,448]{1,0:T(8,128)S(1)} %get-tuple-element.12), channel_id=1, source_target_pairs={{0,3},{1,2},{2,1},{3,0},{4,7},{5,6},{6,5},{7,4},{8,11},{9,10},{10,... | collective-permute-start | bytes 43016 | tf_op jit(solution)/shard_map/ppermute | solution.py:145
  55.2 3.1 %collective-permute-start.11 = (f32[8,448]{1,0:T(8,128)S(1)}, f32[8,448]{1,0:T(8,128)S(1)}, u32[]{:S(2)}, u32[]{:S(2)}) collective-permute-start(f32[8,448]{1,0:T(8,128)S(1)} %select_select_fusion), channel_id=1, source_target_pairs={{0,1},{1,0},{2,3},{3,2},{4,5},{5,4},{6,7},{7,6},{8,9},{9,8},{10,11... | collective-permute-start | bytes 43016 | tf_op jit(solution)/shard_map/ppermute | solution.py:145
